TPU v7x, 256 devices: a whole 4x4x8 slice. The times are simulated.
256 devices in a mesh: dom: 64 (over z, x, core), sub: 4 (over y).
Axes of the slice: x: 4, y: 4, z: 8, core: 2. Of those that a mesh axis runs over, the one named last changes fastest.
Arguments:
- excitation: bfloat16 [64, 1536, 64], P('dom', 'sub'), may hold values from -6 to 6
- local_inverse: bfloat16 [64, 1536, 1536], P('dom', 'sub'), as said below
- aggregation: bfloat16 [64, 1024, 1536], P('dom', None, 'sub'), may hold values from -0.15625 to 0.15625
- disaggregation: bfloat16 [64, 1536, 1024], P('dom', 'sub'), may hold values from -0.1875 to 0.1875
- translation: float32 [64, 6, 2, 512], P('dom'), may hold values from -1.5 to 1.5
- partners: int32 [64, 6], P('dom'), may hold values from 0 to 63, as said below
- list_counts: int32 [64], P('dom'), may hold values from 2 to 6
- sweep_order: int32 [64], replicated, may hold values from 0 to 63, as said below
Outputs:
- currents: float32 [64, 1536, 64], P('dom', 'sub')
Inputs may be any that keep to these rules, and one draw needn't show every extreme that they name: `partners`: row d names 6 different subdomains, none equal to d; only its first list_counts[d] slots are used. `local_inverse`: each subdomain's matrix is the identity plus independent entries of spread 0.6 / sqrt(1536). `sweep_order`: every subdomain has a position of its own.
All inputs are finite; a program needn't handle non-finite values.
Results may differ from a plain program's by a relative error of at most 0.03.
Values may be sent and summed in bfloat16 or wider, within the bound.
No kernel may reach another device: no remote copies, remote signals or barrier semaphores. Data moves between devices by JAX's collectives and lax.ppermute only.
A program may use at most 64 MiB of HBM per device.

v0:
```python
import jax
import jax.numpy as jnp
from jax import lax
from jax.sharding import PartitionSpec as P

SEGMENTS = 8


CONTRACT_FIRST = (((0,), (1,)), ((), ()))
CONTRACT_LAST = (((1,), (1,)), ((), ()))


def rotate(real_weight, imag_weight, pattern):
    samples = real_weight.shape[-1]
    values = pattern.astype(jnp.float32)
    real_part = values[..., :samples]
    imag_part = values[..., samples:]
    return jnp.concatenate(
        [
            real_weight * real_part - imag_weight * imag_part,
            real_weight * imag_part + imag_weight * real_part,
        ],
        axis=-1,
    )


def local(
    excitation,
    local_inverse,
    aggregation,
    disaggregation,
    translation,
    partners,
    list_counts,
    sweep_order,
):
    excite_rows = excitation[0]
    inverse_rows = local_inverse[0]
    agg_columns = aggregation[0]
    disagg_rows = disaggregation[0]
    trans_rows = translation[0]
    partner_row = partners[0]

    def apply_inverse(shard_rows):
        return jnp.dot(inverse_rows, shard_rows, preferred_element_type=jnp.float32)

    solved = apply_inverse(lax.all_gather(excite_rows, "sub", axis=0, tiled=True))
    solved_half = solved.astype(jnp.bfloat16)
    incident = lax.psum_scatter(
        lax.dot_general(
            solved_half, agg_columns, CONTRACT_FIRST, preferred_element_type=jnp.float32
        ).astype(jnp.bfloat16),
        "sub",
        scatter_dimension=0,
        tiled=True,
    ).astype(jnp.float32)
    spread = apply_inverse(lax.all_gather(disagg_rows, "sub", axis=0, tiled=True))
    spread_half = spread.astype(jnp.bfloat16)
    partial_map = lax.dot_general(
        spread_half, agg_columns, CONTRACT_FIRST, preferred_element_type=jnp.float32
    )
    coupling = lax.psum(partial_map.astype(jnp.bfloat16), "sub")
    domains = sweep_order.shape[0]
    segment_of = sweep_order * SEGMENTS // domains
    own_index = lax.axis_index("dom")
    my_segment = segment_of[own_index]
    slot_live = jnp.arange(partner_row.shape[0], dtype=jnp.int32) < list_counts[0]
    domain_ids = jnp.arange(domains, dtype=jnp.int32)
    incoming = jnp.zeros(incident.shape, jnp.float32)
    for segment_k in range(SEGMENTS - 1):
        pattern = (
            incident
            - jnp.dot(incoming.astype(jnp.bfloat16), coupling, preferred_element_type=jnp.float32)
        ).astype(jnp.bfloat16)
        pattern = jnp.where(my_segment == segment_k, pattern, jnp.zeros_like(pattern))
        make_piece = lax.all_gather(pattern[None], "dom", axis=0, tiled=True)
        count = make_piece.shape[0]
        make_senders = jnp.arange(count, dtype=jnp.int32)
        sender_segment = jnp.sum(
            jnp.where(domain_ids[None, :] == make_senders[:, None], segment_of[None, :], 0), axis=1
        )
        sender_live = sender_segment == segment_k
        match = (
            (partner_row[:, None] == make_senders[None, :])
            & slot_live[:, None]
            & sender_live[None, :]
            & (segment_k < my_segment)
        )
        weights = jnp.sum(
            jnp.where(match[:, :, None, None], trans_rows[:, None, :, :], 0.0), axis=0
        )
        terms = rotate(weights[:, 0][:, None, :], weights[:, 1][:, None, :], make_piece)
        incoming = incoming + jnp.sum(terms, axis=0)
    fields = lax.all_gather(incoming.astype(jnp.bfloat16), "sub", axis=0, tiled=True)
    currents = solved - lax.dot_general(
        spread_half, fields, CONTRACT_LAST, preferred_element_type=jnp.float32
    )
    return currents[None]


def solution(mesh):
    in_specs = (
        P("dom", "sub", None),
        P("dom", "sub", None),
        P("dom", None, "sub"),
        P("dom", "sub", None),
        P("dom", None, None, None),
        P("dom", None),
        P("dom"),
        P(),
    )
    out_specs = P("dom", "sub", None)
    return jax.shard_map(local, mesh=mesh, in_specs=in_specs, out_specs=out_specs, check_vma=False)
```

profile of v0, /device:TPU:32, one launch (start us, length us, event | category | flops | bytes accessed | tf_op | source)
XLA Modules:
  0.0 726.2 jit_solution(1331858626277878469)
XLA Ops:
  6.5 0.7 all-gather.18.cloned.1.call-update
  7.3 12.9 %all-gather = bf16[1,1536,64]{1,2,0:T(8,128)(2,1)S(1)} all-gather(bf16[1,384,64]{1,2,0:T(8,128)(2,1)} %param.8), channel_id=2, replica_groups=mesh['dom'=64,'sub'=4] {'sub'}, dimensions={1}, use_global_device_ids=true | all-gather | bytes 245760 | tf_op jit(solution)/shard_map/all_gather | solution.py:47
  20.8 0.6 copy-done.4
  21.4 1.0 convolution_convert_fusion.1
  22.5 31.4 %all-gather.18.cloned.1.call-done = bf16[1,1536,1024]{2,1,0:T(8,128)(2,1)} async-done(((bf16[1,384,1024]{2,1,0:T(8,128)(2,1)}), bf16[1,1536,1024]{2,1,0:T(8,128)(2,1)}) %all-gather.18.cloned.1.call-update) | async-done | bytes 3145744 | tf_op jit(solution)/shard_map/all_gather | solution.py:57
  53.9 3.3 fusion.2
  57.2 0.9 copy-done.6
  58.1 2.6 convolution_convert_fusion
  60.9 0.7 dynamic_slice.3
  62.2 17.4 %reduce-scatter.2.cloned.1.call-done = bf16[16,1024]{1,0:T(8,128)(2,1)} async-done(((bf16[64,1024]{1,0:T(8,128)(2,1)}), bf16[16,1024]{1,0:T(8,128)(2,1)}) %reduce-scatter.2.cloned.1.call-update) | async-done | bytes 32784 | tf_op jit(solution)/shard_map/reduce_scatter | solution.py:49
  79.6 66.1 %all-reduce.2.cloned.1.call-done = bf16[1024,1024]{1,0:T(8,128)(2,1)} async-done(((bf16[1024,1024]{1,0:T(8,128)(2,1)}), bf16[1024,1024]{1,0:T(8,128)(2,1)}) %all-reduce.2.cloned.1.call-update) | async-done | bytes 2097168 | tf_op jit(solution)/shard_map/psum | solution.py:62
  145.7 2.6 fusion.10
  154.8 1.9 select_reduce_fusion
  156.7 67.9 %all-gather.20.cloned.1.call-done = bf16[1024,1024]{1,0:T(8,128)(2,1)} async-done(((bf16[16,1024]{1,0:T(8,128)(2,1)}), bf16[1024,1024]{1,0:T(8,128)(2,1)}) %all-gather.20.cloned.1.call-update) | async-done | bytes 2097168 | tf_op jit(solution)/shard_map/all_gather | solution.py:76
  224.6 2.1 convert
  226.7 0.8 multiply_subtract_fusion.6
  227.7 1.3 copy-done.2
  229.1 1.0 fusion.22
  230.8 1.7 slice_bitcast_fusion.11
  232.5 72.6 %all-gather.22.cloned.1.call-done = bf16[1024,1024]{1,0:T(8,128)(2,1)} async-done(((bf16[16,1024]{1,0:T(8,128)(2,1)}), bf16[1024,1024]{1,0:T(8,128)(2,1)}) %all-gather.22.cloned.1.call-update) | async-done | bytes 2097168 | tf_op jit(solution)/shard_map/all_gather | solution.py:76
  305.2 2.1 convert.1
  307.3 0.8 multiply_subtract_fusion.5
  308.4 0.6 copy-done.9
  309.0 1.0 fusion.21
  310.7 0.7 slice_bitcast_fusion.9
  311.5 73.6 %all-gather.24.cloned.1.call-done = bf16[1024,1024]{1,0:T(8,128)(2,1)} async-done(((bf16[16,1024]{1,0:T(8,128)(2,1)}), bf16[1024,1024]{1,0:T(8,128)(2,1)}) %all-gather.24.cloned.1.call-update) | async-done | bytes 2097168 | tf_op jit(solution)/shard_map/all_gather | solution.py:76
  385.1 2.1 convert.2
  387.2 0.8 multiply_subtract_fusion.4
  388.3 0.6 copy-done.10
  388.9 1.0 fusion.20
  390.7 0.7 slice_bitcast_fusion.7
  391.3 73.7 %all-gather.26.cloned.1.call-done = bf16[1024,1024]{1,0:T(8,128)(2,1)} async-done(((bf16[16,1024]{1,0:T(8,128)(2,1)}), bf16[1024,1024]{1,0:T(8,128)(2,1)}) %all-gather.26.cloned.1.call-update) | async-done | bytes 2097168 | tf_op jit(solution)/shard_map/all_gather | solution.py:76
  465.0 2.1 convert.3
  467.1 0.8 multiply_subtract_fusion.3
  468.2 1.0 fusion.19
  470.1 74.1 %all-gather.28.cloned.1.call-done = bf16[1024,1024]{1,0:T(8,128)(2,1)} async-done(((bf16[16,1024]{1,0:T(8,128)(2,1)}), bf16[1024,1024]{1,0:T(8,128)(2,1)}) %all-gather.28.cloned.1.call-update) | async-done | bytes 2097168 | tf_op jit(solution)/shard_map/all_gather | solution.py:76
  544.3 2.1 convert.4
  546.3 0.8 multiply_subtract_fusion.2
  547.4 1.0 fusion.18
  549.2 74.3 %all-gather.30.cloned.1.call-done = bf16[1024,1024]{1,0:T(8,128)(2,1)} async-done(((bf16[16,1024]{1,0:T(8,128)(2,1)}), bf16[1024,1024]{1,0:T(8,128)(2,1)}) %all-gather.30.cloned.1.call-update) | async-done | bytes 2097168 | tf_op jit(solution)/shard_map/all_gather | solution.py:76
  623.5 2.1 convert.5
  625.6 0.8 multiply_subtract_fusion.1
  626.6 1.0 fusion.17
  627.7 75.0 %all-gather.32.cloned.1.call-done = bf16[1024,1024]{1,0:T(8,128)(2,1)} async-done(((bf16[16,1024]{1,0:T(8,128)(2,1)}), bf16[1024,1024]{1,0:T(8,128)(2,1)}) %all-gather.32.cloned.1.call-update) | async-done | bytes 2097168 | tf_op jit(solution)/shard_map/all_gather | solution.py:76
  702.7 2.1 convert.6
  704.8 0.8 multiply_subtract_fusion
  705.9 12.5 %all_gather.39 = bf16[64,1024]{1,0:T(8,128)(2,1)S(1)} all-gather(bf16[16,1024]{1,0:T(8,128)(2,1)S(1)} %add_convert_fusion), channel_id=1, replica_groups=mesh['dom'=64,'sub'=4] {'sub'}, dimensions={0}, use_global_device_ids=true | all-gather | bytes 163840 | tf_op jit(solution)/shard_map/all_gather | solution.py:94
  718.3 1.0 fusion.8
  (75 shorter events, 3.2 us)
Async XLA Ops:
  6.5 13.7 %copy-start = (bf16[1,384,1536]{2,1,0:T(8,128)(2,1)S(1)}, bf16[1,384,1536]{2,1,0:T(8,128)(2,1)}, u32[]{:S(2)}) copy-start(bf16[1,384,1536]{2,1,0:T(8,128)(2,1)} %param.9) | copy-start | bytes 3538948
  6.5 14.9 %copy-start.8 = (bf16[1,1024,384]{2,1,0:T(8,128)(2,1)S(1)}, bf16[1,1024,384]{2,1,0:T(8,128)(2,1)}, u32[]{:S(2)}) copy-start(bf16[1,1024,384]{2,1,0:T(8,128)(2,1)} %param.10) | copy-start | bytes 2359300
  6.5 47.4 %all-gather.18.cloned.1.call-start = ((), (), s32[]{:S(2)}) async-start(), calls=%async_computation.3 | async-start | bytes 3932160 | tf_op jit(solution)/shard_map/all_gather | solution.py:57
  7.3 72.3 %reduce-scatter.2.cloned.1.call-start = ((), (), s32[]{:S(2)}) async-start(), calls=%async_computation.1 | async-start | bytes 163840 | tf_op jit(solution)/shard_map/reduce_scatter | solution.py:49
  20.8 0.6 copy-start.4
  22.5 123.3 %all-reduce.2.cloned.1.call-start = ((), (), s32[]{:S(2)}) async-start(), calls=%async_computation.2 | async-start | bytes 4194304 | tf_op jit(solution)/shard_map/psum | solution.py:62
  57.2 0.9 copy-start.6
  58.1 2.7 copy-start.18
  60.7 94.0 %copy-start.17 = (s32[1,6]{1,0:T(1,128)S(1)}, s32[1,6]{1,0:T(1,128)}, u32[]{:S(2)}) copy-start(s32[1,6]{1,0:T(1,128)} %param.13) | copy-start | bytes 76
  60.8 94.1 %copy-start.16 = (f32[1,6,2,512]{3,2,1,0:T(2,128)S(1)}, f32[1,6,2,512]{3,2,1,0:T(2,128)}, u32[]{:S(2)}) copy-start(f32[1,6,2,512]{3,2,1,0:T(2,128)} %param.12) | copy-start | bytes 73732
  60.8 163.8 %all-gather.20.cloned.1.call-start = ((), (), s32[]{:S(2)}) async-start(), calls=%async_computation.4 | async-start | bytes 2129920 | tf_op jit(solution)/shard_map/all_gather | solution.py:76
  148.4 156.8 %all-gather.22.cloned.1.call-start = ((), (), s32[]{:S(2)}) async-start(), calls=%async_computation.5 | async-start | bytes 2129920 | tf_op jit(solution)/shard_map/all_gather | solution.py:76
  227.5 1.6 copy-start.2
  227.5 1.6 copy-start.3
  230.1 155.0 %all-gather.24.cloned.1.call-start = ((), (), s32[]{:S(2)}) async-start(), calls=%async_computation.6 | async-start | bytes 2129920 | tf_op jit(solution)/shard_map/all_gather | solution.py:76
  305.2 2.1 copy-start.11
  305.2 2.1 copy-start.12
  308.4 0.6 copy-start.9
  310.0 155.0 %all-gather.26.cloned.1.call-start = ((), (), s32[]{:S(2)}) async-start(), calls=%async_computation.7 | async-start | bytes 2129920 | tf_op jit(solution)/shard_map/all_gather | solution.py:76
  385.1 2.1 copy-start.13
  385.1 2.1 copy-start.14
  388.1 0.8 copy-start.10
  389.9 154.3 %all-gather.28.cloned.1.call-start = ((), (), s32[]{:S(2)}) async-start(), calls=%async_computation.8 | async-start | bytes 2129920 | tf_op jit(solution)/shard_map/all_gather | solution.py:76
  465.0 2.1 copy-start.15
  469.2 154.3 %all-gather.30.cloned.1.call-start = ((), (), s32[]{:S(2)}) async-start(), calls=%async_computation.9 | async-start | bytes 2129920 | tf_op jit(solution)/shard_map/all_gather | solution.py:76
  548.4 154.3 %all-gather.32.cloned.1.call-start = ((), (), s32[]{:S(2)}) async-start(), calls=%async_computation.10 | async-start | bytes 2129920 | tf_op jit(solution)/shard_map/all_gather | solution.py:76
  705.6 13.8 %copy-start.1 = (bf16[1,384,1536]{2,1,0:T(8,128)(2,1)S(1)}, bf16[1,384,1536]{2,1,0:T(8,128)(2,1)}, u32[]{:S(2)}) copy-start(bf16[1,384,1536]{2,1,0:T(8,128)(2,1)} %param.9) | copy-start | bytes 3538948
  705.6 12.7 %copy-start.5 = (f32[384,64]{0,1:T(8,128)S(1)}, f32[384,64]{0,1:T(8,128)}, u32[]{:S(2)}) copy-start(f32[384,64]{0,1:T(8,128)} %copy-done.4) | copy-start | bytes 294916
  705.6 12.7 %copy-start.7 = (bf16[384,1024]{1,0:T(8,128)(2,1)S(1)}, bf16[384,1024]{1,0:T(8,128)(2,1)}, u32[]{:S(2)}) copy-start(bf16[384,1024]{1,0:T(8,128)(2,1)} %copy-done.6) | copy-start | bytes 2359300
Sparse Core Ops, SparseCore 0:
  9.2 44.7 all-gather.17
  56.4 23.1 reduce-scatter.1
  82.1 63.5 all-reduce.1
  148.5 76.0 all-gather.19
  230.2 74.9 all-gather.21
  310.1 74.9 all-gather.23
  390.0 74.9 all-gather.25
  469.3 74.9 all-gather.27
  548.5 74.9 all-gather.29
  627.8 74.9 all-gather.31
where the time goes:
time: 728 us; the launch traced here: 726 us
  waiting for transfers between devices  627 us (86%)
  blocking collectives  25.4 us (3%)
  between operations  24.3 us (3%)
  other arithmetic  23.9 us (3%)
  matrix products  17 us (2%)
  local copies, waits for them, and re-layouts  7.96 us (1%)
    all_gather x7, waiting for transfers between devices, local(): make_piece = lax.all_gather(pattern[None], 'dom', axis=0, tiled=True)  511 us
    psum x1, waiting for transfers between devices, local(): coupling = lax.psum(partial_map.astype(jnp.bfloat16), 'sub')  66.1 us
    all_gather x1, waiting for transfers between devices, local(): lax.all_gather(disagg_rows, 'sub', axis=0, tiled=True)  31.4 us
    reduce_scatter x1, waiting for transfers between devices, local(): lax.psum_scatter(lax.dot_general(solved_half, agg_columns, CONTRACT_FIRST...  17.4 us
    convert_element_type x7, other arithmetic, rotate(): values = pattern.astype(jnp.float32)  14.6 us
  transfers between devices with their start and end apart: 10, of which 10 were waited for; matrix products, arithmetic and copies ran while one was open for 2% of the time, Pallas kernels for 0%

commit v1 on v0

v1 whole, which is shorter than its diff:
```python
import jax
import jax.numpy as jnp
from jax import lax
from jax.sharding import Mesh
from jax.sharding import PartitionSpec as P

SEGMENTS = 8
CORES = 2


CONTRACT_FIRST = (((0,), (1,)), ((), ()))
CONTRACT_LAST = (((1,), (1,)), ((), ()))
DOM = ("zx", "core")


def rotate(real_weight, imag_weight, pattern):
    samples = real_weight.shape[-1]
    values = pattern.astype(jnp.float32)
    real_part = values[..., :samples]
    imag_part = values[..., samples:]
    return jnp.concatenate(
        [
            real_weight * real_part - imag_weight * imag_part,
            real_weight * imag_part + imag_weight * real_part,
        ],
        axis=-1,
    )


def share_slots(slots, chips):
    shape = slots.shape
    swap = [(0, 1), (1, 0)]
    slots = slots + lax.ppermute(slots, "core", swap)
    core = lax.axis_index("core")
    halves = slots.reshape(CORES, -1)
    mine = lax.dynamic_index_in_dim(halves, core, 0, keepdims=False).reshape(chips, -1)
    pieces = lax.all_to_all(mine, "zx", 0, 0, tiled=True)
    total = jnp.sum(pieces, axis=0, keepdims=True)
    spread = jnp.broadcast_to(total, (chips, total.shape[1]))
    gathered = lax.all_to_all(spread, "zx", 0, 0, tiled=True).reshape(-1)
    other = lax.ppermute(gathered, "core", swap)
    whole = jnp.where(
        core == 0,
        jnp.concatenate([gathered, other]),
        jnp.concatenate([other, gathered]),
    )
    return whole.reshape(shape)


def local(
    excitation,
    local_inverse,
    aggregation,
    disaggregation,
    translation,
    partners,
    list_counts,
    sweep_order,
):
    chips = lax.axis_size("zx")
    excite_rows = excitation[0]
    inverse_rows = local_inverse[0]
    agg_columns = aggregation[0]
    disagg_rows = disaggregation[0]
    trans_rows = translation[0]
    partner_row = partners[0]

    def apply_inverse(shard_rows):
        return jnp.dot(inverse_rows, shard_rows, preferred_element_type=jnp.float32)

    solved = apply_inverse(lax.all_gather(excite_rows, "sub", axis=0, tiled=True))
    solved_half = solved.astype(jnp.bfloat16)
    incident = lax.psum_scatter(
        lax.dot_general(
            solved_half, agg_columns, CONTRACT_FIRST, preferred_element_type=jnp.float32
        ).astype(jnp.bfloat16),
        "sub",
        scatter_dimension=0,
        tiled=True,
    ).astype(jnp.float32)
    spread = apply_inverse(lax.all_gather(disagg_rows, "sub", axis=0, tiled=True))
    spread_half = spread.astype(jnp.bfloat16)
    partial_map = lax.dot_general(
        spread_half, agg_columns, CONTRACT_FIRST, preferred_element_type=jnp.float32
    )
    coupling = lax.psum(partial_map.astype(jnp.bfloat16), "sub")

    domains = sweep_order.shape[0]
    members = domains // SEGMENTS
    segment_of = sweep_order * SEGMENTS // domains
    own_index = lax.axis_index("zx") * CORES + lax.axis_index("core")
    my_segment = segment_of[own_index]
    my_slot = sweep_order[own_index] - my_segment * members
    slot_ids = jnp.arange(members, dtype=jnp.int32)
    slot_live = jnp.arange(partner_row.shape[0], dtype=jnp.int32) < list_counts[0]
    partner_pos = sweep_order[partner_row]
    partner_segment = partner_pos * SEGMENTS // domains
    partner_slot = partner_pos - partner_segment * members

    incoming = jnp.zeros(incident.shape, jnp.float32)
    for segment_k in range(SEGMENTS - 1):
        pattern = (
            incident
            - jnp.dot(incoming.astype(jnp.bfloat16), coupling, preferred_element_type=jnp.float32)
        ).astype(jnp.bfloat16)
        mine = (slot_ids == my_slot) & (my_segment == segment_k)
        slots = jnp.where(mine[:, None, None], pattern[None], jnp.zeros_like(pattern)[None])
        slots = share_slots(slots, chips)
        match = (
            (partner_slot[:, None] == slot_ids[None, :])
            & (partner_segment[:, None] == segment_k)
            & slot_live[:, None]
            & (segment_k < my_segment)
        )
        weights = jnp.sum(
            jnp.where(match[:, :, None, None], trans_rows[:, None, :, :], 0.0), axis=0
        )
        terms = rotate(weights[:, 0][:, None, :], weights[:, 1][:, None, :], slots)
        incoming = incoming + jnp.sum(terms, axis=0)
    fields = lax.all_gather(incoming.astype(jnp.bfloat16), "sub", axis=0, tiled=True)
    currents = solved - lax.dot_general(
        spread_half, fields, CONTRACT_LAST, preferred_element_type=jnp.float32
    )
    return currents[None]


def solution(mesh):
    dom_size, sub_size = mesh.devices.shape
    fine = Mesh(mesh.devices.reshape(dom_size // CORES, CORES, sub_size), ("zx", "core", "sub"))
    in_specs = (
        P(DOM, "sub", None),
        P(DOM, "sub", None),
        P(DOM, None, "sub"),
        P(DOM, "sub", None),
        P(DOM, None, None, None),
        P(DOM, None),
        P(DOM),
        P(),
    )
    out_specs = P(DOM, "sub", None)
    return jax.shard_map(local, mesh=fine, in_specs=in_specs, out_specs=out_specs, check_vma=False)
```

time: 728 us -> 550 us (0.76); the launches traced: 726 us -> 539 us
  waiting for transfers between devices: 627 us -> 138 us
  blocking collectives: 25.4 us -> 201 us
  local copies, waits for them, and re-layouts: 7.96 us -> 74.1 us
  other arithmetic: 23.9 us -> 67.5 us
  starting transfers between devices: 0.56 us -> 19.8 us
    all_gather x7 -> x0, waiting for transfers between devices: 511 us -> none  [local(): make_piece = lax.all_gather(pattern[None], 'dom', axis=0, tiled=True)]
    all_to_all x0 -> x12, blocking collectives: none -> 177 us  [the longest x6 91 us: share_slots(): pieces = lax.all_to_all(mine, 'zx', 0, 0, tiled=True)]
    all_to_all x0 -> x14, other arithmetic: none -> 26.4 us  [the longest x7 15.7 us: share_slots(): pieces = lax.all_to_all(mine, 'zx', 0, 0, tiled=True)]
    unnamed x38 -> x87, local copies, waits for them, and re-layouts: 4.14 us -> 26 us
    all_to_all x0 -> x2, starting transfers between devices: none -> 15.3 us  [the longest x1 10.1 us: share_slots(): pieces = lax.all_to_all(mine, 'zx', 0, 0, tiled=True)]
    broadcast_in_dim x0 -> x7, other arithmetic: none -> 13.8 us  [share_slots(): spread = jnp.broadcast_to(total, (chips, total.shape[1]))]
    concatenate x0 -> x14, local copies, waits for them, and re-layouts: none -> 13.5 us  [share_slots(): jnp.concatenate([gathered, other])]
    all_to_all x0 -> x2, waiting for transfers between devices: none -> 13.1 us  [the longest x1 8.62 us: share_slots(): gathered = lax.all_to_all(spread, 'zx', 0, 0, tiled=True).reshape(-1)]
  transfers between devices with their start and end apart: 10 -> 19, of which waited for: 10 -> 13; matrix products, arithmetic and copies ran while one was open for 2% -> 5% of each run, Pallas kernels for 0% -> 0%
where the time goes in v1:
time: 550 us; the launch traced here: 539 us
  blocking collectives  201 us (37%)
  waiting for transfers between devices  138 us (25%)
  local copies, waits for them, and re-layouts  74.1 us (13%)
  other arithmetic  67.5 us (12%)
  between operations  25.7 us (5%)
  starting transfers between devices  19.8 us (4%)
  matrix products  12.7 us (2%)
    all_to_all x6, blocking collectives, share_slots(): pieces = lax.all_to_all(mine, 'zx', 0, 0, tiled=True)  91 us
    all_to_all x6, blocking collectives, share_slots(): gathered = lax.all_to_all(spread, 'zx', 0, 0, tiled=True).reshape(-1)  85.5 us
    psum x1, waiting for transfers between devices, local(): coupling = lax.psum(partial_map.astype(jnp.bfloat16), 'sub')  66.1 us
    all_gather x1, waiting for transfers between devices, local(): lax.all_gather(disagg_rows, 'sub', axis=0, tiled=True)  32.1 us
    unnamed x87, local copies, waits for them, and re-layouts  26 us
    reduce_scatter x1, waiting for transfers between devices, local(): lax.psum_scatter(lax.dot_general(solved_half, agg_columns, CONTRACT_FIRST...  16.4 us
    all_to_all x7, other arithmetic, share_slots(): pieces = lax.all_to_all(mine, 'zx', 0, 0, tiled=True)  15.7 us
    broadcast_in_dim x7, other arithmetic, share_slots(): spread = jnp.broadcast_to(total, (chips, total.shape[1]))  13.8 us
  transfers between devices with their start and end apart: 19, of which 13 were waited for; matrix products, arithmetic and copies ran while one was open for 5% of the time, Pallas kernels for 0%

profile of v1, /device:TPU:32, one launch (start us, length us, event | category | flops | bytes accessed | tf_op | source)
XLA Modules:
  0.0 538.9 jit_solution(2973069429768945431)
XLA Ops:
  7.3 12.9 %all-gather = bf16[1,1536,64]{1,2,0:T(8,128)(2,1)S(1)} all-gather(bf16[1,384,64]{1,2,0:T(8,128)(2,1)} %param.8), channel_id=2, replica_groups=mesh['zx'=32,'core'=2,'sub'=4] {'sub'}, dimensions={1}, use_global_device_ids=true | all-gather | bytes 245760 | tf_op jit(solution)/shard_map/all_gather | solution.py:71
  21.9 32.1 %all-gather.4.cloned.1.call-done = bf16[1,1536,1024]{2,1,0:T(8,128)(2,1)} async-done(((bf16[1,384,1024]{2,1,0:T(8,128)(2,1)}), bf16[1,1536,1024]{2,1,0:T(8,128)(2,1)}) %all-gather.4.cloned.1.call-update) | async-done | bytes 3145744 | tf_op jit(solution)/shard_map/all_gather | solution.py:81
  53.9 3.3 fusion.2
  57.3 2.6 convolution_convert_fusion
  63.2 16.4 %reduce-scatter.2.cloned.1.call-done = bf16[16,1024]{1,0:T(8,128)(2,1)} async-done(((bf16[64,1024]{1,0:T(8,128)(2,1)}), bf16[16,1024]{1,0:T(8,128)(2,1)}) %reduce-scatter.2.cloned.1.call-update) | async-done | bytes 32784 | tf_op jit(solution)/shard_map/reduce_scatter | solution.py:73
  79.6 66.1 %all-reduce.2.cloned.1.call-done = bf16[1024,1024]{1,0:T(8,128)(2,1)} async-done(((bf16[1024,1024]{1,0:T(8,128)(2,1)}), bf16[1024,1024]{1,0:T(8,128)(2,1)}) %all-reduce.2.cloned.1.call-update) | async-done | bytes 2097168 | tf_op jit(solution)/shard_map/psum | solution.py:86
  145.7 2.0 fusion.9
  152.5 10.1 %all-to-all-start = ((bf16[32,2,1024]{2,1,0:T(2,128)(2,1)}), bf16[32,2,1024]{2,1,0:T(2,128)(2,1)S(1)}, u32[]{:S(2)}, u32[]{:S(2)}) async-start(bf16[32,2,1024]{2,1,0:T(2,128)(2,1)} %reshape.728), calls=%async_computation.1 | async-start | bytes 262144 | tf_op jit(solution)/shard_map/all_to_all | solution.py:37
  168.0 4.5 all-to-all-done
  175.0 5.3 all-to-all-start.1
  181.2 8.6 %all-to-all-done.1 = bf16[32,2,1024]{2,1,0:T(2,128)(2,1)S(1)} async-done(((bf16[32,2,1024]{2,1,0:T(2,128)(2,1)}), bf16[32,2,1024]{2,1,0:T(2,128)(2,1)S(1)}, u32[]{:S(2)}, u32[]{:S(2)}) %all-to-all-start.1) | async-done | bytes 131104 | tf_op jit(solution)/shard_map/all_to_all | solution.py:40
  190.7 1.7 reduce.14
  203.3 1.8 reshape.692
  205.2 1.9 constant_dynamic-slice_fusion.5
  207.1 2.2 reduce.30
  210.1 15.2 %all_to_all.105 = bf16[32,2,1024]{2,1,0:T(2,128)(2,1)S(1)} all-to-all(bf16[32,2,1024]{2,1,0:T(2,128)(2,1)} %reshape.732), channel_id=1, replica_groups=mesh['zx'=32,'core'=2,'sub'=4] {'zx'}, dimensions={0} | all-to-all | bytes 262144 | tf_op jit(solution)/shard_map/all_to_all | solution.py:37
  228.1 2.2 reduce.31
  231.1 14.3 %all_to_all.106 = bf16[32,2,1024]{2,1,0:T(2,128)(2,1)S(1)} all-to-all(bf16[32,2,1024]{2,1,0:T(2,128)(2,1)} %reshape.734), channel_id=1, replica_groups=mesh['zx'=32,'core'=2,'sub'=4] {'zx'}, dimensions={0} | all-to-all | bytes 262144 | tf_op jit(solution)/shard_map/all_to_all | solution.py:40
  246.2 1.7 reduce.16
  258.5 1.8 reshape.694
  260.4 1.9 constant_dynamic-slice_fusion.4
  262.3 2.9 reduce.32
  266.8 15.3 %all_to_all.107 = bf16[32,2,1024]{2,1,0:T(2,128)(2,1)S(1)} all-to-all(bf16[32,2,1024]{2,1,0:T(2,128)(2,1)} %reshape.736), channel_id=1, replica_groups=mesh['zx'=32,'core'=2,'sub'=4] {'zx'}, dimensions={0} | all-to-all | bytes 262144 | tf_op jit(solution)/shard_map/all_to_all | solution.py:37
  284.9 2.2 reduce.33
  287.8 14.3 %all_to_all.108 = bf16[32,2,1024]{2,1,0:T(2,128)(2,1)S(1)} all-to-all(bf16[32,2,1024]{2,1,0:T(2,128)(2,1)} %reshape.738), channel_id=1, replica_groups=mesh['zx'=32,'core'=2,'sub'=4] {'zx'}, dimensions={0} | all-to-all | bytes 262144 | tf_op jit(solution)/shard_map/all_to_all | solution.py:40
  302.9 1.7 reduce.18
  315.4 1.8 reshape.696
  317.3 1.9 constant_dynamic-slice_fusion.3
  319.2 2.9 reduce.34
  323.7 15.3 %all_to_all.109 = bf16[32,2,1024]{2,1,0:T(2,128)(2,1)S(1)} all-to-all(bf16[32,2,1024]{2,1,0:T(2,128)(2,1)} %reshape.740), channel_id=1, replica_groups=mesh['zx'=32,'core'=2,'sub'=4] {'zx'}, dimensions={0} | all-to-all | bytes 262144 | tf_op jit(solution)/shard_map/all_to_all | solution.py:37
  341.8 2.2 reduce.35
  344.7 14.3 %all_to_all.110 = bf16[32,2,1024]{2,1,0:T(2,128)(2,1)S(1)} all-to-all(bf16[32,2,1024]{2,1,0:T(2,128)(2,1)} %reshape.742), channel_id=1, replica_groups=mesh['zx'=32,'core'=2,'sub'=4] {'zx'}, dimensions={0} | all-to-all | bytes 262144 | tf_op jit(solution)/shard_map/all_to_all | solution.py:40
  359.8 1.7 reduce.20
  372.1 1.8 reshape.698
  374.0 1.9 constant_dynamic-slice_fusion.2
  375.9 2.9 reduce.36
  380.4 15.3 %all_to_all.111 = bf16[32,2,1024]{2,1,0:T(2,128)(2,1)S(1)} all-to-all(bf16[32,2,1024]{2,1,0:T(2,128)(2,1)} %reshape.744), channel_id=1, replica_groups=mesh['zx'=32,'core'=2,'sub'=4] {'zx'}, dimensions={0} | all-to-all | bytes 262144 | tf_op jit(solution)/shard_map/all_to_all | solution.py:37
  398.5 2.2 reduce.37
  401.4 14.5 %all_to_all.112 = bf16[32,2,1024]{2,1,0:T(2,128)(2,1)S(1)} all-to-all(bf16[32,2,1024]{2,1,0:T(2,128)(2,1)} %reshape.746), channel_id=1, replica_groups=mesh['zx'=32,'core'=2,'sub'=4] {'zx'}, dimensions={0} | all-to-all | bytes 262144 | tf_op jit(solution)/shard_map/all_to_all | solution.py:40
  429.7 1.8 reshape.700
  431.6 1.9 constant_dynamic-slice_fusion.1
  433.5 2.2 reduce.38
  436.5 15.3 %all_to_all.113 = bf16[32,2,1024]{2,1,0:T(2,128)(2,1)S(1)} all-to-all(bf16[32,2,1024]{2,1,0:T(2,128)(2,1)} %reshape.748), channel_id=1, replica_groups=mesh['zx'=32,'core'=2,'sub'=4] {'zx'}, dimensions={0} | all-to-all | bytes 262144 | tf_op jit(solution)/shard_map/all_to_all | solution.py:37
  454.6 2.2 reduce.39
  457.5 14.3 %all_to_all.114 = bf16[32,2,1024]{2,1,0:T(2,128)(2,1)S(1)} all-to-all(bf16[32,2,1024]{2,1,0:T(2,128)(2,1)} %reshape.750), channel_id=1, replica_groups=mesh['zx'=32,'core'=2,'sub'=4] {'zx'}, dimensions={0} | all-to-all | bytes 262144 | tf_op jit(solution)/shard_map/all_to_all | solution.py:40
  486.1 14.6 %all_to_all.115 = bf16[32,2,1024]{2,1,0:T(2,128)(2,1)S(1)} all-to-all(bf16[32,2,1024]{2,1,0:T(2,128)(2,1)S(1)} %reshape.752), channel_id=1, replica_groups=mesh['zx'=32,'core'=2,'sub'=4] {'zx'}, dimensions={0} | all-to-all | bytes 262144 | tf_op jit(solution)/shard_map/all_to_all | solution.py:37
  502.6 13.7 %all_to_all.116 = bf16[32,2,1024]{2,1,0:T(2,128)(2,1)S(1)} all-to-all(bf16[32,2,1024]{2,1,0:T(2,128)(2,1)S(1)} %reshape.754), channel_id=1, replica_groups=mesh['zx'=32,'core'=2,'sub'=4] {'zx'}, dimensions={0} | all-to-all | bytes 262144 | tf_op jit(solution)/shard_map/all_to_all | solution.py:40
  518.9 12.0 %all_gather.11 = bf16[64,1024]{1,0:T(8,128)(2,1)S(1)} all-gather(bf16[16,1024]{1,0:T(8,128)(2,1)S(1)} %add_convert_fusion), channel_id=1, replica_groups=mesh['zx'=32,'core'=2,'sub'=4] {'sub'}, dimensions={0}, use_global_device_ids=true | all-gather | bytes 163840 | tf_op jit(solution)/shard_map/all_gather | solution.py:120
  (236 shorter events, 111.0 us)
Async XLA Ops:
  6.5 13.7 %copy-start = (bf16[1,384,1536]{2,1,0:T(8,128)(2,1)S(1)}, bf16[1,384,1536]{2,1,0:T(8,128)(2,1)}, u32[]{:S(2)}) copy-start(bf16[1,384,1536]{2,1,0:T(8,128)(2,1)} %param.9) | copy-start | bytes 3538948
  6.5 14.2 %copy-start.6 = (bf16[1,1024,384]{2,1,0:T(8,128)(2,1)S(1)}, bf16[1,1024,384]{2,1,0:T(8,128)(2,1)}, u32[]{:S(2)}) copy-start(bf16[1,1024,384]{2,1,0:T(8,128)(2,1)} %param.10) | copy-start | bytes 2359300
  6.5 47.4 %all-gather.4.cloned.1.call-start = ((), (), s32[]{:S(2)}) async-start(), calls=%async_computation.17 | async-start | bytes 3932160 | tf_op jit(solution)/shard_map/all_gather | solution.py:81
  7.3 72.3 %reduce-scatter.2.cloned.1.call-start = ((), (), s32[]{:S(2)}) async-start(), calls=%async_computation.15 | async-start | bytes 163840 | tf_op jit(solution)/shard_map/reduce_scatter | solution.py:73
  21.8 123.9 %all-reduce.2.cloned.1.call-start = ((), (), s32[]{:S(2)}) async-start(), calls=%async_computation.16 | async-start | bytes 4194304 | tf_op jit(solution)/shard_map/psum | solution.py:86
  57.2 2.7 copy-start.4
  57.2 2.7 copy-start.1
  57.2 5.9 %copy-start.25 = (s32[1,6]{1,0:T(1,128)S(1)}, s32[1,6]{1,0:T(1,128)}, u32[]{:S(2)}) copy-start(s32[1,6]{1,0:T(1,128)} %param.13) | copy-start | bytes 76
  147.8 1.6 collective-permute-start
  148.6 31.8 %copy-start.18 = (f32[1,6,2,512]{3,2,1,0:T(2,128)S(1)}, f32[1,6,2,512]{3,2,1,0:T(2,128)}, u32[]{:S(2)}) copy-start(f32[1,6,2,512]{3,2,1,0:T(2,128)} %param.12) | copy-start | bytes 73732
  152.5 19.9 %all-to-all-start = ((bf16[32,2,1024]{2,1,0:T(2,128)(2,1)}), bf16[32,2,1024]{2,1,0:T(2,128)(2,1)S(1)}, u32[]{:S(2)}, u32[]{:S(2)}) async-start(bf16[32,2,1024]{2,1,0:T(2,128)(2,1)} %reshape.728), calls=%async_computation.1 | async-start | bytes 262144 | tf_op jit(solution)/shard_map/all_to_all | solution.py:37
  175.0 14.8 %all-to-all-start.1 = ((bf16[32,2,1024]{2,1,0:T(2,128)(2,1)}), bf16[32,2,1024]{2,1,0:T(2,128)(2,1)S(1)}, u32[]{:S(2)}, u32[]{:S(2)}) async-start(bf16[32,2,1024]{2,1,0:T(2,128)(2,1)} %reshape.730), calls=%async_computation.2 | async-start | bytes 262144 | tf_op jit(solution)/shard_map/all_to_all | solution.py:40
  181.2 18.6 %copy-start.2 = (bf16[1024,1024]{1,0:T(8,128)(2,1)S(1)}, bf16[1024,1024]{1,0:T(8,128)(2,1)}, u32[]{:S(2)}) copy-start(bf16[1024,1024]{1,0:T(8,128)(2,1)} %all-reduce.2.cloned.1.call-done) | copy-start | bytes 6291460
  181.2 18.6 %copy-start.3 = (bf16[16,1024]{1,0:T(8,128)(2,1)S(1)}, bf16[16,1024]{1,0:T(8,128)(2,1)}, u32[]{:S(2)}) copy-start(bf16[16,1024]{1,0:T(8,128)(2,1)} %reduce-scatter.2.cloned.1.call-done) | copy-start | bytes 98308
  193.0 3.3 collective-permute-start.1
  198.3 1.9 copy-start.24
  199.2 0.6 copy-start.9
  200.3 2.2 collective-permute-start.2
  248.5 3.3 collective-permute-start.3
  251.8 3.7 copy-start.10
  254.6 1.3 copy-start.20
  255.5 9.7 %copy-start.11 = (f32[16,1024]{1,0:T(8,128)}, f32[16,1024]{1,0:T(8,128)S(1)}, u32[]{:S(2)}) copy-start(f32[16,1024]{1,0:T(8,128)S(1)} %add.126) | copy-start | bytes 196612
  256.0 1.8 collective-permute-start.4
  305.3 3.4 collective-permute-start.5
  308.7 3.7 copy-start.12
  311.5 1.3 copy-start.21
  312.4 9.7 %copy-start.13 = (f32[16,1024]{1,0:T(8,128)}, f32[16,1024]{1,0:T(8,128)S(1)}, u32[]{:S(2)}) copy-start(f32[16,1024]{1,0:T(8,128)S(1)} %add.129) | copy-start | bytes 196612
  312.9 1.7 collective-permute-start.6
  362.2 3.2 collective-permute-start.7
  365.4 3.7 copy-start.14
  368.2 1.3 copy-start.22
  369.1 9.7 %copy-start.15 = (f32[16,1024]{1,0:T(8,128)}, f32[16,1024]{1,0:T(8,128)S(1)}, u32[]{:S(2)}) copy-start(f32[16,1024]{1,0:T(8,128)S(1)} %add.132) | copy-start | bytes 196612
  369.6 1.8 collective-permute-start.8
  419.1 3.3 collective-permute-start.9
  422.4 3.7 copy-start.16
  425.2 1.9 copy-start.23
  426.1 0.6 copy-start.7
  427.2 1.8 collective-permute-start.10
  475.0 3.3 collective-permute-start.11
  478.2 3.7 copy-start.8
  481.0 1.3 copy-start.19
  482.4 1.8 collective-permute-start.12
  484.5 32.9 %copy-start.17 = (f32[8,2,512]{2,0,1:T(8,128)S(1)}, f32[8,2,512]{2,0,1:T(8,128)}, u32[]{:S(2)}) copy-start(f32[8,2,512]{2,0,1:T(8,128)} %get-tuple-element.5) | copy-start | bytes 98308
  516.5 14.5 %copy-start.5 = (bf16[384,1024]{1,0:T(8,128)(2,1)S(1)}, bf16[384,1024]{1,0:T(8,128)(2,1)}, u32[]{:S(2)}) copy-start(bf16[384,1024]{1,0:T(8,128)(2,1)} %copy-done.4) | copy-start | bytes 2359300
  517.2 1.4 collective-permute-start.13
Sparse Core Ops, SparseCore 0:
  9.2 44.7 all-gather.3
  56.4 23.1 reduce-scatter.1
  82.1 63.5 all-reduce.1

commit v2 on v1

--- a/solution.py
+++ b/solution.py
@@ -11,40 +11,40 @@
 CONTRACT_FIRST = (((0,), (1,)), ((), ()))
 CONTRACT_LAST = (((1,), (1,)), ((), ()))
 DOM = ("zx", "core")
+LANES = 128
 
 
-def rotate(real_weight, imag_weight, pattern):
-    samples = real_weight.shape[-1]
-    values = pattern.astype(jnp.float32)
-    real_part = values[..., :samples]
-    imag_part = values[..., samples:]
-    return jnp.concatenate(
-        [
-            real_weight * real_part - imag_weight * imag_part,
-            real_weight * imag_part + imag_weight * real_part,
-        ],
-        axis=-1,
-    )
+def to_tiles(rows):
+    lead = rows.shape[:-2]
+    count, width = rows.shape[-2:]
+    tiled = rows.reshape(lead + (count, width // LANES, LANES))
+    return jnp.moveaxis(tiled, -2, -3)
+
+
+def from_tiles(tiles):
+    lead = tiles.shape[:-3]
+    groups, count, lanes = tiles.shape[-3:]
+    return jnp.moveaxis(tiles, -3, -2).reshape(lead + (count, groups * lanes))
 
 
 def share_slots(slots, chips):
-    shape = slots.shape
     swap = [(0, 1), (1, 0)]
     slots = slots + lax.ppermute(slots, "core", swap)
     core = lax.axis_index("core")
-    halves = slots.reshape(CORES, -1)
-    mine = lax.dynamic_index_in_dim(halves, core, 0, keepdims=False).reshape(chips, -1)
-    pieces = lax.all_to_all(mine, "zx", 0, 0, tiled=True)
+    count = slots.shape[0]
+    halves = slots.reshape((CORES, count // CORES) + slots.shape[1:])
+    mine = lax.dynamic_index_in_dim(halves, core, 0, keepdims=False)
+    tile_shape = mine.shape[2:]
+    pieces = lax.all_to_all(mine.reshape((chips,) + tile_shape), "zx", 0, 0, tiled=True)
     total = jnp.sum(pieces, axis=0, keepdims=True)
-    spread = jnp.broadcast_to(total, (chips, total.shape[1]))
-    gathered = lax.all_to_all(spread, "zx", 0, 0, tiled=True).reshape(-1)
+    spread = jnp.broadcast_to(total, (chips,) + tile_shape)
+    gathered = lax.all_to_all(spread, "zx", 0, 0, tiled=True).reshape(mine.shape)
     other = lax.ppermute(gathered, "core", swap)
-    whole = jnp.where(
+    return jnp.where(
         core == 0,
         jnp.concatenate([gathered, other]),
         jnp.concatenate([other, gathered]),
     )
-    return whole.reshape(shape)
 
 
 def local(
@@ -97,15 +97,27 @@
     partner_segment = partner_pos * SEGMENTS // domains
     partner_slot = partner_pos - partner_segment * members
 
-    incoming = jnp.zeros(incident.shape, jnp.float32)
+    half_samples = trans_rows.shape[-1] // LANES
+    trans_tiles = trans_rows.reshape(trans_rows.shape[:2] + (half_samples, 1, LANES))
+    incoming = jnp.zeros(to_tiles(incident).shape, jnp.float32)
     for segment_k in range(SEGMENTS - 1):
-        pattern = (
-            incident
-            - jnp.dot(incoming.astype(jnp.bfloat16), coupling, preferred_element_type=jnp.float32)
-        ).astype(jnp.bfloat16)
+        if segment_k == 0:
+            pattern = incident.astype(jnp.bfloat16)
+        else:
+            pattern = (
+                incident
+                - jnp.dot(
+                    from_tiles(incoming).astype(jnp.bfloat16),
+                    coupling,
+                    preferred_element_type=jnp.float32,
+                )
+            ).astype(jnp.bfloat16)
         mine = (slot_ids == my_slot) & (my_segment == segment_k)
-        slots = jnp.where(mine[:, None, None], pattern[None], jnp.zeros_like(pattern)[None])
-        slots = share_slots(slots, chips)
+        pattern_tiles = to_tiles(pattern)
+        slots = jnp.where(
+            mine[:, None, None, None], pattern_tiles[None], jnp.zeros_like(pattern_tiles)[None]
+        )
+        slots = share_slots(slots, chips).astype(jnp.float32)
         match = (
             (partner_slot[:, None] == slot_ids[None, :])
             & (partner_segment[:, None] == segment_k)
@@ -113,10 +125,20 @@
             & (segment_k < my_segment)
         )
         weights = jnp.sum(
-            jnp.where(match[:, :, None, None], trans_rows[:, None, :, :], 0.0), axis=0
+            jnp.where(match[:, :, None, None, None, None], trans_tiles[:, None], 0.0), axis=0
         )
-        terms = rotate(weights[:, 0][:, None, :], weights[:, 1][:, None, :], slots)
-        incoming = incoming + jnp.sum(terms, axis=0)
+        real_weight = weights[:, 0]
+        imag_weight = weights[:, 1]
+        real_part = slots[:, :half_samples]
+        imag_part = slots[:, half_samples:]
+        incoming = incoming + jnp.concatenate(
+            [
+                jnp.sum(real_weight * real_part - imag_weight * imag_part, axis=0),
+                jnp.sum(real_weight * imag_part + imag_weight * real_part, axis=0),
+            ],
+            axis=0,
+        )
+    incoming = from_tiles(incoming)
     fields = lax.all_gather(incoming.astype(jnp.bfloat16), "sub", axis=0, tiled=True)
     currents = solved - lax.dot_general(
         spread_half, fields, CONTRACT_LAST, preferred_element_type=jnp.float32

time: 550 us -> 389 us (0.71); the launches traced: 539 us -> 388 us
  local copies, waits for them, and re-layouts: 74.1 us -> 6.69 us
  other arithmetic: 67.5 us -> 9.43 us
  waiting for transfers between devices: 138 us -> 115 us
    psum x1, waiting for transfers between devices: 66.1 us -> 26 us  [local(): coupling = lax.psum(partial_map.astype(jnp.bfloat16), 'sub')]
    all_to_all x14 -> x0, other arithmetic: 26.4 us -> none  [the longest x7 15.7 us: share_slots(): pieces = lax.all_to_all(mine, 'zx', 0, 0, tiled=True)]
    unnamed x87 -> x35, local copies, waits for them, and re-layouts: 26 us -> 0.88 us
    broadcast_in_dim x7 -> x0, other arithmetic: 13.8 us -> none  [share_slots(): spread = jnp.broadcast_to(total, (chips, total.shape[1]))]
    concatenate x14 -> x0, local copies, waits for them, and re-layouts: 13.5 us -> none  [share_slots(): jnp.concatenate([gathered, other])]
    all_gather x1, waiting for transfers between devices: 32.1 us -> 42.8 us  [local(): lax.all_gather(disagg_rows, 'sub', axis=0, tiled=True)]
    reshape x7 -> x0, local copies, waits for them, and re-layouts: 9.57 us -> none  [share_slots(): halves = slots.reshape(CORES, -1)]
    dynamic_slice x7, local copies, waits for them, and re-layouts: 10.2 us -> 0.78 us  [share_slots(): mine = lax.dynamic_index_in_dim(halves, core, 0, keepdims=False)]
  transfers between devices with their start and end apart: 19 -> 19, of which waited for: 13 -> 16; matrix products, arithmetic and copies ran while one was open for 5% -> 3% of each run, Pallas kernels for 0% -> 0%
where the time goes in v2:
time: 389 us; the launch traced here: 388 us
  blocking collectives  201 us (52%)
  waiting for transfers between devices  115 us (30%)
  between operations  24.7 us (6%)
  starting transfers between devices  17.7 us (5%)
  matrix products  13.5 us (3%)
  other arithmetic  9.43 us (2%)
  local copies, waits for them, and re-layouts  6.69 us (2%)
    all_to_all x6, blocking collectives, share_slots(): lax.all_to_all(mine.reshape((chips,) + tile_shape), 'zx', 0, 0, tiled=True)  93.8 us
    all_to_all x6, blocking collectives, share_slots(): lax.all_to_all(spread, 'zx', 0, 0, tiled=True).reshape(mine.shape)  82.1 us
    all_gather x1, waiting for transfers between devices, local(): lax.all_gather(disagg_rows, 'sub', axis=0, tiled=True)  42.8 us
    psum x1, waiting for transfers between devices, local(): coupling = lax.psum(partial_map.astype(jnp.bfloat16), 'sub')  26 us
    reduce_scatter x1, waiting for transfers between devices, local(): lax.psum_scatter(lax.dot_general(solved_half, agg_columns, CONTRACT_FIRST...  21 us
    all_gather x1, blocking collectives, local(): lax.all_gather(excite_rows, 'sub', axis=0, tiled=True)  13.1 us
    all_gather x1, blocking collectives, local(): lax.all_gather(incoming.astype(jnp.bfloat16), 'sub', axis=0, tiled=True)  12 us
    all_to_all x1, starting transfers between devices, share_slots(): lax.all_to_all(mine.reshape((chips,) + tile_shape), 'zx', 0, 0, tiled=True)  10.1 us
  transfers between devices with their start and end apart: 19, of which 16 were waited for; matrix products, arithmetic and copies ran while one was open for 3% of the time, Pallas kernels for 0%

profile of v2, /device:TPU:32, one launch (start us, length us, event | category | flops | bytes accessed | tf_op | source)
XLA Modules:
  0.0 388.1 jit_solution(12698541871713571364)
XLA Ops:
  6.5 13.1 %all-gather = bf16[1,1536,64]{1,2,0:T(8,128)(2,1)S(1)} all-gather(bf16[1,384,64]{1,2,0:T(8,128)(2,1)} %param.8), channel_id=2, replica_groups=mesh['zx'=32,'core'=2,'sub'=4] {'sub'}, dimensions={1}, use_global_device_ids=true | all-gather | bytes 245760 | tf_op jit(solution)/shard_map/all_gather | solution.py:71
  20.1 2.1 convolution_convert_fusion.1
  22.4 0.7 all-gather.4.cloned.1.call-update
  26.3 21.0 %reduce-scatter.2.cloned.1.call-done = bf16[16,1024]{1,0:T(8,128)(2,1)} async-done(((bf16[64,1024]{1,0:T(8,128)(2,1)}), bf16[16,1024]{1,0:T(8,128)(2,1)}) %reduce-scatter.2.cloned.1.call-update) | async-done | bytes 32784 | tf_op jit(solution)/shard_map/reduce_scatter | solution.py:73
  47.3 0.8 copy.58
  48.3 42.8 %all-gather.4.cloned.1.call-done = bf16[1,1536,1024]{2,1,0:T(8,128)(2,1)} async-done(((bf16[1,384,1024]{2,1,0:T(8,128)(2,1)}), bf16[1,1536,1024]{2,1,0:T(8,128)(2,1)}) %all-gather.4.cloned.1.call-update) | async-done | bytes 3145744 | tf_op jit(solution)/shard_map/all_gather | solution.py:81
  91.2 3.3 fusion.2
  94.5 2.6 convolution_convert_fusion
  97.9 0.7 constant_dynamic-slice_fusion.6
  98.6 10.1 %all-to-all-start = ((bf16[32,16,128]{2,1,0:T(8,128)(2,1)}), bf16[32,16,128]{2,1,0:T(8,128)(2,1)S(1)}, u32[]{:S(2)}, u32[]{:S(2)}) async-start(bf16[32,16,128]{2,1,0:T(8,128)(2,1)} %bitcast.14), calls=%async_computation.1 | async-start | bytes 262144 | tf_op jit(solution)/shard_map/all_to_all | solution.py:38
  113.8 4.5 %all-to-all-done = bf16[32,16,128]{2,1,0:T(8,128)(2,1)S(1)} async-done(((bf16[32,16,128]{2,1,0:T(8,128)(2,1)}), bf16[32,16,128]{2,1,0:T(8,128)(2,1)S(1)}, u32[]{:S(2)}, u32[]{:S(2)}) %all-to-all-start) | async-done | bytes 131104 | tf_op jit(solution)/shard_map/all_to_all | solution.py:38
  118.3 0.7 broadcast_in_dim.280
  119.0 5.3 %all-to-all-start.1 = ((bf16[32,16,128]{2,1,0:T(8,128)(2,1)}), bf16[32,16,128]{2,1,0:T(8,128)(2,1)S(1)}, u32[]{:S(2)}, u32[]{:S(2)}) async-start(bf16[32,16,128]{2,1,0:T(8,128)(2,1)} %broadcast_in_dim.280), calls=%async_computation.2 | async-start | bytes 262144 | tf_op jit(solution)/shard_map/all_to_all | solution.py:41
  124.4 0.8 select_reduce_fusion
  125.2 8.7 %all-to-all-done.1 = bf16[32,16,128]{2,1,0:T(8,128)(2,1)S(1)} async-done(((bf16[32,16,128]{2,1,0:T(8,128)(2,1)}), bf16[32,16,128]{2,1,0:T(8,128)(2,1)S(1)}, u32[]{:S(2)}, u32[]{:S(2)}) %all-to-all-start.1) | async-done | bytes 131104 | tf_op jit(solution)/shard_map/all_to_all | solution.py:41
  135.3 26.0 %all-reduce.2.cloned.1.call-done = bf16[1024,1024]{1,0:T(8,128)(2,1)} async-done(((bf16[1024,1024]{1,0:T(8,128)(2,1)}), bf16[1024,1024]{1,0:T(8,128)(2,1)}) %all-reduce.2.cloned.1.call-update) | async-done | bytes 2097168 | tf_op jit(solution)/shard_map/psum | solution.py:86
  161.3 2.0 fusion.20
  163.5 1.5 collective-permute-done.2
  165.2 19.8 %all_to_all.70 = bf16[32,16,128]{2,1,0:T(8,128)(2,1)} all-to-all(bf16[32,16,128]{2,1,0:T(8,128)(2,1)S(1)} %bitcast.199), channel_id=1, replica_groups=mesh['zx'=32,'core'=2,'sub'=4] {'zx'}, dimensions={0} | all-to-all | bytes 262144 | tf_op jit(solution)/shard_map/all_to_all | solution.py:38
  185.0 0.9 reduce_sum.294
  186.0 13.7 %all_to_all.71 = bf16[32,16,128]{2,1,0:T(8,128)(2,1)S(1)} all-to-all(bf16[32,16,128]{2,1,0:T(8,128)(2,1)S(1)} %broadcast_in_dim.284), channel_id=1, replica_groups=mesh['zx'=32,'core'=2,'sub'=4] {'zx'}, dimensions={0} | all-to-all | bytes 262144 | tf_op jit(solution)/shard_map/all_to_all | solution.py:41
  200.4 0.7 collective-permute-done.3
  202.0 1.4 collective-permute-done.4
  203.5 14.8 %all_to_all.72 = bf16[32,16,128]{2,1,0:T(8,128)(2,1)} all-to-all(bf16[32,16,128]{2,1,0:T(8,128)(2,1)S(1)} %bitcast.200), channel_id=1, replica_groups=mesh['zx'=32,'core'=2,'sub'=4] {'zx'}, dimensions={0} | all-to-all | bytes 262144 | tf_op jit(solution)/shard_map/all_to_all | solution.py:38
  218.3 0.9 reduce_sum.299
  219.3 13.7 %all_to_all.73 = bf16[32,16,128]{2,1,0:T(8,128)(2,1)S(1)} all-to-all(bf16[32,16,128]{2,1,0:T(8,128)(2,1)S(1)} %broadcast_in_dim.288), channel_id=1, replica_groups=mesh['zx'=32,'core'=2,'sub'=4] {'zx'}, dimensions={0} | all-to-all | bytes 262144 | tf_op jit(solution)/shard_map/all_to_all | solution.py:41
  234.4 0.8 convert_bitcast_fusion.3
  236.2 1.4 collective-permute-done.6
  237.7 14.8 %all_to_all.74 = bf16[32,16,128]{2,1,0:T(8,128)(2,1)} all-to-all(bf16[32,16,128]{2,1,0:T(8,128)(2,1)S(1)} %bitcast.201), channel_id=1, replica_groups=mesh['zx'=32,'core'=2,'sub'=4] {'zx'}, dimensions={0} | all-to-all | bytes 262144 | tf_op jit(solution)/shard_map/all_to_all | solution.py:38
  252.5 0.9 reduce_sum.304
  253.5 13.7 %all_to_all.75 = bf16[32,16,128]{2,1,0:T(8,128)(2,1)S(1)} all-to-all(bf16[32,16,128]{2,1,0:T(8,128)(2,1)S(1)} %broadcast_in_dim.292), channel_id=1, replica_groups=mesh['zx'=32,'core'=2,'sub'=4] {'zx'}, dimensions={0} | all-to-all | bytes 262144 | tf_op jit(solution)/shard_map/all_to_all | solution.py:41
  267.2 0.7 slice_bitcast_fusion.7
  269.9 1.2 collective-permute-done.8
  271.1 15.1 %all_to_all.76 = bf16[32,16,128]{2,1,0:T(8,128)(2,1)} all-to-all(bf16[32,16,128]{2,1,0:T(8,128)(2,1)S(1)} %bitcast.202), channel_id=1, replica_groups=mesh['zx'=32,'core'=2,'sub'=4] {'zx'}, dimensions={0} | all-to-all | bytes 262144 | tf_op jit(solution)/shard_map/all_to_all | solution.py:38
  286.2 0.9 reduce_sum.309
  287.2 13.7 %all_to_all.77 = bf16[32,16,128]{2,1,0:T(8,128)(2,1)S(1)} all-to-all(bf16[32,16,128]{2,1,0:T(8,128)(2,1)S(1)} %broadcast_in_dim.296), channel_id=1, replica_groups=mesh['zx'=32,'core'=2,'sub'=4] {'zx'}, dimensions={0} | all-to-all | bytes 262144 | tf_op jit(solution)/shard_map/all_to_all | solution.py:41
  300.9 0.7 slice_bitcast_fusion.5
  302.4 0.8 convert_bitcast_fusion.1
  304.3 1.2 collective-permute-done.10
  305.6 15.1 %all_to_all.78 = bf16[32,16,128]{2,1,0:T(8,128)(2,1)} all-to-all(bf16[32,16,128]{2,1,0:T(8,128)(2,1)S(1)} %bitcast.203), channel_id=1, replica_groups=mesh['zx'=32,'core'=2,'sub'=4] {'zx'}, dimensions={0} | all-to-all | bytes 262144 | tf_op jit(solution)/shard_map/all_to_all | solution.py:38
  320.7 0.9 reduce_sum.314
  321.7 13.7 %all_to_all.79 = bf16[32,16,128]{2,1,0:T(8,128)(2,1)S(1)} all-to-all(bf16[32,16,128]{2,1,0:T(8,128)(2,1)S(1)} %broadcast_in_dim.300), channel_id=1, replica_groups=mesh['zx'=32,'core'=2,'sub'=4] {'zx'}, dimensions={0} | all-to-all | bytes 262144 | tf_op jit(solution)/shard_map/all_to_all | solution.py:41
  337.6 1.4 collective-permute-done.12
  339.1 14.1 %all_to_all.80 = bf16[32,16,128]{2,1,0:T(8,128)(2,1)S(1)} all-to-all(bf16[32,16,128]{2,1,0:T(8,128)(2,1)S(1)} %bitcast.198), channel_id=1, replica_groups=mesh['zx'=32,'core'=2,'sub'=4] {'zx'}, dimensions={0} | all-to-all | bytes 262144 | tf_op jit(solution)/shard_map/all_to_all | solution.py:38
  353.3 13.7 %all_to_all.81 = bf16[32,16,128]{2,1,0:T(8,128)(2,1)S(1)} all-to-all(bf16[32,16,128]{2,1,0:T(8,128)(2,1)S(1)} %broadcast_in_dim.304), channel_id=1, replica_groups=mesh['zx'=32,'core'=2,'sub'=4] {'zx'}, dimensions={0} | all-to-all | bytes 262144 | tf_op jit(solution)/shard_map/all_to_all | solution.py:41
  367.0 0.7 slice_bitcast_fusion.1
  368.5 12.0 %all_gather.11 = bf16[64,1024]{1,0:T(8,128)(2,1)S(1)} all-gather(bf16[16,1024]{1,0:T(8,128)(2,1)S(1)} %copy_bitcast_fusion), channel_id=1, replica_groups=mesh['zx'=32,'core'=2,'sub'=4] {'sub'}, dimensions={0}, use_global_device_ids=true | all-gather | bytes 163840 | tf_op jit(solution)/shard_map/all_gather | solution.py:142
  380.5 1.0 fusion.8
  (152 shorter events, 12.1 us)
Async XLA Ops:
  6.5 13.1 %copy-start = (bf16[1,384,1536]{2,1,0:T(8,128)(2,1)S(1)}, bf16[1,384,1536]{2,1,0:T(8,128)(2,1)}, u32[]{:S(2)}) copy-start(bf16[1,384,1536]{2,1,0:T(8,128)(2,1)} %param.9) | copy-start | bytes 3538948
  6.5 16.6 %copy-start.1 = (s32[64]{0:T(128)S(1)}, s32[64]{0:T(128)}, u32[]{:S(2)}) copy-start(s32[64]{0:T(128)} %param.15) | copy-start | bytes 772
  6.5 19.7 %copy-start.13 = (s32[1,6]{1,0:T(1,128)S(1)}, s32[1,6]{1,0:T(1,128)}, u32[]{:S(2)}) copy-start(s32[1,6]{1,0:T(1,128)} %param.13) | copy-start | bytes 76
  6.5 40.8 %reduce-scatter.2.cloned.1.call-start = ((), (), s32[]{:S(2)}) async-start(), calls=%async_computation.15 | async-start | bytes 163840 | tf_op jit(solution)/shard_map/reduce_scatter | solution.py:73
  22.3 68.9 %all-gather.4.cloned.1.call-start = ((), (), s32[]{:S(2)}) async-start(), calls=%async_computation.17 | async-start | bytes 3932160 | tf_op jit(solution)/shard_map/all_gather | solution.py:81
  23.1 138.2 %all-reduce.2.cloned.1.call-start = ((), (), s32[]{:S(2)}) async-start(), calls=%async_computation.16 | async-start | bytes 4194304 | tf_op jit(solution)/shard_map/psum | solution.py:86
  48.2 46.2 %copy-start.6 = (bf16[1,1024,384]{2,1,0:T(8,128)(2,1)S(1)}, bf16[1,1024,384]{2,1,0:T(8,128)(2,1)}, u32[]{:S(2)}) copy-start(bf16[1,1024,384]{2,1,0:T(8,128)(2,1)} %param.10) | copy-start | bytes 2359300
  48.2 49.6 %collective-permute-start = (bf16[8,8,16,128]{3,2,1,0:T(8,128)(2,1)S(1)}, bf16[8,8,16,128]{3,2,1,0:T(8,128)(2,1)S(1)}, u32[]{:S(2)}, u32[]{:S(2)}) collective-permute-start(bf16[8,8,16,128]{3,2,1,0:T(8,128)(2,1)S(1)} %broadcast_select_fusion.6), channel_id=1, source_target_pairs={{0,4},{4,0},{1,5},{5,1},{2,6},{6,2},{3,7},{7,3},{8,12},{12,8},{9,1... | collective-permute-start | bytes 786440 | tf_op jit(solution)/shard_map/ppermute | solution.py:32
  94.5 2.6 copy-start.4
  97.1 12.2 %copy-start.12 = (f32[1,6,2,512]{3,2,1,0:T(2,128)S(1)}, f32[1,6,2,512]{3,2,1,0:T(2,128)}, u32[]{:S(2)}) copy-start(f32[1,6,2,512]{3,2,1,0:T(2,128)} %param.12) | copy-start | bytes 73732
  97.1 64.2 %copy-start.3 = (bf16[16,1024]{1,0:T(8,128)(2,1)S(1)}, bf16[16,1024]{1,0:T(8,128)(2,1)}, u32[]{:S(2)}) copy-start(bf16[16,1024]{1,0:T(8,128)(2,1)} %reduce-scatter.2.cloned.1.call-done) | copy-start | bytes 98308
  98.6 19.7 %all-to-all-start = ((bf16[32,16,128]{2,1,0:T(8,128)(2,1)}), bf16[32,16,128]{2,1,0:T(8,128)(2,1)S(1)}, u32[]{:S(2)}, u32[]{:S(2)}) async-start(bf16[32,16,128]{2,1,0:T(8,128)(2,1)} %bitcast.14), calls=%async_computation.1 | async-start | bytes 262144 | tf_op jit(solution)/shard_map/all_to_all | solution.py:38
  119.0 14.9 %all-to-all-start.1 = ((bf16[32,16,128]{2,1,0:T(8,128)(2,1)}), bf16[32,16,128]{2,1,0:T(8,128)(2,1)S(1)}, u32[]{:S(2)}, u32[]{:S(2)}) async-start(bf16[32,16,128]{2,1,0:T(8,128)(2,1)} %broadcast_in_dim.280), calls=%async_computation.2 | async-start | bytes 262144 | tf_op jit(solution)/shard_map/all_to_all | solution.py:41
  133.9 1.3 collective-permute-start.1
  163.3 37.9 %copy-start.2 = (bf16[1024,1024]{1,0:T(8,128)(2,1)S(1)}, bf16[1024,1024]{1,0:T(8,128)(2,1)}, u32[]{:S(2)}) copy-start(bf16[1024,1024]{1,0:T(8,128)(2,1)} %all-reduce.2.cloned.1.call-done) | copy-start | bytes 6291460
  163.4 1.6 collective-permute-start.2
  199.7 1.3 collective-permute-start.3
  201.2 2.3 copy-start.7
  201.2 2.3 copy-start.8
  201.7 1.6 collective-permute-start.4
  233.0 1.3 collective-permute-start.5
  235.8 1.8 collective-permute-start.6
  267.2 1.4 collective-permute-start.7
  268.7 32.1 %copy-start.9 = (f32[4,16,128]{2,1,0:T(8,128)}, f32[4,16,128]{2,1,0:T(8,128)S(1)}, u32[]{:S(2)}) copy-start(f32[4,16,128]{2,1,0:T(8,128)S(1)} %get-tuple-element.11) | copy-start | bytes 98308
  268.7 32.1 %copy-start.10 = (f32[4,16,128]{2,1,0:T(8,128)}, f32[4,16,128]{2,1,0:T(8,128)S(1)}, u32[]{:S(2)}) copy-start(f32[4,16,128]{2,1,0:T(8,128)S(1)} %get-tuple-element.12) | copy-start | bytes 98308
  269.3 1.8 collective-permute-start.8
  300.9 1.4 collective-permute-start.9
  303.2 32.1 %copy-start.11 = (f32[8,2,4,128]{3,0,2,1:T(8,128)S(1)}, f32[8,2,4,128]{3,0,2,1:T(8,128)}, u32[]{:S(2)}) copy-start(f32[8,2,4,128]{3,0,2,1:T(8,128)} %get-tuple-element.24) | copy-start | bytes 98308
  303.8 1.8 collective-permute-start.10
  335.3 1.3 collective-permute-start.11
  337.2 43.3 %copy-start.5 = (bf16[384,1024]{1,0:T(8,128)(2,1)S(1)}, bf16[384,1024]{1,0:T(8,128)(2,1)}, u32[]{:S(2)}) copy-start(bf16[384,1024]{1,0:T(8,128)(2,1)} %copy-done.4) | copy-start | bytes 2359300
  337.3 1.6 collective-permute-start.12
  367.0 1.3 collective-permute-start.13
Sparse Core Ops, SparseCore 0:
  22.4 24.8 reduce-scatter.1
  49.3 41.8 all-gather.3
  97.2 64.0 all-reduce.1

commit v3 on v2

--- a/solution.py
+++ b/solution.py
@@ -47,6 +47,12 @@
     )
 
 
+def gather_rows(rows, subs):
+    copies = jnp.broadcast_to(rows[None], (subs,) + rows.shape)
+    pieces = lax.all_to_all(copies, "sub", 0, 0, tiled=True)
+    return pieces.reshape((subs * rows.shape[0],) + rows.shape[1:])
+
+
 def local(
     excitation,
     local_inverse,
@@ -68,16 +74,16 @@
     def apply_inverse(shard_rows):
         return jnp.dot(inverse_rows, shard_rows, preferred_element_type=jnp.float32)
 
-    solved = apply_inverse(lax.all_gather(excite_rows, "sub", axis=0, tiled=True))
+    subs = lax.axis_size("sub")
+    solved = apply_inverse(gather_rows(excite_rows, subs))
     solved_half = solved.astype(jnp.bfloat16)
-    incident = lax.psum_scatter(
-        lax.dot_general(
-            solved_half, agg_columns, CONTRACT_FIRST, preferred_element_type=jnp.float32
-        ).astype(jnp.bfloat16),
-        "sub",
-        scatter_dimension=0,
-        tiled=True,
-    ).astype(jnp.float32)
+    partial_incident = lax.dot_general(
+        solved_half, agg_columns, CONTRACT_FIRST, preferred_element_type=jnp.float32
+    ).astype(jnp.bfloat16)
+    incident_pieces = lax.all_to_all(
+        partial_incident.reshape((subs, -1) + partial_incident.shape[1:]), "sub", 0, 0, tiled=True
+    )
+    incident = jnp.sum(incident_pieces.astype(jnp.float32), axis=0)
     spread = apply_inverse(lax.all_gather(disagg_rows, "sub", axis=0, tiled=True))
     spread_half = spread.astype(jnp.bfloat16)
     partial_map = lax.dot_general(
@@ -139,7 +145,7 @@
             axis=0,
         )
     incoming = from_tiles(incoming)
-    fields = lax.all_gather(incoming.astype(jnp.bfloat16), "sub", axis=0, tiled=True)
+    fields = gather_rows(incoming.astype(jnp.bfloat16), subs)
     currents = solved - lax.dot_general(
         spread_half, fields, CONTRACT_LAST, preferred_element_type=jnp.float32
     )

time: 389 us -> 352 us (0.905)
  waiting for transfers between devices: 115 us -> 81.4 us
  blocking collectives: 201 us -> 185 us
  starting transfers between devices: 17.7 us -> 26.4 us
    all_gather x2 -> x0, blocking collectives: 25.1 us -> none  [the longest x1 13.1 us: local(): lax.all_gather(excite_rows, 'sub', axis=0, tiled=True)]
    reduce_scatter x1 -> x0, waiting for transfers between devices: 21 us -> none  [local(): lax.psum_scatter(lax.dot_general(solved_half, agg_columns, CONTRACT_FIRST...]
    all_gather x1, waiting for transfers between devices: 42.8 us -> 22.8 us  [local(): lax.all_gather(disagg_rows, 'sub', axis=0, tiled=True)]
    all_to_all x0 -> x1, blocking collectives: none -> 8.57 us  [gather_rows(): pieces = lax.all_to_all(copies, 'sub', 0, 0, tiled=True)]
    all_to_all x0 -> x2, waiting for transfers between devices: none -> 8.4 us  [the longest x1 7.17 us: local(): lax.all_to_all(partial_incident.reshape((subs, -1) + partial_incident.sha...]
    all_to_all x0 -> x2, starting transfers between devices: none -> 8.04 us  [the longest x1 4.46 us: gather_rows(): pieces = lax.all_to_all(copies, 'sub', 0, 0, tiled=True)]
  transfers between devices with their start and end apart: 19 -> 20, of which waited for: 16 -> 16; matrix products, arithmetic and copies ran while one was open for 3% -> 5% of each run, Pallas kernels for 0% -> 0%
where the time goes in v3:
time: 352 us; the launch traced here: 350 us
  blocking collectives  185 us (53%)
  waiting for transfers between devices  81.4 us (23%)
  starting transfers between devices  26.4 us (8%)
  between operations  25.1 us (7%)
  matrix products  12.3 us (3%)
  other arithmetic  10.8 us (3%)
  local copies, waits for them, and re-layouts  8.86 us (3%)
    all_to_all x6, blocking collectives, share_slots(): lax.all_to_all(mine.reshape((chips,) + tile_shape), 'zx', 0, 0, tiled=True)  94 us
    all_to_all x6, blocking collectives, share_slots(): lax.all_to_all(spread, 'zx', 0, 0, tiled=True).reshape(mine.shape)  82.1 us
    psum x1, waiting for transfers between devices, local(): coupling = lax.psum(partial_map.astype(jnp.bfloat16), 'sub')  25.9 us
    all_gather x1, waiting for transfers between devices, local(): lax.all_gather(disagg_rows, 'sub', axis=0, tiled=True)  22.8 us
    all_to_all x1, starting transfers between devices, share_slots(): lax.all_to_all(mine.reshape((chips,) + tile_shape), 'zx', 0, 0, tiled=True)  10.4 us
    all_to_all x1, waiting for transfers between devices, share_slots(): lax.all_to_all(spread, 'zx', 0, 0, tiled=True).reshape(mine.shape)  8.67 us
    all_to_all x1, blocking collectives, gather_rows(): pieces = lax.all_to_all(copies, 'sub', 0, 0, tiled=True)  8.57 us
    ppermute x7, waiting for transfers between devices, share_slots(): slots = slots + lax.ppermute(slots, 'core', swap)  7.79 us
  transfers between devices with their start and end apart: 20, of which 16 were waited for; matrix products, arithmetic and copies ran while one was open for 5% of the time, Pallas kernels for 0%

profile of v3, /device:TPU:32, one launch (start us, length us, event | category | flops | bytes accessed | tf_op | source)
XLA Modules:
  0.0 349.8 jit_solution(12650105834274853256)
XLA Ops:
  7.3 1.5 broadcast_in_dim.287
  8.8 4.5 %all-to-all-start = ((bf16[4,384,64]{1,2,0:T(8,128)(2,1)}), bf16[4,384,64]{1,2,0:T(8,128)(2,1)S(1)}, u32[]{:S(2)}, u32[]{:S(2)}) async-start(bf16[4,384,64]{1,2,0:T(8,128)(2,1)} %broadcast_in_dim.287), calls=%async_computation | async-start | bytes 393216 | tf_op jit(solution)/shard_map/all_to_all | solution.py:52
  13.2 1.2 dynamic_slice.29
  18.3 1.2 all-to-all-done
  20.1 1.0 convolution_convert_fusion.1
  21.1 3.6 %all-to-all-start.1 = ((bf16[4,16,1024]{2,1,0:T(8,128)(2,1)}), bf16[4,16,1024]{2,1,0:T(8,128)(2,1)S(1)}, u32[]{:S(2)}, u32[]{:S(2)}) async-start(bf16[4,16,1024]{2,1,0:T(8,128)(2,1)} %bitcast.12), calls=%async_computation.1 | async-start | bytes 262144 | tf_op jit(solution)/shard_map/all_to_all | solution.py:83
  24.7 7.2 %all-to-all-done.1 = bf16[4,16,1024]{2,1,0:T(8,128)(2,1)S(1)} async-done(((bf16[4,16,1024]{2,1,0:T(8,128)(2,1)}), bf16[4,16,1024]{2,1,0:T(8,128)(2,1)S(1)}, u32[]{:S(2)}, u32[]{:S(2)}) %all-to-all-start.1) | async-done | bytes 131104 | tf_op jit(solution)/shard_map/all_to_all | solution.py:83
  32.1 22.8 %all-gather.3.cloned.1.call-done = bf16[1,1536,1024]{2,1,0:T(8,128)(2,1)} async-done(((bf16[1,384,1024]{2,1,0:T(8,128)(2,1)}), bf16[1,1536,1024]{2,1,0:T(8,128)(2,1)}) %all-gather.3.cloned.1.call-update) | async-done | bytes 3145744 | tf_op jit(solution)/shard_map/all_gather | solution.py:87
  55.0 3.3 fusion.2
  58.3 2.6 convolution_convert_fusion
  62.4 10.4 %all-to-all-start.2 = ((bf16[32,16,128]{2,1,0:T(8,128)(2,1)}), bf16[32,16,128]{2,1,0:T(8,128)(2,1)S(1)}, u32[]{:S(2)}, u32[]{:S(2)}) async-start(bf16[32,16,128]{2,1,0:T(8,128)(2,1)} %bitcast.15), calls=%async_computation.2 | async-start | bytes 262144 | tf_op jit(solution)/shard_map/all_to_all | solution.py:38
  78.0 4.5 %all-to-all-done.2 = bf16[32,16,128]{2,1,0:T(8,128)(2,1)S(1)} async-done(((bf16[32,16,128]{2,1,0:T(8,128)(2,1)}), bf16[32,16,128]{2,1,0:T(8,128)(2,1)S(1)}, u32[]{:S(2)}, u32[]{:S(2)}) %all-to-all-start.2) | async-done | bytes 131104 | tf_op jit(solution)/shard_map/all_to_all | solution.py:38
  83.2 5.3 %all-to-all-start.3 = ((bf16[32,16,128]{2,1,0:T(8,128)(2,1)}), bf16[32,16,128]{2,1,0:T(8,128)(2,1)S(1)}, u32[]{:S(2)}, u32[]{:S(2)}) async-start(bf16[32,16,128]{2,1,0:T(8,128)(2,1)} %broadcast_in_dim.295), calls=%async_computation.3 | async-start | bytes 262144 | tf_op jit(solution)/shard_map/all_to_all | solution.py:41
  88.6 0.8 select_reduce_fusion
  89.4 8.7 %all-to-all-done.3 = bf16[32,16,128]{2,1,0:T(8,128)(2,1)S(1)} async-done(((bf16[32,16,128]{2,1,0:T(8,128)(2,1)}), bf16[32,16,128]{2,1,0:T(8,128)(2,1)S(1)}, u32[]{:S(2)}, u32[]{:S(2)}) %all-to-all-start.3) | async-done | bytes 131104 | tf_op jit(solution)/shard_map/all_to_all | solution.py:41
  99.5 25.9 %all-reduce.2.cloned.1.call-done = bf16[1024,1024]{1,0:T(8,128)(2,1)} async-done(((bf16[1024,1024]{1,0:T(8,128)(2,1)}), bf16[1024,1024]{1,0:T(8,128)(2,1)}) %all-reduce.2.cloned.1.call-update) | async-done | bytes 2097168 | tf_op jit(solution)/shard_map/psum | solution.py:92
  125.5 2.0 fusion.20
  127.7 1.5 collective-permute-done.2
  129.3 19.8 %all_to_all.85 = bf16[32,16,128]{2,1,0:T(8,128)(2,1)} all-to-all(bf16[32,16,128]{2,1,0:T(8,128)(2,1)S(1)} %bitcast.205), channel_id=1, replica_groups=mesh['zx'=32,'core'=2,'sub'=4] {'zx'}, dimensions={0} | all-to-all | bytes 262144 | tf_op jit(solution)/shard_map/all_to_all | solution.py:38
  149.2 0.9 reduce_sum.304
  150.1 13.7 %all_to_all.86 = bf16[32,16,128]{2,1,0:T(8,128)(2,1)S(1)} all-to-all(bf16[32,16,128]{2,1,0:T(8,128)(2,1)S(1)} %broadcast_in_dim.299), channel_id=1, replica_groups=mesh['zx'=32,'core'=2,'sub'=4] {'zx'}, dimensions={0} | all-to-all | bytes 262144 | tf_op jit(solution)/shard_map/all_to_all | solution.py:41
  163.9 0.7 slice_bitcast_fusion.11
  166.6 1.2 collective-permute-done.4
  167.9 15.1 %all_to_all.87 = bf16[32,16,128]{2,1,0:T(8,128)(2,1)} all-to-all(bf16[32,16,128]{2,1,0:T(8,128)(2,1)S(1)} %bitcast.206), channel_id=1, replica_groups=mesh['zx'=32,'core'=2,'sub'=4] {'zx'}, dimensions={0} | all-to-all | bytes 262144 | tf_op jit(solution)/shard_map/all_to_all | solution.py:38
  183.0 0.9 reduce_sum.309
  183.9 13.7 %all_to_all.88 = bf16[32,16,128]{2,1,0:T(8,128)(2,1)S(1)} all-to-all(bf16[32,16,128]{2,1,0:T(8,128)(2,1)S(1)} %broadcast_in_dim.303), channel_id=1, replica_groups=mesh['zx'=32,'core'=2,'sub'=4] {'zx'}, dimensions={0} | all-to-all | bytes 262144 | tf_op jit(solution)/shard_map/all_to_all | solution.py:41
  199.1 0.8 convert_bitcast_fusion.3
  200.8 1.4 collective-permute-done.6
  202.3 14.8 %all_to_all.89 = bf16[32,16,128]{2,1,0:T(8,128)(2,1)} all-to-all(bf16[32,16,128]{2,1,0:T(8,128)(2,1)S(1)} %bitcast.207), channel_id=1, replica_groups=mesh['zx'=32,'core'=2,'sub'=4] {'zx'}, dimensions={0} | all-to-all | bytes 262144 | tf_op jit(solution)/shard_map/all_to_all | solution.py:38
  217.2 0.9 reduce_sum.314
  218.1 13.7 %all_to_all.90 = bf16[32,16,128]{2,1,0:T(8,128)(2,1)S(1)} all-to-all(bf16[32,16,128]{2,1,0:T(8,128)(2,1)S(1)} %broadcast_in_dim.307), channel_id=1, replica_groups=mesh['zx'=32,'core'=2,'sub'=4] {'zx'}, dimensions={0} | all-to-all | bytes 262144 | tf_op jit(solution)/shard_map/all_to_all | solution.py:41
  231.8 0.7 slice_bitcast_fusion.7
  234.5 1.2 collective-permute-done.8
  235.8 15.1 %all_to_all.91 = bf16[32,16,128]{2,1,0:T(8,128)(2,1)} all-to-all(bf16[32,16,128]{2,1,0:T(8,128)(2,1)S(1)} %bitcast.208), channel_id=1, replica_groups=mesh['zx'=32,'core'=2,'sub'=4] {'zx'}, dimensions={0} | all-to-all | bytes 262144 | tf_op jit(solution)/shard_map/all_to_all | solution.py:38
  250.9 0.9 reduce_sum.319
  251.9 13.7 %all_to_all.92 = bf16[32,16,128]{2,1,0:T(8,128)(2,1)S(1)} all-to-all(bf16[32,16,128]{2,1,0:T(8,128)(2,1)S(1)} %broadcast_in_dim.311), channel_id=1, replica_groups=mesh['zx'=32,'core'=2,'sub'=4] {'zx'}, dimensions={0} | all-to-all | bytes 262144 | tf_op jit(solution)/shard_map/all_to_all | solution.py:41
  265.5 0.7 slice_bitcast_fusion.5
  267.1 0.9 convert_bitcast_fusion.1
  269.1 1.2 collective-permute-done.10
  270.4 15.1 %all_to_all.93 = bf16[32,16,128]{2,1,0:T(8,128)(2,1)} all-to-all(bf16[32,16,128]{2,1,0:T(8,128)(2,1)S(1)} %bitcast.209), channel_id=1, replica_groups=mesh['zx'=32,'core'=2,'sub'=4] {'zx'}, dimensions={0} | all-to-all | bytes 262144 | tf_op jit(solution)/shard_map/all_to_all | solution.py:38
  285.5 0.9 reduce_sum.324
  286.4 13.7 %all_to_all.94 = bf16[32,16,128]{2,1,0:T(8,128)(2,1)S(1)} all-to-all(bf16[32,16,128]{2,1,0:T(8,128)(2,1)S(1)} %broadcast_in_dim.315), channel_id=1, replica_groups=mesh['zx'=32,'core'=2,'sub'=4] {'zx'}, dimensions={0} | all-to-all | bytes 262144 | tf_op jit(solution)/shard_map/all_to_all | solution.py:41
  302.3 1.4 collective-permute-done.12
  303.9 14.1 %all_to_all.95 = bf16[32,16,128]{2,1,0:T(8,128)(2,1)S(1)} all-to-all(bf16[32,16,128]{2,1,0:T(8,128)(2,1)S(1)} %bitcast.204), channel_id=1, replica_groups=mesh['zx'=32,'core'=2,'sub'=4] {'zx'}, dimensions={0} | all-to-all | bytes 262144 | tf_op jit(solution)/shard_map/all_to_all | solution.py:38
  318.1 13.7 %all_to_all.96 = bf16[32,16,128]{2,1,0:T(8,128)(2,1)S(1)} all-to-all(bf16[32,16,128]{2,1,0:T(8,128)(2,1)S(1)} %broadcast_in_dim.319), channel_id=1, replica_groups=mesh['zx'=32,'core'=2,'sub'=4] {'zx'}, dimensions={0} | all-to-all | bytes 262144 | tf_op jit(solution)/shard_map/all_to_all | solution.py:41
  331.8 0.7 slice_bitcast_fusion.1
  333.3 8.6 %all_to_all.97 = bf16[4,16,1024]{2,1,0:T(8,128)(2,1)S(1)} all-to-all(bf16[4,16,1024]{2,1,0:T(8,128)(2,1)S(1)} %broadcast_in_dim.320), channel_id=1, replica_groups=mesh['zx'=32,'core'=2,'sub'=4] {'sub'}, dimensions={0} | all-to-all | bytes 262144 | tf_op jit(solution)/shard_map/all_to_all | solution.py:52
  341.9 1.0 fusion.8
  (163 shorter events, 15.2 us)
Async XLA Ops:
  6.5 13.0 %copy-start = (bf16[1,384,1536]{2,1,0:T(8,128)(2,1)S(1)}, bf16[1,384,1536]{2,1,0:T(8,128)(2,1)}, u32[]{:S(2)}) copy-start(bf16[1,384,1536]{2,1,0:T(8,128)(2,1)} %param.9) | copy-start | bytes 3538948
  6.5 13.6 %copy-start.5 = (bf16[1,1024,384]{2,1,0:T(8,128)(2,1)S(1)}, bf16[1,1024,384]{2,1,0:T(8,128)(2,1)}, u32[]{:S(2)}) copy-start(bf16[1,1024,384]{2,1,0:T(8,128)(2,1)} %param.10) | copy-start | bytes 2359300
  6.5 48.5 %all-gather.3.cloned.1.call-start = ((), (), s32[]{:S(2)}) async-start(), calls=%async_computation.18 | async-start | bytes 3932160 | tf_op jit(solution)/shard_map/all_gather | solution.py:87
  8.8 10.8 %all-to-all-start = ((bf16[4,384,64]{1,2,0:T(8,128)(2,1)}), bf16[4,384,64]{1,2,0:T(8,128)(2,1)S(1)}, u32[]{:S(2)}, u32[]{:S(2)}) async-start(bf16[4,384,64]{1,2,0:T(8,128)(2,1)} %broadcast_in_dim.287), calls=%async_computation | async-start | bytes 393216 | tf_op jit(solution)/shard_map/all_to_all | solution.py:52
  21.1 10.8 %all-to-all-start.1 = ((bf16[4,16,1024]{2,1,0:T(8,128)(2,1)}), bf16[4,16,1024]{2,1,0:T(8,128)(2,1)S(1)}, u32[]{:S(2)}, u32[]{:S(2)}) async-start(bf16[4,16,1024]{2,1,0:T(8,128)(2,1)} %bitcast.12), calls=%async_computation.1 | async-start | bytes 262144 | tf_op jit(solution)/shard_map/all_to_all | solution.py:83
  24.7 100.8 %all-reduce.2.cloned.1.call-start = ((), (), s32[]{:S(2)}) async-start(), calls=%async_computation.17 | async-start | bytes 4194304 | tf_op jit(solution)/shard_map/psum | solution.py:92
  32.0 29.6 %collective-permute-start = (bf16[8,8,16,128]{3,2,1,0:T(8,128)(2,1)S(1)}, bf16[8,8,16,128]{3,2,1,0:T(8,128)(2,1)S(1)}, u32[]{:S(2)}, u32[]{:S(2)}) collective-permute-start(bf16[8,8,16,128]{3,2,1,0:T(8,128)(2,1)S(1)} %broadcast_select_fusion.6), channel_id=1, source_target_pairs={{0,4},{4,0},{1,5},{5,1},{2,6},{6,2},{3,7},{7,3},{8,12},{12,8},{9,1... | collective-permute-start | bytes 786440 | tf_op jit(solution)/shard_map/ppermute | solution.py:32
  58.3 2.7 copy-start.3
  58.3 2.7 copy-start.1
  60.9 12.6 %copy-start.16 = (f32[1,6,2,512]{3,2,1,0:T(2,128)S(1)}, f32[1,6,2,512]{3,2,1,0:T(2,128)}, u32[]{:S(2)}) copy-start(f32[1,6,2,512]{3,2,1,0:T(2,128)} %param.12) | copy-start | bytes 73732
  62.4 20.1 %all-to-all-start.2 = ((bf16[32,16,128]{2,1,0:T(8,128)(2,1)}), bf16[32,16,128]{2,1,0:T(8,128)(2,1)S(1)}, u32[]{:S(2)}, u32[]{:S(2)}) async-start(bf16[32,16,128]{2,1,0:T(8,128)(2,1)} %bitcast.15), calls=%async_computation.2 | async-start | bytes 262144 | tf_op jit(solution)/shard_map/all_to_all | solution.py:38
  83.2 14.9 %all-to-all-start.3 = ((bf16[32,16,128]{2,1,0:T(8,128)(2,1)}), bf16[32,16,128]{2,1,0:T(8,128)(2,1)S(1)}, u32[]{:S(2)}, u32[]{:S(2)}) async-start(bf16[32,16,128]{2,1,0:T(8,128)(2,1)} %broadcast_in_dim.295), calls=%async_computation.3 | async-start | bytes 262144 | tf_op jit(solution)/shard_map/all_to_all | solution.py:41
  98.0 1.3 collective-permute-start.1
  99.5 65.9 %copy-start.7 = (f32[4,16,128]{2,1,0:T(8,128)}, f32[4,16,128]{2,1,0:T(8,128)S(1)}, u32[]{:S(2)}) copy-start(f32[4,16,128]{2,1,0:T(8,128)S(1)} %get-tuple-element.18) | copy-start | bytes 98308
  127.4 38.0 %copy-start.2 = (bf16[1024,1024]{1,0:T(8,128)(2,1)S(1)}, bf16[1024,1024]{1,0:T(8,128)(2,1)}, u32[]{:S(2)}) copy-start(bf16[1024,1024]{1,0:T(8,128)(2,1)} %all-reduce.2.cloned.1.call-done) | copy-start | bytes 6291460
  127.6 1.6 collective-permute-start.2
  163.9 1.4 collective-permute-start.3
  165.4 2.4 copy-start.8
  165.4 2.4 copy-start.9
  166.0 1.8 collective-permute-start.4
  197.6 1.3 collective-permute-start.5
  199.9 33.5 %copy-start.6 = (f32[8,16,128]{2,1,0:T(8,128)}, f32[8,16,128]{2,1,0:T(8,128)S(1)}, u32[]{:S(2)}) copy-start(f32[8,16,128]{2,1,0:T(8,128)S(1)} %get-tuple-element.29) | copy-start | bytes 196612
  200.4 1.8 collective-permute-start.6
  231.8 1.4 collective-permute-start.7
  233.4 2.4 copy-start.11
  233.4 32.1 %copy-start.10 = (f32[4,16,128]{2,1,0:T(8,128)}, f32[4,16,128]{2,1,0:T(8,128)S(1)}, u32[]{:S(2)}) copy-start(f32[4,16,128]{2,1,0:T(8,128)S(1)} %get-tuple-element.11) | copy-start | bytes 98308
  233.9 1.8 collective-permute-start.8
  235.8 31.3 %copy-start.12 = (f32[4,16,128]{2,1,0:T(8,128)S(1)}, f32[4,16,128]{2,1,0:T(8,128)}, u32[]{:S(2)}) copy-start(f32[4,16,128]{2,1,0:T(8,128)} %copy-done.11) | copy-start | bytes 98308
  265.5 1.4 collective-permute-start.9
  268.0 32.1 %copy-start.15 = (f32[8,2,4,128]{3,0,2,1:T(8,128)S(1)}, f32[8,2,4,128]{3,0,2,1:T(8,128)}, u32[]{:S(2)}) copy-start(f32[8,2,4,128]{3,0,2,1:T(8,128)} %get-tuple-element.24) | copy-start | bytes 98308
  268.5 1.8 collective-permute-start.10
  300.1 1.3 collective-permute-start.11
  301.6 2.3 copy-start.13
  302.0 39.9 %copy-start.4 = (bf16[384,1024]{1,0:T(8,128)(2,1)S(1)}, bf16[384,1024]{1,0:T(8,128)(2,1)}, u32[]{:S(2)}) copy-start(bf16[384,1024]{1,0:T(8,128)(2,1)} %copy-done.3) | copy-start | bytes 2359300
  302.1 1.6 collective-permute-start.12
  303.9 29.4 %copy-start.14 = (f32[4,16,128]{2,1,0:T(8,128)S(1)}, f32[4,16,128]{2,1,0:T(8,128)}, u32[]{:S(2)}) copy-start(f32[4,16,128]{2,1,0:T(8,128)} %copy-done.13) | copy-start | bytes 98308
  331.8 1.3 collective-permute-start.13
Sparse Core Ops, SparseCore 0:
  9.2 45.7 all-gather.2
  61.1 64.3 all-reduce.1

commit v4 on v3

--- a/solution.py
+++ b/solution.py
@@ -84,12 +84,25 @@
         partial_incident.reshape((subs, -1) + partial_incident.shape[1:]), "sub", 0, 0, tiled=True
     )
     incident = jnp.sum(incident_pieces.astype(jnp.float32), axis=0)
-    spread = apply_inverse(lax.all_gather(disagg_rows, "sub", axis=0, tiled=True))
+    sub_index = lax.axis_index("sub")
+    block = disagg_rows.shape[0]
+    spread = jnp.zeros((inverse_rows.shape[0], disagg_rows.shape[1]), jnp.float32)
+    for hop in range(subs):
+        if hop == 0:
+            rows = disagg_rows
+        else:
+            rows = lax.ppermute(disagg_rows, "sub", [(i, i ^ hop) for i in range(subs)])
+        columns = lax.dynamic_slice_in_dim(inverse_rows, (sub_index ^ hop) * block, block, axis=1)
+        spread = spread + jnp.dot(columns, rows, preferred_element_type=jnp.float32)
     spread_half = spread.astype(jnp.bfloat16)
     partial_map = lax.dot_general(
         spread_half, agg_columns, CONTRACT_FIRST, preferred_element_type=jnp.float32
+    ).astype(jnp.bfloat16)
+    map_pieces = lax.all_to_all(
+        partial_map.reshape((subs, -1) + partial_map.shape[1:]), "sub", 0, 0, tiled=True
     )
-    coupling = lax.psum(partial_map.astype(jnp.bfloat16), "sub")
+    map_share = jnp.sum(map_pieces.astype(jnp.float32), axis=0).astype(jnp.bfloat16)
+    coupling = gather_rows(map_share, subs)
 
     domains = sweep_order.shape[0]
     members = domains // SEGMENTS

time: 352 us -> 372 us (1.057)
  starting transfers between devices: 26.4 us -> 43.6 us
  between operations: 25.1 us -> 12.7 us
  waiting for transfers between devices: 81.4 us -> 93.1 us
    all_to_all x1 -> x2, waiting for transfers between devices: 1.23 us -> 45.8 us  [gather_rows(): pieces = lax.all_to_all(copies, 'sub', 0, 0, tiled=True)]
    psum x1 -> x0, waiting for transfers between devices: 25.9 us -> none  [local(): coupling = lax.psum(partial_map.astype(jnp.bfloat16), 'sub')]
    all_to_all x0 -> x1, waiting for transfers between devices: none -> 25 us  [local(): lax.all_to_all(partial_map.reshape((subs, -1) + partial_map.shape[1:]), '...]
    all_gather x1 -> x0, waiting for transfers between devices: 22.8 us -> none  [local(): lax.all_gather(disagg_rows, 'sub', axis=0, tiled=True)]
    dot_general x0 -> x4, matrix products: none -> 7.04 us  [local(): spread = spread + jnp.dot(columns, rows, preferred_element_type=jnp.float32)]
    all_to_all x1, waiting for transfers between devices: 8.67 us -> 2.03 us  [share_slots(): lax.all_to_all(spread, 'zx', 0, 0, tiled=True).reshape(mine.shape)]
    all_to_all x0 -> x1, starting transfers between devices: none -> 4.59 us  [local(): lax.all_to_all(partial_map.reshape((subs, -1) + partial_map.shape[1:]), '...]
    ppermute x0 -> x3, starting transfers between devices: none -> 4.25 us  [local(): rows = lax.ppermute(disagg_rows, 'sub', [(i, i ^ hop) for i in range(subs)])]
  transfers between devices with their start and end apart: 20 -> 23, of which waited for: 16 -> 18; matrix products, arithmetic and copies ran while one was open for 5% -> 6% of each run, Pallas kernels for 0% -> 0%
where the time goes in v4:
time: 372 us; the launch traced here: 369 us
  blocking collectives  183 us (49%)
  waiting for transfers between devices  93.1 us (25%)
  starting transfers between devices  43.6 us (12%)
  matrix products  14.6 us (4%)
  other arithmetic  13.3 us (4%)
  between operations  12.7 us (3%)
  local copies, waits for them, and re-layouts  9.21 us (2%)
    all_to_all x6, blocking collectives, share_slots(): lax.all_to_all(mine.reshape((chips,) + tile_shape), 'zx', 0, 0, tiled=True)  92.3 us
    all_to_all x6, blocking collectives, share_slots(): lax.all_to_all(spread, 'zx', 0, 0, tiled=True).reshape(mine.shape)  82.2 us
    all_to_all x2, waiting for transfers between devices, gather_rows(): pieces = lax.all_to_all(copies, 'sub', 0, 0, tiled=True)  45.8 us
    all_to_all x1, waiting for transfers between devices, local(): lax.all_to_all(partial_map.reshape((subs, -1) + partial_map.shape[1:]), '...  25 us
    all_to_all x1, starting transfers between devices, share_slots(): lax.all_to_all(mine.reshape((chips,) + tile_shape), 'zx', 0, 0, tiled=True)  11.2 us
    all_to_all x1, starting transfers between devices, share_slots(): lax.all_to_all(spread, 'zx', 0, 0, tiled=True).reshape(mine.shape)  9.44 us
    all_to_all x1, blocking collectives, gather_rows(): pieces = lax.all_to_all(copies, 'sub', 0, 0, tiled=True)  8.36 us
    ppermute x7, waiting for transfers between devices, share_slots(): slots = slots + lax.ppermute(slots, 'core', swap)  8.24 us
  transfers between devices with their start and end apart: 23, of which 18 were waited for; matrix products, arithmetic and copies ran while one was open for 6% of the time, Pallas kernels for 0%

profile of v4, /device:TPU:32, one launch (start us, length us, event | category | flops | bytes accessed | tf_op | source)
XLA Modules:
  0.0 369.2 jit_solution(7070830581616124504)
XLA Ops:
  0.0 3.2 collective-permute-start.1
  4.3 1.5 broadcast_in_dim.293
  5.7 4.3 %all-to-all-start = ((bf16[4,384,64]{1,2,0:T(8,128)(2,1)}), bf16[4,384,64]{1,2,0:T(8,128)(2,1)S(1)}, u32[]{:S(2)}, u32[]{:S(2)}) async-start(bf16[4,384,64]{1,2,0:T(8,128)(2,1)} %broadcast_in_dim.293), calls=%async_computation | async-start | bytes 393216 | tf_op jit(solution)/shard_map/all_to_all | solution.py:52
  10.1 1.2 dynamic_slice.57
  14.7 25.3 %all-to-all-done = bf16[4,384,64]{1,2,0:T(8,128)(2,1)S(1)} async-done(((bf16[4,384,64]{1,2,0:T(8,128)(2,1)}), bf16[4,384,64]{1,2,0:T(8,128)(2,1)S(1)}, u32[]{:S(2)}, u32[]{:S(2)}) %all-to-all-start) | async-done | bytes 196640 | tf_op jit(solution)/shard_map/all_to_all | solution.py:52
  40.6 1.0 convolution_convert_fusion.1
  41.6 4.5 %all-to-all-start.1 = ((bf16[4,16,1024]{2,1,0:T(8,128)(2,1)}), bf16[4,16,1024]{2,1,0:T(8,128)(2,1)S(1)}, u32[]{:S(2)}, u32[]{:S(2)}) async-start(bf16[4,16,1024]{2,1,0:T(8,128)(2,1)} %bitcast.16), calls=%async_computation.1 | async-start | bytes 262144 | tf_op jit(solution)/shard_map/all_to_all | solution.py:83
  46.1 6.0 %all-to-all-done.1 = bf16[4,16,1024]{2,1,0:T(8,128)(2,1)S(1)} async-done(((bf16[4,16,1024]{2,1,0:T(8,128)(2,1)}), bf16[4,16,1024]{2,1,0:T(8,128)(2,1)S(1)}, u32[]{:S(2)}, u32[]{:S(2)}) %all-to-all-start.1) | async-done | bytes 131104 | tf_op jit(solution)/shard_map/all_to_all | solution.py:83
  52.3 1.7 fusion.25
  54.8 11.2 %all-to-all-start.2 = ((bf16[32,16,128]{2,1,0:T(8,128)(2,1)}), bf16[32,16,128]{2,1,0:T(8,128)(2,1)S(1)}, u32[]{:S(2)}, u32[]{:S(2)}) async-start(bf16[32,16,128]{2,1,0:T(8,128)(2,1)} %bitcast.19), calls=%async_computation.2 | async-start | bytes 262144 | tf_op jit(solution)/shard_map/all_to_all | solution.py:38
  66.0 1.7 fusion.21
  67.7 1.7 fusion.23
  69.4 1.9 add_convert_fusion
  72.2 2.7 convolution_convert_fusion
  74.9 1.3 all-to-all-done.2
  76.2 4.6 %all-to-all-start.4 = ((bf16[4,256,1024]{2,1,0:T(8,128)(2,1)}), bf16[4,256,1024]{2,1,0:T(8,128)(2,1)}, u32[]{:S(2)}, u32[]{:S(2)}) async-start(bf16[4,256,1024]{2,1,0:T(8,128)(2,1)} %bitcast.215), calls=%async_computation.4 | async-start | bytes 4194304 | tf_op jit(solution)/shard_map/all_to_all | solution.py:101
  81.6 25.0 %all-to-all-done.4 = bf16[4,256,1024]{2,1,0:T(8,128)(2,1)} async-done(((bf16[4,256,1024]{2,1,0:T(8,128)(2,1)}), bf16[4,256,1024]{2,1,0:T(8,128)(2,1)}, u32[]{:S(2)}, u32[]{:S(2)}) %all-to-all-start.4) | async-done | bytes 2097184 | tf_op jit(solution)/shard_map/all_to_all | solution.py:101
  107.3 9.4 %all-to-all-start.3 = ((bf16[32,16,128]{2,1,0:T(8,128)(2,1)}), bf16[32,16,128]{2,1,0:T(8,128)(2,1)S(1)}, u32[]{:S(2)}, u32[]{:S(2)}) async-start(bf16[32,16,128]{2,1,0:T(8,128)(2,1)} %broadcast_in_dim.301), calls=%async_computation.3 | async-start | bytes 262144 | tf_op jit(solution)/shard_map/all_to_all | solution.py:41
  122.3 2.0 reduce_sum.316
  124.3 2.0 all-to-all-done.3
  126.3 1.6 broadcast_in_dim.304
  127.9 3.6 all-to-all-start.5
  134.2 1.1 fusion.31
  135.4 20.5 %all-to-all-done.5 = bf16[4,256,1024]{2,1,0:T(8,128)(2,1)S(1)} async-done(((bf16[4,256,1024]{2,1,0:T(8,128)(2,1)}), bf16[4,256,1024]{2,1,0:T(8,128)(2,1)S(1)}, u32[]{:S(2)}, u32[]{:S(2)}) %all-to-all-start.5) | async-done | bytes 2097184 | tf_op jit(solution)/shard_map/all_to_all | solution.py:52
  156.5 1.5 collective-permute-done.5
  158.2 18.4 %all_to_all.95 = bf16[32,16,128]{2,1,0:T(8,128)(2,1)} all-to-all(bf16[32,16,128]{2,1,0:T(8,128)(2,1)S(1)} %bitcast.230), channel_id=1, replica_groups=mesh['zx'=32,'core'=2,'sub'=4] {'zx'}, dimensions={0} | all-to-all | bytes 262144 | tf_op jit(solution)/shard_map/all_to_all | solution.py:38
  176.6 0.9 reduce_sum.317
  177.6 13.7 %all_to_all.96 = bf16[32,16,128]{2,1,0:T(8,128)(2,1)S(1)} all-to-all(bf16[32,16,128]{2,1,0:T(8,128)(2,1)S(1)} %broadcast_in_dim.306), channel_id=1, replica_groups=mesh['zx'=32,'core'=2,'sub'=4] {'zx'}, dimensions={0} | all-to-all | bytes 262144 | tf_op jit(solution)/shard_map/all_to_all | solution.py:41
  194.1 1.2 collective-permute-done.7
  195.4 15.1 %all_to_all.97 = bf16[32,16,128]{2,1,0:T(8,128)(2,1)} all-to-all(bf16[32,16,128]{2,1,0:T(8,128)(2,1)S(1)} %bitcast.231), channel_id=1, replica_groups=mesh['zx'=32,'core'=2,'sub'=4] {'zx'}, dimensions={0} | all-to-all | bytes 262144 | tf_op jit(solution)/shard_map/all_to_all | solution.py:38
  210.4 0.9 reduce_sum.322
  211.4 13.7 %all_to_all.98 = bf16[32,16,128]{2,1,0:T(8,128)(2,1)S(1)} all-to-all(bf16[32,16,128]{2,1,0:T(8,128)(2,1)S(1)} %broadcast_in_dim.310), channel_id=1, replica_groups=mesh['zx'=32,'core'=2,'sub'=4] {'zx'}, dimensions={0} | all-to-all | bytes 262144 | tf_op jit(solution)/shard_map/all_to_all | solution.py:41
  228.1 1.4 collective-permute-done.9
  229.6 14.8 %all_to_all.99 = bf16[32,16,128]{2,1,0:T(8,128)(2,1)} all-to-all(bf16[32,16,128]{2,1,0:T(8,128)(2,1)S(1)} %bitcast.232), channel_id=1, replica_groups=mesh['zx'=32,'core'=2,'sub'=4] {'zx'}, dimensions={0} | all-to-all | bytes 262144 | tf_op jit(solution)/shard_map/all_to_all | solution.py:38
  245.5 13.7 %all_to_all.100 = bf16[32,16,128]{2,1,0:T(8,128)(2,1)S(1)} all-to-all(bf16[32,16,128]{2,1,0:T(8,128)(2,1)S(1)} %broadcast_in_dim.314), channel_id=1, replica_groups=mesh['zx'=32,'core'=2,'sub'=4] {'zx'}, dimensions={0} | all-to-all | bytes 262144 | tf_op jit(solution)/shard_map/all_to_all | solution.py:41
  261.4 1.4 collective-permute-done.11
  262.9 14.8 %all_to_all.101 = bf16[32,16,128]{2,1,0:T(8,128)(2,1)} all-to-all(bf16[32,16,128]{2,1,0:T(8,128)(2,1)S(1)} %bitcast.233), channel_id=1, replica_groups=mesh['zx'=32,'core'=2,'sub'=4] {'zx'}, dimensions={0} | all-to-all | bytes 262144 | tf_op jit(solution)/shard_map/all_to_all | solution.py:38
  277.7 0.9 reduce_sum.332
  278.7 13.7 %all_to_all.102 = bf16[32,16,128]{2,1,0:T(8,128)(2,1)S(1)} all-to-all(bf16[32,16,128]{2,1,0:T(8,128)(2,1)S(1)} %broadcast_in_dim.318), channel_id=1, replica_groups=mesh['zx'=32,'core'=2,'sub'=4] {'zx'}, dimensions={0} | all-to-all | bytes 262144 | tf_op jit(solution)/shard_map/all_to_all | solution.py:41
  295.5 1.4 collective-permute-done.13
  297.0 14.8 %all_to_all.103 = bf16[32,16,128]{2,1,0:T(8,128)(2,1)} all-to-all(bf16[32,16,128]{2,1,0:T(8,128)(2,1)S(1)} %bitcast.234), channel_id=1, replica_groups=mesh['zx'=32,'core'=2,'sub'=4] {'zx'}, dimensions={0} | all-to-all | bytes 262144 | tf_op jit(solution)/shard_map/all_to_all | solution.py:38
  312.8 13.7 %all_to_all.104 = bf16[32,16,128]{2,1,0:T(8,128)(2,1)S(1)} all-to-all(bf16[32,16,128]{2,1,0:T(8,128)(2,1)S(1)} %broadcast_in_dim.322), channel_id=1, replica_groups=mesh['zx'=32,'core'=2,'sub'=4] {'zx'}, dimensions={0} | all-to-all | bytes 262144 | tf_op jit(solution)/shard_map/all_to_all | solution.py:41
  328.7 1.4 collective-permute-done.15
  330.3 14.3 %all_to_all.105 = bf16[32,16,128]{2,1,0:T(8,128)(2,1)S(1)} all-to-all(bf16[32,16,128]{2,1,0:T(8,128)(2,1)S(1)} %bitcast.229), channel_id=1, replica_groups=mesh['zx'=32,'core'=2,'sub'=4] {'zx'}, dimensions={0} | all-to-all | bytes 262144 | tf_op jit(solution)/shard_map/all_to_all | solution.py:38
  344.6 13.7 %all_to_all.106 = bf16[32,16,128]{2,1,0:T(8,128)(2,1)S(1)} all-to-all(bf16[32,16,128]{2,1,0:T(8,128)(2,1)S(1)} %broadcast_in_dim.326), channel_id=1, replica_groups=mesh['zx'=32,'core'=2,'sub'=4] {'zx'}, dimensions={0} | all-to-all | bytes 262144 | tf_op jit(solution)/shard_map/all_to_all | solution.py:41
  358.4 1.3 collective-permute-done.16
  359.8 8.4 %all_to_all.107 = bf16[4,16,1024]{2,1,0:T(8,128)(2,1)S(1)} all-to-all(bf16[4,16,1024]{2,1,0:T(8,128)(2,1)S(1)} %broadcast_in_dim.327), channel_id=1, replica_groups=mesh['zx'=32,'core'=2,'sub'=4] {'sub'}, dimensions={0} | all-to-all | bytes 262144 | tf_op jit(solution)/shard_map/all_to_all | solution.py:52
  368.2 1.0 fusion.2
  (186 shorter events, 21.2 us)
Async XLA Ops:
  0.0 40.0 %copy-start = (bf16[1,384,1536]{2,1,0:T(8,128)(2,1)S(1)}, bf16[1,384,1536]{2,1,0:T(8,128)(2,1)}, u32[]{:S(2)}) copy-start(bf16[1,384,1536]{2,1,0:T(8,128)(2,1)} %param.9) | copy-start | bytes 3538948
  0.0 40.6 %copy-start.4 = (bf16[1,1024,384]{2,1,0:T(8,128)(2,1)S(1)}, bf16[1,1024,384]{2,1,0:T(8,128)(2,1)}, u32[]{:S(2)}) copy-start(bf16[1,1024,384]{2,1,0:T(8,128)(2,1)} %param.10) | copy-start | bytes 2359300
  0.0 66.0 %collective-permute-start.1 = (bf16[384,1024]{1,0:T(8,128)(2,1)}, bf16[384,1024]{1,0:T(8,128)(2,1)}, u32[]{:S(2)}, u32[]{:S(2)}) collective-permute-start(bf16[384,1024]{1,0:T(8,128)(2,1)} %bitcast.217), channel_id=1, source_target_pairs={{0,2},{1,3},{2,0},{3,1},{4,6},{5,7},{6,4},{7,5},{8,10},{9,11},{10,... | collective-permute-start | bytes 2359304 | tf_op jit(solution)/shard_map/ppermute | solution.py:94
  3.2 64.5 %collective-permute-start = (bf16[384,1024]{1,0:T(8,128)(2,1)}, bf16[384,1024]{1,0:T(8,128)(2,1)}, u32[]{:S(2)}, u32[]{:S(2)}) collective-permute-start(bf16[384,1024]{1,0:T(8,128)(2,1)} %bitcast.218), channel_id=1, source_target_pairs={{0,1},{1,0},{2,3},{3,2},{4,5},{5,4},{6,7},{7,6},{8,9},{9,8},{10,11... | collective-permute-start | bytes 2359304 | tf_op jit(solution)/shard_map/ppermute | solution.py:94
  3.9 65.6 %collective-permute-start.2 = (bf16[384,1024]{1,0:T(8,128)(2,1)}, bf16[384,1024]{1,0:T(8,128)(2,1)}, u32[]{:S(2)}, u32[]{:S(2)}) collective-permute-start(bf16[384,1024]{1,0:T(8,128)(2,1)} %bitcast.219), channel_id=1, source_target_pairs={{0,3},{1,2},{2,1},{3,0},{4,7},{5,6},{6,5},{7,4},{8,11},{9,10},{10,... | collective-permute-start | bytes 2359304 | tf_op jit(solution)/shard_map/ppermute | solution.py:94
  5.7 34.3 %all-to-all-start = ((bf16[4,384,64]{1,2,0:T(8,128)(2,1)}), bf16[4,384,64]{1,2,0:T(8,128)(2,1)S(1)}, u32[]{:S(2)}, u32[]{:S(2)}) async-start(bf16[4,384,64]{1,2,0:T(8,128)(2,1)} %broadcast_in_dim.293), calls=%async_computation | async-start | bytes 393216 | tf_op jit(solution)/shard_map/all_to_all | solution.py:52
  41.6 10.4 %all-to-all-start.1 = ((bf16[4,16,1024]{2,1,0:T(8,128)(2,1)}), bf16[4,16,1024]{2,1,0:T(8,128)(2,1)S(1)}, u32[]{:S(2)}, u32[]{:S(2)}) async-start(bf16[4,16,1024]{2,1,0:T(8,128)(2,1)} %bitcast.16), calls=%async_computation.1 | async-start | bytes 262144 | tf_op jit(solution)/shard_map/all_to_all | solution.py:83
  52.2 1.8 collective-permute-start.3
  54.8 21.4 %all-to-all-start.2 = ((bf16[32,16,128]{2,1,0:T(8,128)(2,1)}), bf16[32,16,128]{2,1,0:T(8,128)(2,1)S(1)}, u32[]{:S(2)}, u32[]{:S(2)}) async-start(bf16[32,16,128]{2,1,0:T(8,128)(2,1)} %bitcast.19), calls=%async_computation.2 | async-start | bytes 262144 | tf_op jit(solution)/shard_map/all_to_all | solution.py:38
  69.4 2.8 copy-start.5
  71.4 0.9 copy-start.2
  76.2 5.3 %copy-start.22 = (f32[1,6,2,512]{3,2,1,0:T(2,128)S(1)}, f32[1,6,2,512]{3,2,1,0:T(2,128)}, u32[]{:S(2)}) copy-start(f32[1,6,2,512]{3,2,1,0:T(2,128)} %param.12) | copy-start | bytes 73732
  76.2 40.5 %copy-start.23 = (s32[1,6]{1,0:T(1,128)S(1)}, s32[1,6]{1,0:T(1,128)}, u32[]{:S(2)}) copy-start(s32[1,6]{1,0:T(1,128)} %param.13) | copy-start | bytes 76
  76.2 40.6 %copy-start.1 = (s32[64]{0:T(128)S(1)}, s32[64]{0:T(128)}, u32[]{:S(2)}) copy-start(s32[64]{0:T(128)} %param.15) | copy-start | bytes 772
  76.2 30.4 %all-to-all-start.4 = ((bf16[4,256,1024]{2,1,0:T(8,128)(2,1)}), bf16[4,256,1024]{2,1,0:T(8,128)(2,1)}, u32[]{:S(2)}, u32[]{:S(2)}) async-start(bf16[4,256,1024]{2,1,0:T(8,128)(2,1)} %bitcast.215), calls=%async_computation.4 | async-start | bytes 4194304 | tf_op jit(solution)/shard_map/all_to_all | solution.py:101
  107.3 19.0 %all-to-all-start.3 = ((bf16[32,16,128]{2,1,0:T(8,128)(2,1)}), bf16[32,16,128]{2,1,0:T(8,128)(2,1)S(1)}, u32[]{:S(2)}, u32[]{:S(2)}) async-start(bf16[32,16,128]{2,1,0:T(8,128)(2,1)} %broadcast_in_dim.301), calls=%async_computation.3 | async-start | bytes 262144 | tf_op jit(solution)/shard_map/all_to_all | solution.py:41
  126.3 1.6 copy-start.8
  127.9 28.0 %all-to-all-start.5 = ((bf16[4,256,1024]{2,1,0:T(8,128)(2,1)}), bf16[4,256,1024]{2,1,0:T(8,128)(2,1)S(1)}, u32[]{:S(2)}, u32[]{:S(2)}) async-start(bf16[4,256,1024]{2,1,0:T(8,128)(2,1)} %broadcast_in_dim.304), calls=%async_computation.5 | async-start | bytes 4194304 | tf_op jit(solution)/shard_map/all_to_all | solution.py:52
  132.5 1.7 collective-permute-start.4
  135.4 57.5 %copy-start.7 = (f32[4,16,128]{2,1,0:T(8,128)}, f32[4,16,128]{2,1,0:T(8,128)S(1)}, u32[]{:S(2)}) copy-start(f32[4,16,128]{2,1,0:T(8,128)S(1)} %get-tuple-element.18) | copy-start | bytes 98308
  156.4 1.6 collective-permute-start.5
  191.3 1.5 collective-permute-start.6
  192.9 2.4 copy-start.9
  192.9 2.4 copy-start.11
  193.4 31.7 %copy-start.21 = (f32[8,2,4,128]{3,0,2,1:T(8,128)S(1)}, f32[8,2,4,128]{3,0,2,1:T(8,128)}, u32[]{:S(2)}) copy-start(f32[8,2,4,128]{3,0,2,1:T(8,128)} %get-tuple-element.21) | copy-start | bytes 98308
  193.5 1.8 collective-permute-start.7
  211.4 15.2 %copy-start.10 = (f32[4,16,128]{2,1,0:T(8,128)S(1)}, f32[4,16,128]{2,1,0:T(8,128)}, u32[]{:S(2)}) copy-start(f32[4,16,128]{2,1,0:T(8,128)} %copy-done.9) | copy-start | bytes 98308
  211.4 15.2 %copy-start.12 = (f32[4,16,128]{2,1,0:T(8,128)S(1)}, f32[4,16,128]{2,1,0:T(8,128)}, u32[]{:S(2)}) copy-start(f32[4,16,128]{2,1,0:T(8,128)} %copy-done.11) | copy-start | bytes 98308
  225.1 1.3 collective-permute-start.8
  227.4 33.2 %copy-start.6 = (f32[8,16,128]{2,1,0:T(8,128)}, f32[8,16,128]{2,1,0:T(8,128)S(1)}, u32[]{:S(2)}) copy-start(f32[8,16,128]{2,1,0:T(8,128)S(1)} %get-tuple-element.29) | copy-start | bytes 196612
  227.8 31.4 %copy-start.20 = (f32[8,2,4,128]{3,0,2,1:T(8,128)S(1)}, f32[8,2,4,128]{3,0,2,1:T(8,128)}, u32[]{:S(2)}) copy-start(f32[8,2,4,128]{3,0,2,1:T(8,128)} %get-tuple-element.22) | copy-start | bytes 98308
  227.9 1.6 collective-permute-start.9
  259.1 1.3 collective-permute-start.10
  260.6 2.3 copy-start.13
  261.0 31.4 %copy-start.19 = (f32[8,2,4,128]{3,0,2,1:T(8,128)S(1)}, f32[8,2,4,128]{3,0,2,1:T(8,128)}, u32[]{:S(2)}) copy-start(f32[8,2,4,128]{3,0,2,1:T(8,128)} %get-tuple-element.23) | copy-start | bytes 98308
  261.1 1.6 collective-permute-start.11
  278.7 15.2 %copy-start.14 = (f32[4,16,128]{2,1,0:T(8,128)S(1)}, f32[4,16,128]{2,1,0:T(8,128)}, u32[]{:S(2)}) copy-start(f32[4,16,128]{2,1,0:T(8,128)} %copy-done.13) | copy-start | bytes 98308
  292.4 1.3 collective-permute-start.12
  295.1 31.4 %copy-start.18 = (f32[8,2,4,128]{3,0,2,1:T(8,128)S(1)}, f32[8,2,4,128]{3,0,2,1:T(8,128)}, u32[]{:S(2)}) copy-start(f32[8,2,4,128]{3,0,2,1:T(8,128)} %get-tuple-element.24) | copy-start | bytes 98308
  295.2 1.6 collective-permute-start.13
  326.5 1.3 collective-permute-start.14
  327.9 2.3 copy-start.15
  328.4 30.0 %copy-start.17 = (f32[8,2,4,128]{3,0,2,1:T(8,128)S(1)}, f32[8,2,4,128]{3,0,2,1:T(8,128)}, u32[]{:S(2)}) copy-start(f32[8,2,4,128]{3,0,2,1:T(8,128)} %get-tuple-element.19) | copy-start | bytes 98308
  328.5 1.6 collective-permute-start.15
  330.2 29.6 %copy-start.16 = (f32[4,16,128]{2,1,0:T(8,128)S(1)}, f32[4,16,128]{2,1,0:T(8,128)}, u32[]{:S(2)}) copy-start(f32[4,16,128]{2,1,0:T(8,128)} %copy-done.15) | copy-start | bytes 98308
  330.2 38.0 %copy-start.3 = (bf16[384,1024]{1,0:T(8,128)(2,1)S(1)}, bf16[384,1024]{1,0:T(8,128)(2,1)}, u32[]{:S(2)}) copy-start(bf16[384,1024]{1,0:T(8,128)(2,1)} %copy-done.2) | copy-start | bytes 2359300
  358.3 1.3 collective-permute-start.16

commit v5 on v3

--- a/solution.py
+++ b/solution.py
@@ -28,23 +28,15 @@
 
 
 def share_slots(slots, chips):
-    swap = [(0, 1), (1, 0)]
-    slots = slots + lax.ppermute(slots, "core", swap)
-    core = lax.axis_index("core")
-    count = slots.shape[0]
-    halves = slots.reshape((CORES, count // CORES) + slots.shape[1:])
-    mine = lax.dynamic_index_in_dim(halves, core, 0, keepdims=False)
-    tile_shape = mine.shape[2:]
-    pieces = lax.all_to_all(mine.reshape((chips,) + tile_shape), "zx", 0, 0, tiled=True)
-    total = jnp.sum(pieces, axis=0, keepdims=True)
-    spread = jnp.broadcast_to(total, (chips,) + tile_shape)
-    gathered = lax.all_to_all(spread, "zx", 0, 0, tiled=True).reshape(mine.shape)
-    other = lax.ppermute(gathered, "core", swap)
-    return jnp.where(
-        core == 0,
-        jnp.concatenate([gathered, other]),
-        jnp.concatenate([other, gathered]),
-    )
+    shape = slots.shape
+    tile_shape = shape[-2:]
+    per_chip = slots.reshape((chips, -1) + tile_shape)
+    pieces = lax.all_to_all(per_chip, "zx", 0, 0, tiled=True)
+    total = jnp.sum(pieces, axis=0)
+    total = total + lax.ppermute(total, "core", [(0, 1), (1, 0)])
+    spread = jnp.broadcast_to(total[None], per_chip.shape)
+    gathered = lax.all_to_all(spread, "zx", 0, 0, tiled=True)
+    return gathered.reshape(shape)
 
 
 def gather_rows(rows, subs):

time: 352 us -> 387 us (1.099)
  blocking collectives: 185 us -> 110 us
  waiting for transfers between devices: 81.4 us -> 144 us
  starting transfers between devices: 26.4 us -> 54.6 us
  local copies, waits for them, and re-layouts: 8.86 us -> 19.3 us
  other arithmetic: 10.8 us -> 20 us
    all_to_all x12 -> x6, blocking collectives: 176 us -> 102 us  [share_slots(): pieces = lax.all_to_all(per_chip, 'zx', 0, 0, tiled=True)]
    all_to_all x2 -> x8, waiting for transfers between devices: 13.2 us -> 86.3 us  [the longest x7 75.5 us: share_slots(): gathered = lax.all_to_all(spread, 'zx', 0, 0, tiled=True)]
    all_to_all x2 -> x8, starting transfers between devices: 15.7 us -> 46.1 us  [the longest x7 35.7 us: share_slots(): gathered = lax.all_to_all(spread, 'zx', 0, 0, tiled=True)]
    broadcast_in_dim x7 -> x28, local copies, waits for them, and re-layouts: 0.8 us -> 10.1 us  [the longest x7 5.17 us: share_slots(): spread = jnp.broadcast_to(total[None], per_chip.shape)]
    psum x1, waiting for transfers between devices: 25.9 us -> 18.5 us  [local(): coupling = lax.psum(partial_map.astype(jnp.bfloat16), 'sub')]
    convert_element_type x7, other arithmetic: 0.28 us -> 5 us  [local(): slots = share_slots(slots, chips).astype(jnp.float32)]
    ppermute x14 -> x7, waiting for transfers between devices: 10.4 us -> 6.96 us  [share_slots(): total = total + lax.ppermute(total, 'core', [(0, 1), (1, 0)])]
  transfers between devices with their start and end apart: 20 -> 19, of which waited for: 16 -> 18; matrix products, arithmetic and copies ran while one was open for 5% -> 5% of each run, Pallas kernels for 0% -> 0%
where the time goes in v5:
time: 387 us; the launch traced here: 385 us
  waiting for transfers between devices  144 us (37%)
  blocking collectives  110 us (28%)
  starting transfers between devices  54.6 us (14%)
  between operations  24.1 us (6%)
  other arithmetic  20 us (5%)
  local copies, waits for them, and re-layouts  19.3 us (5%)
  matrix products  12.3 us (3%)
    all_to_all x6, blocking collectives, share_slots(): pieces = lax.all_to_all(per_chip, 'zx', 0, 0, tiled=True)  102 us
    all_to_all x7, waiting for transfers between devices, share_slots(): gathered = lax.all_to_all(spread, 'zx', 0, 0, tiled=True)  75.5 us
    all_to_all x7, starting transfers between devices, share_slots(): gathered = lax.all_to_all(spread, 'zx', 0, 0, tiled=True)  35.7 us
    all_gather x1, waiting for transfers between devices, local(): lax.all_gather(disagg_rows, 'sub', axis=0, tiled=True)  23.2 us
    psum x1, waiting for transfers between devices, local(): coupling = lax.psum(partial_map.astype(jnp.bfloat16), 'sub')  18.5 us
    all_to_all x1, waiting for transfers between devices, share_slots(): pieces = lax.all_to_all(per_chip, 'zx', 0, 0, tiled=True)  10.8 us
    all_to_all x1, starting transfers between devices, share_slots(): pieces = lax.all_to_all(per_chip, 'zx', 0, 0, tiled=True)  10.5 us
    all_to_all x1, blocking collectives, gather_rows(): pieces = lax.all_to_all(copies, 'sub', 0, 0, tiled=True)  8.57 us
  transfers between devices with their start and end apart: 19, of which 18 were waited for; matrix products, arithmetic and copies ran while one was open for 5% of the time, Pallas kernels for 0%

profile of v5, /device:TPU:32, one launch (start us, length us, event | category | flops | bytes accessed | tf_op | source)
XLA Modules:
  0.0 384.9 jit_solution(6606111834428144270)
XLA Ops:
  7.3 1.5 broadcast_in_dim.329
  8.8 4.5 %all-to-all-start = ((bf16[4,384,64]{1,2,0:T(8,128)(2,1)}), bf16[4,384,64]{1,2,0:T(8,128)(2,1)S(1)}, u32[]{:S(2)}, u32[]{:S(2)}) async-start(bf16[4,384,64]{1,2,0:T(8,128)(2,1)} %broadcast_in_dim.329), calls=%async_computation | async-start | bytes 393216 | tf_op jit(solution)/shard_map/all_to_all | solution.py:44
  13.2 1.3 dynamic_slice.7
  18.2 1.4 all-to-all-done
  20.1 1.0 convolution_convert_fusion.1
  21.1 3.4 all-to-all-start.1
  24.7 7.0 %all-to-all-done.1 = bf16[4,16,1024]{2,1,0:T(8,128)(2,1)S(1)} async-done(((bf16[4,16,1024]{2,1,0:T(8,128)(2,1)}), bf16[4,16,1024]{2,1,0:T(8,128)(2,1)S(1)}, u32[]{:S(2)}, u32[]{:S(2)}) %all-to-all-start.1) | async-done | bytes 131104 | tf_op jit(solution)/shard_map/all_to_all | solution.py:75
  31.8 23.2 %all-gather.3.cloned.1.call-done = bf16[1,1536,1024]{2,1,0:T(8,128)(2,1)} async-done(((bf16[1,384,1024]{2,1,0:T(8,128)(2,1)}), bf16[1,1536,1024]{2,1,0:T(8,128)(2,1)}) %all-gather.3.cloned.1.call-update) | async-done | bytes 3145744 | tf_op jit(solution)/shard_map/all_gather | solution.py:79
  54.9 3.3 fusion.2
  59.1 2.6 convolution_convert_fusion
  62.6 10.5 %all-to-all-start.2 = ((bf16[32,2,16,128]{3,2,1,0:T(8,128)(2,1)}), bf16[32,2,16,128]{3,2,1,0:T(8,128)(2,1)S(1)}, u32[]{:S(2)}, u32[]{:S(2)}) async-start(bf16[32,2,16,128]{3,2,1,0:T(8,128)(2,1)} %broadcast_select_fusion.6), calls=%async_computation.2 | async-start | bytes 524288 | tf_op jit(solution)/shard_map/all_to_all | solution.py:34
  74.4 10.8 %all-to-all-done.2 = bf16[32,2,16,128]{3,2,1,0:T(8,128)(2,1)S(1)} async-done(((bf16[32,2,16,128]{3,2,1,0:T(8,128)(2,1)}), bf16[32,2,16,128]{3,2,1,0:T(8,128)(2,1)S(1)}, u32[]{:S(2)}, u32[]{:S(2)}) %all-to-all-start.2) | async-done | bytes 262176 | tf_op jit(solution)/shard_map/all_to_all | solution.py:34
  90.2 4.6 %all-to-all-start.3 = ((bf16[32,2,16,128]{3,2,1,0:T(8,128)(2,1)}), bf16[32,2,16,128]{3,2,1,0:T(8,128)(2,1)S(1)}, u32[]{:S(2)}, u32[]{:S(2)}) async-start(bf16[32,2,16,128]{3,2,1,0:T(8,128)(2,1)} %broadcast_in_dim.340), calls=%async_computation.3 | async-start | bytes 524288 | tf_op jit(solution)/shard_map/all_to_all | solution.py:38
  97.7 10.0 %all-to-all-done.3 = bf16[32,2,16,128]{3,2,1,0:T(8,128)(2,1)S(1)} async-done(((bf16[32,2,16,128]{3,2,1,0:T(8,128)(2,1)}), bf16[32,2,16,128]{3,2,1,0:T(8,128)(2,1)S(1)}, u32[]{:S(2)}, u32[]{:S(2)}) %all-to-all-start.3) | async-done | bytes 262176 | tf_op jit(solution)/shard_map/all_to_all | solution.py:38
  107.8 18.5 %all-reduce.2.cloned.1.call-done = bf16[1024,1024]{1,0:T(8,128)(2,1)} async-done(((bf16[1024,1024]{1,0:T(8,128)(2,1)}), bf16[1024,1024]{1,0:T(8,128)(2,1)}) %all-reduce.2.cloned.1.call-update) | async-done | bytes 2097168 | tf_op jit(solution)/shard_map/psum | solution.py:84
  126.3 2.0 fusion.20
  128.5 22.3 %all_to_all.85 = bf16[32,2,16,128]{3,2,1,0:T(8,128)(2,1)} all-to-all(bf16[32,2,16,128]{3,2,1,0:T(8,128)(2,1)S(1)} %broadcast_select_fusion.5), channel_id=1, replica_groups=mesh['zx'=32,'core'=2,'sub'=4] {'zx'}, dimensions={0} | all-to-all | bytes 524288 | tf_op jit(solution)/shard_map/all_to_all | solution.py:34
  150.7 1.0 reduce_sum.304
  151.8 1.2 collective-permute-done.1
  153.7 4.9 %all-to-all-start.5 = ((bf16[32,2,16,128]{3,2,1,0:T(8,128)(2,1)}), bf16[32,2,16,128]{3,2,1,0:T(8,128)(2,1)}, u32[]{:S(2)}, u32[]{:S(2)}) async-start(bf16[32,2,16,128]{3,2,1,0:T(8,128)(2,1)} %broadcast_in_dim.347), calls=%async_computation.5 | async-start | bytes 524288 | tf_op jit(solution)/shard_map/all_to_all | solution.py:38
  161.5 10.1 %all-to-all-done.5 = bf16[32,2,16,128]{3,2,1,0:T(8,128)(2,1)} async-done(((bf16[32,2,16,128]{3,2,1,0:T(8,128)(2,1)}), bf16[32,2,16,128]{3,2,1,0:T(8,128)(2,1)}, u32[]{:S(2)}, u32[]{:S(2)}) %all-to-all-start.5) | async-done | bytes 262176 | tf_op jit(solution)/shard_map/all_to_all | solution.py:38
  174.0 15.9 %all_to_all.86 = bf16[32,2,16,128]{3,2,1,0:T(8,128)(2,1)} all-to-all(bf16[32,2,16,128]{3,2,1,0:T(8,128)(2,1)S(1)} %broadcast_select_fusion.4), channel_id=1, replica_groups=mesh['zx'=32,'core'=2,'sub'=4] {'zx'}, dimensions={0} | all-to-all | bytes 524288 | tf_op jit(solution)/shard_map/all_to_all | solution.py:34
  190.0 1.0 reduce_sum.309
  191.1 1.2 collective-permute-done.2
  193.0 5.3 %all-to-all-start.7 = ((bf16[32,2,16,128]{3,2,1,0:T(8,128)(2,1)}), bf16[32,2,16,128]{3,2,1,0:T(8,128)(2,1)}, u32[]{:S(2)}, u32[]{:S(2)}) async-start(bf16[32,2,16,128]{3,2,1,0:T(8,128)(2,1)} %broadcast_in_dim.354), calls=%async_computation.7 | async-start | bytes 524288 | tf_op jit(solution)/shard_map/all_to_all | solution.py:38
  200.9 10.3 %all-to-all-done.7 = bf16[32,2,16,128]{3,2,1,0:T(8,128)(2,1)} async-done(((bf16[32,2,16,128]{3,2,1,0:T(8,128)(2,1)}), bf16[32,2,16,128]{3,2,1,0:T(8,128)(2,1)}, u32[]{:S(2)}, u32[]{:S(2)}) %all-to-all-start.7) | async-done | bytes 262176 | tf_op jit(solution)/shard_map/all_to_all | solution.py:38
  213.7 15.9 %all_to_all.87 = bf16[32,2,16,128]{3,2,1,0:T(8,128)(2,1)} all-to-all(bf16[32,2,16,128]{3,2,1,0:T(8,128)(2,1)S(1)} %broadcast_select_fusion.3), channel_id=1, replica_groups=mesh['zx'=32,'core'=2,'sub'=4] {'zx'}, dimensions={0} | all-to-all | bytes 524288 | tf_op jit(solution)/shard_map/all_to_all | solution.py:34
  229.7 1.0 reduce_sum.314
  230.8 1.2 collective-permute-done.3
  232.7 5.4 %all-to-all-start.9 = ((bf16[32,2,16,128]{3,2,1,0:T(8,128)(2,1)}), bf16[32,2,16,128]{3,2,1,0:T(8,128)(2,1)}, u32[]{:S(2)}, u32[]{:S(2)}) async-start(bf16[32,2,16,128]{3,2,1,0:T(8,128)(2,1)} %broadcast_in_dim.361), calls=%async_computation.9 | async-start | bytes 524288 | tf_op jit(solution)/shard_map/all_to_all | solution.py:38
  240.0 11.0 %all-to-all-done.9 = bf16[32,2,16,128]{3,2,1,0:T(8,128)(2,1)} async-done(((bf16[32,2,16,128]{3,2,1,0:T(8,128)(2,1)}), bf16[32,2,16,128]{3,2,1,0:T(8,128)(2,1)}, u32[]{:S(2)}, u32[]{:S(2)}) %all-to-all-start.9) | async-done | bytes 262176 | tf_op jit(solution)/shard_map/all_to_all | solution.py:38
  250.9 1.0 bitcast_convert_fusion.3
  253.3 15.9 %all_to_all.88 = bf16[32,2,16,128]{3,2,1,0:T(8,128)(2,1)} all-to-all(bf16[32,2,16,128]{3,2,1,0:T(8,128)(2,1)S(1)} %broadcast_select_fusion.2), channel_id=1, replica_groups=mesh['zx'=32,'core'=2,'sub'=4] {'zx'}, dimensions={0} | all-to-all | bytes 524288 | tf_op jit(solution)/shard_map/all_to_all | solution.py:34
  269.3 1.0 reduce_sum.319
  270.4 1.2 collective-permute-done.4
  272.3 5.3 %all-to-all-start.11 = ((bf16[32,2,16,128]{3,2,1,0:T(8,128)(2,1)}), bf16[32,2,16,128]{3,2,1,0:T(8,128)(2,1)}, u32[]{:S(2)}, u32[]{:S(2)}) async-start(bf16[32,2,16,128]{3,2,1,0:T(8,128)(2,1)} %broadcast_in_dim.368), calls=%async_computation.11 | async-start | bytes 524288 | tf_op jit(solution)/shard_map/all_to_all | solution.py:38
  280.2 10.3 %all-to-all-done.11 = bf16[32,2,16,128]{3,2,1,0:T(8,128)(2,1)} async-done(((bf16[32,2,16,128]{3,2,1,0:T(8,128)(2,1)}), bf16[32,2,16,128]{3,2,1,0:T(8,128)(2,1)}, u32[]{:S(2)}, u32[]{:S(2)}) %all-to-all-start.11) | async-done | bytes 262176 | tf_op jit(solution)/shard_map/all_to_all | solution.py:38
  293.1 15.9 %all_to_all.89 = bf16[32,2,16,128]{3,2,1,0:T(8,128)(2,1)} all-to-all(bf16[32,2,16,128]{3,2,1,0:T(8,128)(2,1)S(1)} %broadcast_select_fusion.1), channel_id=1, replica_groups=mesh['zx'=32,'core'=2,'sub'=4] {'zx'}, dimensions={0} | all-to-all | bytes 524288 | tf_op jit(solution)/shard_map/all_to_all | solution.py:34
  309.0 1.0 reduce_sum.324
  310.1 1.2 collective-permute-done.5
  312.0 5.3 %all-to-all-start.13 = ((bf16[32,2,16,128]{3,2,1,0:T(8,128)(2,1)}), bf16[32,2,16,128]{3,2,1,0:T(8,128)(2,1)}, u32[]{:S(2)}, u32[]{:S(2)}) async-start(bf16[32,2,16,128]{3,2,1,0:T(8,128)(2,1)} %broadcast_in_dim.375), calls=%async_computation.13 | async-start | bytes 524288 | tf_op jit(solution)/shard_map/all_to_all | solution.py:38
  319.3 11.0 %all-to-all-done.13 = bf16[32,2,16,128]{3,2,1,0:T(8,128)(2,1)} async-done(((bf16[32,2,16,128]{3,2,1,0:T(8,128)(2,1)}), bf16[32,2,16,128]{3,2,1,0:T(8,128)(2,1)}, u32[]{:S(2)}, u32[]{:S(2)}) %all-to-all-start.13) | async-done | bytes 262176 | tf_op jit(solution)/shard_map/all_to_all | solution.py:38
  332.7 16.0 %all_to_all.90 = bf16[32,2,16,128]{3,2,1,0:T(8,128)(2,1)S(1)} all-to-all(bf16[32,2,16,128]{3,2,1,0:T(8,128)(2,1)S(1)} %broadcast_select_fusion), channel_id=1, replica_groups=mesh['zx'=32,'core'=2,'sub'=4] {'zx'}, dimensions={0} | all-to-all | bytes 524288 | tf_op jit(solution)/shard_map/all_to_all | solution.py:34
  348.8 1.2 collective-permute-done.6
  350.7 4.7 %all-to-all-start.15 = ((bf16[32,2,16,128]{3,2,1,0:T(8,128)(2,1)}), bf16[32,2,16,128]{3,2,1,0:T(8,128)(2,1)S(1)}, u32[]{:S(2)}, u32[]{:S(2)}) async-start(bf16[32,2,16,128]{3,2,1,0:T(8,128)(2,1)} %broadcast_in_dim.382), calls=%async_computation.15 | async-start | bytes 524288 | tf_op jit(solution)/shard_map/all_to_all | solution.py:38
  355.4 12.8 %all-to-all-done.15 = bf16[32,2,16,128]{3,2,1,0:T(8,128)(2,1)S(1)} async-done(((bf16[32,2,16,128]{3,2,1,0:T(8,128)(2,1)}), bf16[32,2,16,128]{3,2,1,0:T(8,128)(2,1)S(1)}, u32[]{:S(2)}, u32[]{:S(2)}) %all-to-all-start.15) | async-done | bytes 262176 | tf_op jit(solution)/shard_map/all_to_all | solution.py:38
  368.4 8.6 %all_to_all.91 = bf16[4,16,1024]{2,1,0:T(8,128)(2,1)S(1)} all-to-all(bf16[4,16,1024]{2,1,0:T(8,128)(2,1)S(1)} %broadcast_in_dim.383), channel_id=1, replica_groups=mesh['zx'=32,'core'=2,'sub'=4] {'sub'}, dimensions={0} | all-to-all | bytes 262144 | tf_op jit(solution)/shard_map/all_to_all | solution.py:44
  377.0 1.0 fusion.8
  (172 shorter events, 34.3 us)
Async XLA Ops:
  6.5 13.0 %copy-start = (bf16[1,384,1536]{2,1,0:T(8,128)(2,1)S(1)}, bf16[1,384,1536]{2,1,0:T(8,128)(2,1)}, u32[]{:S(2)}) copy-start(bf16[1,384,1536]{2,1,0:T(8,128)(2,1)} %param.9) | copy-start | bytes 3538948
  6.5 13.6 %copy-start.5 = (bf16[1,1024,384]{2,1,0:T(8,128)(2,1)S(1)}, bf16[1,1024,384]{2,1,0:T(8,128)(2,1)}, u32[]{:S(2)}) copy-start(bf16[1,1024,384]{2,1,0:T(8,128)(2,1)} %param.10) | copy-start | bytes 2359300
  6.5 48.4 %all-gather.3.cloned.1.call-start = ((), (), s32[]{:S(2)}) async-start(), calls=%async_computation.18 | async-start | bytes 3932160 | tf_op jit(solution)/shard_map/all_gather | solution.py:79
  8.8 10.8 %all-to-all-start = ((bf16[4,384,64]{1,2,0:T(8,128)(2,1)}), bf16[4,384,64]{1,2,0:T(8,128)(2,1)S(1)}, u32[]{:S(2)}, u32[]{:S(2)}) async-start(bf16[4,384,64]{1,2,0:T(8,128)(2,1)} %broadcast_in_dim.329), calls=%async_computation | async-start | bytes 393216 | tf_op jit(solution)/shard_map/all_to_all | solution.py:44
  21.1 10.6 %all-to-all-start.1 = ((bf16[4,16,1024]{2,1,0:T(8,128)(2,1)}), bf16[4,16,1024]{2,1,0:T(8,128)(2,1)S(1)}, u32[]{:S(2)}, u32[]{:S(2)}) async-start(bf16[4,16,1024]{2,1,0:T(8,128)(2,1)} %bitcast.12), calls=%async_computation.1 | async-start | bytes 262144 | tf_op jit(solution)/shard_map/all_to_all | solution.py:75
  24.6 101.8 %all-reduce.2.cloned.1.call-start = ((), (), s32[]{:S(2)}) async-start(), calls=%async_computation.17 | async-start | bytes 4194304 | tf_op jit(solution)/shard_map/psum | solution.py:84
  58.2 0.9 copy-start.3
  61.7 11.4 %copy-start.1 = (s32[64]{0:T(128)S(1)}, s32[64]{0:T(128)}, u32[]{:S(2)}) copy-start(s32[64]{0:T(128)} %param.15) | copy-start | bytes 772
  61.7 34.4 %copy-start.16 = (f32[1,6,2,512]{3,2,1,0:T(2,128)S(1)}, f32[1,6,2,512]{3,2,1,0:T(2,128)}, u32[]{:S(2)}) copy-start(f32[1,6,2,512]{3,2,1,0:T(2,128)} %param.12) | copy-start | bytes 73732
  62.6 22.6 %all-to-all-start.2 = ((bf16[32,2,16,128]{3,2,1,0:T(8,128)(2,1)}), bf16[32,2,16,128]{3,2,1,0:T(8,128)(2,1)S(1)}, u32[]{:S(2)}, u32[]{:S(2)}) async-start(bf16[32,2,16,128]{3,2,1,0:T(8,128)(2,1)} %broadcast_select_fusion.6), calls=%async_computation.2 | async-start | bytes 524288 | tf_op jit(solution)/shard_map/all_to_all | solution.py:34
  85.3 4.1 %collective-permute-start = (bf16[2,16,128]{2,1,0:T(8,128)(2,1)S(1)}, bf16[2,16,128]{2,1,0:T(8,128)(2,1)S(1)}, u32[]{:S(2)}, u32[]{:S(2)}) collective-permute-start(bf16[2,16,128]{2,1,0:T(8,128)(2,1)S(1)} %reduce_sum.299), channel_id=1, source_target_pairs={{0,4},{4,0},{1,5},{5,1},{2,6},{6,2},{3,7},{7,3},{8,12},{12,8},{9,1... | collective-permute-start | bytes 24584 | tf_op jit(solution)/shard_map/ppermute | solution.py:36
  90.2 17.5 %all-to-all-start.3 = ((bf16[32,2,16,128]{3,2,1,0:T(8,128)(2,1)}), bf16[32,2,16,128]{3,2,1,0:T(8,128)(2,1)S(1)}, u32[]{:S(2)}, u32[]{:S(2)}) async-start(bf16[32,2,16,128]{3,2,1,0:T(8,128)(2,1)} %broadcast_in_dim.340), calls=%async_computation.3 | async-start | bytes 524288 | tf_op jit(solution)/shard_map/all_to_all | solution.py:38
  107.8 65.6 %copy-start.7 = (f32[4,16,128]{2,1,0:T(8,128)}, f32[4,16,128]{2,1,0:T(8,128)S(1)}, u32[]{:S(2)}) copy-start(f32[4,16,128]{2,1,0:T(8,128)S(1)} %get-tuple-element.18) | copy-start | bytes 98308
  128.3 45.1 %copy-start.2 = (bf16[1024,1024]{1,0:T(8,128)(2,1)S(1)}, bf16[1024,1024]{1,0:T(8,128)(2,1)}, u32[]{:S(2)}) copy-start(bf16[1024,1024]{1,0:T(8,128)(2,1)} %all-reduce.2.cloned.1.call-done) | copy-start | bytes 6291460
  151.7 1.3 collective-permute-start.1
  153.7 17.9 %all-to-all-start.5 = ((bf16[32,2,16,128]{3,2,1,0:T(8,128)(2,1)}), bf16[32,2,16,128]{3,2,1,0:T(8,128)(2,1)}, u32[]{:S(2)}, u32[]{:S(2)}) async-start(bf16[32,2,16,128]{3,2,1,0:T(8,128)(2,1)} %broadcast_in_dim.347), calls=%async_computation.5 | async-start | bytes 524288 | tf_op jit(solution)/shard_map/all_to_all | solution.py:38
  171.6 2.3 copy-start.19
  173.4 0.6 copy-start.10
  173.4 19.6 %copy-start.9 = (f32[4,16,128]{2,1,0:T(8,128)}, f32[4,16,128]{2,1,0:T(8,128)S(1)}, u32[]{:S(2)}) copy-start(f32[4,16,128]{2,1,0:T(8,128)S(1)} %get-tuple-element.15) | copy-start | bytes 98308
  191.0 1.3 collective-permute-start.2
  193.0 18.3 %all-to-all-start.7 = ((bf16[32,2,16,128]{3,2,1,0:T(8,128)(2,1)}), bf16[32,2,16,128]{3,2,1,0:T(8,128)(2,1)}, u32[]{:S(2)}, u32[]{:S(2)}) async-start(bf16[32,2,16,128]{3,2,1,0:T(8,128)(2,1)} %broadcast_in_dim.354), calls=%async_computation.7 | async-start | bytes 524288 | tf_op jit(solution)/shard_map/all_to_all | solution.py:38
  213.1 39.6 %copy-start.6 = (f32[8,16,128]{2,1,0:T(8,128)}, f32[8,16,128]{2,1,0:T(8,128)S(1)}, u32[]{:S(2)}) copy-start(f32[8,16,128]{2,1,0:T(8,128)S(1)} %get-tuple-element.29) | copy-start | bytes 196612
  213.1 24.9 %copy-start.15 = (f32[8,2,4,128]{3,0,2,1:T(8,128)S(1)}, f32[8,2,4,128]{3,0,2,1:T(8,128)}, u32[]{:S(2)}) copy-start(f32[8,2,4,128]{3,0,2,1:T(8,128)} %get-tuple-element.22) | copy-start | bytes 98308
  230.7 1.3 collective-permute-start.3
  232.7 18.3 %all-to-all-start.9 = ((bf16[32,2,16,128]{3,2,1,0:T(8,128)(2,1)}), bf16[32,2,16,128]{3,2,1,0:T(8,128)(2,1)}, u32[]{:S(2)}, u32[]{:S(2)}) async-start(bf16[32,2,16,128]{3,2,1,0:T(8,128)(2,1)} %broadcast_in_dim.361), calls=%async_computation.9 | async-start | bytes 524288 | tf_op jit(solution)/shard_map/all_to_all | solution.py:38
  250.9 2.3 copy-start.18
  252.7 0.6 copy-start.8
  270.3 1.3 collective-permute-start.4
  272.3 18.3 %all-to-all-start.11 = ((bf16[32,2,16,128]{3,2,1,0:T(8,128)(2,1)}), bf16[32,2,16,128]{3,2,1,0:T(8,128)(2,1)}, u32[]{:S(2)}, u32[]{:S(2)}) async-start(bf16[32,2,16,128]{3,2,1,0:T(8,128)(2,1)} %broadcast_in_dim.368), calls=%async_computation.11 | async-start | bytes 524288 | tf_op jit(solution)/shard_map/all_to_all | solution.py:38
  292.5 24.9 %copy-start.14 = (f32[8,2,4,128]{3,0,2,1:T(8,128)S(1)}, f32[8,2,4,128]{3,0,2,1:T(8,128)}, u32[]{:S(2)}) copy-start(f32[8,2,4,128]{3,0,2,1:T(8,128)} %get-tuple-element.24) | copy-start | bytes 98308
  310.0 1.3 collective-permute-start.5
  312.0 18.3 %all-to-all-start.13 = ((bf16[32,2,16,128]{3,2,1,0:T(8,128)(2,1)}), bf16[32,2,16,128]{3,2,1,0:T(8,128)(2,1)}, u32[]{:S(2)}, u32[]{:S(2)}) async-start(bf16[32,2,16,128]{3,2,1,0:T(8,128)(2,1)} %broadcast_in_dim.375), calls=%async_computation.13 | async-start | bytes 524288 | tf_op jit(solution)/shard_map/all_to_all | solution.py:38
  330.3 2.3 copy-start.17
  332.1 0.6 copy-start.11
  332.5 22.9 %copy-start.13 = (f32[8,2,4,128]{3,0,2,1:T(8,128)S(1)}, f32[8,2,4,128]{3,0,2,1:T(8,128)}, u32[]{:S(2)}) copy-start(f32[8,2,4,128]{3,0,2,1:T(8,128)} %get-tuple-element.19) | copy-start | bytes 98308
  332.6 44.5 %copy-start.4 = (bf16[384,1024]{1,0:T(8,128)(2,1)S(1)}, bf16[384,1024]{1,0:T(8,128)(2,1)}, u32[]{:S(2)}) copy-start(bf16[384,1024]{1,0:T(8,128)(2,1)} %copy-done.3) | copy-start | bytes 2359300
  348.6 19.7 %copy-start.12 = (f32[4,16,128]{2,1,0:T(8,128)S(1)}, f32[4,16,128]{2,1,0:T(8,128)}, u32[]{:S(2)}) copy-start(f32[4,16,128]{2,1,0:T(8,128)} %copy-done.11) | copy-start | bytes 98308
  348.7 1.3 collective-permute-start.6
  350.7 17.6 %all-to-all-start.15 = ((bf16[32,2,16,128]{3,2,1,0:T(8,128)(2,1)}), bf16[32,2,16,128]{3,2,1,0:T(8,128)(2,1)S(1)}, u32[]{:S(2)}, u32[]{:S(2)}) async-start(bf16[32,2,16,128]{3,2,1,0:T(8,128)(2,1)} %broadcast_in_dim.382), calls=%async_computation.15 | async-start | bytes 524288 | tf_op jit(solution)/shard_map/all_to_all | solution.py:38
Sparse Core Ops, SparseCore 0:
  9.2 45.7 all-gather.2
  61.9 64.3 all-reduce.1

commit v6 on v3

--- a/solution.py
+++ b/solution.py
@@ -88,8 +88,8 @@
     spread_half = spread.astype(jnp.bfloat16)
     partial_map = lax.dot_general(
         spread_half, agg_columns, CONTRACT_FIRST, preferred_element_type=jnp.float32
-    )
-    coupling = lax.psum(partial_map.astype(jnp.bfloat16), "sub")
+    ).astype(jnp.bfloat16)
+    coupling = lax.psum(partial_map, "sub")
 
     domains = sweep_order.shape[0]
     members = domains // SEGMENTS
@@ -109,6 +109,13 @@
     for segment_k in range(SEGMENTS - 1):
         if segment_k == 0:
             pattern = incident.astype(jnp.bfloat16)
+        elif segment_k == 1:
+            all_fields = gather_rows(from_tiles(incoming).astype(jnp.bfloat16), subs)
+            products = jnp.dot(all_fields, partial_map, preferred_element_type=jnp.float32)
+            product_pieces = lax.all_to_all(
+                products.reshape((subs, -1) + products.shape[1:]), "sub", 0, 0, tiled=True
+            )
+            pattern = (incident - jnp.sum(product_pieces, axis=0)).astype(jnp.bfloat16)
         else:
             pattern = (
                 incident

time: 352 us -> 347 us (0.986)
  waiting for transfers between devices: 81.4 us -> 65.5 us
  starting transfers between devices: 26.4 us -> 35.4 us
    all_gather x1, waiting for transfers between devices: 22.8 us -> 0.02 us  [local(): lax.all_gather(disagg_rows, 'sub', axis=0, tiled=True)]
    all_to_all x0 -> x1, waiting for transfers between devices: none -> 6.05 us  [local(): lax.all_to_all(products.reshape((subs, -1) + products.shape[1:]), 'sub',...]
    all_to_all x0 -> x1, starting transfers between devices: none -> 4.3 us  [local(): lax.all_to_all(products.reshape((subs, -1) + products.shape[1:]), 'sub',...]
    all_to_all x1 -> x2, starting transfers between devices: 4.46 us -> 8.53 us  [gather_rows(): pieces = lax.all_to_all(copies, 'sub', 0, 0, tiled=True)]
  transfers between devices with their start and end apart: 20 -> 22, of which waited for: 16 -> 19; matrix products, arithmetic and copies ran while one was open for 5% -> 5% of each run, Pallas kernels for 0% -> 0%
where the time goes in v6:
time: 347 us; the launch traced here: 344 us
  blocking collectives  184 us (53%)
  waiting for transfers between devices  65.5 us (19%)
  starting transfers between devices  35.4 us (10%)
  between operations  26 us (7%)
  matrix products  13 us (4%)
  other arithmetic  10.9 us (3%)
  local copies, waits for them, and re-layouts  9.71 us (3%)
    all_to_all x6, blocking collectives, share_slots(): lax.all_to_all(mine.reshape((chips,) + tile_shape), 'zx', 0, 0, tiled=True)  93.1 us
    all_to_all x6, blocking collectives, share_slots(): lax.all_to_all(spread, 'zx', 0, 0, tiled=True).reshape(mine.shape)  82.2 us
    psum x1, waiting for transfers between devices, local(): coupling = lax.psum(partial_map, 'sub')  24.2 us
    all_to_all x1, starting transfers between devices, share_slots(): lax.all_to_all(mine.reshape((chips,) + tile_shape), 'zx', 0, 0, tiled=True)  11.3 us
    ppermute x7, waiting for transfers between devices, share_slots(): slots = slots + lax.ppermute(slots, 'core', swap)  8.98 us
    all_to_all x1, waiting for transfers between devices, share_slots(): lax.all_to_all(spread, 'zx', 0, 0, tiled=True).reshape(mine.shape)  8.66 us
    all_to_all x1, blocking collectives, gather_rows(): pieces = lax.all_to_all(copies, 'sub', 0, 0, tiled=True)  8.57 us
    all_to_all x2, starting transfers between devices, gather_rows(): pieces = lax.all_to_all(copies, 'sub', 0, 0, tiled=True)  8.53 us
  transfers between devices with their start and end apart: 22, of which 19 were waited for; matrix products, arithmetic and copies ran while one was open for 5% of the time, Pallas kernels for 0%

profile of v6, /device:TPU:32, one launch (start us, length us, event | category | flops | bytes accessed | tf_op | source)
XLA Modules:
  0.0 344.4 jit_solution(4358067043961779807)
XLA Ops:
  7.3 1.5 broadcast_in_dim.293
  8.8 4.6 %all-to-all-start = ((bf16[4,384,64]{1,2,0:T(8,128)(2,1)}), bf16[4,384,64]{1,2,0:T(8,128)(2,1)S(1)}, u32[]{:S(2)}, u32[]{:S(2)}) async-start(bf16[4,384,64]{1,2,0:T(8,128)(2,1)} %broadcast_in_dim.293), calls=%async_computation | async-start | bytes 393216 | tf_op jit(solution)/shard_map/all_to_all | solution.py:52
  13.4 1.2 dynamic_slice.29
  18.6 1.1 all-to-all-done
  20.3 1.0 convolution_convert_fusion.1
  21.3 3.7 %all-to-all-start.1 = ((bf16[4,16,1024]{2,1,0:T(8,128)(2,1)}), bf16[4,16,1024]{2,1,0:T(8,128)(2,1)S(1)}, u32[]{:S(2)}, u32[]{:S(2)}) async-start(bf16[4,16,1024]{2,1,0:T(8,128)(2,1)} %bitcast.12), calls=%async_computation.1 | async-start | bytes 262144 | tf_op jit(solution)/shard_map/all_to_all | solution.py:83
  25.0 7.3 %all-to-all-done.1 = bf16[4,16,1024]{2,1,0:T(8,128)(2,1)S(1)} async-done(((bf16[4,16,1024]{2,1,0:T(8,128)(2,1)}), bf16[4,16,1024]{2,1,0:T(8,128)(2,1)S(1)}, u32[]{:S(2)}, u32[]{:S(2)}) %all-to-all-start.1) | async-done | bytes 131104 | tf_op jit(solution)/shard_map/all_to_all | solution.py:83
  33.2 0.8 collective-permute-done
  34.8 11.3 %all-to-all-start.2 = ((bf16[32,16,128]{2,1,0:T(8,128)(2,1)}), bf16[32,16,128]{2,1,0:T(8,128)(2,1)S(1)}, u32[]{:S(2)}, u32[]{:S(2)}) async-start(bf16[32,16,128]{2,1,0:T(8,128)(2,1)} %bitcast.15), calls=%async_computation.2 | async-start | bytes 262144 | tf_op jit(solution)/shard_map/all_to_all | solution.py:38
  51.6 4.3 %all-to-all-done.2 = bf16[32,16,128]{2,1,0:T(8,128)(2,1)S(1)} async-done(((bf16[32,16,128]{2,1,0:T(8,128)(2,1)}), bf16[32,16,128]{2,1,0:T(8,128)(2,1)S(1)}, u32[]{:S(2)}, u32[]{:S(2)}) %all-to-all-start.2) | async-done | bytes 131104 | tf_op jit(solution)/shard_map/all_to_all | solution.py:38
  56.7 5.5 %all-to-all-start.3 = ((bf16[32,16,128]{2,1,0:T(8,128)(2,1)}), bf16[32,16,128]{2,1,0:T(8,128)(2,1)S(1)}, u32[]{:S(2)}, u32[]{:S(2)}) async-start(bf16[32,16,128]{2,1,0:T(8,128)(2,1)} %broadcast_in_dim.301), calls=%async_computation.3 | async-start | bytes 262144 | tf_op jit(solution)/shard_map/all_to_all | solution.py:41
  63.0 8.7 %all-to-all-done.3 = bf16[32,16,128]{2,1,0:T(8,128)(2,1)S(1)} async-done(((bf16[32,16,128]{2,1,0:T(8,128)(2,1)}), bf16[32,16,128]{2,1,0:T(8,128)(2,1)S(1)}, u32[]{:S(2)}, u32[]{:S(2)}) %all-to-all-start.3) | async-done | bytes 131104 | tf_op jit(solution)/shard_map/all_to_all | solution.py:41
  71.7 1.3 collective-permute-done.1
  73.9 3.9 %all-to-all-start.4 = ((bf16[4,16,1024]{2,1,0:T(8,128)(2,1)}), bf16[4,16,1024]{2,1,0:T(8,128)(2,1)}, u32[]{:S(2)}, u32[]{:S(2)}) async-start(bf16[4,16,1024]{2,1,0:T(8,128)(2,1)} %broadcast_in_dim.304), calls=%async_computation.4 | async-start | bytes 262144 | tf_op jit(solution)/shard_map/all_to_all | solution.py:52
  77.8 3.3 fusion.4
  81.2 0.9 copy-done.4
  82.1 1.3 convolution_convert_fusion
  83.8 2.3 fusion.2
  86.1 4.3 %all-to-all-start.5 = ((f32[4,16,1024]{2,1,0:T(8,128)}), f32[4,16,1024]{2,1,0:T(8,128)}, u32[]{:S(2)}, u32[]{:S(2)}) async-start(f32[4,16,1024]{2,1,0:T(8,128)} %fusion.2), calls=%async_computation.5 | async-start | bytes 524288 | tf_op jit(solution)/shard_map/all_to_all | solution.py:115
  91.2 6.0 %all-to-all-done.5 = f32[4,16,1024]{2,1,0:T(8,128)} async-done(((f32[4,16,1024]{2,1,0:T(8,128)}), f32[4,16,1024]{2,1,0:T(8,128)}, u32[]{:S(2)}, u32[]{:S(2)}) %all-to-all-start.5) | async-done | bytes 262176 | tf_op jit(solution)/shard_map/all_to_all | solution.py:115
  97.2 1.0 reduce_sum.313
  98.4 1.5 collective-permute-done.2
  100.1 14.1 %all_to_all.95 = bf16[32,16,128]{2,1,0:T(8,128)(2,1)S(1)} all-to-all(bf16[32,16,128]{2,1,0:T(8,128)(2,1)S(1)} %bitcast.206), channel_id=1, replica_groups=mesh['zx'=32,'core'=2,'sub'=4] {'zx'}, dimensions={0} | all-to-all | bytes 262144 | tf_op jit(solution)/shard_map/all_to_all | solution.py:38
  114.3 13.7 %all_to_all.96 = bf16[32,16,128]{2,1,0:T(8,128)(2,1)S(1)} all-to-all(bf16[32,16,128]{2,1,0:T(8,128)(2,1)S(1)} %broadcast_in_dim.306), channel_id=1, replica_groups=mesh['zx'=32,'core'=2,'sub'=4] {'zx'}, dimensions={0} | all-to-all | bytes 262144 | tf_op jit(solution)/shard_map/all_to_all | solution.py:41
  129.5 24.2 %all-reduce.2.cloned.1.call-done = bf16[1024,1024]{1,0:T(8,128)(2,1)} async-done(((bf16[1024,1024]{1,0:T(8,128)(2,1)}), bf16[1024,1024]{1,0:T(8,128)(2,1)}) %all-reduce.2.cloned.1.call-update) | async-done | bytes 2097168 | tf_op jit(solution)/shard_map/psum | solution.py:92
  153.7 2.0 fusion.20
  155.9 1.5 collective-permute-done.4
  157.6 19.8 %all_to_all.97 = bf16[32,16,128]{2,1,0:T(8,128)(2,1)} all-to-all(bf16[32,16,128]{2,1,0:T(8,128)(2,1)S(1)} %bitcast.207), channel_id=1, replica_groups=mesh['zx'=32,'core'=2,'sub'=4] {'zx'}, dimensions={0} | all-to-all | bytes 262144 | tf_op jit(solution)/shard_map/all_to_all | solution.py:38
  177.4 0.9 reduce_sum.319
  178.4 13.7 %all_to_all.98 = bf16[32,16,128]{2,1,0:T(8,128)(2,1)S(1)} all-to-all(bf16[32,16,128]{2,1,0:T(8,128)(2,1)S(1)} %broadcast_in_dim.310), channel_id=1, replica_groups=mesh['zx'=32,'core'=2,'sub'=4] {'zx'}, dimensions={0} | all-to-all | bytes 262144 | tf_op jit(solution)/shard_map/all_to_all | solution.py:41
  195.4 1.4 collective-permute-done.6
  196.9 14.8 %all_to_all.99 = bf16[32,16,128]{2,1,0:T(8,128)(2,1)} all-to-all(bf16[32,16,128]{2,1,0:T(8,128)(2,1)S(1)} %bitcast.208), channel_id=1, replica_groups=mesh['zx'=32,'core'=2,'sub'=4] {'zx'}, dimensions={0} | all-to-all | bytes 262144 | tf_op jit(solution)/shard_map/all_to_all | solution.py:38
  211.7 0.9 reduce_sum.324
  212.7 13.7 %all_to_all.100 = bf16[32,16,128]{2,1,0:T(8,128)(2,1)S(1)} all-to-all(bf16[32,16,128]{2,1,0:T(8,128)(2,1)S(1)} %broadcast_in_dim.314), channel_id=1, replica_groups=mesh['zx'=32,'core'=2,'sub'=4] {'zx'}, dimensions={0} | all-to-all | bytes 262144 | tf_op jit(solution)/shard_map/all_to_all | solution.py:41
  229.1 1.2 collective-permute-done.8
  230.4 15.1 %all_to_all.101 = bf16[32,16,128]{2,1,0:T(8,128)(2,1)} all-to-all(bf16[32,16,128]{2,1,0:T(8,128)(2,1)S(1)} %bitcast.209), channel_id=1, replica_groups=mesh['zx'=32,'core'=2,'sub'=4] {'zx'}, dimensions={0} | all-to-all | bytes 262144 | tf_op jit(solution)/shard_map/all_to_all | solution.py:38
  245.5 0.9 reduce_sum.329
  246.4 13.7 %all_to_all.102 = bf16[32,16,128]{2,1,0:T(8,128)(2,1)S(1)} all-to-all(bf16[32,16,128]{2,1,0:T(8,128)(2,1)S(1)} %broadcast_in_dim.318), channel_id=1, replica_groups=mesh['zx'=32,'core'=2,'sub'=4] {'zx'}, dimensions={0} | all-to-all | bytes 262144 | tf_op jit(solution)/shard_map/all_to_all | solution.py:41
  261.8 0.9 convert_bitcast_fusion.1
  263.7 1.2 collective-permute-done.10
  265.0 15.1 %all_to_all.103 = bf16[32,16,128]{2,1,0:T(8,128)(2,1)} all-to-all(bf16[32,16,128]{2,1,0:T(8,128)(2,1)S(1)} %bitcast.210), channel_id=1, replica_groups=mesh['zx'=32,'core'=2,'sub'=4] {'zx'}, dimensions={0} | all-to-all | bytes 262144 | tf_op jit(solution)/shard_map/all_to_all | solution.py:38
  280.1 0.9 reduce_sum.334
  281.1 13.7 %all_to_all.104 = bf16[32,16,128]{2,1,0:T(8,128)(2,1)S(1)} all-to-all(bf16[32,16,128]{2,1,0:T(8,128)(2,1)S(1)} %broadcast_in_dim.322), channel_id=1, replica_groups=mesh['zx'=32,'core'=2,'sub'=4] {'zx'}, dimensions={0} | all-to-all | bytes 262144 | tf_op jit(solution)/shard_map/all_to_all | solution.py:41
  297.0 1.4 collective-permute-done.12
  298.5 14.1 %all_to_all.105 = bf16[32,16,128]{2,1,0:T(8,128)(2,1)S(1)} all-to-all(bf16[32,16,128]{2,1,0:T(8,128)(2,1)S(1)} %bitcast.205), channel_id=1, replica_groups=mesh['zx'=32,'core'=2,'sub'=4] {'zx'}, dimensions={0} | all-to-all | bytes 262144 | tf_op jit(solution)/shard_map/all_to_all | solution.py:38
  312.7 13.7 %all_to_all.106 = bf16[32,16,128]{2,1,0:T(8,128)(2,1)S(1)} all-to-all(bf16[32,16,128]{2,1,0:T(8,128)(2,1)S(1)} %broadcast_in_dim.326), channel_id=1, replica_groups=mesh['zx'=32,'core'=2,'sub'=4] {'zx'}, dimensions={0} | all-to-all | bytes 262144 | tf_op jit(solution)/shard_map/all_to_all | solution.py:41
  328.0 8.6 %all_to_all.107 = bf16[4,16,1024]{2,1,0:T(8,128)(2,1)S(1)} all-to-all(bf16[4,16,1024]{2,1,0:T(8,128)(2,1)S(1)} %broadcast_in_dim.327), channel_id=1, replica_groups=mesh['zx'=32,'core'=2,'sub'=4] {'sub'}, dimensions={0} | all-to-all | bytes 262144 | tf_op jit(solution)/shard_map/all_to_all | solution.py:52
  336.5 1.0 fusion.10
  (177 shorter events, 19.2 us)
Async XLA Ops:
  6.5 13.2 %copy-start = (bf16[1,384,1536]{2,1,0:T(8,128)(2,1)S(1)}, bf16[1,384,1536]{2,1,0:T(8,128)(2,1)}, u32[]{:S(2)}) copy-start(bf16[1,384,1536]{2,1,0:T(8,128)(2,1)} %param.9) | copy-start | bytes 3538948
  6.5 13.7 %copy-start.6 = (bf16[1,1024,384]{2,1,0:T(8,128)(2,1)S(1)}, bf16[1,1024,384]{2,1,0:T(8,128)(2,1)}, u32[]{:S(2)}) copy-start(bf16[1,1024,384]{2,1,0:T(8,128)(2,1)} %param.10) | copy-start | bytes 2359300
  6.5 71.3 %all-gather.3.cloned.1.call-start = ((), (), s32[]{:S(2)}) async-start(), calls=%async_computation.20 | async-start | bytes 3932160 | tf_op jit(solution)/shard_map/all_gather | solution.py:87
  8.8 23.8 %copy-start.1 = (s32[64]{0:T(128)S(1)}, s32[64]{0:T(128)}, u32[]{:S(2)}) copy-start(s32[64]{0:T(128)} %param.15) | copy-start | bytes 772
  8.8 10.9 %all-to-all-start = ((bf16[4,384,64]{1,2,0:T(8,128)(2,1)}), bf16[4,384,64]{1,2,0:T(8,128)(2,1)S(1)}, u32[]{:S(2)}, u32[]{:S(2)}) async-start(bf16[4,384,64]{1,2,0:T(8,128)(2,1)} %broadcast_in_dim.293), calls=%async_computation | async-start | bytes 393216 | tf_op jit(solution)/shard_map/all_to_all | solution.py:52
  20.2 31.3 %copy-start.19 = (f32[1,6,2,512]{3,2,1,0:T(2,128)S(1)}, f32[1,6,2,512]{3,2,1,0:T(2,128)}, u32[]{:S(2)}) copy-start(f32[1,6,2,512]{3,2,1,0:T(2,128)} %param.12) | copy-start | bytes 73732
  21.3 11.0 %all-to-all-start.1 = ((bf16[4,16,1024]{2,1,0:T(8,128)(2,1)}), bf16[4,16,1024]{2,1,0:T(8,128)(2,1)S(1)}, u32[]{:S(2)}, u32[]{:S(2)}) async-start(bf16[4,16,1024]{2,1,0:T(8,128)(2,1)} %bitcast.12), calls=%async_computation.1 | async-start | bytes 262144 | tf_op jit(solution)/shard_map/all_to_all | solution.py:83
  32.4 1.6 collective-permute-start
  34.8 21.1 %all-to-all-start.2 = ((bf16[32,16,128]{2,1,0:T(8,128)(2,1)}), bf16[32,16,128]{2,1,0:T(8,128)(2,1)S(1)}, u32[]{:S(2)}, u32[]{:S(2)}) async-start(bf16[32,16,128]{2,1,0:T(8,128)(2,1)} %bitcast.15), calls=%async_computation.2 | async-start | bytes 262144 | tf_op jit(solution)/shard_map/all_to_all | solution.py:38
  56.7 15.0 %all-to-all-start.3 = ((bf16[32,16,128]{2,1,0:T(8,128)(2,1)}), bf16[32,16,128]{2,1,0:T(8,128)(2,1)S(1)}, u32[]{:S(2)}, u32[]{:S(2)}) async-start(bf16[32,16,128]{2,1,0:T(8,128)(2,1)} %broadcast_in_dim.301), calls=%async_computation.3 | async-start | bytes 262144 | tf_op jit(solution)/shard_map/all_to_all | solution.py:41
  71.7 1.3 collective-permute-start.1
  73.2 80.5 %copy-start.9 = (f32[4,16,128]{2,1,0:T(8,128)}, f32[4,16,128]{2,1,0:T(8,128)S(1)}, u32[]{:S(2)}) copy-start(f32[4,16,128]{2,1,0:T(8,128)S(1)} %get-tuple-element.18) | copy-start | bytes 98308
  73.9 10.0 %all-to-all-start.4 = ((bf16[4,16,1024]{2,1,0:T(8,128)(2,1)}), bf16[4,16,1024]{2,1,0:T(8,128)(2,1)}, u32[]{:S(2)}, u32[]{:S(2)}) async-start(bf16[4,16,1024]{2,1,0:T(8,128)(2,1)} %broadcast_in_dim.304), calls=%async_computation.4 | async-start | bytes 262144 | tf_op jit(solution)/shard_map/all_to_all | solution.py:52
  77.8 4.2 %copy-start.7 = (bf16[1,1024,384]{2,1,0:T(8,128)(2,1)S(1)}, bf16[1,1024,384]{2,1,0:T(8,128)(2,1)}, u32[]{:S(2)}) copy-start(bf16[1,1024,384]{2,1,0:T(8,128)(2,1)} %param.10) | copy-start | bytes 2359300
  81.2 0.9 copy-start.4
  83.4 7.7 %copy-start.3 = (bf16[1024,1024]{1,0:T(8,128)(2,1)}, bf16[1024,1024]{1,0:T(8,128)(2,1)S(1)}, u32[]{:S(2)}) copy-start(bf16[1024,1024]{1,0:T(8,128)(2,1)S(1)} %convolution_convert_fusion) | copy-start | bytes 6291460
  86.1 11.1 %all-to-all-start.5 = ((f32[4,16,1024]{2,1,0:T(8,128)}), f32[4,16,1024]{2,1,0:T(8,128)}, u32[]{:S(2)}, u32[]{:S(2)}) async-start(f32[4,16,1024]{2,1,0:T(8,128)} %fusion.2), calls=%async_computation.5 | async-start | bytes 524288 | tf_op jit(solution)/shard_map/all_to_all | solution.py:115
  90.4 63.3 %all-reduce.2.cloned.1.call-start = ((), (), s32[]{:S(2)}) async-start(), calls=%async_computation.19 | async-start | bytes 4194304 | tf_op jit(solution)/shard_map/psum | solution.py:92
  91.1 36.9 %copy-start.18 = (f32[8,2,4,128]{3,0,2,1:T(8,128)S(1)}, f32[8,2,4,128]{3,0,2,1:T(8,128)}, u32[]{:S(2)}) copy-start(f32[8,2,4,128]{3,0,2,1:T(8,128)} %get-tuple-element.20) | copy-start | bytes 98308
  98.3 1.6 collective-permute-start.2
  128.0 1.3 collective-permute-start.3
  129.5 24.2 %copy-start.10 = (f32[4,16,128]{2,1,0:T(8,128)}, f32[4,16,128]{2,1,0:T(8,128)S(1)}, u32[]{:S(2)}) copy-start(f32[4,16,128]{2,1,0:T(8,128)S(1)} %get-tuple-element.15) | copy-start | bytes 98308
  129.5 24.2 %copy-start.11 = (f32[4,16,128]{2,1,0:T(8,128)}, f32[4,16,128]{2,1,0:T(8,128)S(1)}, u32[]{:S(2)}) copy-start(f32[4,16,128]{2,1,0:T(8,128)S(1)} %get-tuple-element.16) | copy-start | bytes 98308
  155.7 38.7 %copy-start.2 = (bf16[1024,1024]{1,0:T(8,128)(2,1)S(1)}, bf16[1024,1024]{1,0:T(8,128)(2,1)}, u32[]{:S(2)}) copy-start(bf16[1024,1024]{1,0:T(8,128)(2,1)} %all-reduce.2.cloned.1.call-done) | copy-start | bytes 6291460
  155.8 1.6 collective-permute-start.4
  192.1 1.3 collective-permute-start.5
  194.4 33.6 %copy-start.8 = (f32[8,16,128]{2,1,0:T(8,128)}, f32[8,16,128]{2,1,0:T(8,128)S(1)}, u32[]{:S(2)}) copy-start(f32[8,16,128]{2,1,0:T(8,128)S(1)} %get-tuple-element.29) | copy-start | bytes 196612
  194.9 1.8 collective-permute-start.6
  226.3 1.5 collective-permute-start.7
  228.0 2.4 copy-start.13
  228.0 32.1 %copy-start.12 = (f32[4,16,128]{2,1,0:T(8,128)}, f32[4,16,128]{2,1,0:T(8,128)S(1)}, u32[]{:S(2)}) copy-start(f32[4,16,128]{2,1,0:T(8,128)S(1)} %get-tuple-element.11) | copy-start | bytes 98308
  228.5 1.8 collective-permute-start.8
  230.4 31.3 %copy-start.14 = (f32[4,16,128]{2,1,0:T(8,128)S(1)}, f32[4,16,128]{2,1,0:T(8,128)}, u32[]{:S(2)}) copy-start(f32[4,16,128]{2,1,0:T(8,128)} %copy-done.13) | copy-start | bytes 98308
  260.1 1.5 collective-permute-start.9
  262.6 32.1 %copy-start.17 = (f32[8,2,4,128]{3,0,2,1:T(8,128)S(1)}, f32[8,2,4,128]{3,0,2,1:T(8,128)}, u32[]{:S(2)}) copy-start(f32[8,2,4,128]{3,0,2,1:T(8,128)} %get-tuple-element.24) | copy-start | bytes 98308
  263.1 1.8 collective-permute-start.10
  294.7 1.3 collective-permute-start.11
  296.2 2.3 copy-start.15
  296.6 39.9 %copy-start.5 = (bf16[384,1024]{1,0:T(8,128)(2,1)S(1)}, bf16[384,1024]{1,0:T(8,128)(2,1)}, u32[]{:S(2)}) copy-start(bf16[384,1024]{1,0:T(8,128)(2,1)} %copy-done.4) | copy-start | bytes 2359300
  296.7 1.6 collective-permute-start.12
  298.5 29.4 %copy-start.16 = (f32[4,16,128]{2,1,0:T(8,128)S(1)}, f32[4,16,128]{2,1,0:T(8,128)}, u32[]{:S(2)}) copy-start(f32[4,16,128]{2,1,0:T(8,128)} %copy-done.15) | copy-start | bytes 98308
  326.4 1.3 collective-permute-start.13
Sparse Core Ops, SparseCore 0:
  9.2 45.8 all-gather.2
  93.6 60.0 all-reduce.1

commit v7 on v6

--- a/solution.py
+++ b/solution.py
@@ -12,6 +12,7 @@
 CONTRACT_LAST = (((1,), (1,)), ((), ()))
 DOM = ("zx", "core")
 LANES = 128
+PARTIAL_ROUNDS = 3
 
 
 def to_tiles(rows):
@@ -109,7 +110,7 @@
     for segment_k in range(SEGMENTS - 1):
         if segment_k == 0:
             pattern = incident.astype(jnp.bfloat16)
-        elif segment_k == 1:
+        elif segment_k < PARTIAL_ROUNDS:
             all_fields = gather_rows(from_tiles(incoming).astype(jnp.bfloat16), subs)
             products = jnp.dot(all_fields, partial_map, preferred_element_type=jnp.float32)
             product_pieces = lax.all_to_all(

time: 347 us -> 367 us (1.058)
  waiting for transfers between devices: 65.5 us -> 74.7 us
  blocking collectives: 184 us -> 192 us
    all_to_all x1 -> x2, blocking collectives: 8.57 us -> 16.9 us  [gather_rows(): pieces = lax.all_to_all(copies, 'sub', 0, 0, tiled=True)]
    all_to_all x1 -> x2, waiting for transfers between devices: 6.05 us -> 12 us  [local(): lax.all_to_all(products.reshape((subs, -1) + products.shape[1:]), 'sub',...]
    all_to_all x1 -> x2, starting transfers between devices: 4.3 us -> 7.71 us  [local(): lax.all_to_all(products.reshape((subs, -1) + products.shape[1:]), 'sub',...]
  transfers between devices with their start and end apart: 22 -> 23, of which waited for: 19 -> 21; matrix products, arithmetic and copies ran while one was open for 5% -> 5% of each run, Pallas kernels for 0% -> 0%
where the time goes in v7:
time: 367 us; the launch traced here: 364 us
  blocking collectives  192 us (52%)
  waiting for transfers between devices  74.7 us (20%)
  starting transfers between devices  37.7 us (10%)
  between operations  25.2 us (7%)
  matrix products  13.8 us (4%)
  other arithmetic  11.7 us (3%)
  local copies, waits for them, and re-layouts  8.97 us (2%)
    all_to_all x6, blocking collectives, share_slots(): lax.all_to_all(mine.reshape((chips,) + tile_shape), 'zx', 0, 0, tiled=True)  92.8 us
    all_to_all x6, blocking collectives, share_slots(): lax.all_to_all(spread, 'zx', 0, 0, tiled=True).reshape(mine.shape)  82.2 us
    psum x1, waiting for transfers between devices, local(): coupling = lax.psum(partial_map, 'sub')  25.2 us
    all_to_all x2, blocking collectives, gather_rows(): pieces = lax.all_to_all(copies, 'sub', 0, 0, tiled=True)  16.9 us
    all_to_all x2, waiting for transfers between devices, local(): lax.all_to_all(products.reshape((subs, -1) + products.shape[1:]), 'sub',...  12 us
    all_to_all x1, starting transfers between devices, share_slots(): lax.all_to_all(mine.reshape((chips,) + tile_shape), 'zx', 0, 0, tiled=True)  11.3 us
    ppermute x7, waiting for transfers between devices, share_slots(): slots = slots + lax.ppermute(slots, 'core', swap)  9.34 us
    all_to_all x1, waiting for transfers between devices, share_slots(): lax.all_to_all(spread, 'zx', 0, 0, tiled=True).reshape(mine.shape)  8.66 us
  transfers between devices with their start and end apart: 23, of which 21 were waited for; matrix products, arithmetic and copies ran while one was open for 5% of the time, Pallas kernels for 0%

profile of v7, /device:TPU:32, one launch (start us, length us, event | category | flops | bytes accessed | tf_op | source)
XLA Modules:
  0.0 364.1 jit_solution(16582661585140710051)
XLA Ops:
  7.3 1.5 broadcast_in_dim.299
  8.8 4.6 %all-to-all-start = ((bf16[4,384,64]{1,2,0:T(8,128)(2,1)}), bf16[4,384,64]{1,2,0:T(8,128)(2,1)S(1)}, u32[]{:S(2)}, u32[]{:S(2)}) async-start(bf16[4,384,64]{1,2,0:T(8,128)(2,1)} %broadcast_in_dim.299), calls=%async_computation | async-start | bytes 393216 | tf_op jit(solution)/shard_map/all_to_all | solution.py:53
  13.4 1.2 dynamic_slice.29
  18.5 1.2 all-to-all-done
  20.3 1.0 convolution_convert_fusion.1
  21.3 3.6 all-to-all-start.1
  24.9 7.2 %all-to-all-done.1 = bf16[4,16,1024]{2,1,0:T(8,128)(2,1)S(1)} async-done(((bf16[4,16,1024]{2,1,0:T(8,128)(2,1)}), bf16[4,16,1024]{2,1,0:T(8,128)(2,1)S(1)}, u32[]{:S(2)}, u32[]{:S(2)}) %all-to-all-start.1) | async-done | bytes 131104 | tf_op jit(solution)/shard_map/all_to_all | solution.py:84
  34.7 11.3 %all-to-all-start.2 = ((bf16[32,16,128]{2,1,0:T(8,128)(2,1)}), bf16[32,16,128]{2,1,0:T(8,128)(2,1)S(1)}, u32[]{:S(2)}, u32[]{:S(2)}) async-start(bf16[32,16,128]{2,1,0:T(8,128)(2,1)} %bitcast.15), calls=%async_computation.2 | async-start | bytes 262144 | tf_op jit(solution)/shard_map/all_to_all | solution.py:39
  51.2 4.7 %all-to-all-done.2 = bf16[32,16,128]{2,1,0:T(8,128)(2,1)S(1)} async-done(((bf16[32,16,128]{2,1,0:T(8,128)(2,1)}), bf16[32,16,128]{2,1,0:T(8,128)(2,1)S(1)}, u32[]{:S(2)}, u32[]{:S(2)}) %all-to-all-start.2) | async-done | bytes 131104 | tf_op jit(solution)/shard_map/all_to_all | solution.py:39
  56.6 5.1 %all-to-all-start.3 = ((bf16[32,16,128]{2,1,0:T(8,128)(2,1)}), bf16[32,16,128]{2,1,0:T(8,128)(2,1)S(1)}, u32[]{:S(2)}, u32[]{:S(2)}) async-start(bf16[32,16,128]{2,1,0:T(8,128)(2,1)} %broadcast_in_dim.307), calls=%async_computation.3 | async-start | bytes 262144 | tf_op jit(solution)/shard_map/all_to_all | solution.py:42
  62.5 8.7 %all-to-all-done.3 = bf16[32,16,128]{2,1,0:T(8,128)(2,1)S(1)} async-done(((bf16[32,16,128]{2,1,0:T(8,128)(2,1)}), bf16[32,16,128]{2,1,0:T(8,128)(2,1)S(1)}, u32[]{:S(2)}, u32[]{:S(2)}) %all-to-all-start.3) | async-done | bytes 131104 | tf_op jit(solution)/shard_map/all_to_all | solution.py:42
  71.2 1.3 collective-permute-done.1
  73.4 3.9 %all-to-all-start.4 = ((bf16[4,16,1024]{2,1,0:T(8,128)(2,1)}), bf16[4,16,1024]{2,1,0:T(8,128)(2,1)}, u32[]{:S(2)}, u32[]{:S(2)}) async-start(bf16[4,16,1024]{2,1,0:T(8,128)(2,1)} %broadcast_in_dim.310), calls=%async_computation.4 | async-start | bytes 262144 | tf_op jit(solution)/shard_map/all_to_all | solution.py:53
  77.4 3.3 fusion.6
  81.6 1.3 convolution_convert_fusion
  83.4 2.3 fusion.4
  85.6 4.3 %all-to-all-start.5 = ((f32[4,16,1024]{2,1,0:T(8,128)}), f32[4,16,1024]{2,1,0:T(8,128)}, u32[]{:S(2)}, u32[]{:S(2)}) async-start(f32[4,16,1024]{2,1,0:T(8,128)} %fusion.4), calls=%async_computation.5 | async-start | bytes 524288 | tf_op jit(solution)/shard_map/all_to_all | solution.py:116
  90.6 6.2 %all-to-all-done.5 = f32[4,16,1024]{2,1,0:T(8,128)} async-done(((f32[4,16,1024]{2,1,0:T(8,128)}), f32[4,16,1024]{2,1,0:T(8,128)}, u32[]{:S(2)}, u32[]{:S(2)}) %all-to-all-start.5) | async-done | bytes 262176 | tf_op jit(solution)/shard_map/all_to_all | solution.py:116
  96.7 1.6 reduce_sum.322
  99.4 1.5 collective-permute-done.2
  101.0 14.8 %all_to_all.105 = bf16[32,16,128]{2,1,0:T(8,128)(2,1)} all-to-all(bf16[32,16,128]{2,1,0:T(8,128)(2,1)S(1)} %bitcast.206), channel_id=1, replica_groups=mesh['zx'=32,'core'=2,'sub'=4] {'zx'}, dimensions={0} | all-to-all | bytes 262144 | tf_op jit(solution)/shard_map/all_to_all | solution.py:39
  115.9 0.9 reduce_sum.323
  116.8 13.7 %all_to_all.106 = bf16[32,16,128]{2,1,0:T(8,128)(2,1)S(1)} all-to-all(bf16[32,16,128]{2,1,0:T(8,128)(2,1)S(1)} %broadcast_in_dim.312), channel_id=1, replica_groups=mesh['zx'=32,'core'=2,'sub'=4] {'zx'}, dimensions={0} | all-to-all | bytes 262144 | tf_op jit(solution)/shard_map/all_to_all | solution.py:42
  130.5 1.3 collective-permute-done.3
  132.0 8.4 %all_to_all.107 = bf16[4,16,1024]{2,1,0:T(8,128)(2,1)S(1)} all-to-all(bf16[4,16,1024]{2,1,0:T(8,128)(2,1)S(1)} %broadcast_in_dim.315), channel_id=1, replica_groups=mesh['zx'=32,'core'=2,'sub'=4] {'sub'}, dimensions={0} | all-to-all | bytes 262144 | tf_op jit(solution)/shard_map/all_to_all | solution.py:53
  140.4 1.2 fusion.2
  141.6 3.4 all-to-all-start.9
  145.8 5.9 %all-to-all-done.9 = f32[4,16,1024]{2,1,0:T(8,128)S(1)} async-done(((f32[4,16,1024]{2,1,0:T(8,128)}), f32[4,16,1024]{2,1,0:T(8,128)S(1)}, u32[]{:S(2)}, u32[]{:S(2)}) %all-to-all-start.9) | async-done | bytes 262176 | tf_op jit(solution)/shard_map/all_to_all | solution.py:116
  151.9 1.5 collective-permute-done.4
  153.6 14.1 %all_to_all.108 = bf16[32,16,128]{2,1,0:T(8,128)(2,1)S(1)} all-to-all(bf16[32,16,128]{2,1,0:T(8,128)(2,1)S(1)} %bitcast.207), channel_id=1, replica_groups=mesh['zx'=32,'core'=2,'sub'=4] {'zx'}, dimensions={0} | all-to-all | bytes 262144 | tf_op jit(solution)/shard_map/all_to_all | solution.py:39
  167.8 13.7 %all_to_all.109 = bf16[32,16,128]{2,1,0:T(8,128)(2,1)S(1)} all-to-all(bf16[32,16,128]{2,1,0:T(8,128)(2,1)S(1)} %broadcast_in_dim.317), channel_id=1, replica_groups=mesh['zx'=32,'core'=2,'sub'=4] {'zx'}, dimensions={0} | all-to-all | bytes 262144 | tf_op jit(solution)/shard_map/all_to_all | solution.py:42
  183.1 25.2 %all-reduce.2.cloned.1.call-done = bf16[1024,1024]{1,0:T(8,128)(2,1)} async-done(((bf16[1024,1024]{1,0:T(8,128)(2,1)}), bf16[1024,1024]{1,0:T(8,128)(2,1)}) %all-reduce.2.cloned.1.call-update) | async-done | bytes 2097168 | tf_op jit(solution)/shard_map/psum | solution.py:93
  208.3 2.0 fusion.20
  210.5 1.5 collective-permute-done.6
  212.1 19.8 %all_to_all.110 = bf16[32,16,128]{2,1,0:T(8,128)(2,1)} all-to-all(bf16[32,16,128]{2,1,0:T(8,128)(2,1)S(1)} %bitcast.208), channel_id=1, replica_groups=mesh['zx'=32,'core'=2,'sub'=4] {'zx'}, dimensions={0} | all-to-all | bytes 262144 | tf_op jit(solution)/shard_map/all_to_all | solution.py:39
  232.0 0.9 reduce_sum.334
  232.9 13.7 %all_to_all.111 = bf16[32,16,128]{2,1,0:T(8,128)(2,1)S(1)} all-to-all(bf16[32,16,128]{2,1,0:T(8,128)(2,1)S(1)} %broadcast_in_dim.321), channel_id=1, replica_groups=mesh['zx'=32,'core'=2,'sub'=4] {'zx'}, dimensions={0} | all-to-all | bytes 262144 | tf_op jit(solution)/shard_map/all_to_all | solution.py:42
  248.9 1.4 collective-permute-done.8
  250.4 14.8 %all_to_all.112 = bf16[32,16,128]{2,1,0:T(8,128)(2,1)} all-to-all(bf16[32,16,128]{2,1,0:T(8,128)(2,1)S(1)} %bitcast.209), channel_id=1, replica_groups=mesh['zx'=32,'core'=2,'sub'=4] {'zx'}, dimensions={0} | all-to-all | bytes 262144 | tf_op jit(solution)/shard_map/all_to_all | solution.py:39
  266.2 13.7 %all_to_all.113 = bf16[32,16,128]{2,1,0:T(8,128)(2,1)S(1)} all-to-all(bf16[32,16,128]{2,1,0:T(8,128)(2,1)S(1)} %broadcast_in_dim.325), channel_id=1, replica_groups=mesh['zx'=32,'core'=2,'sub'=4] {'zx'}, dimensions={0} | all-to-all | bytes 262144 | tf_op jit(solution)/shard_map/all_to_all | solution.py:42
  283.5 1.2 collective-permute-done.10
  284.8 15.1 %all_to_all.114 = bf16[32,16,128]{2,1,0:T(8,128)(2,1)} all-to-all(bf16[32,16,128]{2,1,0:T(8,128)(2,1)S(1)} %bitcast.210), channel_id=1, replica_groups=mesh['zx'=32,'core'=2,'sub'=4] {'zx'}, dimensions={0} | all-to-all | bytes 262144 | tf_op jit(solution)/shard_map/all_to_all | solution.py:39
  300.8 13.7 %all_to_all.115 = bf16[32,16,128]{2,1,0:T(8,128)(2,1)S(1)} all-to-all(bf16[32,16,128]{2,1,0:T(8,128)(2,1)S(1)} %broadcast_in_dim.329), channel_id=1, replica_groups=mesh['zx'=32,'core'=2,'sub'=4] {'zx'}, dimensions={0} | all-to-all | bytes 262144 | tf_op jit(solution)/shard_map/all_to_all | solution.py:42
  316.7 1.4 collective-permute-done.12
  318.2 14.1 %all_to_all.116 = bf16[32,16,128]{2,1,0:T(8,128)(2,1)S(1)} all-to-all(bf16[32,16,128]{2,1,0:T(8,128)(2,1)S(1)} %bitcast.205), channel_id=1, replica_groups=mesh['zx'=32,'core'=2,'sub'=4] {'zx'}, dimensions={0} | all-to-all | bytes 262144 | tf_op jit(solution)/shard_map/all_to_all | solution.py:39
  332.4 13.7 %all_to_all.117 = bf16[32,16,128]{2,1,0:T(8,128)(2,1)S(1)} all-to-all(bf16[32,16,128]{2,1,0:T(8,128)(2,1)S(1)} %broadcast_in_dim.333), channel_id=1, replica_groups=mesh['zx'=32,'core'=2,'sub'=4] {'zx'}, dimensions={0} | all-to-all | bytes 262144 | tf_op jit(solution)/shard_map/all_to_all | solution.py:42
  347.7 8.6 %all_to_all.118 = bf16[4,16,1024]{2,1,0:T(8,128)(2,1)S(1)} all-to-all(bf16[4,16,1024]{2,1,0:T(8,128)(2,1)S(1)} %broadcast_in_dim.334), channel_id=1, replica_groups=mesh['zx'=32,'core'=2,'sub'=4] {'sub'}, dimensions={0} | all-to-all | bytes 262144 | tf_op jit(solution)/shard_map/all_to_all | solution.py:53
  356.3 1.0 fusion.12
  (184 shorter events, 22.2 us)
Async XLA Ops:
  6.5 13.2 %copy-start = (bf16[1,384,1536]{2,1,0:T(8,128)(2,1)S(1)}, bf16[1,384,1536]{2,1,0:T(8,128)(2,1)}, u32[]{:S(2)}) copy-start(bf16[1,384,1536]{2,1,0:T(8,128)(2,1)} %param.9) | copy-start | bytes 3538948
  6.5 13.7 %copy-start.6 = (bf16[1,1024,384]{2,1,0:T(8,128)(2,1)S(1)}, bf16[1,1024,384]{2,1,0:T(8,128)(2,1)}, u32[]{:S(2)}) copy-start(bf16[1,1024,384]{2,1,0:T(8,128)(2,1)} %param.10) | copy-start | bytes 2359300
  6.5 70.8 %all-gather.3.cloned.1.call-start = ((), (), s32[]{:S(2)}) async-start(), calls=%async_computation.22 | async-start | bytes 3932160 | tf_op jit(solution)/shard_map/all_gather | solution.py:88
  8.8 23.7 %copy-start.1 = (s32[64]{0:T(128)S(1)}, s32[64]{0:T(128)}, u32[]{:S(2)}) copy-start(s32[64]{0:T(128)} %param.15) | copy-start | bytes 772
  8.8 10.9 %all-to-all-start = ((bf16[4,384,64]{1,2,0:T(8,128)(2,1)}), bf16[4,384,64]{1,2,0:T(8,128)(2,1)S(1)}, u32[]{:S(2)}, u32[]{:S(2)}) async-start(bf16[4,384,64]{1,2,0:T(8,128)(2,1)} %broadcast_in_dim.299), calls=%async_computation | async-start | bytes 393216 | tf_op jit(solution)/shard_map/all_to_all | solution.py:53
  20.2 30.8 %copy-start.19 = (f32[1,6,2,512]{3,2,1,0:T(2,128)S(1)}, f32[1,6,2,512]{3,2,1,0:T(2,128)}, u32[]{:S(2)}) copy-start(f32[1,6,2,512]{3,2,1,0:T(2,128)} %param.12) | copy-start | bytes 73732
  21.3 10.8 %all-to-all-start.1 = ((bf16[4,16,1024]{2,1,0:T(8,128)(2,1)}), bf16[4,16,1024]{2,1,0:T(8,128)(2,1)S(1)}, u32[]{:S(2)}, u32[]{:S(2)}) async-start(bf16[4,16,1024]{2,1,0:T(8,128)(2,1)} %bitcast.12), calls=%async_computation.1 | async-start | bytes 262144 | tf_op jit(solution)/shard_map/all_to_all | solution.py:84
  32.3 1.6 collective-permute-start
  34.7 21.2 %all-to-all-start.2 = ((bf16[32,16,128]{2,1,0:T(8,128)(2,1)}), bf16[32,16,128]{2,1,0:T(8,128)(2,1)S(1)}, u32[]{:S(2)}, u32[]{:S(2)}) async-start(bf16[32,16,128]{2,1,0:T(8,128)(2,1)} %bitcast.15), calls=%async_computation.2 | async-start | bytes 262144 | tf_op jit(solution)/shard_map/all_to_all | solution.py:39
  56.6 14.6 %all-to-all-start.3 = ((bf16[32,16,128]{2,1,0:T(8,128)(2,1)}), bf16[32,16,128]{2,1,0:T(8,128)(2,1)S(1)}, u32[]{:S(2)}, u32[]{:S(2)}) async-start(bf16[32,16,128]{2,1,0:T(8,128)(2,1)} %broadcast_in_dim.307), calls=%async_computation.3 | async-start | bytes 262144 | tf_op jit(solution)/shard_map/all_to_all | solution.py:42
  71.2 1.3 collective-permute-start.1
  72.7 59.3 %copy-start.9 = (f32[4,16,128]{2,1,0:T(8,128)}, f32[4,16,128]{2,1,0:T(8,128)S(1)}, u32[]{:S(2)}) copy-start(f32[4,16,128]{2,1,0:T(8,128)S(1)} %get-tuple-element.18) | copy-start | bytes 98308
  73.4 10.0 %all-to-all-start.4 = ((bf16[4,16,1024]{2,1,0:T(8,128)(2,1)}), bf16[4,16,1024]{2,1,0:T(8,128)(2,1)}, u32[]{:S(2)}, u32[]{:S(2)}) async-start(bf16[4,16,1024]{2,1,0:T(8,128)(2,1)} %broadcast_in_dim.310), calls=%async_computation.4 | async-start | bytes 262144 | tf_op jit(solution)/shard_map/all_to_all | solution.py:53
  77.3 4.2 %copy-start.7 = (bf16[1,1024,384]{2,1,0:T(8,128)(2,1)S(1)}, bf16[1,1024,384]{2,1,0:T(8,128)(2,1)}, u32[]{:S(2)}) copy-start(bf16[1,1024,384]{2,1,0:T(8,128)(2,1)} %param.10) | copy-start | bytes 2359300
  80.7 0.9 copy-start.4
  82.9 57.5 %copy-start.3 = (bf16[1024,1024]{1,0:T(8,128)(2,1)}, bf16[1024,1024]{1,0:T(8,128)(2,1)S(1)}, u32[]{:S(2)}) copy-start(bf16[1024,1024]{1,0:T(8,128)(2,1)S(1)} %convolution_convert_fusion) | copy-start | bytes 6291460
  85.6 11.1 %all-to-all-start.5 = ((f32[4,16,1024]{2,1,0:T(8,128)}), f32[4,16,1024]{2,1,0:T(8,128)}, u32[]{:S(2)}, u32[]{:S(2)}) async-start(f32[4,16,1024]{2,1,0:T(8,128)} %fusion.4), calls=%async_computation.5 | async-start | bytes 524288 | tf_op jit(solution)/shard_map/all_to_all | solution.py:116
  99.3 1.6 collective-permute-start.2
  130.5 1.3 collective-permute-start.3
  132.0 8.4 %copy-start.14 = (f32[4,16,128]{2,1,0:T(8,128)}, f32[4,16,128]{2,1,0:T(8,128)S(1)}, u32[]{:S(2)}) copy-start(f32[4,16,128]{2,1,0:T(8,128)S(1)} %get-tuple-element.16) | copy-start | bytes 98308
  141.6 10.1 %all-to-all-start.9 = ((f32[4,16,1024]{2,1,0:T(8,128)}), f32[4,16,1024]{2,1,0:T(8,128)S(1)}, u32[]{:S(2)}, u32[]{:S(2)}) async-start(f32[4,16,1024]{2,1,0:T(8,128)} %fusion.2), calls=%async_computation.9 | async-start | bytes 524288 | tf_op jit(solution)/shard_map/all_to_all | solution.py:116
  145.0 63.2 %all-reduce.2.cloned.1.call-start = ((), (), s32[]{:S(2)}) async-start(), calls=%async_computation.21 | async-start | bytes 4194304 | tf_op jit(solution)/shard_map/psum | solution.py:93
  145.7 35.8 %copy-start.18 = (f32[8,2,4,128]{3,0,2,1:T(8,128)S(1)}, f32[8,2,4,128]{3,0,2,1:T(8,128)}, u32[]{:S(2)}) copy-start(f32[8,2,4,128]{3,0,2,1:T(8,128)} %get-tuple-element.21) | copy-start | bytes 98308
  145.8 37.2 %copy-start.10 = (f32[4,16,128]{2,1,0:T(8,128)S(1)}, f32[4,16,128]{2,1,0:T(8,128)}, u32[]{:S(2)}) copy-start(f32[4,16,128]{2,1,0:T(8,128)} %copy-done.9) | copy-start | bytes 98308
  145.8 37.2 %copy-start.15 = (f32[4,16,128]{2,1,0:T(8,128)S(1)}, f32[4,16,128]{2,1,0:T(8,128)}, u32[]{:S(2)}) copy-start(f32[4,16,128]{2,1,0:T(8,128)} %copy-done.14) | copy-start | bytes 98308
  151.8 1.6 collective-permute-start.4
  181.5 1.3 collective-permute-start.5
  183.0 65.1 %copy-start.8 = (f32[8,16,128]{2,1,0:T(8,128)}, f32[8,16,128]{2,1,0:T(8,128)S(1)}, u32[]{:S(2)}) copy-start(f32[8,16,128]{2,1,0:T(8,128)S(1)} %get-tuple-element.29) | copy-start | bytes 196612
  208.2 38.4 %copy-start.17 = (f32[8,2,4,128]{3,0,2,1:T(8,128)S(1)}, f32[8,2,4,128]{3,0,2,1:T(8,128)}, u32[]{:S(2)}) copy-start(f32[8,2,4,128]{3,0,2,1:T(8,128)} %get-tuple-element.22) | copy-start | bytes 98308
  210.2 37.9 %copy-start.2 = (bf16[1024,1024]{1,0:T(8,128)(2,1)S(1)}, bf16[1024,1024]{1,0:T(8,128)(2,1)}, u32[]{:S(2)}) copy-start(bf16[1024,1024]{1,0:T(8,128)(2,1)} %all-reduce.2.cloned.1.call-done) | copy-start | bytes 6291460
  210.4 1.6 collective-permute-start.6
  246.7 1.3 collective-permute-start.7
  248.1 2.3 copy-start.11
  248.7 1.6 collective-permute-start.8
  279.9 1.4 collective-permute-start.9
  282.4 32.1 %copy-start.16 = (f32[8,2,4,128]{3,0,2,1:T(8,128)S(1)}, f32[8,2,4,128]{3,0,2,1:T(8,128)}, u32[]{:S(2)}) copy-start(f32[8,2,4,128]{3,0,2,1:T(8,128)} %get-tuple-element.24) | copy-start | bytes 98308
  282.9 1.8 collective-permute-start.10
  314.5 1.3 collective-permute-start.11
  315.9 2.3 copy-start.12
  316.4 39.9 %copy-start.5 = (bf16[384,1024]{1,0:T(8,128)(2,1)S(1)}, bf16[384,1024]{1,0:T(8,128)(2,1)}, u32[]{:S(2)}) copy-start(bf16[384,1024]{1,0:T(8,128)(2,1)} %copy-done.4) | copy-start | bytes 2359300
  316.5 1.6 collective-permute-start.12
  318.2 29.4 %copy-start.13 = (f32[4,16,128]{2,1,0:T(8,128)S(1)}, f32[4,16,128]{2,1,0:T(8,128)}, u32[]{:S(2)}) copy-start(f32[4,16,128]{2,1,0:T(8,128)} %copy-done.12) | copy-start | bytes 98308
  346.2 1.3 collective-permute-start.13
Sparse Core Ops, SparseCore 0:
  9.2 45.7 all-gather.2
  148.2 59.9 all-reduce.1

commit v8 on v6

--- a/solution.py
+++ b/solution.py
@@ -47,10 +47,31 @@
     )
 
 
+def from_partners(value_for, subs):
+    received = [value_for(0)]
+    for hop in range(1, subs):
+        received.append(lax.ppermute(value_for(hop), "sub", [(i, i ^ hop) for i in range(subs)]))
+    return jnp.stack(received)
+
+
 def gather_rows(rows, subs):
+    received = from_partners(lambda hop: rows, subs)
+    order = lax.axis_index("sub") ^ jnp.arange(subs, dtype=jnp.int32)
+    return received[order].reshape((subs * rows.shape[0],) + rows.shape[1:])
+
+
+def broadcast_rows(rows, subs):
     copies = jnp.broadcast_to(rows[None], (subs,) + rows.shape)
     pieces = lax.all_to_all(copies, "sub", 0, 0, tiled=True)
     return pieces.reshape((subs * rows.shape[0],) + rows.shape[1:])
+
+
+def scatter_sum(blocks, subs):
+    own = lax.axis_index("sub")
+    received = from_partners(
+        lambda hop: lax.dynamic_index_in_dim(blocks, own ^ hop, 0, keepdims=False), subs
+    )
+    return jnp.sum(received.astype(jnp.float32), axis=0)
 
 
 def local(
@@ -75,15 +96,12 @@
         return jnp.dot(inverse_rows, shard_rows, preferred_element_type=jnp.float32)
 
     subs = lax.axis_size("sub")
-    solved = apply_inverse(gather_rows(excite_rows, subs))
+    solved = apply_inverse(broadcast_rows(excite_rows, subs))
     solved_half = solved.astype(jnp.bfloat16)
     partial_incident = lax.dot_general(
         solved_half, agg_columns, CONTRACT_FIRST, preferred_element_type=jnp.float32
     ).astype(jnp.bfloat16)
-    incident_pieces = lax.all_to_all(
-        partial_incident.reshape((subs, -1) + partial_incident.shape[1:]), "sub", 0, 0, tiled=True
-    )
-    incident = jnp.sum(incident_pieces.astype(jnp.float32), axis=0)
+    incident = scatter_sum(partial_incident.reshape((subs, -1) + partial_incident.shape[1:]), subs)
     spread = apply_inverse(lax.all_gather(disagg_rows, "sub", axis=0, tiled=True))
     spread_half = spread.astype(jnp.bfloat16)
     partial_map = lax.dot_general(
@@ -112,10 +130,8 @@
         elif segment_k == 1:
             all_fields = gather_rows(from_tiles(incoming).astype(jnp.bfloat16), subs)
             products = jnp.dot(all_fields, partial_map, preferred_element_type=jnp.float32)
-            product_pieces = lax.all_to_all(
-                products.reshape((subs, -1) + products.shape[1:]), "sub", 0, 0, tiled=True
-            )
-            pattern = (incident - jnp.sum(product_pieces, axis=0)).astype(jnp.bfloat16)
+            coupled = scatter_sum(products.reshape((subs, -1) + products.shape[1:]), subs)
+            pattern = (incident - coupled).astype(jnp.bfloat16)
         else:
             pattern = (
                 incident

time: 347 us -> 344 us (level)
  blocking collectives: 184 us -> 175 us
  starting transfers between devices: 35.4 us -> 42.2 us
  local copies, waits for them, and re-layouts: 9.71 us -> 16 us
  waiting for transfers between devices: 65.5 us -> 61.2 us
    ppermute x0 -> x12, starting transfers between devices: none -> 19 us  [from_partners(): lax.ppermute(value_for(hop), 'sub', [(i, i ^ hop) for i in range(subs)])]
    all_to_all x4 -> x1, waiting for transfers between devices: 14.8 us -> 1.13 us  [broadcast_rows(): pieces = lax.all_to_all(copies, 'sub', 0, 0, tiled=True)]
    all_to_all x4 -> x1, starting transfers between devices: 16.6 us -> 4.46 us  [broadcast_rows(): pieces = lax.all_to_all(copies, 'sub', 0, 0, tiled=True)]
    ppermute x0 -> x12, waiting for transfers between devices: none -> 11.3 us  [from_partners(): lax.ppermute(value_for(hop), 'sub', [(i, i ^ hop) for i in range(subs)])]
    all_to_all x1 -> x0, blocking collectives: 8.57 us -> none  [gather_rows(): pieces = lax.all_to_all(copies, 'sub', 0, 0, tiled=True)]
    unnamed x47 -> x51, local copies, waits for them, and re-layouts: 1.03 us -> 6.07 us
  transfers between devices with their start and end apart: 22 -> 31, of which waited for: 19 -> 24; matrix products, arithmetic and copies ran while one was open for 5% -> 5% of each run, Pallas kernels for 0% -> 0%
where the time goes in v8:
time: 344 us; the launch traced here: 342 us
  blocking collectives  175 us (51%)
  waiting for transfers between devices  61.2 us (18%)
  starting transfers between devices  42.2 us (12%)
  between operations  25.1 us (7%)
  local copies, waits for them, and re-layouts  16 us (5%)
  matrix products  12.3 us (4%)
  other arithmetic  10.1 us (3%)
    all_to_all x6, blocking collectives, share_slots(): lax.all_to_all(mine.reshape((chips,) + tile_shape), 'zx', 0, 0, tiled=True)  93.1 us
    all_to_all x6, blocking collectives, share_slots(): lax.all_to_all(spread, 'zx', 0, 0, tiled=True).reshape(mine.shape)  82.2 us
    psum x1, waiting for transfers between devices, local(): coupling = lax.psum(partial_map, 'sub')  21.8 us
    ppermute x12, starting transfers between devices, from_partners(): lax.ppermute(value_for(hop), 'sub', [(i, i ^ hop) for i in range(subs)])  19 us
    all_to_all x1, starting transfers between devices, share_slots(): lax.all_to_all(mine.reshape((chips,) + tile_shape), 'zx', 0, 0, tiled=True)  11.5 us
    ppermute x12, waiting for transfers between devices, from_partners(): lax.ppermute(value_for(hop), 'sub', [(i, i ^ hop) for i in range(subs)])  11.3 us
    ppermute x7, waiting for transfers between devices, share_slots(): slots = slots + lax.ppermute(slots, 'core', swap)  8.98 us
    all_to_all x1, waiting for transfers between devices, share_slots(): lax.all_to_all(spread, 'zx', 0, 0, tiled=True).reshape(mine.shape)  8.64 us
  transfers between devices with their start and end apart: 31, of which 24 were waited for; matrix products, arithmetic and copies ran while one was open for 5% of the time, Pallas kernels for 0%

profile of v8, /device:TPU:32, one launch (start us, length us, event | category | flops | bytes accessed | tf_op | source)
XLA Modules:
  0.0 342.2 jit_solution(2991050584387418596)
XLA Ops:
  7.3 1.5 broadcast_in_dim.283
  8.8 4.5 %all-to-all-start = ((bf16[4,384,64]{1,2,0:T(8,128)(2,1)}), bf16[4,384,64]{1,2,0:T(8,128)(2,1)S(1)}, u32[]{:S(2)}, u32[]{:S(2)}) async-start(bf16[4,384,64]{1,2,0:T(8,128)(2,1)} %broadcast_in_dim.283), calls=%async_computation | async-start | bytes 393216 | tf_op jit(solution)/shard_map/all_to_all | solution.py:65
  13.2 1.3 dynamic_slice.55
  18.4 1.1 all-to-all-done
  21.5 2.7 collective-permute-start.1
  24.2 1.1 collective-permute-start.2
  25.3 1.6 collective-permute-done.1
  26.9 2.7 collective-permute-done.2
  32.1 11.5 %all-to-all-start.1 = ((bf16[32,16,128]{2,1,0:T(8,128)(2,1)}), bf16[32,16,128]{2,1,0:T(8,128)(2,1)S(1)}, u32[]{:S(2)}, u32[]{:S(2)}) async-start(bf16[32,16,128]{2,1,0:T(8,128)(2,1)} %bitcast.21), calls=%async_computation.1 | async-start | bytes 262144 | tf_op jit(solution)/shard_map/all_to_all | solution.py:38
  48.8 4.8 %all-to-all-done.1 = bf16[32,16,128]{2,1,0:T(8,128)(2,1)S(1)} async-done(((bf16[32,16,128]{2,1,0:T(8,128)(2,1)}), bf16[32,16,128]{2,1,0:T(8,128)(2,1)S(1)}, u32[]{:S(2)}, u32[]{:S(2)}) %all-to-all-start.1) | async-done | bytes 131104 | tf_op jit(solution)/shard_map/all_to_all | solution.py:38
  54.3 5.0 %all-to-all-start.2 = ((bf16[32,16,128]{2,1,0:T(8,128)(2,1)}), bf16[32,16,128]{2,1,0:T(8,128)(2,1)S(1)}, u32[]{:S(2)}, u32[]{:S(2)}) async-start(bf16[32,16,128]{2,1,0:T(8,128)(2,1)} %broadcast_in_dim.291), calls=%async_computation.2 | async-start | bytes 262144 | tf_op jit(solution)/shard_map/all_to_all | solution.py:41
  60.2 8.6 %all-to-all-done.2 = bf16[32,16,128]{2,1,0:T(8,128)(2,1)S(1)} async-done(((bf16[32,16,128]{2,1,0:T(8,128)(2,1)}), bf16[32,16,128]{2,1,0:T(8,128)(2,1)S(1)}, u32[]{:S(2)}, u32[]{:S(2)}) %all-to-all-start.2) | async-done | bytes 131104 | tf_op jit(solution)/shard_map/all_to_all | solution.py:41
  68.9 1.3 collective-permute-done.4
  70.4 2.6 collective-permute-start.6
  73.1 2.1 collective-permute-start.7
  75.9 2.2 collective-permute-done.7
  78.2 1.2 gather_fusion.1
  79.4 3.3 fusion.4
  83.6 1.3 convolution_convert_fusion
  85.0 2.3 fusion.2
  87.2 1.6 dynamic-slice_bitcast_fusion.3
  88.8 3.5 %collective-permute-start.9 = (f32[16,1024]{1,0:T(8,128)}, f32[16,1024]{1,0:T(8,128)}, u32[]{:S(2)}, u32[]{:S(2)}) collective-permute-start(f32[16,1024]{1,0:T(8,128)} %get-tuple-element.34), channel_id=1, source_target_pairs={{0,2},{1,3},{2,0},{3,1},{4,6},{5,7},{6,4},{7,5},{8,10},{9,11},{10,... | collective-permute-start | bytes 196616 | tf_op jit(solution)/shard_map/ppermute | solution.py:53
  92.4 1.2 collective-permute-start.10
  96.6 1.6 collective-permute-done.10
  99.4 1.5 collective-permute-done.11
  101.1 14.2 %all_to_all.75 = bf16[32,16,128]{2,1,0:T(8,128)(2,1)S(1)} all-to-all(bf16[32,16,128]{2,1,0:T(8,128)(2,1)S(1)} %bitcast.250), channel_id=1, replica_groups=mesh['zx'=32,'core'=2,'sub'=4] {'zx'}, dimensions={0} | all-to-all | bytes 262144 | tf_op jit(solution)/shard_map/all_to_all | solution.py:38
  115.3 13.7 %all_to_all.76 = bf16[32,16,128]{2,1,0:T(8,128)(2,1)S(1)} all-to-all(bf16[32,16,128]{2,1,0:T(8,128)(2,1)S(1)} %broadcast_in_dim.295), channel_id=1, replica_groups=mesh['zx'=32,'core'=2,'sub'=4] {'zx'}, dimensions={0} | all-to-all | bytes 262144 | tf_op jit(solution)/shard_map/all_to_all | solution.py:41
  130.5 21.8 %all-reduce.2.cloned.1.call-done = bf16[1024,1024]{1,0:T(8,128)(2,1)} async-done(((bf16[1024,1024]{1,0:T(8,128)(2,1)}), bf16[1024,1024]{1,0:T(8,128)(2,1)}) %all-reduce.2.cloned.1.call-update) | async-done | bytes 2097168 | tf_op jit(solution)/shard_map/psum | solution.py:110
  152.3 2.0 fusion.20
  154.5 1.5 collective-permute-done.13
  156.2 19.8 %all_to_all.77 = bf16[32,16,128]{2,1,0:T(8,128)(2,1)} all-to-all(bf16[32,16,128]{2,1,0:T(8,128)(2,1)S(1)} %bitcast.251), channel_id=1, replica_groups=mesh['zx'=32,'core'=2,'sub'=4] {'zx'}, dimensions={0} | all-to-all | bytes 262144 | tf_op jit(solution)/shard_map/all_to_all | solution.py:38
  177.0 13.7 %all_to_all.78 = bf16[32,16,128]{2,1,0:T(8,128)(2,1)S(1)} all-to-all(bf16[32,16,128]{2,1,0:T(8,128)(2,1)S(1)} %broadcast_in_dim.299), channel_id=1, replica_groups=mesh['zx'=32,'core'=2,'sub'=4] {'zx'}, dimensions={0} | all-to-all | bytes 262144 | tf_op jit(solution)/shard_map/all_to_all | solution.py:41
  194.2 1.2 collective-permute-done.15
  195.5 15.1 %all_to_all.79 = bf16[32,16,128]{2,1,0:T(8,128)(2,1)} all-to-all(bf16[32,16,128]{2,1,0:T(8,128)(2,1)S(1)} %bitcast.252), channel_id=1, replica_groups=mesh['zx'=32,'core'=2,'sub'=4] {'zx'}, dimensions={0} | all-to-all | bytes 262144 | tf_op jit(solution)/shard_map/all_to_all | solution.py:38
  211.5 13.7 %all_to_all.80 = bf16[32,16,128]{2,1,0:T(8,128)(2,1)S(1)} all-to-all(bf16[32,16,128]{2,1,0:T(8,128)(2,1)S(1)} %broadcast_in_dim.303), channel_id=1, replica_groups=mesh['zx'=32,'core'=2,'sub'=4] {'zx'}, dimensions={0} | all-to-all | bytes 262144 | tf_op jit(solution)/shard_map/all_to_all | solution.py:41
  227.4 1.4 collective-permute-done.17
  229.0 14.8 %all_to_all.81 = bf16[32,16,128]{2,1,0:T(8,128)(2,1)} all-to-all(bf16[32,16,128]{2,1,0:T(8,128)(2,1)S(1)} %bitcast.253), channel_id=1, replica_groups=mesh['zx'=32,'core'=2,'sub'=4] {'zx'}, dimensions={0} | all-to-all | bytes 262144 | tf_op jit(solution)/shard_map/all_to_all | solution.py:38
  244.8 13.7 %all_to_all.82 = bf16[32,16,128]{2,1,0:T(8,128)(2,1)S(1)} all-to-all(bf16[32,16,128]{2,1,0:T(8,128)(2,1)S(1)} %broadcast_in_dim.307), channel_id=1, replica_groups=mesh['zx'=32,'core'=2,'sub'=4] {'zx'}, dimensions={0} | all-to-all | bytes 262144 | tf_op jit(solution)/shard_map/all_to_all | solution.py:41
  262.0 1.2 collective-permute-done.19
  263.3 15.1 %all_to_all.83 = bf16[32,16,128]{2,1,0:T(8,128)(2,1)} all-to-all(bf16[32,16,128]{2,1,0:T(8,128)(2,1)S(1)} %bitcast.254), channel_id=1, replica_groups=mesh['zx'=32,'core'=2,'sub'=4] {'zx'}, dimensions={0} | all-to-all | bytes 262144 | tf_op jit(solution)/shard_map/all_to_all | solution.py:38
  279.3 13.7 %all_to_all.84 = bf16[32,16,128]{2,1,0:T(8,128)(2,1)S(1)} all-to-all(bf16[32,16,128]{2,1,0:T(8,128)(2,1)S(1)} %broadcast_in_dim.311), channel_id=1, replica_groups=mesh['zx'=32,'core'=2,'sub'=4] {'zx'}, dimensions={0} | all-to-all | bytes 262144 | tf_op jit(solution)/shard_map/all_to_all | solution.py:41
  295.2 1.4 collective-permute-done.21
  296.8 14.1 %all_to_all.85 = bf16[32,16,128]{2,1,0:T(8,128)(2,1)S(1)} all-to-all(bf16[32,16,128]{2,1,0:T(8,128)(2,1)S(1)} %bitcast.249), channel_id=1, replica_groups=mesh['zx'=32,'core'=2,'sub'=4] {'zx'}, dimensions={0} | all-to-all | bytes 262144 | tf_op jit(solution)/shard_map/all_to_all | solution.py:38
  311.0 13.7 %all_to_all.86 = bf16[32,16,128]{2,1,0:T(8,128)(2,1)S(1)} all-to-all(bf16[32,16,128]{2,1,0:T(8,128)(2,1)S(1)} %broadcast_in_dim.315), channel_id=1, replica_groups=mesh['zx'=32,'core'=2,'sub'=4] {'zx'}, dimensions={0} | all-to-all | bytes 262144 | tf_op jit(solution)/shard_map/all_to_all | solution.py:41
  326.6 2.0 collective-permute-start.24
  328.6 2.4 collective-permute-start.25
  332.0 1.7 collective-permute-done.25
  334.3 1.0 fusion.10
  (208 shorter events, 32.1 us)
Async XLA Ops:
  6.5 13.0 %copy-start = (bf16[1,384,1536]{2,1,0:T(8,128)(2,1)S(1)}, bf16[1,384,1536]{2,1,0:T(8,128)(2,1)}, u32[]{:S(2)}) copy-start(bf16[1,384,1536]{2,1,0:T(8,128)(2,1)} %param.9) | copy-start | bytes 3538948
  6.5 13.6 %copy-start.6 = (bf16[1,1024,384]{2,1,0:T(8,128)(2,1)S(1)}, bf16[1,1024,384]{2,1,0:T(8,128)(2,1)}, u32[]{:S(2)}) copy-start(bf16[1,1024,384]{2,1,0:T(8,128)(2,1)} %param.10) | copy-start | bytes 2359300
  6.5 72.9 %all-gather.3.cloned.1.call-start = ((), (), s32[]{:S(2)}) async-start(), calls=%async_computation.16 | async-start | bytes 3932160 | tf_op jit(solution)/shard_map/all_gather | solution.py:105
  8.8 10.8 %all-to-all-start = ((bf16[4,384,64]{1,2,0:T(8,128)(2,1)}), bf16[4,384,64]{1,2,0:T(8,128)(2,1)S(1)}, u32[]{:S(2)}, u32[]{:S(2)}) async-start(bf16[4,384,64]{1,2,0:T(8,128)(2,1)} %broadcast_in_dim.283), calls=%async_computation | async-start | bytes 393216 | tf_op jit(solution)/shard_map/all_to_all | solution.py:65
  13.2 16.7 %copy-start.1 = (s32[64]{0:T(128)S(1)}, s32[64]{0:T(128)}, u32[]{:S(2)}) copy-start(s32[64]{0:T(128)} %param.15) | copy-start | bytes 772
  20.1 28.6 %copy-start.19 = (f32[1,6,2,512]{3,2,1,0:T(2,128)S(1)}, f32[1,6,2,512]{3,2,1,0:T(2,128)}, u32[]{:S(2)}) copy-start(f32[1,6,2,512]{3,2,1,0:T(2,128)} %param.12) | copy-start | bytes 73732
  20.5 4.8 %collective-permute-start = (bf16[16,1024]{1,0:T(8,128)(2,1)S(1)}, bf16[16,1024]{1,0:T(8,128)(2,1)S(1)}, u32[]{:S(2)}, u32[]{:S(2)}) collective-permute-start(bf16[16,1024]{1,0:T(8,128)(2,1)S(1)} %get-tuple-element.39), channel_id=1, source_target_pairs={{0,1},{1,0},{2,3},{3,2},{4,5},{5,4},{6,7},{7,6},{8,9},{9,8},{10,11... | collective-permute-start | bytes 98312 | tf_op jit(solution)/shard_map/ppermute | solution.py:53
  21.5 5.4 %collective-permute-start.1 = (bf16[16,1024]{1,0:T(8,128)(2,1)S(1)}, bf16[16,1024]{1,0:T(8,128)(2,1)S(1)}, u32[]{:S(2)}, u32[]{:S(2)}) collective-permute-start(bf16[16,1024]{1,0:T(8,128)(2,1)S(1)} %get-tuple-element.38), channel_id=1, source_target_pairs={{0,2},{1,3},{2,0},{3,1},{4,6},{5,7},{6,4},{7,5},{8,10},{9,11},{10,... | collective-permute-start | bytes 98312 | tf_op jit(solution)/shard_map/ppermute | solution.py:53
  24.2 5.4 %collective-permute-start.2 = (bf16[16,1024]{1,0:T(8,128)(2,1)S(1)}, bf16[16,1024]{1,0:T(8,128)(2,1)S(1)}, u32[]{:S(2)}, u32[]{:S(2)}) collective-permute-start(bf16[16,1024]{1,0:T(8,128)(2,1)S(1)} %get-tuple-element.37), channel_id=1, source_target_pairs={{0,3},{1,2},{2,1},{3,0},{4,7},{5,6},{6,5},{7,4},{8,11},{9,10},{10,... | collective-permute-start | bytes 98312 | tf_op jit(solution)/shard_map/ppermute | solution.py:53
  29.8 1.6 collective-permute-start.3
  32.1 21.4 %all-to-all-start.1 = ((bf16[32,16,128]{2,1,0:T(8,128)(2,1)}), bf16[32,16,128]{2,1,0:T(8,128)(2,1)S(1)}, u32[]{:S(2)}, u32[]{:S(2)}) async-start(bf16[32,16,128]{2,1,0:T(8,128)(2,1)} %bitcast.21), calls=%async_computation.1 | async-start | bytes 262144 | tf_op jit(solution)/shard_map/all_to_all | solution.py:38
  54.3 14.5 %all-to-all-start.2 = ((bf16[32,16,128]{2,1,0:T(8,128)(2,1)}), bf16[32,16,128]{2,1,0:T(8,128)(2,1)S(1)}, u32[]{:S(2)}, u32[]{:S(2)}) async-start(bf16[32,16,128]{2,1,0:T(8,128)(2,1)} %broadcast_in_dim.291), calls=%async_computation.2 | async-start | bytes 262144 | tf_op jit(solution)/shard_map/all_to_all | solution.py:41
  68.8 1.3 collective-permute-start.4
  70.3 9.1 %copy-start.11 = (f32[4,16,128]{2,1,0:T(8,128)}, f32[4,16,128]{2,1,0:T(8,128)S(1)}, u32[]{:S(2)}) copy-start(f32[4,16,128]{2,1,0:T(8,128)S(1)} %get-tuple-element.18) | copy-start | bytes 98308
  70.3 5.5 %collective-permute-start.5 = (bf16[16,1024]{1,0:T(8,128)(2,1)S(1)}, bf16[16,1024]{1,0:T(8,128)(2,1)S(1)}, u32[]{:S(2)}, u32[]{:S(2)}) collective-permute-start(bf16[16,1024]{1,0:T(8,128)(2,1)S(1)} %bitcast.285), channel_id=1, source_target_pairs={{0,1},{1,0},{2,3},{3,2},{4,5},{5,4},{6,7},{7,6},{8,9},{9,8},{10,11... | collective-permute-start | bytes 98312 | tf_op jit(solution)/shard_map/ppermute | solution.py:53
  70.4 5.5 %collective-permute-start.6 = (bf16[16,1024]{1,0:T(8,128)(2,1)S(1)}, bf16[16,1024]{1,0:T(8,128)(2,1)S(1)}, u32[]{:S(2)}, u32[]{:S(2)}) collective-permute-start(bf16[16,1024]{1,0:T(8,128)(2,1)S(1)} %bitcast.286), channel_id=1, source_target_pairs={{0,2},{1,3},{2,0},{3,1},{4,6},{5,7},{6,4},{7,5},{8,10},{9,11},{10,... | collective-permute-start | bytes 98312 | tf_op jit(solution)/shard_map/ppermute | solution.py:53
  73.1 5.1 %collective-permute-start.7 = (bf16[16,1024]{1,0:T(8,128)(2,1)S(1)}, bf16[16,1024]{1,0:T(8,128)(2,1)S(1)}, u32[]{:S(2)}, u32[]{:S(2)}) collective-permute-start(bf16[16,1024]{1,0:T(8,128)(2,1)S(1)} %bitcast.287), channel_id=1, source_target_pairs={{0,3},{1,2},{2,1},{3,0},{4,7},{5,6},{6,5},{7,4},{8,11},{9,10},{10,... | collective-permute-start | bytes 98312 | tf_op jit(solution)/shard_map/ppermute | solution.py:53
  79.4 4.2 %copy-start.7 = (bf16[1,1024,384]{2,1,0:T(8,128)(2,1)S(1)}, bf16[1,1024,384]{2,1,0:T(8,128)(2,1)}, u32[]{:S(2)}) copy-start(bf16[1,1024,384]{2,1,0:T(8,128)(2,1)} %param.10) | copy-start | bytes 2359300
  85.0 8.6 %copy-start.3 = (bf16[1024,1024]{1,0:T(8,128)(2,1)}, bf16[1024,1024]{1,0:T(8,128)(2,1)S(1)}, u32[]{:S(2)}) copy-start(bf16[1024,1024]{1,0:T(8,128)(2,1)S(1)} %convolution_convert_fusion) | copy-start | bytes 6291460
  87.2 65.1 %all-reduce.2.cloned.1.call-start = ((), (), s32[]{:S(2)}) async-start(), calls=%async_computation.15 | async-start | bytes 4194304 | tf_op jit(solution)/shard_map/psum | solution.py:110
  88.8 5.6 %collective-permute-start.8 = (f32[16,1024]{1,0:T(8,128)}, f32[16,1024]{1,0:T(8,128)}, u32[]{:S(2)}, u32[]{:S(2)}) collective-permute-start(f32[16,1024]{1,0:T(8,128)} %get-tuple-element.35), channel_id=1, source_target_pairs={{0,1},{1,0},{2,3},{3,2},{4,5},{5,4},{6,7},{7,6},{8,9},{9,8},{10,11... | collective-permute-start | bytes 196616 | tf_op jit(solution)/shard_map/ppermute | solution.py:53
  88.8 6.9 %collective-permute-start.9 = (f32[16,1024]{1,0:T(8,128)}, f32[16,1024]{1,0:T(8,128)}, u32[]{:S(2)}, u32[]{:S(2)}) collective-permute-start(f32[16,1024]{1,0:T(8,128)} %get-tuple-element.34), channel_id=1, source_target_pairs={{0,2},{1,3},{2,0},{3,1},{4,6},{5,7},{6,4},{7,5},{8,10},{9,11},{10,... | collective-permute-start | bytes 196616 | tf_op jit(solution)/shard_map/ppermute | solution.py:53
  92.4 5.8 %collective-permute-start.10 = (f32[16,1024]{1,0:T(8,128)}, f32[16,1024]{1,0:T(8,128)}, u32[]{:S(2)}, u32[]{:S(2)}) collective-permute-start(f32[16,1024]{1,0:T(8,128)} %get-tuple-element.33), channel_id=1, source_target_pairs={{0,3},{1,2},{2,1},{3,0},{4,7},{5,6},{6,5},{7,4},{8,11},{9,10},{10,... | collective-permute-start | bytes 196616 | tf_op jit(solution)/shard_map/ppermute | solution.py:53
  93.6 35.4 %copy-start.18 = (f32[8,2,4,128]{3,0,2,1:T(8,128)S(1)}, f32[8,2,4,128]{3,0,2,1:T(8,128)}, u32[]{:S(2)}) copy-start(f32[8,2,4,128]{3,0,2,1:T(8,128)} %get-tuple-element.20) | copy-start | bytes 98308
  95.3 57.0 %copy-start.12 = (f32[4,16,128]{2,1,0:T(8,128)S(1)}, f32[4,16,128]{2,1,0:T(8,128)}, u32[]{:S(2)}) copy-start(f32[4,16,128]{2,1,0:T(8,128)} %copy-done.11) | copy-start | bytes 98308
  99.2 1.8 collective-permute-start.11
  129.0 1.3 collective-permute-start.12
  130.5 21.8 %copy-start.13 = (f32[4,16,128]{2,1,0:T(8,128)}, f32[4,16,128]{2,1,0:T(8,128)S(1)}, u32[]{:S(2)}) copy-start(f32[4,16,128]{2,1,0:T(8,128)S(1)} %get-tuple-element.15) | copy-start | bytes 98308
  130.5 21.8 %copy-start.14 = (f32[4,16,128]{2,1,0:T(8,128)}, f32[4,16,128]{2,1,0:T(8,128)S(1)}, u32[]{:S(2)}) copy-start(f32[4,16,128]{2,1,0:T(8,128)S(1)} %get-tuple-element.16) | copy-start | bytes 98308
  154.3 38.8 %copy-start.2 = (bf16[1024,1024]{1,0:T(8,128)(2,1)S(1)}, bf16[1024,1024]{1,0:T(8,128)(2,1)}, u32[]{:S(2)}) copy-start(bf16[1024,1024]{1,0:T(8,128)(2,1)} %all-reduce.2.cloned.1.call-done) | copy-start | bytes 6291460
  154.4 1.6 collective-permute-start.13
  190.7 1.4 collective-permute-start.14
  193.1 33.6 %copy-start.8 = (f32[8,16,128]{2,1,0:T(8,128)}, f32[8,16,128]{2,1,0:T(8,128)S(1)}, u32[]{:S(2)}) copy-start(f32[8,16,128]{2,1,0:T(8,128)S(1)} %get-tuple-element.29) | copy-start | bytes 196612
  193.1 32.1 %copy-start.17 = (f32[8,2,4,128]{3,0,2,1:T(8,128)S(1)}, f32[8,2,4,128]{3,0,2,1:T(8,128)}, u32[]{:S(2)}) copy-start(f32[8,2,4,128]{3,0,2,1:T(8,128)} %get-tuple-element.22) | copy-start | bytes 98308
  193.6 1.8 collective-permute-start.15
  225.2 1.3 collective-permute-start.16
  227.2 1.6 collective-permute-start.17
  258.5 1.4 collective-permute-start.18
  260.9 32.1 %copy-start.16 = (f32[8,2,4,128]{3,0,2,1:T(8,128)S(1)}, f32[8,2,4,128]{3,0,2,1:T(8,128)}, u32[]{:S(2)}) copy-start(f32[8,2,4,128]{3,0,2,1:T(8,128)} %get-tuple-element.24) | copy-start | bytes 98308
  261.4 1.8 collective-permute-start.19
  293.0 1.3 collective-permute-start.20
  295.0 39.3 %copy-start.5 = (bf16[384,1024]{1,0:T(8,128)(2,1)S(1)}, bf16[384,1024]{1,0:T(8,128)(2,1)}, u32[]{:S(2)}) copy-start(bf16[384,1024]{1,0:T(8,128)(2,1)} %copy-done.4) | copy-start | bytes 2359300
  295.0 1.6 collective-permute-start.21
  296.8 29.4 %copy-start.10 = (f32[4,16,128]{2,1,0:T(8,128)S(1)}, f32[4,16,128]{2,1,0:T(8,128)}, u32[]{:S(2)}) copy-start(f32[4,16,128]{2,1,0:T(8,128)} %copy-done.9) | copy-start | bytes 98308
  324.7 1.3 collective-permute-start.22
  326.2 4.9 %collective-permute-start.23 = (bf16[16,1024]{1,0:T(8,128)(2,1)S(1)}, bf16[16,1024]{1,0:T(8,128)(2,1)S(1)}, u32[]{:S(2)}, u32[]{:S(2)}) collective-permute-start(bf16[16,1024]{1,0:T(8,128)(2,1)S(1)} %copy_bitcast_fusion), channel_id=1, source_target_pairs={{0,1},{1,0},{2,3},{3,2},{4,5},{5,4},{6,7},{7,6},{8,9},{9,8},{10,11... | collective-permute-start | bytes 98312 | tf_op jit(solution)/shard_map/ppermute | solution.py:53
  326.6 5.4 %collective-permute-start.24 = (bf16[16,1024]{1,0:T(8,128)(2,1)S(1)}, bf16[16,1024]{1,0:T(8,128)(2,1)S(1)}, u32[]{:S(2)}, u32[]{:S(2)}) collective-permute-start(bf16[16,1024]{1,0:T(8,128)(2,1)S(1)} %copy_bitcast_fusion), channel_id=1, source_target_pairs={{0,2},{1,3},{2,0},{3,1},{4,6},{5,7},{6,4},{7,5},{8,10},{9,11},{10,... | collective-permute-start | bytes 98312 | tf_op jit(solution)/shard_map/ppermute | solution.py:53
  328.6 5.1 %collective-permute-start.25 = (bf16[16,1024]{1,0:T(8,128)(2,1)S(1)}, bf16[16,1024]{1,0:T(8,128)(2,1)S(1)}, u32[]{:S(2)}, u32[]{:S(2)}) collective-permute-start(bf16[16,1024]{1,0:T(8,128)(2,1)S(1)} %copy_bitcast_fusion), channel_id=1, source_target_pairs={{0,3},{1,2},{2,1},{3,0},{4,7},{5,6},{6,5},{7,4},{8,11},{9,10},{10,... | collective-permute-start | bytes 98312 | tf_op jit(solution)/shard_map/ppermute | solution.py:53
  (3 other events, 5.5 us)
Sparse Core Ops, SparseCore 0:
  9.2 45.1 all-gather.2
  93.7 58.5 all-reduce.1

commit v9 on v8

--- a/solution.py
+++ b/solution.py
@@ -102,12 +102,19 @@
         solved_half, agg_columns, CONTRACT_FIRST, preferred_element_type=jnp.float32
     ).astype(jnp.bfloat16)
     incident = scatter_sum(partial_incident.reshape((subs, -1) + partial_incident.shape[1:]), subs)
-    spread = apply_inverse(lax.all_gather(disagg_rows, "sub", axis=0, tiled=True))
+    sub_index = lax.axis_index("sub")
+    block = disagg_rows.shape[0]
+    disagg_parts = from_partners(lambda hop: disagg_rows, subs)
+    spread = jnp.zeros((inverse_rows.shape[0], disagg_rows.shape[1]), jnp.float32)
+    for hop in range(subs):
+        columns = lax.dynamic_slice_in_dim(inverse_rows, (sub_index ^ hop) * block, block, axis=1)
+        spread = spread + jnp.dot(columns, disagg_parts[hop], preferred_element_type=jnp.float32)
     spread_half = spread.astype(jnp.bfloat16)
     partial_map = lax.dot_general(
         spread_half, agg_columns, CONTRACT_FIRST, preferred_element_type=jnp.float32
     ).astype(jnp.bfloat16)
-    coupling = lax.psum(partial_map, "sub")
+    map_share = scatter_sum(partial_map.reshape((subs, -1) + partial_map.shape[1:]), subs)
+    coupling = gather_rows(map_share.astype(jnp.bfloat16), subs)
 
     domains = sweep_order.shape[0]
     members = domains // SEGMENTS

time: 344 us -> 365 us (1.061)
  blocking collectives: 175 us -> 143 us
  starting transfers between devices: 42.2 us -> 68.9 us
  waiting for transfers between devices: 61.2 us -> 79.8 us
  between operations: 25.1 us -> 12.8 us
  other arithmetic: 10.1 us -> 19.8 us
  local copies, waits for them, and re-layouts: 16 us -> 20.7 us
  matrix products: 12.3 us -> 16.8 us
    psum x1 -> x0, waiting for transfers between devices: 21.8 us -> none  [local(): coupling = lax.psum(partial_map, 'sub')]
    ppermute x12 -> x21, waiting for transfers between devices: 11.3 us -> 32.9 us  [from_partners(): lax.ppermute(value_for(hop), 'sub', [(i, i ^ hop) for i in range(subs)])]
    all_to_all x6 -> x5, blocking collectives: 93.1 us -> 74.9 us  [share_slots(): lax.all_to_all(mine.reshape((chips,) + tile_shape), 'zx', 0, 0, tiled=True)]
    ppermute x12 -> x21, starting transfers between devices: 19 us -> 35.6 us  [from_partners(): lax.ppermute(value_for(hop), 'sub', [(i, i ^ hop) for i in range(subs)])]
    all_to_all x1, waiting for transfers between devices: 1.13 us -> 17.4 us  [broadcast_rows(): pieces = lax.all_to_all(copies, 'sub', 0, 0, tiled=True)]
    all_to_all x6 -> x5, blocking collectives: 82.2 us -> 68.5 us  [share_slots(): lax.all_to_all(spread, 'zx', 0, 0, tiled=True).reshape(mine.shape)]
    dot_general x0 -> x4, matrix products: none -> 10.2 us  [local(): jnp.dot(columns, disagg_parts[hop], preferred_element_type=jnp.float32)]
    unnamed x51 -> x47, local copies, waits for them, and re-layouts: 6.07 us -> 0.23 us
  transfers between devices with their start and end apart: 31 -> 40, of which waited for: 24 -> 23; matrix products, arithmetic and copies ran while one was open for 5% -> 11% of each run, Pallas kernels for 0% -> 0%
where the time goes in v9:
time: 365 us; the launch traced here: 362 us
  blocking collectives  143 us (39%)
  waiting for transfers between devices  79.8 us (22%)
  starting transfers between devices  68.9 us (19%)
  local copies, waits for them, and re-layouts  20.7 us (6%)
  other arithmetic  19.8 us (5%)
  matrix products  16.8 us (5%)
  between operations  12.8 us (4%)
    all_to_all x5, blocking collectives, share_slots(): lax.all_to_all(mine.reshape((chips,) + tile_shape), 'zx', 0, 0, tiled=True)  74.9 us
    all_to_all x5, blocking collectives, share_slots(): lax.all_to_all(spread, 'zx', 0, 0, tiled=True).reshape(mine.shape)  68.5 us
    ppermute x21, starting transfers between devices, from_partners(): lax.ppermute(value_for(hop), 'sub', [(i, i ^ hop) for i in range(subs)])  35.6 us
    ppermute x21, waiting for transfers between devices, from_partners(): lax.ppermute(value_for(hop), 'sub', [(i, i ^ hop) for i in range(subs)])  32.9 us
    all_to_all x1, waiting for transfers between devices, broadcast_rows(): pieces = lax.all_to_all(copies, 'sub', 0, 0, tiled=True)  17.4 us
    all_to_all x2, starting transfers between devices, share_slots(): lax.all_to_all(mine.reshape((chips,) + tile_shape), 'zx', 0, 0, tiled=True)  17.2 us
    all_to_all x2, waiting for transfers between devices, share_slots(): lax.all_to_all(spread, 'zx', 0, 0, tiled=True).reshape(mine.shape)  12.2 us
    all_to_all x2, starting transfers between devices, share_slots(): lax.all_to_all(spread, 'zx', 0, 0, tiled=True).reshape(mine.shape)  10.7 us
  transfers between devices with their start and end apart: 40, of which 23 were waited for; matrix products, arithmetic and copies ran while one was open for 11% of the time, Pallas kernels for 0%

profile of v9, /device:TPU:32, one launch (start us, length us, event | category | flops | bytes accessed | tf_op | source)
XLA Modules:
  0.0 362.2 jit_solution(14174391249101680463)
XLA Ops:
  0.0 3.2 collective-permute-start.1
  5.4 3.4 all-to-all-start
  22.6 17.4 %all-to-all-done = bf16[4,384,64]{1,2,0:T(8,128)(2,1)S(1)} async-done(((bf16[4,384,64]{1,2,0:T(8,128)(2,1)}), bf16[4,384,64]{1,2,0:T(8,128)(2,1)S(1)}, u32[]{:S(2)}, u32[]{:S(2)}) %all-to-all-start) | async-done | bytes 196640 | tf_op jit(solution)/shard_map/all_to_all | solution.py:65
  41.0 1.7 collective-permute-start.3
  42.6 2.9 collective-permute-start.4
  45.8 3.1 collective-permute-start.2
  48.9 2.2 collective-permute-done.5
  53.6 11.2 %all-to-all-start.1 = ((bf16[32,16,128]{2,1,0:T(8,128)(2,1)}), bf16[32,16,128]{2,1,0:T(8,128)(2,1)S(1)}, u32[]{:S(2)}, u32[]{:S(2)}) async-start(bf16[32,16,128]{2,1,0:T(8,128)(2,1)} %bitcast.25), calls=%async_computation.1 | async-start | bytes 262144 | tf_op jit(solution)/shard_map/all_to_all | solution.py:38
  64.8 1.7 fusion.27
  66.5 8.2 %all-to-all-done.1 = bf16[32,16,128]{2,1,0:T(8,128)(2,1)S(1)} async-done(((bf16[32,16,128]{2,1,0:T(8,128)(2,1)}), bf16[32,16,128]{2,1,0:T(8,128)(2,1)S(1)}, u32[]{:S(2)}, u32[]{:S(2)}) %all-to-all-start.1) | async-done | bytes 131104 | tf_op jit(solution)/shard_map/all_to_all | solution.py:38
  75.4 4.7 %all-to-all-start.2 = ((bf16[32,16,128]{2,1,0:T(8,128)(2,1)}), bf16[32,16,128]{2,1,0:T(8,128)(2,1)S(1)}, u32[]{:S(2)}, u32[]{:S(2)}) async-start(bf16[32,16,128]{2,1,0:T(8,128)(2,1)} %broadcast_in_dim.292), calls=%async_computation.2 | async-start | bytes 262144 | tf_op jit(solution)/shard_map/all_to_all | solution.py:41
  80.1 2.9 fusion.23
  83.0 2.9 fusion.25
  85.9 3.9 %all-to-all-done.2 = bf16[32,16,128]{2,1,0:T(8,128)(2,1)S(1)} async-done(((bf16[32,16,128]{2,1,0:T(8,128)(2,1)}), bf16[32,16,128]{2,1,0:T(8,128)(2,1)S(1)}, u32[]{:S(2)}, u32[]{:S(2)}) %all-to-all-start.2) | async-done | bytes 131104 | tf_op jit(solution)/shard_map/all_to_all | solution.py:41
  89.7 2.8 add_convert_fusion
  94.8 3.3 collective-permute-start.10
  103.0 2.1 gather_fusion.1
  106.8 3.5 collective-permute-start.12
  111.5 1.9 collective-permute-done.12
  113.4 2.4 collective-permute-done.13
  117.2 2.6 collective-permute-start.17
  119.8 2.1 collective-permute-start.18
  122.7 6.1 %all-to-all-start.3 = ((bf16[32,16,128]{2,1,0:T(8,128)(2,1)}), bf16[32,16,128]{2,1,0:T(8,128)(2,1)}, u32[]{:S(2)}, u32[]{:S(2)}) async-start(bf16[32,16,128]{2,1,0:T(8,128)(2,1)} %bitcast.287), calls=%async_computation.3 | async-start | bytes 262144 | tf_op jit(solution)/shard_map/all_to_all | solution.py:38
  128.8 3.5 collective-permute-done.16
  132.3 11.5 %collective-permute-done.17 = bf16[256,1024]{1,0:T(8,128)(2,1)} collective-permute-done((bf16[256,1024]{1,0:T(8,128)(2,1)}, bf16[256,1024]{1,0:T(8,128)(2,1)}, u32[]{:S(2)}, u32[]{:S(2)}) %collective-permute-start.17) | collective-permute-done | bytes 524320 | tf_op jit(solution)/shard_map/ppermute | solution.py:53
  143.8 2.6 collective-permute-done.18
  146.4 2.3 fusion.18
  148.6 3.6 collective-permute-start.20
  155.6 6.1 %all-to-all-start.4 = ((bf16[32,16,128]{2,1,0:T(8,128)(2,1)}), bf16[32,16,128]{2,1,0:T(8,128)(2,1)}, u32[]{:S(2)}, u32[]{:S(2)}) async-start(bf16[32,16,128]{2,1,0:T(8,128)(2,1)} %broadcast_in_dim.296), calls=%async_computation.4 | async-start | bytes 262144 | tf_op jit(solution)/shard_map/all_to_all | solution.py:41
  163.0 8.4 %all-to-all-done.4 = bf16[32,16,128]{2,1,0:T(8,128)(2,1)} async-done(((bf16[32,16,128]{2,1,0:T(8,128)(2,1)}), bf16[32,16,128]{2,1,0:T(8,128)(2,1)}, u32[]{:S(2)}, u32[]{:S(2)}) %all-to-all-start.4) | async-done | bytes 131104 | tf_op jit(solution)/shard_map/all_to_all | solution.py:41
  171.3 3.3 collective-permute-done.20
  174.6 2.6 collective-permute-done.21
  177.2 2.6 pad_maximum_fusion
  179.8 2.4 gather_fusion.2
  184.9 1.5 collective-permute-done.22
  186.5 15.8 %all_to_all.75 = bf16[32,16,128]{2,1,0:T(8,128)(2,1)} all-to-all(bf16[32,16,128]{2,1,0:T(8,128)(2,1)S(1)} %bitcast.289), channel_id=1, replica_groups=mesh['zx'=32,'core'=2,'sub'=4] {'zx'}, dimensions={0} | all-to-all | bytes 262144 | tf_op jit(solution)/shard_map/all_to_all | solution.py:38
  203.3 13.7 %all_to_all.76 = bf16[32,16,128]{2,1,0:T(8,128)(2,1)S(1)} all-to-all(bf16[32,16,128]{2,1,0:T(8,128)(2,1)S(1)} %broadcast_in_dim.300), channel_id=1, replica_groups=mesh['zx'=32,'core'=2,'sub'=4] {'zx'}, dimensions={0} | all-to-all | bytes 262144 | tf_op jit(solution)/shard_map/all_to_all | solution.py:41
  221.9 15.1 %all_to_all.77 = bf16[32,16,128]{2,1,0:T(8,128)(2,1)} all-to-all(bf16[32,16,128]{2,1,0:T(8,128)(2,1)S(1)} %bitcast.290), channel_id=1, replica_groups=mesh['zx'=32,'core'=2,'sub'=4] {'zx'}, dimensions={0} | all-to-all | bytes 262144 | tf_op jit(solution)/shard_map/all_to_all | solution.py:38
  237.9 13.7 %all_to_all.78 = bf16[32,16,128]{2,1,0:T(8,128)(2,1)S(1)} all-to-all(bf16[32,16,128]{2,1,0:T(8,128)(2,1)S(1)} %broadcast_in_dim.304), channel_id=1, replica_groups=mesh['zx'=32,'core'=2,'sub'=4] {'zx'}, dimensions={0} | all-to-all | bytes 262144 | tf_op jit(solution)/shard_map/all_to_all | solution.py:41
  255.3 14.8 %all_to_all.79 = bf16[32,16,128]{2,1,0:T(8,128)(2,1)} all-to-all(bf16[32,16,128]{2,1,0:T(8,128)(2,1)S(1)} %bitcast.291), channel_id=1, replica_groups=mesh['zx'=32,'core'=2,'sub'=4] {'zx'}, dimensions={0} | all-to-all | bytes 262144 | tf_op jit(solution)/shard_map/all_to_all | solution.py:38
  271.1 13.7 %all_to_all.80 = bf16[32,16,128]{2,1,0:T(8,128)(2,1)S(1)} all-to-all(bf16[32,16,128]{2,1,0:T(8,128)(2,1)S(1)} %broadcast_in_dim.308), channel_id=1, replica_groups=mesh['zx'=32,'core'=2,'sub'=4] {'zx'}, dimensions={0} | all-to-all | bytes 262144 | tf_op jit(solution)/shard_map/all_to_all | solution.py:41
  289.7 15.1 %all_to_all.81 = bf16[32,16,128]{2,1,0:T(8,128)(2,1)} all-to-all(bf16[32,16,128]{2,1,0:T(8,128)(2,1)S(1)} %bitcast.292), channel_id=1, replica_groups=mesh['zx'=32,'core'=2,'sub'=4] {'zx'}, dimensions={0} | all-to-all | bytes 262144 | tf_op jit(solution)/shard_map/all_to_all | solution.py:38
  305.7 13.7 %all_to_all.82 = bf16[32,16,128]{2,1,0:T(8,128)(2,1)S(1)} all-to-all(bf16[32,16,128]{2,1,0:T(8,128)(2,1)S(1)} %broadcast_in_dim.312), channel_id=1, replica_groups=mesh['zx'=32,'core'=2,'sub'=4] {'zx'}, dimensions={0} | all-to-all | bytes 262144 | tf_op jit(solution)/shard_map/all_to_all | solution.py:41
  323.2 14.1 %all_to_all.83 = bf16[32,16,128]{2,1,0:T(8,128)(2,1)S(1)} all-to-all(bf16[32,16,128]{2,1,0:T(8,128)(2,1)S(1)} %bitcast.288), channel_id=1, replica_groups=mesh['zx'=32,'core'=2,'sub'=4] {'zx'}, dimensions={0} | all-to-all | bytes 262144 | tf_op jit(solution)/shard_map/all_to_all | solution.py:38
  337.4 13.7 %all_to_all.84 = bf16[32,16,128]{2,1,0:T(8,128)(2,1)S(1)} all-to-all(bf16[32,16,128]{2,1,0:T(8,128)(2,1)S(1)} %broadcast_in_dim.316), channel_id=1, replica_groups=mesh['zx'=32,'core'=2,'sub'=4] {'zx'}, dimensions={0} | all-to-all | bytes 262144 | tf_op jit(solution)/shard_map/all_to_all | solution.py:41
  352.7 2.6 collective-permute-start.33
  355.3 2.1 collective-permute-start.34
  358.2 2.2 collective-permute-done.34
  (225 shorter events, 52.9 us)
Async XLA Ops:
  0.0 40.0 %copy-start = (bf16[1,384,1536]{2,1,0:T(8,128)(2,1)S(1)}, bf16[1,384,1536]{2,1,0:T(8,128)(2,1)}, u32[]{:S(2)}) copy-start(bf16[1,384,1536]{2,1,0:T(8,128)(2,1)} %param.9) | copy-start | bytes 3538948
  0.0 40.6 %copy-start.3 = (bf16[1,1024,384]{2,1,0:T(8,128)(2,1)S(1)}, bf16[1,1024,384]{2,1,0:T(8,128)(2,1)}, u32[]{:S(2)}) copy-start(bf16[1,1024,384]{2,1,0:T(8,128)(2,1)} %param.10) | copy-start | bytes 2359300
  0.0 80.1 %collective-permute-start.1 = (bf16[384,1024]{1,0:T(8,128)(2,1)}, bf16[384,1024]{1,0:T(8,128)(2,1)}, u32[]{:S(2)}, u32[]{:S(2)}) collective-permute-start(bf16[384,1024]{1,0:T(8,128)(2,1)} %bitcast.3), channel_id=1, source_target_pairs={{0,2},{1,3},{2,0},{3,1},{4,6},{5,7},{6,4},{7,5},{8,10},{9,11},{10,... | collective-permute-start | bytes 2359304 | tf_op jit(solution)/shard_map/ppermute | solution.py:53
  3.2 79.8 %collective-permute-start = (bf16[384,1024]{1,0:T(8,128)(2,1)}, bf16[384,1024]{1,0:T(8,128)(2,1)}, u32[]{:S(2)}, u32[]{:S(2)}) collective-permute-start(bf16[384,1024]{1,0:T(8,128)(2,1)} %bitcast.3), channel_id=1, source_target_pairs={{0,1},{1,0},{2,3},{3,2},{4,5},{5,4},{6,7},{7,6},{8,9},{9,8},{10,11... | collective-permute-start | bytes 2359304 | tf_op jit(solution)/shard_map/ppermute | solution.py:53
  5.4 34.6 %all-to-all-start = ((bf16[4,384,64]{1,2,0:T(8,128)(2,1)}), bf16[4,384,64]{1,2,0:T(8,128)(2,1)S(1)}, u32[]{:S(2)}, u32[]{:S(2)}) async-start(bf16[4,384,64]{1,2,0:T(8,128)(2,1)} %broadcast_in_dim.284), calls=%async_computation | async-start | bytes 393216 | tf_op jit(solution)/shard_map/all_to_all | solution.py:65
  41.0 4.8 %collective-permute-start.3 = (bf16[16,1024]{1,0:T(8,128)(2,1)S(1)}, bf16[16,1024]{1,0:T(8,128)(2,1)S(1)}, u32[]{:S(2)}, u32[]{:S(2)}) collective-permute-start(bf16[16,1024]{1,0:T(8,128)(2,1)S(1)} %get-tuple-element.42), channel_id=1, source_target_pairs={{0,1},{1,0},{2,3},{3,2},{4,5},{5,4},{6,7},{7,6},{8,9},{9,8},{10,11... | collective-permute-start | bytes 98312 | tf_op jit(solution)/shard_map/ppermute | solution.py:53
  42.6 6.2 %collective-permute-start.4 = (bf16[16,1024]{1,0:T(8,128)(2,1)S(1)}, bf16[16,1024]{1,0:T(8,128)(2,1)S(1)}, u32[]{:S(2)}, u32[]{:S(2)}) collective-permute-start(bf16[16,1024]{1,0:T(8,128)(2,1)S(1)} %get-tuple-element.41), channel_id=1, source_target_pairs={{0,2},{1,3},{2,0},{3,1},{4,6},{5,7},{6,4},{7,5},{8,10},{9,11},{10,... | collective-permute-start | bytes 98312 | tf_op jit(solution)/shard_map/ppermute | solution.py:53
  45.5 5.5 %collective-permute-start.5 = (bf16[16,1024]{1,0:T(8,128)(2,1)S(1)}, bf16[16,1024]{1,0:T(8,128)(2,1)S(1)}, u32[]{:S(2)}, u32[]{:S(2)}) collective-permute-start(bf16[16,1024]{1,0:T(8,128)(2,1)S(1)} %get-tuple-element.40), channel_id=1, source_target_pairs={{0,3},{1,2},{2,1},{3,0},{4,7},{5,6},{6,5},{7,4},{8,11},{9,10},{10,... | collective-permute-start | bytes 98312 | tf_op jit(solution)/shard_map/ppermute | solution.py:53
  45.8 44.0 %collective-permute-start.2 = (bf16[384,1024]{1,0:T(8,128)(2,1)}, bf16[384,1024]{1,0:T(8,128)(2,1)}, u32[]{:S(2)}, u32[]{:S(2)}) collective-permute-start(bf16[384,1024]{1,0:T(8,128)(2,1)} %bitcast.3), channel_id=1, source_target_pairs={{0,3},{1,2},{2,1},{3,0},{4,7},{5,6},{6,5},{7,4},{8,11},{9,10},{10,... | collective-permute-start | bytes 2359304 | tf_op jit(solution)/shard_map/ppermute | solution.py:53
  51.2 1.6 collective-permute-start.6
  52.1 50.8 %copy-start.16 = (s32[1024]{0:T(1024)}, s32[1024]{0:T(1024)S(1)}, u32[]{:S(2)}) copy-start(s32[1024]{0:T(1024)S(1)} %pad_clamp_fusion) | copy-start | bytes 12292
  53.6 21.1 %all-to-all-start.1 = ((bf16[32,16,128]{2,1,0:T(8,128)(2,1)}), bf16[32,16,128]{2,1,0:T(8,128)(2,1)S(1)}, u32[]{:S(2)}, u32[]{:S(2)}) async-start(bf16[32,16,128]{2,1,0:T(8,128)(2,1)} %bitcast.25), calls=%async_computation.1 | async-start | bytes 262144 | tf_op jit(solution)/shard_map/all_to_all | solution.py:38
  75.4 14.3 %all-to-all-start.2 = ((bf16[32,16,128]{2,1,0:T(8,128)(2,1)}), bf16[32,16,128]{2,1,0:T(8,128)(2,1)S(1)}, u32[]{:S(2)}, u32[]{:S(2)}) async-start(bf16[32,16,128]{2,1,0:T(8,128)(2,1)} %broadcast_in_dim.292), calls=%async_computation.2 | async-start | bytes 262144 | tf_op jit(solution)/shard_map/all_to_all | solution.py:41
  89.7 2.8 collective-permute-start.7
  93.4 8.0 %collective-permute-start.8 = (bf16[16,1024]{1,0:T(8,128)(2,1)}, bf16[16,1024]{1,0:T(8,128)(2,1)}, u32[]{:S(2)}, u32[]{:S(2)}) collective-permute-start(bf16[16,1024]{1,0:T(8,128)(2,1)} %bitcast.267), channel_id=1, source_target_pairs={{0,1},{1,0},{2,3},{3,2},{4,5},{5,4},{6,7},{7,6},{8,9},{9,8},{10,11... | collective-permute-start | bytes 98312 | tf_op jit(solution)/shard_map/ppermute | solution.py:53
  93.4 8.0 %collective-permute-start.9 = (bf16[16,1024]{1,0:T(8,128)(2,1)}, bf16[16,1024]{1,0:T(8,128)(2,1)}, u32[]{:S(2)}, u32[]{:S(2)}) collective-permute-start(bf16[16,1024]{1,0:T(8,128)(2,1)} %bitcast.267), channel_id=1, source_target_pairs={{0,2},{1,3},{2,0},{3,1},{4,6},{5,7},{6,4},{7,5},{8,10},{9,11},{10,... | collective-permute-start | bytes 98312 | tf_op jit(solution)/shard_map/ppermute | solution.py:53
  94.8 6.6 %collective-permute-start.10 = (bf16[16,1024]{1,0:T(8,128)(2,1)}, bf16[16,1024]{1,0:T(8,128)(2,1)}, u32[]{:S(2)}, u32[]{:S(2)}) collective-permute-start(bf16[16,1024]{1,0:T(8,128)(2,1)} %bitcast.267), channel_id=1, source_target_pairs={{0,3},{1,2},{2,1},{3,0},{4,7},{5,6},{6,5},{7,4},{8,11},{9,10},{10,... | collective-permute-start | bytes 98312 | tf_op jit(solution)/shard_map/ppermute | solution.py:53
  106.5 5.0 %collective-permute-start.11 = (f32[16,1024]{1,0:T(8,128)S(1)}, f32[16,1024]{1,0:T(8,128)S(1)}, u32[]{:S(2)}, u32[]{:S(2)}) collective-permute-start(f32[16,1024]{1,0:T(8,128)S(1)} %get-tuple-element.38), channel_id=1, source_target_pairs={{0,1},{1,0},{2,3},{3,2},{4,5},{5,4},{6,7},{7,6},{8,9},{9,8},{10,11... | collective-permute-start | bytes 196616 | tf_op jit(solution)/shard_map/ppermute | solution.py:53
  106.8 6.6 %collective-permute-start.12 = (f32[16,1024]{1,0:T(8,128)S(1)}, f32[16,1024]{1,0:T(8,128)S(1)}, u32[]{:S(2)}, u32[]{:S(2)}) collective-permute-start(f32[16,1024]{1,0:T(8,128)S(1)} %get-tuple-element.37), channel_id=1, source_target_pairs={{0,2},{1,3},{2,0},{3,1},{4,6},{5,7},{6,4},{7,5},{8,10},{9,11},{10,... | collective-permute-start | bytes 196616 | tf_op jit(solution)/shard_map/ppermute | solution.py:53
  110.3 5.5 %collective-permute-start.13 = (f32[16,1024]{1,0:T(8,128)S(1)}, f32[16,1024]{1,0:T(8,128)S(1)}, u32[]{:S(2)}, u32[]{:S(2)}) collective-permute-start(f32[16,1024]{1,0:T(8,128)S(1)} %get-tuple-element.36), channel_id=1, source_target_pairs={{0,3},{1,2},{2,1},{3,0},{4,7},{5,6},{6,5},{7,4},{8,11},{9,10},{10,... | collective-permute-start | bytes 196616 | tf_op jit(solution)/shard_map/ppermute | solution.py:53
  115.9 6.0 %collective-permute-start.14 = (bf16[8,8,16,128]{3,2,1,0:T(8,128)(2,1)S(1)}, bf16[8,8,16,128]{3,2,1,0:T(8,128)(2,1)S(1)}, u32[]{:S(2)}, u32[]{:S(2)}) collective-permute-start(bf16[8,8,16,128]{3,2,1,0:T(8,128)(2,1)S(1)} %broadcast_select_fusion.5), channel_id=1, source_target_pairs={{0,4},{4,0},{1,5},{5,1},{2,6},{6,2},{3,7},{7,3},{8,12},{12,8},{9,1... | collective-permute-start | bytes 786440 | tf_op jit(solution)/shard_map/ppermute | solution.py:32
  117.2 15.0 %collective-permute-start.16 = (bf16[256,1024]{1,0:T(8,128)(2,1)}, bf16[256,1024]{1,0:T(8,128)(2,1)}, u32[]{:S(2)}, u32[]{:S(2)}) collective-permute-start(bf16[256,1024]{1,0:T(8,128)(2,1)} %get-tuple-element.32), channel_id=1, source_target_pairs={{0,1},{1,0},{2,3},{3,2},{4,5},{5,4},{6,7},{7,6},{8,9},{9,8},{10,11... | collective-permute-start | bytes 1572872 | tf_op jit(solution)/shard_map/ppermute | solution.py:53
  117.2 26.5 %collective-permute-start.17 = (bf16[256,1024]{1,0:T(8,128)(2,1)}, bf16[256,1024]{1,0:T(8,128)(2,1)}, u32[]{:S(2)}, u32[]{:S(2)}) collective-permute-start(bf16[256,1024]{1,0:T(8,128)(2,1)} %get-tuple-element.34), channel_id=1, source_target_pairs={{0,2},{1,3},{2,0},{3,1},{4,6},{5,7},{6,4},{7,5},{8,10},{9,11},{10,... | collective-permute-start | bytes 1572872 | tf_op jit(solution)/shard_map/ppermute | solution.py:53
  119.8 41.9 %copy-start.15 = (f32[8,2,4,128]{3,0,2,1:T(8,128)S(1)}, f32[8,2,4,128]{3,0,2,1:T(8,128)}, u32[]{:S(2)}) copy-start(f32[8,2,4,128]{3,0,2,1:T(8,128)} %get-tuple-element.20) | copy-start | bytes 98308
  119.8 26.5 %collective-permute-start.18 = (bf16[256,1024]{1,0:T(8,128)(2,1)}, bf16[256,1024]{1,0:T(8,128)(2,1)}, u32[]{:S(2)}, u32[]{:S(2)}) collective-permute-start(bf16[256,1024]{1,0:T(8,128)(2,1)} %get-tuple-element.33), channel_id=1, source_target_pairs={{0,3},{1,2},{2,1},{3,0},{4,7},{5,6},{6,5},{7,4},{8,11},{9,10},{10,... | collective-permute-start | bytes 1572872 | tf_op jit(solution)/shard_map/ppermute | solution.py:53
  122.7 31.3 %all-to-all-start.3 = ((bf16[32,16,128]{2,1,0:T(8,128)(2,1)}), bf16[32,16,128]{2,1,0:T(8,128)(2,1)}, u32[]{:S(2)}, u32[]{:S(2)}) async-start(bf16[32,16,128]{2,1,0:T(8,128)(2,1)} %bitcast.287), calls=%async_computation.3 | async-start | bytes 262144 | tf_op jit(solution)/shard_map/all_to_all | solution.py:38
  148.6 22.7 %collective-permute-start.19 = (bf16[256,1024]{1,0:T(8,128)(2,1)}, bf16[256,1024]{1,0:T(8,128)(2,1)S(1)}, u32[]{:S(2)}, u32[]{:S(2)}) collective-permute-start(bf16[256,1024]{1,0:T(8,128)(2,1)} %fusion.18), channel_id=1, source_target_pairs={{0,1},{1,0},{2,3},{3,2},{4,5},{5,4},{6,7},{7,6},{8,9},{9,8},{10,11... | collective-permute-start | bytes 1572872 | tf_op jit(solution)/shard_map/ppermute | solution.py:53
  148.6 26.0 %collective-permute-start.20 = (bf16[256,1024]{1,0:T(8,128)(2,1)}, bf16[256,1024]{1,0:T(8,128)(2,1)S(1)}, u32[]{:S(2)}, u32[]{:S(2)}) collective-permute-start(bf16[256,1024]{1,0:T(8,128)(2,1)} %fusion.18), channel_id=1, source_target_pairs={{0,2},{1,3},{2,0},{3,1},{4,6},{5,7},{6,4},{7,5},{8,10},{9,11},{10,... | collective-permute-start | bytes 1572872 | tf_op jit(solution)/shard_map/ppermute | solution.py:53
  152.2 25.0 %collective-permute-start.21 = (bf16[256,1024]{1,0:T(8,128)(2,1)}, bf16[256,1024]{1,0:T(8,128)(2,1)S(1)}, u32[]{:S(2)}, u32[]{:S(2)}) collective-permute-start(bf16[256,1024]{1,0:T(8,128)(2,1)} %fusion.18), channel_id=1, source_target_pairs={{0,3},{1,2},{2,1},{3,0},{4,7},{5,6},{6,5},{7,4},{8,11},{9,10},{10,... | collective-permute-start | bytes 1572872 | tf_op jit(solution)/shard_map/ppermute | solution.py:53
  155.6 15.7 %all-to-all-start.4 = ((bf16[32,16,128]{2,1,0:T(8,128)(2,1)}), bf16[32,16,128]{2,1,0:T(8,128)(2,1)}, u32[]{:S(2)}, u32[]{:S(2)}) async-start(bf16[32,16,128]{2,1,0:T(8,128)(2,1)} %broadcast_in_dim.296), calls=%async_computation.4 | async-start | bytes 262144 | tf_op jit(solution)/shard_map/all_to_all | solution.py:41
  171.3 10.9 %collective-permute-start.15 = (bf16[4,8,16,128]{3,2,1,0:T(8,128)(2,1)}, bf16[4,8,16,128]{3,2,1,0:T(8,128)(2,1)}, u32[]{:S(2)}, u32[]{:S(2)}) collective-permute-start(bf16[4,8,16,128]{3,2,1,0:T(8,128)(2,1)} %bitcast.44), channel_id=1, source_target_pairs={{0,4},{4,0},{1,5},{5,1},{2,6},{6,2},{3,7},{7,3},{8,12},{12,8},{9,1... | collective-permute-start | bytes 393224 | tf_op jit(solution)/shard_map/ppermute | solution.py:42
  184.2 32.8 %copy-start.10 = (f32[4,16,128]{2,1,0:T(8,128)}, f32[4,16,128]{2,1,0:T(8,128)S(1)}, u32[]{:S(2)}) copy-start(f32[4,16,128]{2,1,0:T(8,128)S(1)} %get-tuple-element.15) | copy-start | bytes 98308
  184.8 1.6 collective-permute-start.22
  217.0 1.5 collective-permute-start.23
  219.5 67.0 %copy-start.5 = (f32[8,16,128]{2,1,0:T(8,128)}, f32[8,16,128]{2,1,0:T(8,128)S(1)}, u32[]{:S(2)}) copy-start(f32[8,16,128]{2,1,0:T(8,128)S(1)} %get-tuple-element.29) | copy-start | bytes 196612
  220.0 1.8 collective-permute-start.24
  251.6 1.3 collective-permute-start.25
  253.6 1.6 collective-permute-start.26
  284.8 1.5 collective-permute-start.27
  287.3 32.1 %copy-start.13 = (f32[8,2,4,128]{3,0,2,1:T(8,128)S(1)}, f32[8,2,4,128]{3,0,2,1:T(8,128)}, u32[]{:S(2)}) copy-start(f32[8,2,4,128]{3,0,2,1:T(8,128)} %get-tuple-element.24) | copy-start | bytes 98308
  287.8 1.8 collective-permute-start.28
  319.4 1.3 collective-permute-start.29
  321.4 39.7 %copy-start.2 = (bf16[384,1024]{1,0:T(8,128)(2,1)S(1)}, bf16[384,1024]{1,0:T(8,128)(2,1)}, u32[]{:S(2)}) copy-start(bf16[384,1024]{1,0:T(8,128)(2,1)} %copy-done.1) | copy-start | bytes 2359300
  321.4 1.6 collective-permute-start.30
  351.1 1.3 collective-permute-start.31
  352.6 4.9 %collective-permute-start.32 = (bf16[16,1024]{1,0:T(8,128)(2,1)S(1)}, bf16[16,1024]{1,0:T(8,128)(2,1)S(1)}, u32[]{:S(2)}, u32[]{:S(2)}) collective-permute-start(bf16[16,1024]{1,0:T(8,128)(2,1)S(1)} %copy_bitcast_fusion), channel_id=1, source_target_pairs={{0,1},{1,0},{2,3},{3,2},{4,5},{5,4},{6,7},{7,6},{8,9},{9,8},{10,11... | collective-permute-start | bytes 98312 | tf_op jit(solution)/shard_map/ppermute | solution.py:53
  352.7 5.5 %collective-permute-start.33 = (bf16[16,1024]{1,0:T(8,128)(2,1)S(1)}, bf16[16,1024]{1,0:T(8,128)(2,1)S(1)}, u32[]{:S(2)}, u32[]{:S(2)}) collective-permute-start(bf16[16,1024]{1,0:T(8,128)(2,1)S(1)} %copy_bitcast_fusion), channel_id=1, source_target_pairs={{0,2},{1,3},{2,0},{3,1},{4,6},{5,7},{6,4},{7,5},{8,10},{9,11},{10,... | collective-permute-start | bytes 98312 | tf_op jit(solution)/shard_map/ppermute | solution.py:53
  355.3 5.1 %collective-permute-start.34 = (bf16[16,1024]{1,0:T(8,128)(2,1)S(1)}, bf16[16,1024]{1,0:T(8,128)(2,1)S(1)}, u32[]{:S(2)}, u32[]{:S(2)}) collective-permute-start(bf16[16,1024]{1,0:T(8,128)(2,1)S(1)} %copy_bitcast_fusion), channel_id=1, source_target_pairs={{0,3},{1,2},{2,1},{3,0},{4,7},{5,6},{6,5},{7,4},{8,11},{9,10},{10,... | collective-permute-start | bytes 98312 | tf_op jit(solution)/shard_map/ppermute | solution.py:53
  (10 other events, 92.7 us)

commit v10 on v8

--- a/solution.py
+++ b/solution.py
@@ -29,11 +29,12 @@
 
 def share_slots(slots, chips):
     swap = [(0, 1), (1, 0)]
-    slots = slots + lax.ppermute(slots, "core", swap)
     core = lax.axis_index("core")
     count = slots.shape[0]
     halves = slots.reshape((CORES, count // CORES) + slots.shape[1:])
+    wanted = lax.dynamic_index_in_dim(halves, 1 - core, 0, keepdims=False)
     mine = lax.dynamic_index_in_dim(halves, core, 0, keepdims=False)
+    mine = mine + lax.ppermute(wanted, "core", swap)
     tile_shape = mine.shape[2:]
     pieces = lax.all_to_all(mine.reshape((chips,) + tile_shape), "zx", 0, 0, tiled=True)
     total = jnp.sum(pieces, axis=0, keepdims=True)

time: 344 us -> 341 us (level)
  local copies, waits for them, and re-layouts: 16 us -> 11.2 us
    unnamed x51, local copies, waits for them, and re-layouts: 6.07 us -> 2.05 us
  transfers between devices with their start and end apart: 31 -> 31, of which waited for: 24 -> 23; matrix products, arithmetic and copies ran while one was open for 5% -> 4% of each run, Pallas kernels for 0% -> 0%
where the time goes in v10:
time: 341 us; the launch traced here: 339 us
  blocking collectives  175 us (51%)
  waiting for transfers between devices  61.6 us (18%)
  starting transfers between devices  42.5 us (12%)
  between operations  26.1 us (8%)
  matrix products  12.3 us (4%)
  local copies, waits for them, and re-layouts  11.2 us (3%)
  other arithmetic  10.1 us (3%)
    all_to_all x6, blocking collectives, share_slots(): lax.all_to_all(mine.reshape((chips,) + tile_shape), 'zx', 0, 0, tiled=True)  93.3 us
    all_to_all x6, blocking collectives, share_slots(): lax.all_to_all(spread, 'zx', 0, 0, tiled=True).reshape(mine.shape)  82.2 us
    psum x1, waiting for transfers between devices, local(): coupling = lax.psum(partial_map, 'sub')  19.7 us
    ppermute x12, starting transfers between devices, from_partners(): lax.ppermute(value_for(hop), 'sub', [(i, i ^ hop) for i in range(subs)])  19.1 us
    ppermute x12, waiting for transfers between devices, from_partners(): lax.ppermute(value_for(hop), 'sub', [(i, i ^ hop) for i in range(subs)])  12.2 us
    all_to_all x1, starting transfers between devices, share_slots(): lax.all_to_all(mine.reshape((chips,) + tile_shape), 'zx', 0, 0, tiled=True)  11.5 us
    all_to_all x1, waiting for transfers between devices, share_slots(): lax.all_to_all(spread, 'zx', 0, 0, tiled=True).reshape(mine.shape)  8.66 us
    ppermute x7, waiting for transfers between devices, share_slots(): mine = mine + lax.ppermute(wanted, 'core', swap)  8.36 us
  transfers between devices with their start and end apart: 31, of which 23 were waited for; matrix products, arithmetic and copies ran while one was open for 4% of the time, Pallas kernels for 0%

profile of v10, /device:TPU:32, one launch (start us, length us, event | category | flops | bytes accessed | tf_op | source)
XLA Modules:
  0.0 339.4 jit_solution(2868509288090377741)
XLA Ops:
  7.3 1.5 broadcast_in_dim.283
  8.8 4.5 %all-to-all-start = ((bf16[4,384,64]{1,2,0:T(8,128)(2,1)}), bf16[4,384,64]{1,2,0:T(8,128)(2,1)S(1)}, u32[]{:S(2)}, u32[]{:S(2)}) async-start(bf16[4,384,64]{1,2,0:T(8,128)(2,1)} %broadcast_in_dim.283), calls=%async_computation | async-start | bytes 393216 | tf_op jit(solution)/shard_map/all_to_all | solution.py:66
  14.6 1.2 dynamic_slice.76
  20.5 1.1 collective-permute-start
  21.6 2.7 collective-permute-start.1
  26.0 1.1 collective-permute-done.1
  27.1 2.7 collective-permute-done.2
  30.1 1.3 collective-permute-done.3
  32.0 11.5 %all-to-all-start.1 = ((bf16[32,16,128]{2,1,0:T(8,128)(2,1)}), bf16[32,16,128]{2,1,0:T(8,128)(2,1)S(1)}, u32[]{:S(2)}, u32[]{:S(2)}) async-start(bf16[32,16,128]{2,1,0:T(8,128)(2,1)} %bitcast.22), calls=%async_computation.1 | async-start | bytes 262144 | tf_op jit(solution)/shard_map/all_to_all | solution.py:39
  49.1 4.3 %all-to-all-done.1 = bf16[32,16,128]{2,1,0:T(8,128)(2,1)S(1)} async-done(((bf16[32,16,128]{2,1,0:T(8,128)(2,1)}), bf16[32,16,128]{2,1,0:T(8,128)(2,1)S(1)}, u32[]{:S(2)}, u32[]{:S(2)}) %all-to-all-start.1) | async-done | bytes 131104 | tf_op jit(solution)/shard_map/all_to_all | solution.py:39
  54.2 5.5 %all-to-all-start.2 = ((bf16[32,16,128]{2,1,0:T(8,128)(2,1)}), bf16[32,16,128]{2,1,0:T(8,128)(2,1)S(1)}, u32[]{:S(2)}, u32[]{:S(2)}) async-start(bf16[32,16,128]{2,1,0:T(8,128)(2,1)} %broadcast_in_dim.291), calls=%async_computation.2 | async-start | bytes 262144 | tf_op jit(solution)/shard_map/all_to_all | solution.py:42
  60.5 8.7 %all-to-all-done.2 = bf16[32,16,128]{2,1,0:T(8,128)(2,1)S(1)} async-done(((bf16[32,16,128]{2,1,0:T(8,128)(2,1)}), bf16[32,16,128]{2,1,0:T(8,128)(2,1)S(1)}, u32[]{:S(2)}, u32[]{:S(2)}) %all-to-all-start.2) | async-done | bytes 131104 | tf_op jit(solution)/shard_map/all_to_all | solution.py:42
  69.2 1.3 collective-permute-done.4
  70.8 2.5 collective-permute-start.6
  73.3 2.2 collective-permute-start.7
  77.0 1.5 collective-permute-done.7
  78.4 1.2 gather_fusion.1
  79.6 3.3 fusion.4
  83.9 1.3 convolution_convert_fusion
  85.2 2.3 fusion.2
  89.3 3.6 %collective-permute-start.9 = (f32[16,1024]{1,0:T(8,128)S(1)}, f32[16,1024]{1,0:T(8,128)S(1)}, u32[]{:S(2)}, u32[]{:S(2)}) collective-permute-start(f32[16,1024]{1,0:T(8,128)S(1)} %get-tuple-element.34), channel_id=1, source_target_pairs={{0,2},{1,3},{2,0},{3,1},{4,6},{5,7},{6,4},{7,5},{8,10},{9,11},{10,... | collective-permute-start | bytes 196616 | tf_op jit(solution)/shard_map/ppermute | solution.py:54
  92.9 1.0 collective-permute-start.10
  94.0 1.9 collective-permute-done.9
  96.0 2.4 collective-permute-done.10
  98.7 1.3 collective-permute-done.11
  100.0 14.3 %all_to_all.75 = bf16[32,16,128]{2,1,0:T(8,128)(2,1)S(1)} all-to-all(bf16[32,16,128]{2,1,0:T(8,128)(2,1)S(1)} %bitcast.264), channel_id=1, replica_groups=mesh['zx'=32,'core'=2,'sub'=4] {'zx'}, dimensions={0} | all-to-all | bytes 262144 | tf_op jit(solution)/shard_map/all_to_all | solution.py:39
  114.4 13.7 %all_to_all.76 = bf16[32,16,128]{2,1,0:T(8,128)(2,1)S(1)} all-to-all(bf16[32,16,128]{2,1,0:T(8,128)(2,1)S(1)} %broadcast_in_dim.295), channel_id=1, replica_groups=mesh['zx'=32,'core'=2,'sub'=4] {'zx'}, dimensions={0} | all-to-all | bytes 262144 | tf_op jit(solution)/shard_map/all_to_all | solution.py:42
  128.2 1.3 collective-permute-done.12
  129.6 19.7 %all-reduce.2.cloned.1.call-done = bf16[1024,1024]{1,0:T(8,128)(2,1)} async-done(((bf16[1024,1024]{1,0:T(8,128)(2,1)}), bf16[1024,1024]{1,0:T(8,128)(2,1)}) %all-reduce.2.cloned.1.call-update) | async-done | bytes 2097168 | tf_op jit(solution)/shard_map/psum | solution.py:111
  149.4 2.0 fusion.20
  151.6 1.3 collective-permute-done.13
  153.0 19.9 %all_to_all.77 = bf16[32,16,128]{2,1,0:T(8,128)(2,1)} all-to-all(bf16[32,16,128]{2,1,0:T(8,128)(2,1)S(1)} %bitcast.265), channel_id=1, replica_groups=mesh['zx'=32,'core'=2,'sub'=4] {'zx'}, dimensions={0} | all-to-all | bytes 262144 | tf_op jit(solution)/shard_map/all_to_all | solution.py:39
  173.8 13.7 %all_to_all.78 = bf16[32,16,128]{2,1,0:T(8,128)(2,1)S(1)} all-to-all(bf16[32,16,128]{2,1,0:T(8,128)(2,1)S(1)} %broadcast_in_dim.299), channel_id=1, replica_groups=mesh['zx'=32,'core'=2,'sub'=4] {'zx'}, dimensions={0} | all-to-all | bytes 262144 | tf_op jit(solution)/shard_map/all_to_all | solution.py:42
  192.8 15.1 %all_to_all.79 = bf16[32,16,128]{2,1,0:T(8,128)(2,1)} all-to-all(bf16[32,16,128]{2,1,0:T(8,128)(2,1)S(1)} %bitcast.266), channel_id=1, replica_groups=mesh['zx'=32,'core'=2,'sub'=4] {'zx'}, dimensions={0} | all-to-all | bytes 262144 | tf_op jit(solution)/shard_map/all_to_all | solution.py:39
  208.9 13.7 %all_to_all.80 = bf16[32,16,128]{2,1,0:T(8,128)(2,1)S(1)} all-to-all(bf16[32,16,128]{2,1,0:T(8,128)(2,1)S(1)} %broadcast_in_dim.303), channel_id=1, replica_groups=mesh['zx'=32,'core'=2,'sub'=4] {'zx'}, dimensions={0} | all-to-all | bytes 262144 | tf_op jit(solution)/shard_map/all_to_all | solution.py:42
  222.6 1.3 collective-permute-done.16
  224.8 1.2 collective-permute-done.17
  226.0 14.8 %all_to_all.81 = bf16[32,16,128]{2,1,0:T(8,128)(2,1)} all-to-all(bf16[32,16,128]{2,1,0:T(8,128)(2,1)S(1)} %bitcast.267), channel_id=1, replica_groups=mesh['zx'=32,'core'=2,'sub'=4] {'zx'}, dimensions={0} | all-to-all | bytes 262144 | tf_op jit(solution)/shard_map/all_to_all | solution.py:39
  241.8 13.7 %all_to_all.82 = bf16[32,16,128]{2,1,0:T(8,128)(2,1)S(1)} all-to-all(bf16[32,16,128]{2,1,0:T(8,128)(2,1)S(1)} %broadcast_in_dim.307), channel_id=1, replica_groups=mesh['zx'=32,'core'=2,'sub'=4] {'zx'}, dimensions={0} | all-to-all | bytes 262144 | tf_op jit(solution)/shard_map/all_to_all | solution.py:42
  260.8 15.1 %all_to_all.83 = bf16[32,16,128]{2,1,0:T(8,128)(2,1)} all-to-all(bf16[32,16,128]{2,1,0:T(8,128)(2,1)S(1)} %bitcast.268), channel_id=1, replica_groups=mesh['zx'=32,'core'=2,'sub'=4] {'zx'}, dimensions={0} | all-to-all | bytes 262144 | tf_op jit(solution)/shard_map/all_to_all | solution.py:39
  276.9 13.7 %all_to_all.84 = bf16[32,16,128]{2,1,0:T(8,128)(2,1)S(1)} all-to-all(bf16[32,16,128]{2,1,0:T(8,128)(2,1)S(1)} %broadcast_in_dim.311), channel_id=1, replica_groups=mesh['zx'=32,'core'=2,'sub'=4] {'zx'}, dimensions={0} | all-to-all | bytes 262144 | tf_op jit(solution)/shard_map/all_to_all | solution.py:42
  290.6 1.3 collective-permute-done.20
  292.8 1.2 collective-permute-done.21
  294.1 14.1 %all_to_all.85 = bf16[32,16,128]{2,1,0:T(8,128)(2,1)S(1)} all-to-all(bf16[32,16,128]{2,1,0:T(8,128)(2,1)S(1)} %bitcast.263), channel_id=1, replica_groups=mesh['zx'=32,'core'=2,'sub'=4] {'zx'}, dimensions={0} | all-to-all | bytes 262144 | tf_op jit(solution)/shard_map/all_to_all | solution.py:39
  308.3 13.7 %all_to_all.86 = bf16[32,16,128]{2,1,0:T(8,128)(2,1)S(1)} all-to-all(bf16[32,16,128]{2,1,0:T(8,128)(2,1)S(1)} %broadcast_in_dim.315), channel_id=1, replica_groups=mesh['zx'=32,'core'=2,'sub'=4] {'zx'}, dimensions={0} | all-to-all | bytes 262144 | tf_op jit(solution)/shard_map/all_to_all | solution.py:42
  323.9 2.0 collective-permute-start.24
  325.9 2.4 collective-permute-start.25
  329.3 1.7 collective-permute-done.25
  (205 shorter events, 30.5 us)
Async XLA Ops:
  6.5 13.1 %copy-start = (bf16[1,384,1536]{2,1,0:T(8,128)(2,1)S(1)}, bf16[1,384,1536]{2,1,0:T(8,128)(2,1)}, u32[]{:S(2)}) copy-start(bf16[1,384,1536]{2,1,0:T(8,128)(2,1)} %param.9) | copy-start | bytes 3538948
  6.5 13.6 %copy-start.6 = (bf16[1,1024,384]{2,1,0:T(8,128)(2,1)S(1)}, bf16[1,1024,384]{2,1,0:T(8,128)(2,1)}, u32[]{:S(2)}) copy-start(bf16[1,1024,384]{2,1,0:T(8,128)(2,1)} %param.10) | copy-start | bytes 2359300
  6.5 73.1 %all-gather.3.cloned.1.call-start = ((), (), s32[]{:S(2)}) async-start(), calls=%async_computation.16 | async-start | bytes 3932160 | tf_op jit(solution)/shard_map/all_gather | solution.py:106
  7.3 18.1 %copy-start.1 = (s32[64]{0:T(128)S(1)}, s32[64]{0:T(128)}, u32[]{:S(2)}) copy-start(s32[64]{0:T(128)} %param.15) | copy-start | bytes 772
  8.8 10.8 %all-to-all-start = ((bf16[4,384,64]{1,2,0:T(8,128)(2,1)}), bf16[4,384,64]{1,2,0:T(8,128)(2,1)S(1)}, u32[]{:S(2)}, u32[]{:S(2)}) async-start(bf16[4,384,64]{1,2,0:T(8,128)(2,1)} %broadcast_in_dim.283), calls=%async_computation | async-start | bytes 393216 | tf_op jit(solution)/shard_map/all_to_all | solution.py:66
  20.1 28.9 %copy-start.19 = (f32[1,6,2,512]{3,2,1,0:T(2,128)S(1)}, f32[1,6,2,512]{3,2,1,0:T(2,128)}, u32[]{:S(2)}) copy-start(f32[1,6,2,512]{3,2,1,0:T(2,128)} %param.12) | copy-start | bytes 73732
  20.5 5.4 %collective-permute-start = (bf16[16,1024]{1,0:T(8,128)(2,1)S(1)}, bf16[16,1024]{1,0:T(8,128)(2,1)S(1)}, u32[]{:S(2)}, u32[]{:S(2)}) collective-permute-start(bf16[16,1024]{1,0:T(8,128)(2,1)S(1)} %get-tuple-element.39), channel_id=1, source_target_pairs={{0,1},{1,0},{2,3},{3,2},{4,5},{5,4},{6,7},{7,6},{8,9},{9,8},{10,11... | collective-permute-start | bytes 98312 | tf_op jit(solution)/shard_map/ppermute | solution.py:54
  21.6 5.4 %collective-permute-start.1 = (bf16[16,1024]{1,0:T(8,128)(2,1)S(1)}, bf16[16,1024]{1,0:T(8,128)(2,1)S(1)}, u32[]{:S(2)}, u32[]{:S(2)}) collective-permute-start(bf16[16,1024]{1,0:T(8,128)(2,1)S(1)} %get-tuple-element.38), channel_id=1, source_target_pairs={{0,2},{1,3},{2,0},{3,1},{4,6},{5,7},{6,4},{7,5},{8,10},{9,11},{10,... | collective-permute-start | bytes 98312 | tf_op jit(solution)/shard_map/ppermute | solution.py:54
  24.3 5.5 %collective-permute-start.2 = (bf16[16,1024]{1,0:T(8,128)(2,1)S(1)}, bf16[16,1024]{1,0:T(8,128)(2,1)S(1)}, u32[]{:S(2)}, u32[]{:S(2)}) collective-permute-start(bf16[16,1024]{1,0:T(8,128)(2,1)S(1)} %get-tuple-element.37), channel_id=1, source_target_pairs={{0,3},{1,2},{2,1},{3,0},{4,7},{5,6},{6,5},{7,4},{8,11},{9,10},{10,... | collective-permute-start | bytes 98312 | tf_op jit(solution)/shard_map/ppermute | solution.py:54
  29.9 1.4 collective-permute-start.3
  32.0 21.4 %all-to-all-start.1 = ((bf16[32,16,128]{2,1,0:T(8,128)(2,1)}), bf16[32,16,128]{2,1,0:T(8,128)(2,1)S(1)}, u32[]{:S(2)}, u32[]{:S(2)}) async-start(bf16[32,16,128]{2,1,0:T(8,128)(2,1)} %bitcast.22), calls=%async_computation.1 | async-start | bytes 262144 | tf_op jit(solution)/shard_map/all_to_all | solution.py:39
  54.2 15.0 %all-to-all-start.2 = ((bf16[32,16,128]{2,1,0:T(8,128)(2,1)}), bf16[32,16,128]{2,1,0:T(8,128)(2,1)S(1)}, u32[]{:S(2)}, u32[]{:S(2)}) async-start(bf16[32,16,128]{2,1,0:T(8,128)(2,1)} %broadcast_in_dim.291), calls=%async_computation.2 | async-start | bytes 262144 | tf_op jit(solution)/shard_map/all_to_all | solution.py:42
  69.2 1.3 collective-permute-start.4
  70.7 9.0 %copy-start.11 = (f32[4,16,128]{2,1,0:T(8,128)}, f32[4,16,128]{2,1,0:T(8,128)S(1)}, u32[]{:S(2)}) copy-start(f32[4,16,128]{2,1,0:T(8,128)S(1)} %get-tuple-element.18) | copy-start | bytes 98308
  70.7 6.2 %collective-permute-start.5 = (bf16[16,1024]{1,0:T(8,128)(2,1)S(1)}, bf16[16,1024]{1,0:T(8,128)(2,1)S(1)}, u32[]{:S(2)}, u32[]{:S(2)}) collective-permute-start(bf16[16,1024]{1,0:T(8,128)(2,1)S(1)} %bitcast.302), channel_id=1, source_target_pairs={{0,1},{1,0},{2,3},{3,2},{4,5},{5,4},{6,7},{7,6},{8,9},{9,8},{10,11... | collective-permute-start | bytes 98312 | tf_op jit(solution)/shard_map/ppermute | solution.py:54
  70.8 6.1 %collective-permute-start.6 = (bf16[16,1024]{1,0:T(8,128)(2,1)S(1)}, bf16[16,1024]{1,0:T(8,128)(2,1)S(1)}, u32[]{:S(2)}, u32[]{:S(2)}) collective-permute-start(bf16[16,1024]{1,0:T(8,128)(2,1)S(1)} %bitcast.303), channel_id=1, source_target_pairs={{0,2},{1,3},{2,0},{3,1},{4,6},{5,7},{6,4},{7,5},{8,10},{9,11},{10,... | collective-permute-start | bytes 98312 | tf_op jit(solution)/shard_map/ppermute | solution.py:54
  73.3 5.1 %collective-permute-start.7 = (bf16[16,1024]{1,0:T(8,128)(2,1)S(1)}, bf16[16,1024]{1,0:T(8,128)(2,1)S(1)}, u32[]{:S(2)}, u32[]{:S(2)}) collective-permute-start(bf16[16,1024]{1,0:T(8,128)(2,1)S(1)} %bitcast.304), channel_id=1, source_target_pairs={{0,3},{1,2},{2,1},{3,0},{4,7},{5,6},{6,5},{7,4},{8,11},{9,10},{10,... | collective-permute-start | bytes 98312 | tf_op jit(solution)/shard_map/ppermute | solution.py:54
  79.6 4.2 %copy-start.7 = (bf16[1,1024,384]{2,1,0:T(8,128)(2,1)S(1)}, bf16[1,1024,384]{2,1,0:T(8,128)(2,1)}, u32[]{:S(2)}) copy-start(bf16[1,1024,384]{2,1,0:T(8,128)(2,1)} %param.10) | copy-start | bytes 2359300
  85.2 2.3 copy-start.3
  87.5 61.9 %all-reduce.2.cloned.1.call-start = ((), (), s32[]{:S(2)}) async-start(), calls=%async_computation.15 | async-start | bytes 4194304 | tf_op jit(solution)/shard_map/psum | solution.py:111
  88.2 40.0 %copy-start.18 = (f32[8,2,4,128]{3,0,2,1:T(8,128)S(1)}, f32[8,2,4,128]{3,0,2,1:T(8,128)}, u32[]{:S(2)}) copy-start(f32[8,2,4,128]{3,0,2,1:T(8,128)} %get-tuple-element.20) | copy-start | bytes 98308
  89.2 4.8 %collective-permute-start.8 = (f32[16,1024]{1,0:T(8,128)S(1)}, f32[16,1024]{1,0:T(8,128)S(1)}, u32[]{:S(2)}, u32[]{:S(2)}) collective-permute-start(f32[16,1024]{1,0:T(8,128)S(1)} %get-tuple-element.35), channel_id=1, source_target_pairs={{0,1},{1,0},{2,3},{3,2},{4,5},{5,4},{6,7},{7,6},{8,9},{9,8},{10,11... | collective-permute-start | bytes 196616 | tf_op jit(solution)/shard_map/ppermute | solution.py:54
  89.3 6.7 %collective-permute-start.9 = (f32[16,1024]{1,0:T(8,128)S(1)}, f32[16,1024]{1,0:T(8,128)S(1)}, u32[]{:S(2)}, u32[]{:S(2)}) collective-permute-start(f32[16,1024]{1,0:T(8,128)S(1)} %get-tuple-element.34), channel_id=1, source_target_pairs={{0,2},{1,3},{2,0},{3,1},{4,6},{5,7},{6,4},{7,5},{8,10},{9,11},{10,... | collective-permute-start | bytes 196616 | tf_op jit(solution)/shard_map/ppermute | solution.py:54
  92.9 5.5 %collective-permute-start.10 = (f32[16,1024]{1,0:T(8,128)S(1)}, f32[16,1024]{1,0:T(8,128)S(1)}, u32[]{:S(2)}, u32[]{:S(2)}) collective-permute-start(f32[16,1024]{1,0:T(8,128)S(1)} %get-tuple-element.33), channel_id=1, source_target_pairs={{0,3},{1,2},{2,1},{3,0},{4,7},{5,6},{6,5},{7,4},{8,11},{9,10},{10,... | collective-permute-start | bytes 196616 | tf_op jit(solution)/shard_map/ppermute | solution.py:54
  94.0 55.4 %copy-start.12 = (f32[4,16,128]{2,1,0:T(8,128)S(1)}, f32[4,16,128]{2,1,0:T(8,128)}, u32[]{:S(2)}) copy-start(f32[4,16,128]{2,1,0:T(8,128)} %copy-done.11) | copy-start | bytes 98308
  98.6 1.4 collective-permute-start.11
  128.1 1.3 collective-permute-start.12
  129.6 57.9 %copy-start.13 = (f32[4,16,128]{2,1,0:T(8,128)}, f32[4,16,128]{2,1,0:T(8,128)S(1)}, u32[]{:S(2)}) copy-start(f32[4,16,128]{2,1,0:T(8,128)S(1)} %get-tuple-element.15) | copy-start | bytes 98308
  129.6 57.9 %copy-start.14 = (f32[4,16,128]{2,1,0:T(8,128)}, f32[4,16,128]{2,1,0:T(8,128)S(1)}, u32[]{:S(2)}) copy-start(f32[4,16,128]{2,1,0:T(8,128)S(1)} %get-tuple-element.16) | copy-start | bytes 98308
  151.4 39.3 %copy-start.2 = (bf16[1024,1024]{1,0:T(8,128)(2,1)S(1)}, bf16[1024,1024]{1,0:T(8,128)(2,1)}, u32[]{:S(2)}) copy-start(bf16[1024,1024]{1,0:T(8,128)(2,1)} %all-reduce.2.cloned.1.call-done) | copy-start | bytes 6291460
  151.5 1.4 collective-permute-start.13
  187.5 2.2 collective-permute-start.14
  190.7 67.2 %copy-start.8 = (f32[8,16,128]{2,1,0:T(8,128)}, f32[8,16,128]{2,1,0:T(8,128)S(1)}, u32[]{:S(2)}) copy-start(f32[8,16,128]{2,1,0:T(8,128)S(1)} %get-tuple-element.29) | copy-start | bytes 196612
  190.7 31.9 %copy-start.17 = (f32[8,2,4,128]{3,0,2,1:T(8,128)S(1)}, f32[8,2,4,128]{3,0,2,1:T(8,128)}, u32[]{:S(2)}) copy-start(f32[8,2,4,128]{3,0,2,1:T(8,128)} %get-tuple-element.22) | copy-start | bytes 98308
  191.2 1.6 collective-permute-start.15
  222.5 1.3 collective-permute-start.16
  224.6 1.4 collective-permute-start.17
  255.5 2.2 collective-permute-start.18
  258.7 31.8 %copy-start.16 = (f32[8,2,4,128]{3,0,2,1:T(8,128)S(1)}, f32[8,2,4,128]{3,0,2,1:T(8,128)}, u32[]{:S(2)}) copy-start(f32[8,2,4,128]{3,0,2,1:T(8,128)} %get-tuple-element.24) | copy-start | bytes 98308
  259.2 1.6 collective-permute-start.19
  290.5 1.3 collective-permute-start.20
  292.5 39.1 %copy-start.5 = (bf16[384,1024]{1,0:T(8,128)(2,1)S(1)}, bf16[384,1024]{1,0:T(8,128)(2,1)}, u32[]{:S(2)}) copy-start(bf16[384,1024]{1,0:T(8,128)(2,1)} %copy-done.4) | copy-start | bytes 2359300
  292.6 1.4 collective-permute-start.21
  294.0 29.4 %copy-start.10 = (f32[4,16,128]{2,1,0:T(8,128)S(1)}, f32[4,16,128]{2,1,0:T(8,128)}, u32[]{:S(2)}) copy-start(f32[4,16,128]{2,1,0:T(8,128)} %copy-done.9) | copy-start | bytes 98308
  322.0 1.3 collective-permute-start.22
  323.5 4.9 %collective-permute-start.23 = (bf16[16,1024]{1,0:T(8,128)(2,1)S(1)}, bf16[16,1024]{1,0:T(8,128)(2,1)S(1)}, u32[]{:S(2)}, u32[]{:S(2)}) collective-permute-start(bf16[16,1024]{1,0:T(8,128)(2,1)S(1)} %copy_bitcast_fusion), channel_id=1, source_target_pairs={{0,1},{1,0},{2,3},{3,2},{4,5},{5,4},{6,7},{7,6},{8,9},{9,8},{10,11... | collective-permute-start | bytes 98312 | tf_op jit(solution)/shard_map/ppermute | solution.py:54
  323.9 5.4 %collective-permute-start.24 = (bf16[16,1024]{1,0:T(8,128)(2,1)S(1)}, bf16[16,1024]{1,0:T(8,128)(2,1)S(1)}, u32[]{:S(2)}, u32[]{:S(2)}) collective-permute-start(bf16[16,1024]{1,0:T(8,128)(2,1)S(1)} %copy_bitcast_fusion), channel_id=1, source_target_pairs={{0,2},{1,3},{2,0},{3,1},{4,6},{5,7},{6,4},{7,5},{8,10},{9,11},{10,... | collective-permute-start | bytes 98312 | tf_op jit(solution)/shard_map/ppermute | solution.py:54
  325.9 5.1 %collective-permute-start.25 = (bf16[16,1024]{1,0:T(8,128)(2,1)S(1)}, bf16[16,1024]{1,0:T(8,128)(2,1)S(1)}, u32[]{:S(2)}, u32[]{:S(2)}) collective-permute-start(bf16[16,1024]{1,0:T(8,128)(2,1)S(1)} %copy_bitcast_fusion), channel_id=1, source_target_pairs={{0,3},{1,2},{2,1},{3,0},{4,7},{5,6},{6,5},{7,4},{8,11},{9,10},{10,... | collective-permute-start | bytes 98312 | tf_op jit(solution)/shard_map/ppermute | solution.py:54
  (3 other events, 4.9 us)
Sparse Core Ops, SparseCore 0:
  9.2 45.0 all-gather.2
  90.6 58.6 all-reduce.1

commit v11 on v10

--- a/solution.py
+++ b/solution.py
@@ -41,11 +41,7 @@
     spread = jnp.broadcast_to(total, (chips,) + tile_shape)
     gathered = lax.all_to_all(spread, "zx", 0, 0, tiled=True).reshape(mine.shape)
     other = lax.ppermute(gathered, "core", swap)
-    return jnp.where(
-        core == 0,
-        jnp.concatenate([gathered, other]),
-        jnp.concatenate([other, gathered]),
-    )
+    return gathered, other
 
 
 def from_partners(value_for, subs):
@@ -129,7 +125,7 @@
         if segment_k == 0:
             pattern = incident.astype(jnp.bfloat16)
         elif segment_k == 1:
-            all_fields = gather_rows(from_tiles(incoming).astype(jnp.bfloat16), subs)
+            all_fields = broadcast_rows(from_tiles(incoming).astype(jnp.bfloat16), subs)
             products = jnp.dot(all_fields, partial_map, preferred_element_type=jnp.float32)
             coupled = scatter_sum(products.reshape((subs, -1) + products.shape[1:]), subs)
             pattern = (incident - coupled).astype(jnp.bfloat16)
@@ -147,7 +143,7 @@
         slots = jnp.where(
             mine[:, None, None, None], pattern_tiles[None], jnp.zeros_like(pattern_tiles)[None]
         )
-        slots = share_slots(slots, chips).astype(jnp.float32)
+        gathered, other = share_slots(slots, chips)
         match = (
             (partner_slot[:, None] == slot_ids[None, :])
             & (partner_segment[:, None] == segment_k)
@@ -157,10 +153,19 @@
         weights = jnp.sum(
             jnp.where(match[:, :, None, None, None, None], trans_tiles[:, None], 0.0), axis=0
         )
-        real_weight = weights[:, 0]
-        imag_weight = weights[:, 1]
-        real_part = slots[:, :half_samples]
-        imag_part = slots[:, half_samples:]
+        weight_halves = weights.reshape((CORES, members // CORES) + weights.shape[1:])
+        core = lax.axis_index("core")
+        ordered_weights = jnp.concatenate(
+            [
+                lax.dynamic_index_in_dim(weight_halves, core, 0, keepdims=False),
+                lax.dynamic_index_in_dim(weight_halves, 1 - core, 0, keepdims=False),
+            ]
+        )
+        values = jnp.concatenate([gathered, other]).astype(jnp.float32)
+        real_weight = ordered_weights[:, 0]
+        imag_weight = ordered_weights[:, 1]
+        real_part = values[:, :half_samples]
+        imag_part = values[:, half_samples:]
         incoming = incoming + jnp.concatenate(
             [
                 jnp.sum(real_weight * real_part - imag_weight * imag_part, axis=0),

time: 341 us -> 343 us (level)
  blocking collectives: 175 us -> 134 us
  waiting for transfers between devices: 61.6 us -> 89.9 us
  starting transfers between devices: 42.5 us -> 55.4 us
    all_to_all x6 -> x3, blocking collectives: 82.2 us -> 41 us  [share_slots(): lax.all_to_all(spread, 'zx', 0, 0, tiled=True).reshape(mine.shape)]
    all_to_all x1 -> x4, waiting for transfers between devices: 8.66 us -> 33.2 us  [share_slots(): lax.all_to_all(spread, 'zx', 0, 0, tiled=True).reshape(mine.shape)]
    all_to_all x1 -> x4, starting transfers between devices: 5.45 us -> 20 us  [share_slots(): lax.all_to_all(spread, 'zx', 0, 0, tiled=True).reshape(mine.shape)]
    ppermute x12 -> x9, starting transfers between devices: 19.1 us -> 14.4 us  [from_partners(): lax.ppermute(value_for(hop), 'sub', [(i, i ^ hop) for i in range(subs)])]
    all_to_all x1 -> x2, starting transfers between devices: 4.46 us -> 8.4 us  [broadcast_rows(): pieces = lax.all_to_all(copies, 'sub', 0, 0, tiled=True)]
    ppermute x12 -> x9, waiting for transfers between devices: 12.2 us -> 11 us  [from_partners(): lax.ppermute(value_for(hop), 'sub', [(i, i ^ hop) for i in range(subs)])]
  transfers between devices with their start and end apart: 31 -> 32, of which waited for: 23 -> 28; matrix products, arithmetic and copies ran while one was open for 4% -> 5% of each run, Pallas kernels for 0% -> 0%
where the time goes in v11:
time: 343 us; the launch traced here: 341 us
  blocking collectives  134 us (39%)
  waiting for transfers between devices  89.9 us (26%)
  starting transfers between devices  55.4 us (16%)
  between operations  24.4 us (7%)
  local copies, waits for them, and re-layouts  12.6 us (4%)
  matrix products  12.3 us (4%)
  other arithmetic  12 us (3%)
    all_to_all x6, blocking collectives, share_slots(): lax.all_to_all(mine.reshape((chips,) + tile_shape), 'zx', 0, 0, tiled=True)  93 us
    all_to_all x3, blocking collectives, share_slots(): lax.all_to_all(spread, 'zx', 0, 0, tiled=True).reshape(mine.shape)  41 us
    all_to_all x4, waiting for transfers between devices, share_slots(): lax.all_to_all(spread, 'zx', 0, 0, tiled=True).reshape(mine.shape)  33.2 us
    psum x1, waiting for transfers between devices, local(): coupling = lax.psum(partial_map, 'sub')  20.2 us
    all_to_all x4, starting transfers between devices, share_slots(): lax.all_to_all(spread, 'zx', 0, 0, tiled=True).reshape(mine.shape)  20 us
    ppermute x9, starting transfers between devices, from_partners(): lax.ppermute(value_for(hop), 'sub', [(i, i ^ hop) for i in range(subs)])  14.4 us
    all_to_all x1, starting transfers between devices, share_slots(): lax.all_to_all(mine.reshape((chips,) + tile_shape), 'zx', 0, 0, tiled=True)  11.3 us
    ppermute x9, waiting for transfers between devices, from_partners(): lax.ppermute(value_for(hop), 'sub', [(i, i ^ hop) for i in range(subs)])  11 us
  transfers between devices with their start and end apart: 32, of which 28 were waited for; matrix products, arithmetic and copies ran while one was open for 5% of the time, Pallas kernels for 0%

profile of v11, /device:TPU:32, one launch (start us, length us, event | category | flops | bytes accessed | tf_op | source)
XLA Modules:
  0.0 340.7 jit_solution(4390564253670803062)
XLA Ops:
  7.3 1.5 broadcast_in_dim.288
  8.8 4.5 %all-to-all-start = ((bf16[4,384,64]{1,2,0:T(8,128)(2,1)}), bf16[4,384,64]{1,2,0:T(8,128)(2,1)S(1)}, u32[]{:S(2)}, u32[]{:S(2)}) async-start(bf16[4,384,64]{1,2,0:T(8,128)(2,1)} %broadcast_in_dim.288), calls=%async_computation | async-start | bytes 393216 | tf_op jit(solution)/shard_map/all_to_all | solution.py:62
  14.6 1.2 dynamic_slice.121
  18.2 1.3 all-to-all-done
  21.3 2.7 collective-permute-start.1
  24.0 1.3 collective-permute-start.2
  26.8 2.8 collective-permute-done.2
  29.8 1.3 collective-permute-done.3
  31.8 11.3 %all-to-all-start.1 = ((bf16[32,16,128]{2,1,0:T(8,128)(2,1)}), bf16[32,16,128]{2,1,0:T(8,128)(2,1)S(1)}, u32[]{:S(2)}, u32[]{:S(2)}) async-start(bf16[32,16,128]{2,1,0:T(8,128)(2,1)} %bitcast.24), calls=%async_computation.1 | async-start | bytes 262144 | tf_op jit(solution)/shard_map/all_to_all | solution.py:39
  47.9 5.1 %all-to-all-done.1 = bf16[32,16,128]{2,1,0:T(8,128)(2,1)S(1)} async-done(((bf16[32,16,128]{2,1,0:T(8,128)(2,1)}), bf16[32,16,128]{2,1,0:T(8,128)(2,1)S(1)}, u32[]{:S(2)}, u32[]{:S(2)}) %all-to-all-start.1) | async-done | bytes 131104 | tf_op jit(solution)/shard_map/all_to_all | solution.py:39
  53.8 4.7 %all-to-all-start.2 = ((bf16[32,16,128]{2,1,0:T(8,128)(2,1)}), bf16[32,16,128]{2,1,0:T(8,128)(2,1)S(1)}, u32[]{:S(2)}, u32[]{:S(2)}) async-start(bf16[32,16,128]{2,1,0:T(8,128)(2,1)} %broadcast_in_dim.296), calls=%async_computation.2 | async-start | bytes 262144 | tf_op jit(solution)/shard_map/all_to_all | solution.py:42
  59.4 8.7 %all-to-all-done.2 = bf16[32,16,128]{2,1,0:T(8,128)(2,1)S(1)} async-done(((bf16[32,16,128]{2,1,0:T(8,128)(2,1)}), bf16[32,16,128]{2,1,0:T(8,128)(2,1)S(1)}, u32[]{:S(2)}, u32[]{:S(2)}) %all-to-all-start.2) | async-done | bytes 131104 | tf_op jit(solution)/shard_map/all_to_all | solution.py:42
  70.3 3.9 %all-to-all-start.3 = ((bf16[4,16,1024]{2,1,0:T(8,128)(2,1)}), bf16[4,16,1024]{2,1,0:T(8,128)(2,1)}, u32[]{:S(2)}, u32[]{:S(2)}) async-start(bf16[4,16,1024]{2,1,0:T(8,128)(2,1)} %broadcast_in_dim.299), calls=%async_computation.3 | async-start | bytes 262144 | tf_op jit(solution)/shard_map/all_to_all | solution.py:62
  74.3 3.3 fusion.4
  78.5 1.3 convolution_convert_fusion
  80.4 2.2 fusion.2
  84.3 1.5 collective-permute-start.5
  85.8 2.7 collective-permute-start.6
  89.2 2.8 collective-permute-done.6
  92.0 2.0 collective-permute-done.7
  94.3 1.3 collective-permute-done.8
  95.6 14.2 %all_to_all.80 = bf16[32,16,128]{2,1,0:T(8,128)(2,1)S(1)} all-to-all(bf16[32,16,128]{2,1,0:T(8,128)(2,1)S(1)} %bitcast.301), channel_id=1, replica_groups=mesh['zx'=32,'core'=2,'sub'=4] {'zx'}, dimensions={0} | all-to-all | bytes 262144 | tf_op jit(solution)/shard_map/all_to_all | solution.py:39
  109.9 13.7 %all_to_all.81 = bf16[32,16,128]{2,1,0:T(8,128)(2,1)S(1)} all-to-all(bf16[32,16,128]{2,1,0:T(8,128)(2,1)S(1)} %broadcast_in_dim.301), channel_id=1, replica_groups=mesh['zx'=32,'core'=2,'sub'=4] {'zx'}, dimensions={0} | all-to-all | bytes 262144 | tf_op jit(solution)/shard_map/all_to_all | solution.py:42
  123.6 1.3 collective-permute-done.9
  125.1 20.2 %all-reduce.2.cloned.1.call-done = bf16[1024,1024]{1,0:T(8,128)(2,1)} async-done(((bf16[1024,1024]{1,0:T(8,128)(2,1)}), bf16[1024,1024]{1,0:T(8,128)(2,1)}) %all-reduce.2.cloned.1.call-update) | async-done | bytes 2097168 | tf_op jit(solution)/shard_map/psum | solution.py:107
  145.3 2.0 fusion.20
  147.5 1.3 collective-permute-done.10
  148.9 19.9 %all_to_all.82 = bf16[32,16,128]{2,1,0:T(8,128)(2,1)} all-to-all(bf16[32,16,128]{2,1,0:T(8,128)(2,1)S(1)} %bitcast.302), channel_id=1, replica_groups=mesh['zx'=32,'core'=2,'sub'=4] {'zx'}, dimensions={0} | all-to-all | bytes 262144 | tf_op jit(solution)/shard_map/all_to_all | solution.py:39
  170.3 5.3 %all-to-all-start.7 = ((bf16[32,16,128]{2,1,0:T(8,128)(2,1)}), bf16[32,16,128]{2,1,0:T(8,128)(2,1)}, u32[]{:S(2)}, u32[]{:S(2)}) async-start(bf16[32,16,128]{2,1,0:T(8,128)(2,1)} %broadcast_in_dim.305), calls=%async_computation.7 | async-start | bytes 262144 | tf_op jit(solution)/shard_map/all_to_all | solution.py:42
  177.5 7.8 %all-to-all-done.7 = bf16[32,16,128]{2,1,0:T(8,128)(2,1)} async-done(((bf16[32,16,128]{2,1,0:T(8,128)(2,1)}), bf16[32,16,128]{2,1,0:T(8,128)(2,1)}, u32[]{:S(2)}, u32[]{:S(2)}) %all-to-all-start.7) | async-done | bytes 131104 | tf_op jit(solution)/shard_map/all_to_all | solution.py:42
  185.4 1.5 collective-permute-done.11
  190.8 14.9 %all_to_all.83 = bf16[32,16,128]{2,1,0:T(8,128)(2,1)} all-to-all(bf16[32,16,128]{2,1,0:T(8,128)(2,1)S(1)} %bitcast.303), channel_id=1, replica_groups=mesh['zx'=32,'core'=2,'sub'=4] {'zx'}, dimensions={0} | all-to-all | bytes 262144 | tf_op jit(solution)/shard_map/all_to_all | solution.py:39
  206.6 13.7 %all_to_all.84 = bf16[32,16,128]{2,1,0:T(8,128)(2,1)S(1)} all-to-all(bf16[32,16,128]{2,1,0:T(8,128)(2,1)S(1)} %broadcast_in_dim.309), channel_id=1, replica_groups=mesh['zx'=32,'core'=2,'sub'=4] {'zx'}, dimensions={0} | all-to-all | bytes 262144 | tf_op jit(solution)/shard_map/all_to_all | solution.py:42
  220.4 1.3 collective-permute-done.13
  223.8 14.8 %all_to_all.85 = bf16[32,16,128]{2,1,0:T(8,128)(2,1)} all-to-all(bf16[32,16,128]{2,1,0:T(8,128)(2,1)S(1)} %bitcast.304), channel_id=1, replica_groups=mesh['zx'=32,'core'=2,'sub'=4] {'zx'}, dimensions={0} | all-to-all | bytes 262144 | tf_op jit(solution)/shard_map/all_to_all | solution.py:39
  240.3 5.3 %all-to-all-start.11 = ((bf16[32,16,128]{2,1,0:T(8,128)(2,1)}), bf16[32,16,128]{2,1,0:T(8,128)(2,1)}, u32[]{:S(2)}, u32[]{:S(2)}) async-start(bf16[32,16,128]{2,1,0:T(8,128)(2,1)} %broadcast_in_dim.313), calls=%async_computation.11 | async-start | bytes 262144 | tf_op jit(solution)/shard_map/all_to_all | solution.py:42
  247.5 7.8 %all-to-all-done.11 = bf16[32,16,128]{2,1,0:T(8,128)(2,1)} async-done(((bf16[32,16,128]{2,1,0:T(8,128)(2,1)}), bf16[32,16,128]{2,1,0:T(8,128)(2,1)}, u32[]{:S(2)}, u32[]{:S(2)}) %all-to-all-start.11) | async-done | bytes 131104 | tf_op jit(solution)/shard_map/all_to_all | solution.py:42
  255.4 1.5 collective-permute-done.15
  260.8 14.9 %all_to_all.86 = bf16[32,16,128]{2,1,0:T(8,128)(2,1)} all-to-all(bf16[32,16,128]{2,1,0:T(8,128)(2,1)S(1)} %bitcast.305), channel_id=1, replica_groups=mesh['zx'=32,'core'=2,'sub'=4] {'zx'}, dimensions={0} | all-to-all | bytes 262144 | tf_op jit(solution)/shard_map/all_to_all | solution.py:39
  276.6 13.7 %all_to_all.87 = bf16[32,16,128]{2,1,0:T(8,128)(2,1)S(1)} all-to-all(bf16[32,16,128]{2,1,0:T(8,128)(2,1)S(1)} %broadcast_in_dim.317), channel_id=1, replica_groups=mesh['zx'=32,'core'=2,'sub'=4] {'zx'}, dimensions={0} | all-to-all | bytes 262144 | tf_op jit(solution)/shard_map/all_to_all | solution.py:42
  290.3 1.3 collective-permute-done.17
  293.8 14.4 %all_to_all.88 = bf16[32,16,128]{2,1,0:T(8,128)(2,1)S(1)} all-to-all(bf16[32,16,128]{2,1,0:T(8,128)(2,1)S(1)} %bitcast.306), channel_id=1, replica_groups=mesh['zx'=32,'core'=2,'sub'=4] {'zx'}, dimensions={0} | all-to-all | bytes 262144 | tf_op jit(solution)/shard_map/all_to_all | solution.py:39
  308.8 4.7 %all-to-all-start.15 = ((bf16[32,16,128]{2,1,0:T(8,128)(2,1)}), bf16[32,16,128]{2,1,0:T(8,128)(2,1)S(1)}, u32[]{:S(2)}, u32[]{:S(2)}) async-start(bf16[32,16,128]{2,1,0:T(8,128)(2,1)} %broadcast_in_dim.321), calls=%async_computation.15 | async-start | bytes 262144 | tf_op jit(solution)/shard_map/all_to_all | solution.py:42
  314.3 8.9 %all-to-all-done.15 = bf16[32,16,128]{2,1,0:T(8,128)(2,1)S(1)} async-done(((bf16[32,16,128]{2,1,0:T(8,128)(2,1)}), bf16[32,16,128]{2,1,0:T(8,128)(2,1)S(1)}, u32[]{:S(2)}, u32[]{:S(2)}) %all-to-all-start.15) | async-done | bytes 131104 | tf_op jit(solution)/shard_map/all_to_all | solution.py:42
  323.3 1.3 collective-permute-done.19
  325.1 2.0 collective-permute-start.21
  327.1 2.4 collective-permute-start.22
  330.5 1.7 collective-permute-done.22
  (207 shorter events, 37.0 us)
Async XLA Ops:
  6.5 13.1 %copy-start = (bf16[1,384,1536]{2,1,0:T(8,128)(2,1)S(1)}, bf16[1,384,1536]{2,1,0:T(8,128)(2,1)}, u32[]{:S(2)}) copy-start(bf16[1,384,1536]{2,1,0:T(8,128)(2,1)} %param.9) | copy-start | bytes 3538948
  6.5 13.6 %copy-start.6 = (bf16[1,1024,384]{2,1,0:T(8,128)(2,1)S(1)}, bf16[1,1024,384]{2,1,0:T(8,128)(2,1)}, u32[]{:S(2)}) copy-start(bf16[1,1024,384]{2,1,0:T(8,128)(2,1)} %param.10) | copy-start | bytes 2359300
  6.5 67.7 %all-gather.3.cloned.1.call-start = ((), (), s32[]{:S(2)}) async-start(), calls=%async_computation.17 | async-start | bytes 3932160 | tf_op jit(solution)/shard_map/all_gather | solution.py:102
  7.3 18.1 %copy-start.1 = (s32[64]{0:T(128)S(1)}, s32[64]{0:T(128)}, u32[]{:S(2)}) copy-start(s32[64]{0:T(128)} %param.15) | copy-start | bytes 772
  8.8 10.8 %all-to-all-start = ((bf16[4,384,64]{1,2,0:T(8,128)(2,1)}), bf16[4,384,64]{1,2,0:T(8,128)(2,1)S(1)}, u32[]{:S(2)}, u32[]{:S(2)}) async-start(bf16[4,384,64]{1,2,0:T(8,128)(2,1)} %broadcast_in_dim.288), calls=%async_computation | async-start | bytes 393216 | tf_op jit(solution)/shard_map/all_to_all | solution.py:62
  20.1 27.8 %copy-start.19 = (f32[1,6,2,512]{3,2,1,0:T(2,128)S(1)}, f32[1,6,2,512]{3,2,1,0:T(2,128)}, u32[]{:S(2)}) copy-start(f32[1,6,2,512]{3,2,1,0:T(2,128)} %param.12) | copy-start | bytes 73732
  20.5 5.4 %collective-permute-start = (bf16[16,1024]{1,0:T(8,128)(2,1)S(1)}, bf16[16,1024]{1,0:T(8,128)(2,1)S(1)}, u32[]{:S(2)}, u32[]{:S(2)}) collective-permute-start(bf16[16,1024]{1,0:T(8,128)(2,1)S(1)} %get-tuple-element.39), channel_id=1, source_target_pairs={{0,1},{1,0},{2,3},{3,2},{4,5},{5,4},{6,7},{7,6},{8,9},{9,8},{10,11... | collective-permute-start | bytes 98312 | tf_op jit(solution)/shard_map/ppermute | solution.py:50
  21.3 5.4 %collective-permute-start.1 = (bf16[16,1024]{1,0:T(8,128)(2,1)S(1)}, bf16[16,1024]{1,0:T(8,128)(2,1)S(1)}, u32[]{:S(2)}, u32[]{:S(2)}) collective-permute-start(bf16[16,1024]{1,0:T(8,128)(2,1)S(1)} %get-tuple-element.38), channel_id=1, source_target_pairs={{0,2},{1,3},{2,0},{3,1},{4,6},{5,7},{6,4},{7,5},{8,10},{9,11},{10,... | collective-permute-start | bytes 98312 | tf_op jit(solution)/shard_map/ppermute | solution.py:50
  24.0 5.5 %collective-permute-start.2 = (bf16[16,1024]{1,0:T(8,128)(2,1)S(1)}, bf16[16,1024]{1,0:T(8,128)(2,1)S(1)}, u32[]{:S(2)}, u32[]{:S(2)}) collective-permute-start(bf16[16,1024]{1,0:T(8,128)(2,1)S(1)} %get-tuple-element.37), channel_id=1, source_target_pairs={{0,3},{1,2},{2,1},{3,0},{4,7},{5,6},{6,5},{7,4},{8,11},{9,10},{10,... | collective-permute-start | bytes 98312 | tf_op jit(solution)/shard_map/ppermute | solution.py:50
  29.7 1.4 collective-permute-start.3
  31.8 21.2 %all-to-all-start.1 = ((bf16[32,16,128]{2,1,0:T(8,128)(2,1)}), bf16[32,16,128]{2,1,0:T(8,128)(2,1)S(1)}, u32[]{:S(2)}, u32[]{:S(2)}) async-start(bf16[32,16,128]{2,1,0:T(8,128)(2,1)} %bitcast.24), calls=%async_computation.1 | async-start | bytes 262144 | tf_op jit(solution)/shard_map/all_to_all | solution.py:39
  53.8 14.3 %all-to-all-start.2 = ((bf16[32,16,128]{2,1,0:T(8,128)(2,1)}), bf16[32,16,128]{2,1,0:T(8,128)(2,1)S(1)}, u32[]{:S(2)}, u32[]{:S(2)}) async-start(bf16[32,16,128]{2,1,0:T(8,128)(2,1)} %broadcast_in_dim.296), calls=%async_computation.2 | async-start | bytes 262144 | tf_op jit(solution)/shard_map/all_to_all | solution.py:42
  68.1 1.3 collective-permute-start.4
  69.6 4.7 %copy-start.9 = (f32[4,16,128]{2,1,0:T(8,128)}, f32[4,16,128]{2,1,0:T(8,128)S(1)}, u32[]{:S(2)}) copy-start(f32[4,16,128]{2,1,0:T(8,128)S(1)} %get-tuple-element.18) | copy-start | bytes 98308
  70.3 10.1 %all-to-all-start.3 = ((bf16[4,16,1024]{2,1,0:T(8,128)(2,1)}), bf16[4,16,1024]{2,1,0:T(8,128)(2,1)}, u32[]{:S(2)}, u32[]{:S(2)}) async-start(bf16[4,16,1024]{2,1,0:T(8,128)(2,1)} %broadcast_in_dim.299), calls=%async_computation.3 | async-start | bytes 262144 | tf_op jit(solution)/shard_map/all_to_all | solution.py:62
  74.2 4.3 %copy-start.7 = (bf16[1,1024,384]{2,1,0:T(8,128)(2,1)S(1)}, bf16[1,1024,384]{2,1,0:T(8,128)(2,1)}, u32[]{:S(2)}) copy-start(bf16[1,1024,384]{2,1,0:T(8,128)(2,1)} %param.10) | copy-start | bytes 2359300
  82.6 62.7 %all-reduce.2.cloned.1.call-start = ((), (), s32[]{:S(2)}) async-start(), calls=%async_computation.16 | async-start | bytes 4194304 | tf_op jit(solution)/shard_map/psum | solution.py:107
  83.3 40.2 %copy-start.18 = (f32[8,2,4,128]{3,0,2,1:T(8,128)S(1)}, f32[8,2,4,128]{3,0,2,1:T(8,128)}, u32[]{:S(2)}) copy-start(f32[8,2,4,128]{3,0,2,1:T(8,128)} %get-tuple-element.20) | copy-start | bytes 98308
  84.3 4.8 %collective-permute-start.5 = (f32[16,1024]{1,0:T(8,128)S(1)}, f32[16,1024]{1,0:T(8,128)S(1)}, u32[]{:S(2)}, u32[]{:S(2)}) collective-permute-start(f32[16,1024]{1,0:T(8,128)S(1)} %get-tuple-element.35), channel_id=1, source_target_pairs={{0,1},{1,0},{2,3},{3,2},{4,5},{5,4},{6,7},{7,6},{8,9},{9,8},{10,11... | collective-permute-start | bytes 196616 | tf_op jit(solution)/shard_map/ppermute | solution.py:50
  85.8 6.1 %collective-permute-start.6 = (f32[16,1024]{1,0:T(8,128)S(1)}, f32[16,1024]{1,0:T(8,128)S(1)}, u32[]{:S(2)}, u32[]{:S(2)}) collective-permute-start(f32[16,1024]{1,0:T(8,128)S(1)} %get-tuple-element.34), channel_id=1, source_target_pairs={{0,2},{1,3},{2,0},{3,1},{4,6},{5,7},{6,4},{7,5},{8,10},{9,11},{10,... | collective-permute-start | bytes 196616 | tf_op jit(solution)/shard_map/ppermute | solution.py:50
  88.5 5.5 %collective-permute-start.7 = (f32[16,1024]{1,0:T(8,128)S(1)}, f32[16,1024]{1,0:T(8,128)S(1)}, u32[]{:S(2)}, u32[]{:S(2)}) collective-permute-start(f32[16,1024]{1,0:T(8,128)S(1)} %get-tuple-element.33), channel_id=1, source_target_pairs={{0,3},{1,2},{2,1},{3,0},{4,7},{5,6},{6,5},{7,4},{8,11},{9,10},{10,... | collective-permute-start | bytes 196616 | tf_op jit(solution)/shard_map/ppermute | solution.py:50
  89.1 56.1 %copy-start.10 = (f32[4,16,128]{2,1,0:T(8,128)S(1)}, f32[4,16,128]{2,1,0:T(8,128)}, u32[]{:S(2)}) copy-start(f32[4,16,128]{2,1,0:T(8,128)} %copy-done.9) | copy-start | bytes 98308
  94.2 1.4 collective-permute-start.8
  123.6 1.3 collective-permute-start.9
  125.1 20.2 %copy-start.13 = (f32[4,16,128]{2,1,0:T(8,128)}, f32[4,16,128]{2,1,0:T(8,128)S(1)}, u32[]{:S(2)}) copy-start(f32[4,16,128]{2,1,0:T(8,128)S(1)} %get-tuple-element.15) | copy-start | bytes 98308
  125.1 20.2 %copy-start.14 = (f32[4,16,128]{2,1,0:T(8,128)}, f32[4,16,128]{2,1,0:T(8,128)S(1)}, u32[]{:S(2)}) copy-start(f32[4,16,128]{2,1,0:T(8,128)S(1)} %get-tuple-element.16) | copy-start | bytes 98308
  147.2 41.5 %copy-start.2 = (bf16[1024,1024]{1,0:T(8,128)(2,1)S(1)}, bf16[1024,1024]{1,0:T(8,128)(2,1)}, u32[]{:S(2)}) copy-start(bf16[1024,1024]{1,0:T(8,128)(2,1)} %all-reduce.2.cloned.1.call-done) | copy-start | bytes 6291460
  147.4 1.4 collective-permute-start.10
  170.3 15.0 %all-to-all-start.7 = ((bf16[32,16,128]{2,1,0:T(8,128)(2,1)}), bf16[32,16,128]{2,1,0:T(8,128)(2,1)}, u32[]{:S(2)}, u32[]{:S(2)}) async-start(bf16[32,16,128]{2,1,0:T(8,128)(2,1)} %broadcast_in_dim.305), calls=%async_computation.7 | async-start | bytes 262144 | tf_op jit(solution)/shard_map/all_to_all | solution.py:42
  185.3 1.6 collective-permute-start.11
  188.7 33.1 %copy-start.8 = (f32[8,16,128]{2,1,0:T(8,128)}, f32[8,16,128]{2,1,0:T(8,128)S(1)}, u32[]{:S(2)}) copy-start(f32[8,16,128]{2,1,0:T(8,128)S(1)} %get-tuple-element.29) | copy-start | bytes 196612
  188.7 31.6 %copy-start.17 = (f32[8,2,4,128]{3,0,2,1:T(8,128)S(1)}, f32[8,2,4,128]{3,0,2,1:T(8,128)}, u32[]{:S(2)}) copy-start(f32[8,2,4,128]{3,0,2,1:T(8,128)} %get-tuple-element.22) | copy-start | bytes 98308
  189.3 1.4 collective-permute-start.12
  220.3 1.3 collective-permute-start.13
  222.3 1.4 collective-permute-start.14
  240.3 15.0 %all-to-all-start.11 = ((bf16[32,16,128]{2,1,0:T(8,128)(2,1)}), bf16[32,16,128]{2,1,0:T(8,128)(2,1)}, u32[]{:S(2)}, u32[]{:S(2)}) async-start(bf16[32,16,128]{2,1,0:T(8,128)(2,1)} %broadcast_in_dim.313), calls=%async_computation.11 | async-start | bytes 262144 | tf_op jit(solution)/shard_map/all_to_all | solution.py:42
  255.3 1.6 collective-permute-start.15
  258.8 31.5 %copy-start.16 = (f32[8,2,4,128]{3,0,2,1:T(8,128)S(1)}, f32[8,2,4,128]{3,0,2,1:T(8,128)}, u32[]{:S(2)}) copy-start(f32[8,2,4,128]{3,0,2,1:T(8,128)} %get-tuple-element.24) | copy-start | bytes 98308
  259.3 1.4 collective-permute-start.16
  290.3 1.3 collective-permute-start.17
  292.3 40.5 %copy-start.5 = (bf16[384,1024]{1,0:T(8,128)(2,1)S(1)}, bf16[384,1024]{1,0:T(8,128)(2,1)}, u32[]{:S(2)}) copy-start(bf16[384,1024]{1,0:T(8,128)(2,1)} %copy-done.4) | copy-start | bytes 2359300
  292.3 1.4 collective-permute-start.18
  293.8 30.9 %copy-start.12 = (f32[4,16,128]{2,1,0:T(8,128)S(1)}, f32[4,16,128]{2,1,0:T(8,128)}, u32[]{:S(2)}) copy-start(f32[4,16,128]{2,1,0:T(8,128)} %copy-done.11) | copy-start | bytes 98308
  308.8 14.4 %all-to-all-start.15 = ((bf16[32,16,128]{2,1,0:T(8,128)(2,1)}), bf16[32,16,128]{2,1,0:T(8,128)(2,1)S(1)}, u32[]{:S(2)}, u32[]{:S(2)}) async-start(bf16[32,16,128]{2,1,0:T(8,128)(2,1)} %broadcast_in_dim.321), calls=%async_computation.15 | async-start | bytes 262144 | tf_op jit(solution)/shard_map/all_to_all | solution.py:42
  323.2 1.3 collective-permute-start.19
  324.7 4.9 %collective-permute-start.20 = (bf16[16,1024]{1,0:T(8,128)(2,1)S(1)}, bf16[16,1024]{1,0:T(8,128)(2,1)S(1)}, u32[]{:S(2)}, u32[]{:S(2)}) collective-permute-start(bf16[16,1024]{1,0:T(8,128)(2,1)S(1)} %copy_bitcast_fusion), channel_id=1, source_target_pairs={{0,1},{1,0},{2,3},{3,2},{4,5},{5,4},{6,7},{7,6},{8,9},{9,8},{10,11... | collective-permute-start | bytes 98312 | tf_op jit(solution)/shard_map/ppermute | solution.py:50
  325.1 5.4 %collective-permute-start.21 = (bf16[16,1024]{1,0:T(8,128)(2,1)S(1)}, bf16[16,1024]{1,0:T(8,128)(2,1)S(1)}, u32[]{:S(2)}, u32[]{:S(2)}) collective-permute-start(bf16[16,1024]{1,0:T(8,128)(2,1)S(1)} %copy_bitcast_fusion), channel_id=1, source_target_pairs={{0,2},{1,3},{2,0},{3,1},{4,6},{5,7},{6,4},{7,5},{8,10},{9,11},{10,... | collective-permute-start | bytes 98312 | tf_op jit(solution)/shard_map/ppermute | solution.py:50
  327.1 5.1 %collective-permute-start.22 = (bf16[16,1024]{1,0:T(8,128)(2,1)S(1)}, bf16[16,1024]{1,0:T(8,128)(2,1)S(1)}, u32[]{:S(2)}, u32[]{:S(2)}) collective-permute-start(bf16[16,1024]{1,0:T(8,128)(2,1)S(1)} %copy_bitcast_fusion), channel_id=1, source_target_pairs={{0,3},{1,2},{2,1},{3,0},{4,7},{5,6},{6,5},{7,4},{8,11},{9,10},{10,... | collective-permute-start | bytes 98312 | tf_op jit(solution)/shard_map/ppermute | solution.py:50
  (4 other events, 7.7 us)
Sparse Core Ops, SparseCore 0:
  9.2 45.0 all-gather.2
  85.8 59.4 all-reduce.1

commit v12 on v10

--- a/solution.py
+++ b/solution.py
@@ -97,7 +97,15 @@
         return jnp.dot(inverse_rows, shard_rows, preferred_element_type=jnp.float32)
 
     subs = lax.axis_size("sub")
-    solved = apply_inverse(broadcast_rows(excite_rows, subs))
+    sub_index = lax.axis_index("sub")
+    excite_parts = from_partners(lambda hop: excite_rows, subs)
+    excite_block = excite_rows.shape[0]
+    solved = jnp.zeros((inverse_rows.shape[0], excite_rows.shape[1]), jnp.float32)
+    for hop in range(subs):
+        columns = lax.dynamic_slice_in_dim(
+            inverse_rows, (sub_index ^ hop) * excite_block, excite_block, axis=1
+        )
+        solved = solved + jnp.dot(columns, excite_parts[hop], preferred_element_type=jnp.float32)
     solved_half = solved.astype(jnp.bfloat16)
     partial_incident = lax.dot_general(
         solved_half, agg_columns, CONTRACT_FIRST, preferred_element_type=jnp.float32
@@ -129,7 +137,7 @@
         if segment_k == 0:
             pattern = incident.astype(jnp.bfloat16)
         elif segment_k == 1:
-            all_fields = gather_rows(from_tiles(incoming).astype(jnp.bfloat16), subs)
+            all_fields = broadcast_rows(from_tiles(incoming).astype(jnp.bfloat16), subs)
             products = jnp.dot(all_fields, partial_map, preferred_element_type=jnp.float32)
             coupled = scatter_sum(products.reshape((subs, -1) + products.shape[1:]), subs)
             pattern = (incident - coupled).astype(jnp.bfloat16)

time: 341 us -> 340 us (level)
  blocking collectives: 175 us -> 162 us
  waiting for transfers between devices: 61.6 us -> 69.4 us
  starting transfers between devices: 42.5 us -> 47.4 us
    all_to_all x6 -> x5, blocking collectives: 82.2 us -> 68.5 us  [share_slots(): lax.all_to_all(spread, 'zx', 0, 0, tiled=True).reshape(mine.shape)]
    all_to_all x1 -> x2, waiting for transfers between devices: 8.66 us -> 17.6 us  [share_slots(): lax.all_to_all(spread, 'zx', 0, 0, tiled=True).reshape(mine.shape)]
    all_to_all x1 -> x2, starting transfers between devices: 5.45 us -> 11.5 us  [share_slots(): lax.all_to_all(spread, 'zx', 0, 0, tiled=True).reshape(mine.shape)]
  transfers between devices with their start and end apart: 31 -> 32, of which waited for: 23 -> 23; matrix products, arithmetic and copies ran while one was open for 4% -> 5% of each run, Pallas kernels for 0% -> 0%
where the time goes in v12:
time: 340 us; the launch traced here: 338 us
  blocking collectives  162 us (48%)
  waiting for transfers between devices  69.4 us (20%)
  starting transfers between devices  47.4 us (14%)
  between operations  26.1 us (8%)
  matrix products  13.6 us (4%)
  other arithmetic  10.2 us (3%)
  local copies, waits for them, and re-layouts  9.8 us (3%)
    all_to_all x6, blocking collectives, share_slots(): lax.all_to_all(mine.reshape((chips,) + tile_shape), 'zx', 0, 0, tiled=True)  93.1 us
    all_to_all x5, blocking collectives, share_slots(): lax.all_to_all(spread, 'zx', 0, 0, tiled=True).reshape(mine.shape)  68.5 us
    psum x1, waiting for transfers between devices, local(): coupling = lax.psum(partial_map, 'sub')  20 us
    ppermute x12, starting transfers between devices, from_partners(): lax.ppermute(value_for(hop), 'sub', [(i, i ^ hop) for i in range(subs)])  18.9 us
    all_to_all x2, waiting for transfers between devices, share_slots(): lax.all_to_all(spread, 'zx', 0, 0, tiled=True).reshape(mine.shape)  17.6 us
    ppermute x12, waiting for transfers between devices, from_partners(): lax.ppermute(value_for(hop), 'sub', [(i, i ^ hop) for i in range(subs)])  12.1 us
    all_to_all x2, starting transfers between devices, share_slots(): lax.all_to_all(spread, 'zx', 0, 0, tiled=True).reshape(mine.shape)  11.5 us
    all_to_all x1, starting transfers between devices, share_slots(): lax.all_to_all(mine.reshape((chips,) + tile_shape), 'zx', 0, 0, tiled=True)  11 us
  transfers between devices with their start and end apart: 32, of which 23 were waited for; matrix products, arithmetic and copies ran while one was open for 5% of the time, Pallas kernels for 0%

profile of v12, /device:TPU:32, one launch (start us, length us, event | category | flops | bytes accessed | tf_op | source)
XLA Modules:
  0.0 338.0 jit_solution(8381426654984464099)
XLA Ops:
  7.3 1.7 collective-permute-start
  8.9 2.2 collective-permute-start.2
  13.2 1.0 fusion.26
  14.2 1.2 dynamic_slice.104
  19.3 1.3 collective-permute-start.3
  20.6 2.9 collective-permute-start.4
  24.8 1.3 collective-permute-done.4
  26.1 3.2 collective-permute-done.5
  29.6 1.3 collective-permute-done.6
  31.6 11.0 %all-to-all-start = ((bf16[32,16,128]{2,1,0:T(8,128)(2,1)}), bf16[32,16,128]{2,1,0:T(8,128)(2,1)S(1)}, u32[]{:S(2)}, u32[]{:S(2)}) async-start(bf16[32,16,128]{2,1,0:T(8,128)(2,1)} %bitcast.26), calls=%async_computation | async-start | bytes 262144 | tf_op jit(solution)/shard_map/all_to_all | solution.py:39
  49.5 2.9 all-to-all-done
  53.2 6.8 %all-to-all-start.1 = ((bf16[32,16,128]{2,1,0:T(8,128)(2,1)}), bf16[32,16,128]{2,1,0:T(8,128)(2,1)S(1)}, u32[]{:S(2)}, u32[]{:S(2)}) async-start(bf16[32,16,128]{2,1,0:T(8,128)(2,1)} %broadcast_in_dim.287), calls=%async_computation.1 | async-start | bytes 262144 | tf_op jit(solution)/shard_map/all_to_all | solution.py:42
  60.9 8.7 %all-to-all-done.1 = bf16[32,16,128]{2,1,0:T(8,128)(2,1)S(1)} async-done(((bf16[32,16,128]{2,1,0:T(8,128)(2,1)}), bf16[32,16,128]{2,1,0:T(8,128)(2,1)S(1)}, u32[]{:S(2)}, u32[]{:S(2)}) %all-to-all-start.1) | async-done | bytes 131104 | tf_op jit(solution)/shard_map/all_to_all | solution.py:42
  69.6 1.3 collective-permute-done.7
  71.7 3.9 %all-to-all-start.2 = ((bf16[4,16,1024]{2,1,0:T(8,128)(2,1)}), bf16[4,16,1024]{2,1,0:T(8,128)(2,1)}, u32[]{:S(2)}, u32[]{:S(2)}) async-start(bf16[4,16,1024]{2,1,0:T(8,128)(2,1)} %broadcast_in_dim.290), calls=%async_computation.2 | async-start | bytes 262144 | tf_op jit(solution)/shard_map/all_to_all | solution.py:66
  75.7 3.3 fusion.4
  80.0 1.3 convolution_convert_fusion
  81.7 2.3 fusion.2
  85.7 1.6 collective-permute-start.8
  87.3 2.7 collective-permute-start.9
  90.5 2.7 collective-permute-done.9
  93.3 2.2 collective-permute-done.10
  95.9 1.3 collective-permute-done.11
  97.3 14.1 %all_to_all.75 = bf16[32,16,128]{2,1,0:T(8,128)(2,1)S(1)} all-to-all(bf16[32,16,128]{2,1,0:T(8,128)(2,1)S(1)} %bitcast.270), channel_id=1, replica_groups=mesh['zx'=32,'core'=2,'sub'=4] {'zx'}, dimensions={0} | all-to-all | bytes 262144 | tf_op jit(solution)/shard_map/all_to_all | solution.py:39
  111.5 13.7 %all_to_all.76 = bf16[32,16,128]{2,1,0:T(8,128)(2,1)S(1)} all-to-all(bf16[32,16,128]{2,1,0:T(8,128)(2,1)S(1)} %broadcast_in_dim.292), channel_id=1, replica_groups=mesh['zx'=32,'core'=2,'sub'=4] {'zx'}, dimensions={0} | all-to-all | bytes 262144 | tf_op jit(solution)/shard_map/all_to_all | solution.py:42
  125.2 1.3 collective-permute-done.12
  126.7 20.0 %all-reduce.2.cloned.1.call-done = bf16[1024,1024]{1,0:T(8,128)(2,1)} async-done(((bf16[1024,1024]{1,0:T(8,128)(2,1)}), bf16[1024,1024]{1,0:T(8,128)(2,1)}) %all-reduce.2.cloned.1.call-update) | async-done | bytes 2097168 | tf_op jit(solution)/shard_map/psum | solution.py:119
  146.7 2.0 fusion.19
  149.0 1.3 collective-permute-done.13
  150.3 19.9 %all_to_all.77 = bf16[32,16,128]{2,1,0:T(8,128)(2,1)} all-to-all(bf16[32,16,128]{2,1,0:T(8,128)(2,1)S(1)} %bitcast.271), channel_id=1, replica_groups=mesh['zx'=32,'core'=2,'sub'=4] {'zx'}, dimensions={0} | all-to-all | bytes 262144 | tf_op jit(solution)/shard_map/all_to_all | solution.py:39
  171.1 13.7 %all_to_all.78 = bf16[32,16,128]{2,1,0:T(8,128)(2,1)S(1)} all-to-all(bf16[32,16,128]{2,1,0:T(8,128)(2,1)S(1)} %broadcast_in_dim.296), channel_id=1, replica_groups=mesh['zx'=32,'core'=2,'sub'=4] {'zx'}, dimensions={0} | all-to-all | bytes 262144 | tf_op jit(solution)/shard_map/all_to_all | solution.py:42
  190.2 15.1 %all_to_all.79 = bf16[32,16,128]{2,1,0:T(8,128)(2,1)} all-to-all(bf16[32,16,128]{2,1,0:T(8,128)(2,1)S(1)} %bitcast.272), channel_id=1, replica_groups=mesh['zx'=32,'core'=2,'sub'=4] {'zx'}, dimensions={0} | all-to-all | bytes 262144 | tf_op jit(solution)/shard_map/all_to_all | solution.py:39
  206.2 13.7 %all_to_all.80 = bf16[32,16,128]{2,1,0:T(8,128)(2,1)S(1)} all-to-all(bf16[32,16,128]{2,1,0:T(8,128)(2,1)S(1)} %broadcast_in_dim.300), channel_id=1, replica_groups=mesh['zx'=32,'core'=2,'sub'=4] {'zx'}, dimensions={0} | all-to-all | bytes 262144 | tf_op jit(solution)/shard_map/all_to_all | solution.py:42
  219.9 1.3 collective-permute-done.16
  222.1 1.2 collective-permute-done.17
  223.4 14.8 %all_to_all.81 = bf16[32,16,128]{2,1,0:T(8,128)(2,1)} all-to-all(bf16[32,16,128]{2,1,0:T(8,128)(2,1)S(1)} %bitcast.273), channel_id=1, replica_groups=mesh['zx'=32,'core'=2,'sub'=4] {'zx'}, dimensions={0} | all-to-all | bytes 262144 | tf_op jit(solution)/shard_map/all_to_all | solution.py:39
  239.2 13.7 %all_to_all.82 = bf16[32,16,128]{2,1,0:T(8,128)(2,1)S(1)} all-to-all(bf16[32,16,128]{2,1,0:T(8,128)(2,1)S(1)} %broadcast_in_dim.304), channel_id=1, replica_groups=mesh['zx'=32,'core'=2,'sub'=4] {'zx'}, dimensions={0} | all-to-all | bytes 262144 | tf_op jit(solution)/shard_map/all_to_all | solution.py:42
  258.2 15.1 %all_to_all.83 = bf16[32,16,128]{2,1,0:T(8,128)(2,1)} all-to-all(bf16[32,16,128]{2,1,0:T(8,128)(2,1)S(1)} %bitcast.274), channel_id=1, replica_groups=mesh['zx'=32,'core'=2,'sub'=4] {'zx'}, dimensions={0} | all-to-all | bytes 262144 | tf_op jit(solution)/shard_map/all_to_all | solution.py:39
  274.2 13.7 %all_to_all.84 = bf16[32,16,128]{2,1,0:T(8,128)(2,1)S(1)} all-to-all(bf16[32,16,128]{2,1,0:T(8,128)(2,1)S(1)} %broadcast_in_dim.308), channel_id=1, replica_groups=mesh['zx'=32,'core'=2,'sub'=4] {'zx'}, dimensions={0} | all-to-all | bytes 262144 | tf_op jit(solution)/shard_map/all_to_all | solution.py:42
  287.9 1.3 collective-permute-done.20
  290.2 1.2 collective-permute-done.21
  291.4 14.1 %all_to_all.85 = bf16[32,16,128]{2,1,0:T(8,128)(2,1)S(1)} all-to-all(bf16[32,16,128]{2,1,0:T(8,128)(2,1)S(1)} %bitcast.269), channel_id=1, replica_groups=mesh['zx'=32,'core'=2,'sub'=4] {'zx'}, dimensions={0} | all-to-all | bytes 262144 | tf_op jit(solution)/shard_map/all_to_all | solution.py:39
  306.2 4.7 %all-to-all-start.14 = ((bf16[32,16,128]{2,1,0:T(8,128)(2,1)}), bf16[32,16,128]{2,1,0:T(8,128)(2,1)S(1)}, u32[]{:S(2)}, u32[]{:S(2)}) async-start(bf16[32,16,128]{2,1,0:T(8,128)(2,1)} %broadcast_in_dim.312), calls=%async_computation.14 | async-start | bytes 262144 | tf_op jit(solution)/shard_map/all_to_all | solution.py:42
  311.6 8.9 %all-to-all-done.14 = bf16[32,16,128]{2,1,0:T(8,128)(2,1)S(1)} async-done(((bf16[32,16,128]{2,1,0:T(8,128)(2,1)}), bf16[32,16,128]{2,1,0:T(8,128)(2,1)S(1)}, u32[]{:S(2)}, u32[]{:S(2)}) %all-to-all-start.14) | async-done | bytes 131104 | tf_op jit(solution)/shard_map/all_to_all | solution.py:42
  320.6 1.3 collective-permute-done.22
  322.4 2.0 collective-permute-start.24
  324.4 2.4 collective-permute-start.25
  327.9 1.7 collective-permute-done.25
  (203 shorter events, 31.5 us)
Async XLA Ops:
  6.5 6.6 %copy-start = (bf16[1,384,1536]{2,1,0:T(8,128)(2,1)S(1)}, bf16[1,384,1536]{2,1,0:T(8,128)(2,1)}, u32[]{:S(2)}) copy-start(bf16[1,384,1536]{2,1,0:T(8,128)(2,1)} %param.9) | copy-start | bytes 3538948
  6.5 17.6 %copy-start.1 = (s32[64]{0:T(128)S(1)}, s32[64]{0:T(128)}, u32[]{:S(2)}) copy-start(s32[64]{0:T(128)} %param.15) | copy-start | bytes 772
  6.5 12.4 %copy-start.6 = (bf16[1,1024,384]{2,1,0:T(8,128)(2,1)S(1)}, bf16[1,1024,384]{2,1,0:T(8,128)(2,1)}, u32[]{:S(2)}) copy-start(bf16[1,1024,384]{2,1,0:T(8,128)(2,1)} %param.10) | copy-start | bytes 2359300
  6.5 69.2 %all-gather.3.cloned.1.call-start = ((), (), s32[]{:S(2)}) async-start(), calls=%async_computation.16 | async-start | bytes 3932160 | tf_op jit(solution)/shard_map/all_gather | solution.py:114
  7.3 10.9 %collective-permute-start = (bf16[384,64]{0,1:T(8,128)(2,1)}, bf16[384,64]{0,1:T(8,128)(2,1)S(1)}, u32[]{:S(2)}, u32[]{:S(2)}) collective-permute-start(bf16[384,64]{0,1:T(8,128)(2,1)} %bitcast.307), channel_id=1, source_target_pairs={{0,1},{1,0},{2,3},{3,2},{4,5},{5,4},{6,7},{7,6},{8,9},{9,8},{10,11... | collective-permute-start | bytes 147464 | tf_op jit(solution)/shard_map/ppermute | solution.py:54
  8.9 9.5 %collective-permute-start.2 = (bf16[384,64]{0,1:T(8,128)(2,1)}, bf16[384,64]{0,1:T(8,128)(2,1)S(1)}, u32[]{:S(2)}, u32[]{:S(2)}) collective-permute-start(bf16[384,64]{0,1:T(8,128)(2,1)} %bitcast.308), channel_id=1, source_target_pairs={{0,3},{1,2},{2,1},{3,0},{4,7},{5,6},{6,5},{7,4},{8,11},{9,10},{10,... | collective-permute-start | bytes 147464 | tf_op jit(solution)/shard_map/ppermute | solution.py:54
  11.1 7.6 %collective-permute-start.1 = (bf16[384,64]{0,1:T(8,128)(2,1)}, bf16[384,64]{0,1:T(8,128)(2,1)S(1)}, u32[]{:S(2)}, u32[]{:S(2)}) collective-permute-start(bf16[384,64]{0,1:T(8,128)(2,1)} %bitcast.309), channel_id=1, source_target_pairs={{0,2},{1,3},{2,0},{3,1},{4,6},{5,7},{6,4},{7,5},{8,10},{9,11},{10,... | collective-permute-start | bytes 147464 | tf_op jit(solution)/shard_map/ppermute | solution.py:54
  18.7 30.8 %copy-start.19 = (f32[1,6,2,512]{3,2,1,0:T(2,128)S(1)}, f32[1,6,2,512]{3,2,1,0:T(2,128)}, u32[]{:S(2)}) copy-start(f32[1,6,2,512]{3,2,1,0:T(2,128)} %param.12) | copy-start | bytes 73732
  19.3 5.4 %collective-permute-start.3 = (bf16[16,1024]{1,0:T(8,128)(2,1)S(1)}, bf16[16,1024]{1,0:T(8,128)(2,1)S(1)}, u32[]{:S(2)}, u32[]{:S(2)}) collective-permute-start(bf16[16,1024]{1,0:T(8,128)(2,1)S(1)} %get-tuple-element.39), channel_id=1, source_target_pairs={{0,1},{1,0},{2,3},{3,2},{4,5},{5,4},{6,7},{7,6},{8,9},{9,8},{10,11... | collective-permute-start | bytes 98312 | tf_op jit(solution)/shard_map/ppermute | solution.py:54
  20.6 5.4 %collective-permute-start.4 = (bf16[16,1024]{1,0:T(8,128)(2,1)S(1)}, bf16[16,1024]{1,0:T(8,128)(2,1)S(1)}, u32[]{:S(2)}, u32[]{:S(2)}) collective-permute-start(bf16[16,1024]{1,0:T(8,128)(2,1)S(1)} %get-tuple-element.38), channel_id=1, source_target_pairs={{0,2},{1,3},{2,0},{3,1},{4,6},{5,7},{6,4},{7,5},{8,10},{9,11},{10,... | collective-permute-start | bytes 98312 | tf_op jit(solution)/shard_map/ppermute | solution.py:54
  23.5 5.8 %collective-permute-start.5 = (bf16[16,1024]{1,0:T(8,128)(2,1)S(1)}, bf16[16,1024]{1,0:T(8,128)(2,1)S(1)}, u32[]{:S(2)}, u32[]{:S(2)}) collective-permute-start(bf16[16,1024]{1,0:T(8,128)(2,1)S(1)} %get-tuple-element.37), channel_id=1, source_target_pairs={{0,3},{1,2},{2,1},{3,0},{4,7},{5,6},{6,5},{7,4},{8,11},{9,10},{10,... | collective-permute-start | bytes 98312 | tf_op jit(solution)/shard_map/ppermute | solution.py:54
  29.5 1.4 collective-permute-start.6
  31.6 20.9 %all-to-all-start = ((bf16[32,16,128]{2,1,0:T(8,128)(2,1)}), bf16[32,16,128]{2,1,0:T(8,128)(2,1)S(1)}, u32[]{:S(2)}, u32[]{:S(2)}) async-start(bf16[32,16,128]{2,1,0:T(8,128)(2,1)} %bitcast.26), calls=%async_computation | async-start | bytes 262144 | tf_op jit(solution)/shard_map/all_to_all | solution.py:39
  53.2 16.4 %all-to-all-start.1 = ((bf16[32,16,128]{2,1,0:T(8,128)(2,1)}), bf16[32,16,128]{2,1,0:T(8,128)(2,1)S(1)}, u32[]{:S(2)}, u32[]{:S(2)}) async-start(bf16[32,16,128]{2,1,0:T(8,128)(2,1)} %broadcast_in_dim.287), calls=%async_computation.1 | async-start | bytes 262144 | tf_op jit(solution)/shard_map/all_to_all | solution.py:42
  69.6 1.3 collective-permute-start.7
  71.0 4.7 %copy-start.9 = (f32[4,16,128]{2,1,0:T(8,128)}, f32[4,16,128]{2,1,0:T(8,128)S(1)}, u32[]{:S(2)}) copy-start(f32[4,16,128]{2,1,0:T(8,128)S(1)} %get-tuple-element.18) | copy-start | bytes 98308
  71.7 10.0 %all-to-all-start.2 = ((bf16[4,16,1024]{2,1,0:T(8,128)(2,1)}), bf16[4,16,1024]{2,1,0:T(8,128)(2,1)}, u32[]{:S(2)}, u32[]{:S(2)}) async-start(bf16[4,16,1024]{2,1,0:T(8,128)(2,1)} %broadcast_in_dim.290), calls=%async_computation.2 | async-start | bytes 262144 | tf_op jit(solution)/shard_map/all_to_all | solution.py:66
  75.7 4.2 %copy-start.7 = (bf16[1,1024,384]{2,1,0:T(8,128)(2,1)S(1)}, bf16[1,1024,384]{2,1,0:T(8,128)(2,1)}, u32[]{:S(2)}) copy-start(bf16[1,1024,384]{2,1,0:T(8,128)(2,1)} %param.10) | copy-start | bytes 2359300
  84.0 62.7 %all-reduce.2.cloned.1.call-start = ((), (), s32[]{:S(2)}) async-start(), calls=%async_computation.15 | async-start | bytes 4194304 | tf_op jit(solution)/shard_map/psum | solution.py:119
  84.7 40.5 %copy-start.18 = (f32[8,2,4,128]{3,0,2,1:T(8,128)S(1)}, f32[8,2,4,128]{3,0,2,1:T(8,128)}, u32[]{:S(2)}) copy-start(f32[8,2,4,128]{3,0,2,1:T(8,128)} %get-tuple-element.20) | copy-start | bytes 98308
  85.7 4.8 %collective-permute-start.8 = (f32[16,1024]{1,0:T(8,128)S(1)}, f32[16,1024]{1,0:T(8,128)S(1)}, u32[]{:S(2)}, u32[]{:S(2)}) collective-permute-start(f32[16,1024]{1,0:T(8,128)S(1)} %get-tuple-element.35), channel_id=1, source_target_pairs={{0,1},{1,0},{2,3},{3,2},{4,5},{5,4},{6,7},{7,6},{8,9},{9,8},{10,11... | collective-permute-start | bytes 196616 | tf_op jit(solution)/shard_map/ppermute | solution.py:54
  87.3 5.9 %collective-permute-start.9 = (f32[16,1024]{1,0:T(8,128)S(1)}, f32[16,1024]{1,0:T(8,128)S(1)}, u32[]{:S(2)}, u32[]{:S(2)}) collective-permute-start(f32[16,1024]{1,0:T(8,128)S(1)} %get-tuple-element.34), channel_id=1, source_target_pairs={{0,2},{1,3},{2,0},{3,1},{4,6},{5,7},{6,4},{7,5},{8,10},{9,11},{10,... | collective-permute-start | bytes 196616 | tf_op jit(solution)/shard_map/ppermute | solution.py:54
  90.0 5.5 %collective-permute-start.10 = (f32[16,1024]{1,0:T(8,128)S(1)}, f32[16,1024]{1,0:T(8,128)S(1)}, u32[]{:S(2)}, u32[]{:S(2)}) collective-permute-start(f32[16,1024]{1,0:T(8,128)S(1)} %get-tuple-element.33), channel_id=1, source_target_pairs={{0,3},{1,2},{2,1},{3,0},{4,7},{5,6},{6,5},{7,4},{8,11},{9,10},{10,... | collective-permute-start | bytes 196616 | tf_op jit(solution)/shard_map/ppermute | solution.py:54
  90.5 56.2 %copy-start.10 = (f32[4,16,128]{2,1,0:T(8,128)S(1)}, f32[4,16,128]{2,1,0:T(8,128)}, u32[]{:S(2)}) copy-start(f32[4,16,128]{2,1,0:T(8,128)} %copy-done.9) | copy-start | bytes 98308
  95.6 1.6 collective-permute-start.11
  125.2 1.3 collective-permute-start.12
  126.7 20.0 %copy-start.13 = (f32[4,16,128]{2,1,0:T(8,128)}, f32[4,16,128]{2,1,0:T(8,128)S(1)}, u32[]{:S(2)}) copy-start(f32[4,16,128]{2,1,0:T(8,128)S(1)} %get-tuple-element.15) | copy-start | bytes 98308
  126.7 20.0 %copy-start.14 = (f32[4,16,128]{2,1,0:T(8,128)}, f32[4,16,128]{2,1,0:T(8,128)S(1)}, u32[]{:S(2)}) copy-start(f32[4,16,128]{2,1,0:T(8,128)S(1)} %get-tuple-element.16) | copy-start | bytes 98308
  148.7 39.3 %copy-start.2 = (bf16[1024,1024]{1,0:T(8,128)(2,1)S(1)}, bf16[1024,1024]{1,0:T(8,128)(2,1)}, u32[]{:S(2)}) copy-start(bf16[1024,1024]{1,0:T(8,128)(2,1)} %all-reduce.2.cloned.1.call-done) | copy-start | bytes 6291460
  148.9 1.4 collective-permute-start.13
  184.9 2.2 collective-permute-start.14
  188.0 33.3 %copy-start.8 = (f32[8,16,128]{2,1,0:T(8,128)}, f32[8,16,128]{2,1,0:T(8,128)S(1)}, u32[]{:S(2)}) copy-start(f32[8,16,128]{2,1,0:T(8,128)S(1)} %get-tuple-element.29) | copy-start | bytes 196612
  188.0 31.9 %copy-start.17 = (f32[8,2,4,128]{3,0,2,1:T(8,128)S(1)}, f32[8,2,4,128]{3,0,2,1:T(8,128)}, u32[]{:S(2)}) copy-start(f32[8,2,4,128]{3,0,2,1:T(8,128)} %get-tuple-element.22) | copy-start | bytes 98308
  188.6 1.6 collective-permute-start.15
  219.9 1.3 collective-permute-start.16
  221.9 1.4 collective-permute-start.17
  252.9 2.2 collective-permute-start.18
  256.1 31.8 %copy-start.16 = (f32[8,2,4,128]{3,0,2,1:T(8,128)S(1)}, f32[8,2,4,128]{3,0,2,1:T(8,128)}, u32[]{:S(2)}) copy-start(f32[8,2,4,128]{3,0,2,1:T(8,128)} %get-tuple-element.24) | copy-start | bytes 98308
  256.6 1.6 collective-permute-start.19
  287.9 1.3 collective-permute-start.20
  289.9 40.3 %copy-start.5 = (bf16[384,1024]{1,0:T(8,128)(2,1)S(1)}, bf16[384,1024]{1,0:T(8,128)(2,1)}, u32[]{:S(2)}) copy-start(bf16[384,1024]{1,0:T(8,128)(2,1)} %copy-done.4) | copy-start | bytes 2359300
  289.9 1.4 collective-permute-start.21
  291.4 30.6 %copy-start.12 = (f32[4,16,128]{2,1,0:T(8,128)S(1)}, f32[4,16,128]{2,1,0:T(8,128)}, u32[]{:S(2)}) copy-start(f32[4,16,128]{2,1,0:T(8,128)} %copy-done.11) | copy-start | bytes 98308
  306.2 14.3 %all-to-all-start.14 = ((bf16[32,16,128]{2,1,0:T(8,128)(2,1)}), bf16[32,16,128]{2,1,0:T(8,128)(2,1)S(1)}, u32[]{:S(2)}, u32[]{:S(2)}) async-start(bf16[32,16,128]{2,1,0:T(8,128)(2,1)} %broadcast_in_dim.312), calls=%async_computation.14 | async-start | bytes 262144 | tf_op jit(solution)/shard_map/all_to_all | solution.py:42
  320.5 1.3 collective-permute-start.22
  322.1 4.9 %collective-permute-start.23 = (bf16[16,1024]{1,0:T(8,128)(2,1)S(1)}, bf16[16,1024]{1,0:T(8,128)(2,1)S(1)}, u32[]{:S(2)}, u32[]{:S(2)}) collective-permute-start(bf16[16,1024]{1,0:T(8,128)(2,1)S(1)} %copy_bitcast_fusion), channel_id=1, source_target_pairs={{0,1},{1,0},{2,3},{3,2},{4,5},{5,4},{6,7},{7,6},{8,9},{9,8},{10,11... | collective-permute-start | bytes 98312 | tf_op jit(solution)/shard_map/ppermute | solution.py:54
  322.4 5.4 %collective-permute-start.24 = (bf16[16,1024]{1,0:T(8,128)(2,1)S(1)}, bf16[16,1024]{1,0:T(8,128)(2,1)S(1)}, u32[]{:S(2)}, u32[]{:S(2)}) collective-permute-start(bf16[16,1024]{1,0:T(8,128)(2,1)S(1)} %copy_bitcast_fusion), channel_id=1, source_target_pairs={{0,2},{1,3},{2,0},{3,1},{4,6},{5,7},{6,4},{7,5},{8,10},{9,11},{10,... | collective-permute-start | bytes 98312 | tf_op jit(solution)/shard_map/ppermute | solution.py:54
  324.4 5.1 %collective-permute-start.25 = (bf16[16,1024]{1,0:T(8,128)(2,1)S(1)}, bf16[16,1024]{1,0:T(8,128)(2,1)S(1)}, u32[]{:S(2)}, u32[]{:S(2)}) collective-permute-start(bf16[16,1024]{1,0:T(8,128)(2,1)S(1)} %copy_bitcast_fusion), channel_id=1, source_target_pairs={{0,3},{1,2},{2,1},{3,0},{4,7},{5,6},{6,5},{7,4},{8,11},{9,10},{10,... | collective-permute-start | bytes 98312 | tf_op jit(solution)/shard_map/ppermute | solution.py:54
  (4 other events, 7.6 us)
Sparse Core Ops, SparseCore 0:
  9.2 45.0 all-gather.2
  87.2 59.5 all-reduce.1

commit v13 on v10

--- a/solution.py
+++ b/solution.py
@@ -41,11 +41,7 @@
     spread = jnp.broadcast_to(total, (chips,) + tile_shape)
     gathered = lax.all_to_all(spread, "zx", 0, 0, tiled=True).reshape(mine.shape)
     other = lax.ppermute(gathered, "core", swap)
-    return jnp.where(
-        core == 0,
-        jnp.concatenate([gathered, other]),
-        jnp.concatenate([other, gathered]),
-    )
+    return jnp.concatenate([gathered, other])
 
 
 def from_partners(value_for, subs):
@@ -157,6 +153,14 @@
         weights = jnp.sum(
             jnp.where(match[:, :, None, None, None, None], trans_tiles[:, None], 0.0), axis=0
         )
+        weight_halves = weights.reshape((CORES, members // CORES) + weights.shape[1:])
+        core = lax.axis_index("core")
+        weights = jnp.concatenate(
+            [
+                lax.dynamic_index_in_dim(weight_halves, core, 0, keepdims=False),
+                lax.dynamic_index_in_dim(weight_halves, 1 - core, 0, keepdims=False),
+            ]
+        )
         real_weight = weights[:, 0]
         imag_weight = weights[:, 1]
         real_part = slots[:, :half_samples]

time: 341 us -> 344 us (level)
  blocking collectives: 175 us -> 148 us
  waiting for transfers between devices: 61.6 us -> 81.7 us
  starting transfers between devices: 42.5 us -> 51.7 us
    all_to_all x6 -> x4, blocking collectives: 82.2 us -> 54.8 us  [share_slots(): lax.all_to_all(spread, 'zx', 0, 0, tiled=True).reshape(mine.shape)]
    all_to_all x1 -> x3, waiting for transfers between devices: 8.66 us -> 24.3 us  [share_slots(): lax.all_to_all(spread, 'zx', 0, 0, tiled=True).reshape(mine.shape)]
    all_to_all x1 -> x3, starting transfers between devices: 5.45 us -> 15.3 us  [share_slots(): lax.all_to_all(spread, 'zx', 0, 0, tiled=True).reshape(mine.shape)]
  transfers between devices with their start and end apart: 31 -> 33, of which waited for: 23 -> 27; matrix products, arithmetic and copies ran while one was open for 4% -> 4% of each run, Pallas kernels for 0% -> 0%
where the time goes in v13:
time: 344 us; the launch traced here: 342 us
  blocking collectives  148 us (43%)
  waiting for transfers between devices  81.7 us (24%)
  starting transfers between devices  51.7 us (15%)
  between operations  24.4 us (7%)
  local copies, waits for them, and re-layouts  12.5 us (4%)
  matrix products  12.3 us (4%)
  other arithmetic  12 us (3%)
    all_to_all x6, blocking collectives, share_slots(): lax.all_to_all(mine.reshape((chips,) + tile_shape), 'zx', 0, 0, tiled=True)  92.8 us
    all_to_all x4, blocking collectives, share_slots(): lax.all_to_all(spread, 'zx', 0, 0, tiled=True).reshape(mine.shape)  54.8 us
    all_to_all x3, waiting for transfers between devices, share_slots(): lax.all_to_all(spread, 'zx', 0, 0, tiled=True).reshape(mine.shape)  24.3 us
    psum x1, waiting for transfers between devices, local(): coupling = lax.psum(partial_map, 'sub')  19.7 us
    ppermute x12, starting transfers between devices, from_partners(): lax.ppermute(value_for(hop), 'sub', [(i, i ^ hop) for i in range(subs)])  19.1 us
    all_to_all x3, starting transfers between devices, share_slots(): lax.all_to_all(spread, 'zx', 0, 0, tiled=True).reshape(mine.shape)  15.3 us
    ppermute x12, waiting for transfers between devices, from_partners(): lax.ppermute(value_for(hop), 'sub', [(i, i ^ hop) for i in range(subs)])  12.3 us
    all_to_all x1, starting transfers between devices, share_slots(): lax.all_to_all(mine.reshape((chips,) + tile_shape), 'zx', 0, 0, tiled=True)  11.3 us
  transfers between devices with their start and end apart: 33, of which 27 were waited for; matrix products, arithmetic and copies ran while one was open for 4% of the time, Pallas kernels for 0%

profile of v13, /device:TPU:32, one launch (start us, length us, event | category | flops | bytes accessed | tf_op | source)
XLA Modules:
  0.0 342.2 jit_solution(6576554105979092279)
XLA Ops:
  7.3 1.5 broadcast_in_dim.283
  8.8 4.5 %all-to-all-start = ((bf16[4,384,64]{1,2,0:T(8,128)(2,1)}), bf16[4,384,64]{1,2,0:T(8,128)(2,1)S(1)}, u32[]{:S(2)}, u32[]{:S(2)}) async-start(bf16[4,384,64]{1,2,0:T(8,128)(2,1)} %broadcast_in_dim.283), calls=%async_computation | async-start | bytes 393216 | tf_op jit(solution)/shard_map/all_to_all | solution.py:62
  18.2 1.3 all-to-all-done
  21.3 2.7 collective-permute-start.1
  24.0 1.3 collective-permute-start.2
  26.8 2.8 collective-permute-done.2
  29.9 1.3 collective-permute-done.3
  31.8 11.3 %all-to-all-start.1 = ((bf16[32,16,128]{2,1,0:T(8,128)(2,1)}), bf16[32,16,128]{2,1,0:T(8,128)(2,1)S(1)}, u32[]{:S(2)}, u32[]{:S(2)}) async-start(bf16[32,16,128]{2,1,0:T(8,128)(2,1)} %bitcast.24), calls=%async_computation.1 | async-start | bytes 262144 | tf_op jit(solution)/shard_map/all_to_all | solution.py:39
  47.9 5.2 %all-to-all-done.1 = bf16[32,16,128]{2,1,0:T(8,128)(2,1)S(1)} async-done(((bf16[32,16,128]{2,1,0:T(8,128)(2,1)}), bf16[32,16,128]{2,1,0:T(8,128)(2,1)S(1)}, u32[]{:S(2)}, u32[]{:S(2)}) %all-to-all-start.1) | async-done | bytes 131104 | tf_op jit(solution)/shard_map/all_to_all | solution.py:39
  53.8 4.7 %all-to-all-start.2 = ((bf16[32,16,128]{2,1,0:T(8,128)(2,1)}), bf16[32,16,128]{2,1,0:T(8,128)(2,1)S(1)}, u32[]{:S(2)}, u32[]{:S(2)}) async-start(bf16[32,16,128]{2,1,0:T(8,128)(2,1)} %broadcast_in_dim.291), calls=%async_computation.2 | async-start | bytes 262144 | tf_op jit(solution)/shard_map/all_to_all | solution.py:42
  59.4 8.7 %all-to-all-done.2 = bf16[32,16,128]{2,1,0:T(8,128)(2,1)S(1)} async-done(((bf16[32,16,128]{2,1,0:T(8,128)(2,1)}), bf16[32,16,128]{2,1,0:T(8,128)(2,1)S(1)}, u32[]{:S(2)}, u32[]{:S(2)}) %all-to-all-start.2) | async-done | bytes 131104 | tf_op jit(solution)/shard_map/all_to_all | solution.py:42
  68.1 1.3 collective-permute-done.4
  69.7 2.9 collective-permute-start.6
  72.6 1.8 collective-permute-start.7
  75.6 2.1 collective-permute-done.7
  78.9 3.3 fusion.4
  83.2 1.3 convolution_convert_fusion
  84.5 2.2 fusion.2
  88.6 3.3 collective-permute-start.9
  91.8 1.4 collective-permute-start.10
  93.3 1.5 collective-permute-done.9
  94.9 2.4 collective-permute-done.10
  97.8 1.3 collective-permute-done.11
  99.1 14.2 %all_to_all.75 = bf16[32,16,128]{2,1,0:T(8,128)(2,1)S(1)} all-to-all(bf16[32,16,128]{2,1,0:T(8,128)(2,1)S(1)} %bitcast.305), channel_id=1, replica_groups=mesh['zx'=32,'core'=2,'sub'=4] {'zx'}, dimensions={0} | all-to-all | bytes 262144 | tf_op jit(solution)/shard_map/all_to_all | solution.py:39
  113.4 13.7 %all_to_all.76 = bf16[32,16,128]{2,1,0:T(8,128)(2,1)S(1)} all-to-all(bf16[32,16,128]{2,1,0:T(8,128)(2,1)S(1)} %broadcast_in_dim.295), channel_id=1, replica_groups=mesh['zx'=32,'core'=2,'sub'=4] {'zx'}, dimensions={0} | all-to-all | bytes 262144 | tf_op jit(solution)/shard_map/all_to_all | solution.py:42
  127.1 1.3 collective-permute-done.12
  128.6 19.7 %all-reduce.2.cloned.1.call-done = bf16[1024,1024]{1,0:T(8,128)(2,1)} async-done(((bf16[1024,1024]{1,0:T(8,128)(2,1)}), bf16[1024,1024]{1,0:T(8,128)(2,1)}) %all-reduce.2.cloned.1.call-update) | async-done | bytes 2097168 | tf_op jit(solution)/shard_map/psum | solution.py:107
  148.3 2.0 fusion.20
  150.5 1.3 collective-permute-done.13
  151.9 19.9 %all_to_all.77 = bf16[32,16,128]{2,1,0:T(8,128)(2,1)} all-to-all(bf16[32,16,128]{2,1,0:T(8,128)(2,1)S(1)} %bitcast.306), channel_id=1, replica_groups=mesh['zx'=32,'core'=2,'sub'=4] {'zx'}, dimensions={0} | all-to-all | bytes 262144 | tf_op jit(solution)/shard_map/all_to_all | solution.py:39
  173.3 5.3 %all-to-all-start.6 = ((bf16[32,16,128]{2,1,0:T(8,128)(2,1)}), bf16[32,16,128]{2,1,0:T(8,128)(2,1)}, u32[]{:S(2)}, u32[]{:S(2)}) async-start(bf16[32,16,128]{2,1,0:T(8,128)(2,1)} %broadcast_in_dim.299), calls=%async_computation.6 | async-start | bytes 262144 | tf_op jit(solution)/shard_map/all_to_all | solution.py:42
  180.5 7.8 %all-to-all-done.6 = bf16[32,16,128]{2,1,0:T(8,128)(2,1)} async-done(((bf16[32,16,128]{2,1,0:T(8,128)(2,1)}), bf16[32,16,128]{2,1,0:T(8,128)(2,1)}, u32[]{:S(2)}, u32[]{:S(2)}) %all-to-all-start.6) | async-done | bytes 131104 | tf_op jit(solution)/shard_map/all_to_all | solution.py:42
  188.4 1.5 collective-permute-done.14
  193.8 14.9 %all_to_all.78 = bf16[32,16,128]{2,1,0:T(8,128)(2,1)} all-to-all(bf16[32,16,128]{2,1,0:T(8,128)(2,1)S(1)} %bitcast.307), channel_id=1, replica_groups=mesh['zx'=32,'core'=2,'sub'=4] {'zx'}, dimensions={0} | all-to-all | bytes 262144 | tf_op jit(solution)/shard_map/all_to_all | solution.py:39
  209.6 13.7 %all_to_all.79 = bf16[32,16,128]{2,1,0:T(8,128)(2,1)S(1)} all-to-all(bf16[32,16,128]{2,1,0:T(8,128)(2,1)S(1)} %broadcast_in_dim.303), channel_id=1, replica_groups=mesh['zx'=32,'core'=2,'sub'=4] {'zx'}, dimensions={0} | all-to-all | bytes 262144 | tf_op jit(solution)/shard_map/all_to_all | solution.py:42
  223.4 1.3 collective-permute-done.16
  226.8 14.8 %all_to_all.80 = bf16[32,16,128]{2,1,0:T(8,128)(2,1)} all-to-all(bf16[32,16,128]{2,1,0:T(8,128)(2,1)S(1)} %bitcast.308), channel_id=1, replica_groups=mesh['zx'=32,'core'=2,'sub'=4] {'zx'}, dimensions={0} | all-to-all | bytes 262144 | tf_op jit(solution)/shard_map/all_to_all | solution.py:39
  243.3 5.3 %all-to-all-start.10 = ((bf16[32,16,128]{2,1,0:T(8,128)(2,1)}), bf16[32,16,128]{2,1,0:T(8,128)(2,1)}, u32[]{:S(2)}, u32[]{:S(2)}) async-start(bf16[32,16,128]{2,1,0:T(8,128)(2,1)} %broadcast_in_dim.307), calls=%async_computation.10 | async-start | bytes 262144 | tf_op jit(solution)/shard_map/all_to_all | solution.py:42
  250.5 7.8 %all-to-all-done.10 = bf16[32,16,128]{2,1,0:T(8,128)(2,1)} async-done(((bf16[32,16,128]{2,1,0:T(8,128)(2,1)}), bf16[32,16,128]{2,1,0:T(8,128)(2,1)}, u32[]{:S(2)}, u32[]{:S(2)}) %all-to-all-start.10) | async-done | bytes 131104 | tf_op jit(solution)/shard_map/all_to_all | solution.py:42
  258.4 1.5 collective-permute-done.18
  263.8 14.9 %all_to_all.81 = bf16[32,16,128]{2,1,0:T(8,128)(2,1)} all-to-all(bf16[32,16,128]{2,1,0:T(8,128)(2,1)S(1)} %bitcast.309), channel_id=1, replica_groups=mesh['zx'=32,'core'=2,'sub'=4] {'zx'}, dimensions={0} | all-to-all | bytes 262144 | tf_op jit(solution)/shard_map/all_to_all | solution.py:39
  279.6 13.7 %all_to_all.82 = bf16[32,16,128]{2,1,0:T(8,128)(2,1)S(1)} all-to-all(bf16[32,16,128]{2,1,0:T(8,128)(2,1)S(1)} %broadcast_in_dim.311), channel_id=1, replica_groups=mesh['zx'=32,'core'=2,'sub'=4] {'zx'}, dimensions={0} | all-to-all | bytes 262144 | tf_op jit(solution)/shard_map/all_to_all | solution.py:42
  293.3 1.3 collective-permute-done.20
  296.8 14.1 %all_to_all.83 = bf16[32,16,128]{2,1,0:T(8,128)(2,1)S(1)} all-to-all(bf16[32,16,128]{2,1,0:T(8,128)(2,1)S(1)} %bitcast.310), channel_id=1, replica_groups=mesh['zx'=32,'core'=2,'sub'=4] {'zx'}, dimensions={0} | all-to-all | bytes 262144 | tf_op jit(solution)/shard_map/all_to_all | solution.py:39
  311.0 13.7 %all_to_all.84 = bf16[32,16,128]{2,1,0:T(8,128)(2,1)S(1)} all-to-all(bf16[32,16,128]{2,1,0:T(8,128)(2,1)S(1)} %broadcast_in_dim.315), channel_id=1, replica_groups=mesh['zx'=32,'core'=2,'sub'=4] {'zx'}, dimensions={0} | all-to-all | bytes 262144 | tf_op jit(solution)/shard_map/all_to_all | solution.py:42
  326.6 2.0 collective-permute-start.24
  328.6 2.4 collective-permute-start.25
  332.0 1.7 collective-permute-done.25
  (214 shorter events, 37.8 us)
Async XLA Ops:
  6.5 13.1 %copy-start = (bf16[1,384,1536]{2,1,0:T(8,128)(2,1)S(1)}, bf16[1,384,1536]{2,1,0:T(8,128)(2,1)}, u32[]{:S(2)}) copy-start(bf16[1,384,1536]{2,1,0:T(8,128)(2,1)} %param.9) | copy-start | bytes 3538948
  6.5 13.6 %copy-start.6 = (bf16[1,1024,384]{2,1,0:T(8,128)(2,1)S(1)}, bf16[1,1024,384]{2,1,0:T(8,128)(2,1)}, u32[]{:S(2)}) copy-start(bf16[1,1024,384]{2,1,0:T(8,128)(2,1)} %param.10) | copy-start | bytes 2359300
  6.5 72.4 %all-gather.3.cloned.1.call-start = ((), (), s32[]{:S(2)}) async-start(), calls=%async_computation.16 | async-start | bytes 3932160 | tf_op jit(solution)/shard_map/all_gather | solution.py:102
  7.3 18.1 %copy-start.1 = (s32[64]{0:T(128)S(1)}, s32[64]{0:T(128)}, u32[]{:S(2)}) copy-start(s32[64]{0:T(128)} %param.15) | copy-start | bytes 772
  8.8 10.8 %all-to-all-start = ((bf16[4,384,64]{1,2,0:T(8,128)(2,1)}), bf16[4,384,64]{1,2,0:T(8,128)(2,1)S(1)}, u32[]{:S(2)}, u32[]{:S(2)}) async-start(bf16[4,384,64]{1,2,0:T(8,128)(2,1)} %broadcast_in_dim.283), calls=%async_computation | async-start | bytes 393216 | tf_op jit(solution)/shard_map/all_to_all | solution.py:62
  20.1 38.4 %copy-start.19 = (f32[1,6,2,512]{3,2,1,0:T(2,128)S(1)}, f32[1,6,2,512]{3,2,1,0:T(2,128)}, u32[]{:S(2)}) copy-start(f32[1,6,2,512]{3,2,1,0:T(2,128)} %param.12) | copy-start | bytes 73732
  20.5 5.4 %collective-permute-start = (bf16[16,1024]{1,0:T(8,128)(2,1)S(1)}, bf16[16,1024]{1,0:T(8,128)(2,1)S(1)}, u32[]{:S(2)}, u32[]{:S(2)}) collective-permute-start(bf16[16,1024]{1,0:T(8,128)(2,1)S(1)} %get-tuple-element.39), channel_id=1, source_target_pairs={{0,1},{1,0},{2,3},{3,2},{4,5},{5,4},{6,7},{7,6},{8,9},{9,8},{10,11... | collective-permute-start | bytes 98312 | tf_op jit(solution)/shard_map/ppermute | solution.py:50
  21.3 5.4 %collective-permute-start.1 = (bf16[16,1024]{1,0:T(8,128)(2,1)S(1)}, bf16[16,1024]{1,0:T(8,128)(2,1)S(1)}, u32[]{:S(2)}, u32[]{:S(2)}) collective-permute-start(bf16[16,1024]{1,0:T(8,128)(2,1)S(1)} %get-tuple-element.38), channel_id=1, source_target_pairs={{0,2},{1,3},{2,0},{3,1},{4,6},{5,7},{6,4},{7,5},{8,10},{9,11},{10,... | collective-permute-start | bytes 98312 | tf_op jit(solution)/shard_map/ppermute | solution.py:50
  24.0 5.5 %collective-permute-start.2 = (bf16[16,1024]{1,0:T(8,128)(2,1)S(1)}, bf16[16,1024]{1,0:T(8,128)(2,1)S(1)}, u32[]{:S(2)}, u32[]{:S(2)}) collective-permute-start(bf16[16,1024]{1,0:T(8,128)(2,1)S(1)} %get-tuple-element.37), channel_id=1, source_target_pairs={{0,3},{1,2},{2,1},{3,0},{4,7},{5,6},{6,5},{7,4},{8,11},{9,10},{10,... | collective-permute-start | bytes 98312 | tf_op jit(solution)/shard_map/ppermute | solution.py:50
  29.7 1.4 collective-permute-start.3
  31.8 21.2 %all-to-all-start.1 = ((bf16[32,16,128]{2,1,0:T(8,128)(2,1)}), bf16[32,16,128]{2,1,0:T(8,128)(2,1)S(1)}, u32[]{:S(2)}, u32[]{:S(2)}) async-start(bf16[32,16,128]{2,1,0:T(8,128)(2,1)} %bitcast.24), calls=%async_computation.1 | async-start | bytes 262144 | tf_op jit(solution)/shard_map/all_to_all | solution.py:39
  53.8 14.3 %all-to-all-start.2 = ((bf16[32,16,128]{2,1,0:T(8,128)(2,1)}), bf16[32,16,128]{2,1,0:T(8,128)(2,1)S(1)}, u32[]{:S(2)}, u32[]{:S(2)}) async-start(bf16[32,16,128]{2,1,0:T(8,128)(2,1)} %broadcast_in_dim.291), calls=%async_computation.2 | async-start | bytes 262144 | tf_op jit(solution)/shard_map/all_to_all | solution.py:42
  68.1 1.3 collective-permute-start.4
  69.6 9.4 %copy-start.11 = (f32[4,16,128]{2,1,0:T(8,128)}, f32[4,16,128]{2,1,0:T(8,128)S(1)}, u32[]{:S(2)}) copy-start(f32[4,16,128]{2,1,0:T(8,128)S(1)} %get-tuple-element.18) | copy-start | bytes 98308
  69.6 6.0 %collective-permute-start.5 = (bf16[16,1024]{1,0:T(8,128)(2,1)S(1)}, bf16[16,1024]{1,0:T(8,128)(2,1)S(1)}, u32[]{:S(2)}, u32[]{:S(2)}) collective-permute-start(bf16[16,1024]{1,0:T(8,128)(2,1)S(1)} %bitcast.354), channel_id=1, source_target_pairs={{0,1},{1,0},{2,3},{3,2},{4,5},{5,4},{6,7},{7,6},{8,9},{9,8},{10,11... | collective-permute-start | bytes 98312 | tf_op jit(solution)/shard_map/ppermute | solution.py:50
  69.7 5.9 %collective-permute-start.6 = (bf16[16,1024]{1,0:T(8,128)(2,1)S(1)}, bf16[16,1024]{1,0:T(8,128)(2,1)S(1)}, u32[]{:S(2)}, u32[]{:S(2)}) collective-permute-start(bf16[16,1024]{1,0:T(8,128)(2,1)S(1)} %bitcast.355), channel_id=1, source_target_pairs={{0,2},{1,3},{2,0},{3,1},{4,6},{5,7},{6,4},{7,5},{8,10},{9,11},{10,... | collective-permute-start | bytes 98312 | tf_op jit(solution)/shard_map/ppermute | solution.py:50
  72.6 5.1 %collective-permute-start.7 = (bf16[16,1024]{1,0:T(8,128)(2,1)S(1)}, bf16[16,1024]{1,0:T(8,128)(2,1)S(1)}, u32[]{:S(2)}, u32[]{:S(2)}) collective-permute-start(bf16[16,1024]{1,0:T(8,128)(2,1)S(1)} %bitcast.356), channel_id=1, source_target_pairs={{0,3},{1,2},{2,1},{3,0},{4,7},{5,6},{6,5},{7,4},{8,11},{9,10},{10,... | collective-permute-start | bytes 98312 | tf_op jit(solution)/shard_map/ppermute | solution.py:50
  86.7 61.5 %all-reduce.2.cloned.1.call-start = ((), (), s32[]{:S(2)}) async-start(), calls=%async_computation.15 | async-start | bytes 4194304 | tf_op jit(solution)/shard_map/psum | solution.py:107
  87.5 39.6 %copy-start.18 = (f32[8,2,4,128]{3,0,2,1:T(8,128)S(1)}, f32[8,2,4,128]{3,0,2,1:T(8,128)}, u32[]{:S(2)}) copy-start(f32[8,2,4,128]{3,0,2,1:T(8,128)} %get-tuple-element.20) | copy-start | bytes 98308
  88.5 4.8 %collective-permute-start.8 = (f32[16,1024]{1,0:T(8,128)S(1)}, f32[16,1024]{1,0:T(8,128)S(1)}, u32[]{:S(2)}, u32[]{:S(2)}) collective-permute-start(f32[16,1024]{1,0:T(8,128)S(1)} %get-tuple-element.35), channel_id=1, source_target_pairs={{0,1},{1,0},{2,3},{3,2},{4,5},{5,4},{6,7},{7,6},{8,9},{9,8},{10,11... | collective-permute-start | bytes 196616 | tf_op jit(solution)/shard_map/ppermute | solution.py:50
  88.6 6.3 %collective-permute-start.9 = (f32[16,1024]{1,0:T(8,128)S(1)}, f32[16,1024]{1,0:T(8,128)S(1)}, u32[]{:S(2)}, u32[]{:S(2)}) collective-permute-start(f32[16,1024]{1,0:T(8,128)S(1)} %get-tuple-element.34), channel_id=1, source_target_pairs={{0,2},{1,3},{2,0},{3,1},{4,6},{5,7},{6,4},{7,5},{8,10},{9,11},{10,... | collective-permute-start | bytes 196616 | tf_op jit(solution)/shard_map/ppermute | solution.py:50
  91.8 5.5 %collective-permute-start.10 = (f32[16,1024]{1,0:T(8,128)S(1)}, f32[16,1024]{1,0:T(8,128)S(1)}, u32[]{:S(2)}, u32[]{:S(2)}) collective-permute-start(f32[16,1024]{1,0:T(8,128)S(1)} %get-tuple-element.33), channel_id=1, source_target_pairs={{0,3},{1,2},{2,1},{3,0},{4,7},{5,6},{6,5},{7,4},{8,11},{9,10},{10,... | collective-permute-start | bytes 196616 | tf_op jit(solution)/shard_map/ppermute | solution.py:50
  93.3 55.0 %copy-start.12 = (f32[4,16,128]{2,1,0:T(8,128)S(1)}, f32[4,16,128]{2,1,0:T(8,128)}, u32[]{:S(2)}) copy-start(f32[4,16,128]{2,1,0:T(8,128)} %copy-done.11) | copy-start | bytes 98308
  97.5 1.6 collective-permute-start.11
  127.1 1.3 collective-permute-start.12
  128.5 19.7 %copy-start.13 = (f32[4,16,128]{2,1,0:T(8,128)}, f32[4,16,128]{2,1,0:T(8,128)S(1)}, u32[]{:S(2)}) copy-start(f32[4,16,128]{2,1,0:T(8,128)S(1)} %get-tuple-element.15) | copy-start | bytes 98308
  128.5 19.7 %copy-start.14 = (f32[4,16,128]{2,1,0:T(8,128)}, f32[4,16,128]{2,1,0:T(8,128)S(1)}, u32[]{:S(2)}) copy-start(f32[4,16,128]{2,1,0:T(8,128)S(1)} %get-tuple-element.16) | copy-start | bytes 98308
  150.3 41.5 %copy-start.2 = (bf16[1024,1024]{1,0:T(8,128)(2,1)S(1)}, bf16[1024,1024]{1,0:T(8,128)(2,1)}, u32[]{:S(2)}) copy-start(bf16[1024,1024]{1,0:T(8,128)(2,1)} %all-reduce.2.cloned.1.call-done) | copy-start | bytes 6291460
  150.4 1.4 collective-permute-start.13
  173.3 15.0 %all-to-all-start.6 = ((bf16[32,16,128]{2,1,0:T(8,128)(2,1)}), bf16[32,16,128]{2,1,0:T(8,128)(2,1)}, u32[]{:S(2)}, u32[]{:S(2)}) async-start(bf16[32,16,128]{2,1,0:T(8,128)(2,1)} %broadcast_in_dim.299), calls=%async_computation.6 | async-start | bytes 262144 | tf_op jit(solution)/shard_map/all_to_all | solution.py:42
  188.3 1.6 collective-permute-start.14
  191.7 33.1 %copy-start.8 = (f32[8,16,128]{2,1,0:T(8,128)}, f32[8,16,128]{2,1,0:T(8,128)S(1)}, u32[]{:S(2)}) copy-start(f32[8,16,128]{2,1,0:T(8,128)S(1)} %get-tuple-element.29) | copy-start | bytes 196612
  191.8 31.6 %copy-start.17 = (f32[8,2,4,128]{3,0,2,1:T(8,128)S(1)}, f32[8,2,4,128]{3,0,2,1:T(8,128)}, u32[]{:S(2)}) copy-start(f32[8,2,4,128]{3,0,2,1:T(8,128)} %get-tuple-element.22) | copy-start | bytes 98308
  192.3 1.4 collective-permute-start.15
  223.3 1.3 collective-permute-start.16
  225.4 1.4 collective-permute-start.17
  243.3 15.0 %all-to-all-start.10 = ((bf16[32,16,128]{2,1,0:T(8,128)(2,1)}), bf16[32,16,128]{2,1,0:T(8,128)(2,1)}, u32[]{:S(2)}, u32[]{:S(2)}) async-start(bf16[32,16,128]{2,1,0:T(8,128)(2,1)} %broadcast_in_dim.307), calls=%async_computation.10 | async-start | bytes 262144 | tf_op jit(solution)/shard_map/all_to_all | solution.py:42
  258.3 1.6 collective-permute-start.18
  261.8 31.5 %copy-start.16 = (f32[8,2,4,128]{3,0,2,1:T(8,128)S(1)}, f32[8,2,4,128]{3,0,2,1:T(8,128)}, u32[]{:S(2)}) copy-start(f32[8,2,4,128]{3,0,2,1:T(8,128)} %get-tuple-element.24) | copy-start | bytes 98308
  262.3 1.4 collective-permute-start.19
  293.3 1.3 collective-permute-start.20
  295.3 39.0 %copy-start.5 = (bf16[384,1024]{1,0:T(8,128)(2,1)S(1)}, bf16[384,1024]{1,0:T(8,128)(2,1)}, u32[]{:S(2)}) copy-start(bf16[384,1024]{1,0:T(8,128)(2,1)} %copy-done.4) | copy-start | bytes 2359300
  295.3 1.4 collective-permute-start.21
  296.8 29.4 %copy-start.10 = (f32[4,16,128]{2,1,0:T(8,128)S(1)}, f32[4,16,128]{2,1,0:T(8,128)}, u32[]{:S(2)}) copy-start(f32[4,16,128]{2,1,0:T(8,128)} %copy-done.9) | copy-start | bytes 98308
  324.7 1.3 collective-permute-start.22
  326.2 4.9 %collective-permute-start.23 = (bf16[16,1024]{1,0:T(8,128)(2,1)S(1)}, bf16[16,1024]{1,0:T(8,128)(2,1)S(1)}, u32[]{:S(2)}, u32[]{:S(2)}) collective-permute-start(bf16[16,1024]{1,0:T(8,128)(2,1)S(1)} %copy_bitcast_fusion), channel_id=1, source_target_pairs={{0,1},{1,0},{2,3},{3,2},{4,5},{5,4},{6,7},{7,6},{8,9},{9,8},{10,11... | collective-permute-start | bytes 98312 | tf_op jit(solution)/shard_map/ppermute | solution.py:50
  326.6 5.4 %collective-permute-start.24 = (bf16[16,1024]{1,0:T(8,128)(2,1)S(1)}, bf16[16,1024]{1,0:T(8,128)(2,1)S(1)}, u32[]{:S(2)}, u32[]{:S(2)}) collective-permute-start(bf16[16,1024]{1,0:T(8,128)(2,1)S(1)} %copy_bitcast_fusion), channel_id=1, source_target_pairs={{0,2},{1,3},{2,0},{3,1},{4,6},{5,7},{6,4},{7,5},{8,10},{9,11},{10,... | collective-permute-start | bytes 98312 | tf_op jit(solution)/shard_map/ppermute | solution.py:50
  328.6 5.1 %collective-permute-start.25 = (bf16[16,1024]{1,0:T(8,128)(2,1)S(1)}, bf16[16,1024]{1,0:T(8,128)(2,1)S(1)}, u32[]{:S(2)}, u32[]{:S(2)}) collective-permute-start(bf16[16,1024]{1,0:T(8,128)(2,1)S(1)} %copy_bitcast_fusion), channel_id=1, source_target_pairs={{0,3},{1,2},{2,1},{3,0},{4,7},{5,6},{6,5},{7,4},{8,11},{9,10},{10,... | collective-permute-start | bytes 98312 | tf_op jit(solution)/shard_map/ppermute | solution.py:50
  (5 other events, 11.4 us)
Sparse Core Ops, SparseCore 0:
  9.2 45.0 all-gather.2
  89.9 58.2 all-reduce.1

commit v14 on v10

--- a/solution.py
+++ b/solution.py
@@ -130,7 +130,9 @@
             pattern = incident.astype(jnp.bfloat16)
         elif segment_k == 1:
             all_fields = gather_rows(from_tiles(incoming).astype(jnp.bfloat16), subs)
-            products = jnp.dot(all_fields, partial_map, preferred_element_type=jnp.float32)
+            products = jnp.dot(all_fields, partial_map, preferred_element_type=jnp.float32).astype(
+                jnp.bfloat16
+            )
             coupled = scatter_sum(products.reshape((subs, -1) + products.shape[1:]), subs)
             pattern = (incident - coupled).astype(jnp.bfloat16)
         else:

time: 341 us -> 339 us (level)
  transfers between devices with their start and end apart: 31 -> 31, of which waited for: 23 -> 24; matrix products, arithmetic and copies ran while one was open for 4% -> 4% of each run, Pallas kernels for 0% -> 0%
where the time goes in v14:
time: 339 us; the launch traced here: 337 us
  blocking collectives  175 us (52%)
  waiting for transfers between devices  62.5 us (18%)
  starting transfers between devices  41.4 us (12%)
  between operations  24.3 us (7%)
  matrix products  12.3 us (4%)
  local copies, waits for them, and re-layouts  11 us (3%)
  other arithmetic  10.2 us (3%)
    all_to_all x6, blocking collectives, share_slots(): lax.all_to_all(mine.reshape((chips,) + tile_shape), 'zx', 0, 0, tiled=True)  93.3 us
    all_to_all x6, blocking collectives, share_slots(): lax.all_to_all(spread, 'zx', 0, 0, tiled=True).reshape(mine.shape)  82.2 us
    psum x1, waiting for transfers between devices, local(): coupling = lax.psum(partial_map, 'sub')  20.2 us
    ppermute x12, starting transfers between devices, from_partners(): lax.ppermute(value_for(hop), 'sub', [(i, i ^ hop) for i in range(subs)])  19.1 us
    ppermute x12, waiting for transfers between devices, from_partners(): lax.ppermute(value_for(hop), 'sub', [(i, i ^ hop) for i in range(subs)])  12 us
    all_to_all x1, starting transfers between devices, share_slots(): lax.all_to_all(mine.reshape((chips,) + tile_shape), 'zx', 0, 0, tiled=True)  11.3 us
    all_to_all x1, waiting for transfers between devices, share_slots(): lax.all_to_all(spread, 'zx', 0, 0, tiled=True).reshape(mine.shape)  8.76 us
    ppermute x7, waiting for transfers between devices, share_slots(): mine = mine + lax.ppermute(wanted, 'core', swap)  8.36 us
  transfers between devices with their start and end apart: 31, of which 24 were waited for; matrix products, arithmetic and copies ran while one was open for 4% of the time, Pallas kernels for 0%

profile of v14, /device:TPU:32, one launch (start us, length us, event | category | flops | bytes accessed | tf_op | source)
XLA Modules:
  0.0 337.1 jit_solution(10784173534934538943)
XLA Ops:
  7.3 1.5 broadcast_in_dim.283
  8.8 4.5 %all-to-all-start = ((bf16[4,384,64]{1,2,0:T(8,128)(2,1)}), bf16[4,384,64]{1,2,0:T(8,128)(2,1)S(1)}, u32[]{:S(2)}, u32[]{:S(2)}) async-start(bf16[4,384,64]{1,2,0:T(8,128)(2,1)} %broadcast_in_dim.283), calls=%async_computation | async-start | bytes 393216 | tf_op jit(solution)/shard_map/all_to_all | solution.py:66
  14.6 1.2 dynamic_slice.75
  18.2 1.3 all-to-all-done
  21.3 2.7 collective-permute-start.1
  24.0 1.3 collective-permute-start.2
  26.8 2.8 collective-permute-done.2
  29.8 1.3 collective-permute-done.3
  31.8 11.3 %all-to-all-start.1 = ((bf16[32,16,128]{2,1,0:T(8,128)(2,1)}), bf16[32,16,128]{2,1,0:T(8,128)(2,1)S(1)}, u32[]{:S(2)}, u32[]{:S(2)}) async-start(bf16[32,16,128]{2,1,0:T(8,128)(2,1)} %bitcast.22), calls=%async_computation.1 | async-start | bytes 262144 | tf_op jit(solution)/shard_map/all_to_all | solution.py:39
  47.9 5.2 %all-to-all-done.1 = bf16[32,16,128]{2,1,0:T(8,128)(2,1)S(1)} async-done(((bf16[32,16,128]{2,1,0:T(8,128)(2,1)}), bf16[32,16,128]{2,1,0:T(8,128)(2,1)S(1)}, u32[]{:S(2)}, u32[]{:S(2)}) %all-to-all-start.1) | async-done | bytes 131104 | tf_op jit(solution)/shard_map/all_to_all | solution.py:39
  53.8 4.7 %all-to-all-start.2 = ((bf16[32,16,128]{2,1,0:T(8,128)(2,1)}), bf16[32,16,128]{2,1,0:T(8,128)(2,1)S(1)}, u32[]{:S(2)}, u32[]{:S(2)}) async-start(bf16[32,16,128]{2,1,0:T(8,128)(2,1)} %broadcast_in_dim.291), calls=%async_computation.2 | async-start | bytes 262144 | tf_op jit(solution)/shard_map/all_to_all | solution.py:42
  59.3 8.8 %all-to-all-done.2 = bf16[32,16,128]{2,1,0:T(8,128)(2,1)S(1)} async-done(((bf16[32,16,128]{2,1,0:T(8,128)(2,1)}), bf16[32,16,128]{2,1,0:T(8,128)(2,1)S(1)}, u32[]{:S(2)}, u32[]{:S(2)}) %all-to-all-start.2) | async-done | bytes 131104 | tf_op jit(solution)/shard_map/all_to_all | solution.py:42
  68.1 1.3 collective-permute-done.4
  69.7 2.9 collective-permute-start.6
  72.6 1.8 collective-permute-start.7
  75.6 2.1 collective-permute-done.7
  77.7 1.2 gather_fusion.1
  78.9 3.3 fusion.2
  83.2 1.3 convolution_convert_fusion
  84.5 2.2 convolution_convert_fusion.2
  88.4 3.2 collective-permute-start.9
  91.6 1.4 collective-permute-start.10
  94.0 2.8 collective-permute-done.10
  97.0 1.3 collective-permute-done.11
  98.4 14.4 %all_to_all.75 = bf16[32,16,128]{2,1,0:T(8,128)(2,1)S(1)} all-to-all(bf16[32,16,128]{2,1,0:T(8,128)(2,1)S(1)} %bitcast.250), channel_id=1, replica_groups=mesh['zx'=32,'core'=2,'sub'=4] {'zx'}, dimensions={0} | all-to-all | bytes 262144 | tf_op jit(solution)/shard_map/all_to_all | solution.py:39
  112.8 13.7 %all_to_all.76 = bf16[32,16,128]{2,1,0:T(8,128)(2,1)S(1)} all-to-all(bf16[32,16,128]{2,1,0:T(8,128)(2,1)S(1)} %broadcast_in_dim.295), channel_id=1, replica_groups=mesh['zx'=32,'core'=2,'sub'=4] {'zx'}, dimensions={0} | all-to-all | bytes 262144 | tf_op jit(solution)/shard_map/all_to_all | solution.py:42
  126.5 1.3 collective-permute-done.12
  128.0 20.2 %all-reduce.2.cloned.1.call-done = bf16[1024,1024]{1,0:T(8,128)(2,1)} async-done(((bf16[1024,1024]{1,0:T(8,128)(2,1)}), bf16[1024,1024]{1,0:T(8,128)(2,1)}) %all-reduce.2.cloned.1.call-update) | async-done | bytes 2097168 | tf_op jit(solution)/shard_map/psum | solution.py:111
  148.2 2.0 fusion.18
  150.5 1.3 collective-permute-done.13
  151.8 19.9 %all_to_all.77 = bf16[32,16,128]{2,1,0:T(8,128)(2,1)} all-to-all(bf16[32,16,128]{2,1,0:T(8,128)(2,1)S(1)} %bitcast.251), channel_id=1, replica_groups=mesh['zx'=32,'core'=2,'sub'=4] {'zx'}, dimensions={0} | all-to-all | bytes 262144 | tf_op jit(solution)/shard_map/all_to_all | solution.py:39
  172.6 13.7 %all_to_all.78 = bf16[32,16,128]{2,1,0:T(8,128)(2,1)S(1)} all-to-all(bf16[32,16,128]{2,1,0:T(8,128)(2,1)S(1)} %broadcast_in_dim.299), channel_id=1, replica_groups=mesh['zx'=32,'core'=2,'sub'=4] {'zx'}, dimensions={0} | all-to-all | bytes 262144 | tf_op jit(solution)/shard_map/all_to_all | solution.py:42
  189.7 1.0 collective-permute-done.15
  190.7 15.1 %all_to_all.79 = bf16[32,16,128]{2,1,0:T(8,128)(2,1)} all-to-all(bf16[32,16,128]{2,1,0:T(8,128)(2,1)S(1)} %bitcast.252), channel_id=1, replica_groups=mesh['zx'=32,'core'=2,'sub'=4] {'zx'}, dimensions={0} | all-to-all | bytes 262144 | tf_op jit(solution)/shard_map/all_to_all | solution.py:39
  206.7 13.7 %all_to_all.80 = bf16[32,16,128]{2,1,0:T(8,128)(2,1)S(1)} all-to-all(bf16[32,16,128]{2,1,0:T(8,128)(2,1)S(1)} %broadcast_in_dim.303), channel_id=1, replica_groups=mesh['zx'=32,'core'=2,'sub'=4] {'zx'}, dimensions={0} | all-to-all | bytes 262144 | tf_op jit(solution)/shard_map/all_to_all | solution.py:42
  222.7 1.2 collective-permute-done.17
  223.9 14.8 %all_to_all.81 = bf16[32,16,128]{2,1,0:T(8,128)(2,1)} all-to-all(bf16[32,16,128]{2,1,0:T(8,128)(2,1)S(1)} %bitcast.253), channel_id=1, replica_groups=mesh['zx'=32,'core'=2,'sub'=4] {'zx'}, dimensions={0} | all-to-all | bytes 262144 | tf_op jit(solution)/shard_map/all_to_all | solution.py:39
  239.7 13.7 %all_to_all.82 = bf16[32,16,128]{2,1,0:T(8,128)(2,1)S(1)} all-to-all(bf16[32,16,128]{2,1,0:T(8,128)(2,1)S(1)} %broadcast_in_dim.307), channel_id=1, replica_groups=mesh['zx'=32,'core'=2,'sub'=4] {'zx'}, dimensions={0} | all-to-all | bytes 262144 | tf_op jit(solution)/shard_map/all_to_all | solution.py:42
  258.5 15.1 %all_to_all.83 = bf16[32,16,128]{2,1,0:T(8,128)(2,1)} all-to-all(bf16[32,16,128]{2,1,0:T(8,128)(2,1)S(1)} %bitcast.254), channel_id=1, replica_groups=mesh['zx'=32,'core'=2,'sub'=4] {'zx'}, dimensions={0} | all-to-all | bytes 262144 | tf_op jit(solution)/shard_map/all_to_all | solution.py:39
  274.5 13.7 %all_to_all.84 = bf16[32,16,128]{2,1,0:T(8,128)(2,1)S(1)} all-to-all(bf16[32,16,128]{2,1,0:T(8,128)(2,1)S(1)} %broadcast_in_dim.311), channel_id=1, replica_groups=mesh['zx'=32,'core'=2,'sub'=4] {'zx'}, dimensions={0} | all-to-all | bytes 262144 | tf_op jit(solution)/shard_map/all_to_all | solution.py:42
  288.2 1.3 collective-permute-done.20
  290.5 1.2 collective-permute-done.21
  291.7 14.1 %all_to_all.85 = bf16[32,16,128]{2,1,0:T(8,128)(2,1)S(1)} all-to-all(bf16[32,16,128]{2,1,0:T(8,128)(2,1)S(1)} %bitcast.249), channel_id=1, replica_groups=mesh['zx'=32,'core'=2,'sub'=4] {'zx'}, dimensions={0} | all-to-all | bytes 262144 | tf_op jit(solution)/shard_map/all_to_all | solution.py:39
  305.9 13.7 %all_to_all.86 = bf16[32,16,128]{2,1,0:T(8,128)(2,1)S(1)} all-to-all(bf16[32,16,128]{2,1,0:T(8,128)(2,1)S(1)} %broadcast_in_dim.315), channel_id=1, replica_groups=mesh['zx'=32,'core'=2,'sub'=4] {'zx'}, dimensions={0} | all-to-all | bytes 262144 | tf_op jit(solution)/shard_map/all_to_all | solution.py:42
  321.5 2.0 collective-permute-start.24
  323.5 2.4 collective-permute-start.25
  327.0 1.7 collective-permute-done.25
  329.3 1.0 fusion.8
  (203 shorter events, 29.2 us)
Async XLA Ops:
  6.5 13.1 %copy-start = (bf16[1,384,1536]{2,1,0:T(8,128)(2,1)S(1)}, bf16[1,384,1536]{2,1,0:T(8,128)(2,1)}, u32[]{:S(2)}) copy-start(bf16[1,384,1536]{2,1,0:T(8,128)(2,1)} %param.9) | copy-start | bytes 3538948
  6.5 13.6 %copy-start.6 = (bf16[1,1024,384]{2,1,0:T(8,128)(2,1)S(1)}, bf16[1,1024,384]{2,1,0:T(8,128)(2,1)}, u32[]{:S(2)}) copy-start(bf16[1,1024,384]{2,1,0:T(8,128)(2,1)} %param.10) | copy-start | bytes 2359300
  6.5 72.4 %all-gather.3.cloned.1.call-start = ((), (), s32[]{:S(2)}) async-start(), calls=%async_computation.16 | async-start | bytes 3932160 | tf_op jit(solution)/shard_map/all_gather | solution.py:106
  7.3 18.1 %copy-start.1 = (s32[64]{0:T(128)S(1)}, s32[64]{0:T(128)}, u32[]{:S(2)}) copy-start(s32[64]{0:T(128)} %param.15) | copy-start | bytes 772
  8.8 10.8 %all-to-all-start = ((bf16[4,384,64]{1,2,0:T(8,128)(2,1)}), bf16[4,384,64]{1,2,0:T(8,128)(2,1)S(1)}, u32[]{:S(2)}, u32[]{:S(2)}) async-start(bf16[4,384,64]{1,2,0:T(8,128)(2,1)} %broadcast_in_dim.283), calls=%async_computation | async-start | bytes 393216 | tf_op jit(solution)/shard_map/all_to_all | solution.py:66
  20.1 27.7 %copy-start.19 = (f32[1,6,2,512]{3,2,1,0:T(2,128)S(1)}, f32[1,6,2,512]{3,2,1,0:T(2,128)}, u32[]{:S(2)}) copy-start(f32[1,6,2,512]{3,2,1,0:T(2,128)} %param.12) | copy-start | bytes 73732
  20.5 5.4 %collective-permute-start = (bf16[16,1024]{1,0:T(8,128)(2,1)S(1)}, bf16[16,1024]{1,0:T(8,128)(2,1)S(1)}, u32[]{:S(2)}, u32[]{:S(2)}) collective-permute-start(bf16[16,1024]{1,0:T(8,128)(2,1)S(1)} %get-tuple-element.39), channel_id=1, source_target_pairs={{0,1},{1,0},{2,3},{3,2},{4,5},{5,4},{6,7},{7,6},{8,9},{9,8},{10,11... | collective-permute-start | bytes 98312 | tf_op jit(solution)/shard_map/ppermute | solution.py:54
  21.3 5.4 %collective-permute-start.1 = (bf16[16,1024]{1,0:T(8,128)(2,1)S(1)}, bf16[16,1024]{1,0:T(8,128)(2,1)S(1)}, u32[]{:S(2)}, u32[]{:S(2)}) collective-permute-start(bf16[16,1024]{1,0:T(8,128)(2,1)S(1)} %get-tuple-element.38), channel_id=1, source_target_pairs={{0,2},{1,3},{2,0},{3,1},{4,6},{5,7},{6,4},{7,5},{8,10},{9,11},{10,... | collective-permute-start | bytes 98312 | tf_op jit(solution)/shard_map/ppermute | solution.py:54
  24.0 5.5 %collective-permute-start.2 = (bf16[16,1024]{1,0:T(8,128)(2,1)S(1)}, bf16[16,1024]{1,0:T(8,128)(2,1)S(1)}, u32[]{:S(2)}, u32[]{:S(2)}) collective-permute-start(bf16[16,1024]{1,0:T(8,128)(2,1)S(1)} %get-tuple-element.37), channel_id=1, source_target_pairs={{0,3},{1,2},{2,1},{3,0},{4,7},{5,6},{6,5},{7,4},{8,11},{9,10},{10,... | collective-permute-start | bytes 98312 | tf_op jit(solution)/shard_map/ppermute | solution.py:54
  29.7 1.4 collective-permute-start.3
  31.8 21.2 %all-to-all-start.1 = ((bf16[32,16,128]{2,1,0:T(8,128)(2,1)}), bf16[32,16,128]{2,1,0:T(8,128)(2,1)S(1)}, u32[]{:S(2)}, u32[]{:S(2)}) async-start(bf16[32,16,128]{2,1,0:T(8,128)(2,1)} %bitcast.22), calls=%async_computation.1 | async-start | bytes 262144 | tf_op jit(solution)/shard_map/all_to_all | solution.py:39
  53.8 14.3 %all-to-all-start.2 = ((bf16[32,16,128]{2,1,0:T(8,128)(2,1)}), bf16[32,16,128]{2,1,0:T(8,128)(2,1)S(1)}, u32[]{:S(2)}, u32[]{:S(2)}) async-start(bf16[32,16,128]{2,1,0:T(8,128)(2,1)} %broadcast_in_dim.291), calls=%async_computation.2 | async-start | bytes 262144 | tf_op jit(solution)/shard_map/all_to_all | solution.py:42
  68.1 1.3 collective-permute-start.4
  69.6 78.7 %copy-start.11 = (f32[4,16,128]{2,1,0:T(8,128)}, f32[4,16,128]{2,1,0:T(8,128)S(1)}, u32[]{:S(2)}) copy-start(f32[4,16,128]{2,1,0:T(8,128)S(1)} %get-tuple-element.18) | copy-start | bytes 98308
  69.6 6.0 %collective-permute-start.5 = (bf16[16,1024]{1,0:T(8,128)(2,1)S(1)}, bf16[16,1024]{1,0:T(8,128)(2,1)S(1)}, u32[]{:S(2)}, u32[]{:S(2)}) collective-permute-start(bf16[16,1024]{1,0:T(8,128)(2,1)S(1)} %bitcast.285), channel_id=1, source_target_pairs={{0,1},{1,0},{2,3},{3,2},{4,5},{5,4},{6,7},{7,6},{8,9},{9,8},{10,11... | collective-permute-start | bytes 98312 | tf_op jit(solution)/shard_map/ppermute | solution.py:54
  69.7 5.9 %collective-permute-start.6 = (bf16[16,1024]{1,0:T(8,128)(2,1)S(1)}, bf16[16,1024]{1,0:T(8,128)(2,1)S(1)}, u32[]{:S(2)}, u32[]{:S(2)}) collective-permute-start(bf16[16,1024]{1,0:T(8,128)(2,1)S(1)} %bitcast.286), channel_id=1, source_target_pairs={{0,2},{1,3},{2,0},{3,1},{4,6},{5,7},{6,4},{7,5},{8,10},{9,11},{10,... | collective-permute-start | bytes 98312 | tf_op jit(solution)/shard_map/ppermute | solution.py:54
  72.6 5.1 %collective-permute-start.7 = (bf16[16,1024]{1,0:T(8,128)(2,1)S(1)}, bf16[16,1024]{1,0:T(8,128)(2,1)S(1)}, u32[]{:S(2)}, u32[]{:S(2)}) collective-permute-start(bf16[16,1024]{1,0:T(8,128)(2,1)S(1)} %bitcast.287), channel_id=1, source_target_pairs={{0,3},{1,2},{2,1},{3,0},{4,7},{5,6},{6,5},{7,4},{8,11},{9,10},{10,... | collective-permute-start | bytes 98312 | tf_op jit(solution)/shard_map/ppermute | solution.py:54
  78.9 4.2 %copy-start.7 = (bf16[1,1024,384]{2,1,0:T(8,128)(2,1)S(1)}, bf16[1,1024,384]{2,1,0:T(8,128)(2,1)}, u32[]{:S(2)}) copy-start(bf16[1,1024,384]{2,1,0:T(8,128)(2,1)} %param.10) | copy-start | bytes 2359300
  84.5 2.2 copy-start.3
  86.7 61.5 %all-reduce.2.cloned.1.call-start = ((), (), s32[]{:S(2)}) async-start(), calls=%async_computation.15 | async-start | bytes 4194304 | tf_op jit(solution)/shard_map/psum | solution.py:111
  87.4 39.1 %copy-start.18 = (f32[8,2,4,128]{3,0,2,1:T(8,128)S(1)}, f32[8,2,4,128]{3,0,2,1:T(8,128)}, u32[]{:S(2)}) copy-start(f32[8,2,4,128]{3,0,2,1:T(8,128)} %get-tuple-element.20) | copy-start | bytes 98308
  88.3 4.8 %collective-permute-start.8 = (bf16[16,1024]{1,0:T(8,128)(2,1)S(1)}, bf16[16,1024]{1,0:T(8,128)(2,1)S(1)}, u32[]{:S(2)}, u32[]{:S(2)}) collective-permute-start(bf16[16,1024]{1,0:T(8,128)(2,1)S(1)} %get-tuple-element.35), channel_id=1, source_target_pairs={{0,1},{1,0},{2,3},{3,2},{4,5},{5,4},{6,7},{7,6},{8,9},{9,8},{10,11... | collective-permute-start | bytes 98312 | tf_op jit(solution)/shard_map/ppermute | solution.py:54
  88.4 5.6 %collective-permute-start.9 = (bf16[16,1024]{1,0:T(8,128)(2,1)S(1)}, bf16[16,1024]{1,0:T(8,128)(2,1)S(1)}, u32[]{:S(2)}, u32[]{:S(2)}) collective-permute-start(bf16[16,1024]{1,0:T(8,128)(2,1)S(1)} %get-tuple-element.34), channel_id=1, source_target_pairs={{0,2},{1,3},{2,0},{3,1},{4,6},{5,7},{6,4},{7,5},{8,10},{9,11},{10,... | collective-permute-start | bytes 98312 | tf_op jit(solution)/shard_map/ppermute | solution.py:54
  91.6 5.1 %collective-permute-start.10 = (bf16[16,1024]{1,0:T(8,128)(2,1)S(1)}, bf16[16,1024]{1,0:T(8,128)(2,1)S(1)}, u32[]{:S(2)}, u32[]{:S(2)}) collective-permute-start(bf16[16,1024]{1,0:T(8,128)(2,1)S(1)} %get-tuple-element.33), channel_id=1, source_target_pairs={{0,3},{1,2},{2,1},{3,0},{4,7},{5,6},{6,5},{7,4},{8,11},{9,10},{10,... | collective-permute-start | bytes 98312 | tf_op jit(solution)/shard_map/ppermute | solution.py:54
  96.9 1.4 collective-permute-start.11
  126.5 1.3 collective-permute-start.12
  128.0 20.2 %copy-start.12 = (f32[4,16,128]{2,1,0:T(8,128)}, f32[4,16,128]{2,1,0:T(8,128)S(1)}, u32[]{:S(2)}) copy-start(f32[4,16,128]{2,1,0:T(8,128)S(1)} %get-tuple-element.15) | copy-start | bytes 98308
  128.0 20.2 %copy-start.13 = (f32[4,16,128]{2,1,0:T(8,128)}, f32[4,16,128]{2,1,0:T(8,128)S(1)}, u32[]{:S(2)}) copy-start(f32[4,16,128]{2,1,0:T(8,128)S(1)} %get-tuple-element.16) | copy-start | bytes 98308
  150.2 38.5 %copy-start.2 = (bf16[1024,1024]{1,0:T(8,128)(2,1)S(1)}, bf16[1024,1024]{1,0:T(8,128)(2,1)}, u32[]{:S(2)}) copy-start(bf16[1024,1024]{1,0:T(8,128)(2,1)} %all-reduce.2.cloned.1.call-done) | copy-start | bytes 6291460
  150.4 1.4 collective-permute-start.13
  186.4 1.3 collective-permute-start.14
  188.7 33.2 %copy-start.8 = (f32[8,16,128]{2,1,0:T(8,128)}, f32[8,16,128]{2,1,0:T(8,128)S(1)}, u32[]{:S(2)}) copy-start(f32[8,16,128]{2,1,0:T(8,128)S(1)} %get-tuple-element.29) | copy-start | bytes 196612
  189.2 1.5 collective-permute-start.15
  220.4 1.3 collective-permute-start.16
  221.9 31.5 %copy-start.14 = (f32[4,16,128]{2,1,0:T(8,128)}, f32[4,16,128]{2,1,0:T(8,128)S(1)}, u32[]{:S(2)}) copy-start(f32[4,16,128]{2,1,0:T(8,128)S(1)} %get-tuple-element.11) | copy-start | bytes 98308
  222.4 1.4 collective-permute-start.17
  223.9 31.6 %copy-start.16 = (f32[4,16,128]{2,1,0:T(8,128)S(1)}, f32[4,16,128]{2,1,0:T(8,128)}, u32[]{:S(2)}) copy-start(f32[4,16,128]{2,1,0:T(8,128)} %copy-done.15) | copy-start | bytes 98308
  253.4 1.9 collective-permute-start.18
  256.4 31.8 %copy-start.17 = (f32[8,2,4,128]{3,0,2,1:T(8,128)S(1)}, f32[8,2,4,128]{3,0,2,1:T(8,128)}, u32[]{:S(2)}) copy-start(f32[8,2,4,128]{3,0,2,1:T(8,128)} %get-tuple-element.24) | copy-start | bytes 98308
  256.9 1.6 collective-permute-start.19
  288.2 1.3 collective-permute-start.20
  290.2 39.1 %copy-start.5 = (bf16[384,1024]{1,0:T(8,128)(2,1)S(1)}, bf16[384,1024]{1,0:T(8,128)(2,1)}, u32[]{:S(2)}) copy-start(bf16[384,1024]{1,0:T(8,128)(2,1)} %copy-done.4) | copy-start | bytes 2359300
  290.2 1.4 collective-permute-start.21
  291.7 29.4 %copy-start.10 = (f32[4,16,128]{2,1,0:T(8,128)S(1)}, f32[4,16,128]{2,1,0:T(8,128)}, u32[]{:S(2)}) copy-start(f32[4,16,128]{2,1,0:T(8,128)} %copy-done.9) | copy-start | bytes 98308
  319.7 1.3 collective-permute-start.22
  321.2 4.9 %collective-permute-start.23 = (bf16[16,1024]{1,0:T(8,128)(2,1)S(1)}, bf16[16,1024]{1,0:T(8,128)(2,1)S(1)}, u32[]{:S(2)}, u32[]{:S(2)}) collective-permute-start(bf16[16,1024]{1,0:T(8,128)(2,1)S(1)} %copy_bitcast_fusion), channel_id=1, source_target_pairs={{0,1},{1,0},{2,3},{3,2},{4,5},{5,4},{6,7},{7,6},{8,9},{9,8},{10,11... | collective-permute-start | bytes 98312 | tf_op jit(solution)/shard_map/ppermute | solution.py:54
  321.5 5.4 %collective-permute-start.24 = (bf16[16,1024]{1,0:T(8,128)(2,1)S(1)}, bf16[16,1024]{1,0:T(8,128)(2,1)S(1)}, u32[]{:S(2)}, u32[]{:S(2)}) collective-permute-start(bf16[16,1024]{1,0:T(8,128)(2,1)S(1)} %copy_bitcast_fusion), channel_id=1, source_target_pairs={{0,2},{1,3},{2,0},{3,1},{4,6},{5,7},{6,4},{7,5},{8,10},{9,11},{10,... | collective-permute-start | bytes 98312 | tf_op jit(solution)/shard_map/ppermute | solution.py:54
  323.5 5.1 %collective-permute-start.25 = (bf16[16,1024]{1,0:T(8,128)(2,1)S(1)}, bf16[16,1024]{1,0:T(8,128)(2,1)S(1)}, u32[]{:S(2)}, u32[]{:S(2)}) collective-permute-start(bf16[16,1024]{1,0:T(8,128)(2,1)S(1)} %copy_bitcast_fusion), channel_id=1, source_target_pairs={{0,3},{1,2},{2,1},{3,0},{4,7},{5,6},{6,5},{7,4},{8,11},{9,10},{10,... | collective-permute-start | bytes 98312 | tf_op jit(solution)/shard_map/ppermute | solution.py:54
  (3 other events, 4.9 us)
Sparse Core Ops, SparseCore 0:
  9.2 45.0 all-gather.2
  89.9 58.2 all-reduce.1
